TPU v7x, 32 devices: a whole 2x2x4 slice. The times are simulated.
32 devices in a mesh: seq: 8 (over z, x), grp: 4 (over y, core).
Axes of the slice: x: 2, y: 2, z: 4, core: 2. Of those that a mesh axis runs over, the one named last changes fastest.
Arguments:
- xbc_in: bfloat16 [4096, 4352], P(('grp', 'seq')), parts along dimension 0, may hold values from -6 to 6
- conv_weight: float32 [4, 4352], replicated, may hold values from -3 to 3
- conv_bias: float32 [4352], replicated, may hold values from -2 to 2
- dt_raw: float32 [4096, 64], P(('grp', 'seq')), parts along dimension 0, may hold values from -6 to 358.4
- decay_rate: float32 [64], replicated, may hold values from 0.0001953125 to 0.08
- skip: float32 [64], replicated, may hold values from 0.5 to 2
- level_table: float32 [8, 12, 64], replicated, may hold values from 0.05 to 0.5
- group_class: int32 [64], P(('grp', 'seq')), parts along dimension 0, may hold values from 0 to 7
- cotangent: bfloat16 [4096, 4096], P(('grp', 'seq')), parts along dimension 0, may hold values from -6 to 6
Outputs:
- ssm_out: bfloat16 [4096, 4096], P(('grp', 'seq')), parts along dimension 0
- grad_c_in: float32 [4096, 128], P(('grp', 'seq')), parts along dimension 0
- level_update: float32 [32, 12, 64], P('grp'), parts along dimension 0
There are 4 independent parts, one for each index of `grp`. A program takes and returns all parts, laid end to end along the dimension named above; an argument that names none is the same for every part. Nothing has to cross between parts.
All inputs are finite; a program needn't handle non-finite values.
Results may differ from a plain program's by a relative error of at most 0.0059.
Values may be sent and summed in bfloat16 or wider, within the bound.
No kernel may reach another device: no remote copies, remote signals or barrier semaphores. Data moves between devices by JAX's collectives and lax.ppermute only.
A program may use at most 128 MiB of HBM per device.

v0:
```python
import math

import jax
import jax.numpy as jnp
from jax import lax
from jax.sharding import PartitionSpec as P


def shifted(value, axis, steps):
    count = lax.axis_size(axis)
    leading, last = (max(0, -steps), min(count, count - steps))
    return lax.ppermute(value, axis, [(source, source + steps) for source in range(leading, last)])


def from_partner(value, axis, distance):
    mask = 2**distance
    pairs = [(source, source ^ mask) for source in range(lax.axis_size(axis))]
    return lax.ppermute(value, axis, pairs)


def contract(form, left, right):
    return jnp.einsum(form, left, right, preferred_element_type=jnp.float32)


def exact(form, left, right):
    return jnp.einsum(form, left, right, precision=lax.Precision.HIGHEST)


def conv_forward(window, conv_weight, conv_bias, length):
    result = jnp.zeros((length, window.shape[1]), jnp.float32) + conv_bias[None, :]
    for offset in range(conv_weight.shape[0]):
        result = (
            result
            + window[offset : offset + length].astype(jnp.float32) * conv_weight[offset][None, :]
        )
    return result


def split_act(preact, heads, head_dim, state_dim):
    length = preact.shape[0]
    inner = heads * head_dim
    x_act = jax.nn.silu(preact[:, :inner]).astype(jnp.bfloat16).reshape(length, heads, head_dim)
    b_key = preact[:, inner : inner + state_dim].astype(jnp.bfloat16)
    c_query = preact[:, inner + state_dim :].astype(jnp.bfloat16)
    return (x_act, b_key, c_query)


def local_group(x_part, b_part, c_part, decay_part, grad_part, weight_zero):
    length = x_part.shape[0]
    state_dim = b_part.shape[1]
    cumul = jnp.cumsum(decay_part, axis=0)
    scores = jnp.dot(c_part, b_part.T, preferred_element_type=jnp.float32)
    causal = (jnp.arange(length)[:, None] >= jnp.arange(length)[None, :])[None]
    across = jnp.transpose(cumul)
    spread = across[:, :, None] - across[:, None, :]
    fading = jnp.where(causal, jnp.exp(jnp.where(causal, spread, 0.0)), 0.0)
    basic = fading * scores[None] / state_dim
    intra = (weight_zero[:, None, None] * basic).astype(jnp.bfloat16)
    y_inner = contract("hts,shp->thp", intra, x_part)
    x_faded = (x_part * jnp.exp(cumul[-1][None, :] - cumul)[:, :, None]).astype(jnp.bfloat16)
    group_state = contract("sn,shp->hnp", b_part, x_faded)
    products = contract("thp,shp->hts", grad_part, x_part)
    grad_weight = (
        jnp.sum(weight_zero[:, None, None] * fading * products, axis=0) / state_dim
    ).astype(jnp.bfloat16)
    grad_inner = jnp.dot(grad_weight, b_part, preferred_element_type=jnp.float32)
    level_zero = jnp.sum(basic * products, axis=(1, 2))
    return (y_inner, group_state, cumul, grad_inner, level_zero)


def combine(block, block_decay, other, other_decay, leading, upper):
    grown = upper[..., None, None]
    found = grown * jnp.exp(leading)[..., None, None] * other
    joined = grown * (other * jnp.exp(block_decay)[..., None, None] + block) + (1.0 - grown) * (
        block * jnp.exp(other_decay)[..., None, None] + other
    )
    return (joined, block_decay + other_decay, leading + upper * other_decay, found)


def local(
    xbc_in, conv_weight, conv_bias, dt_raw, decay_rate, skip, level_table, group_class, cotangent
):
    length = xbc_in.shape[0]
    taps = conv_weight.shape[0]
    heads = dt_raw.shape[1]
    inner = cotangent.shape[1]
    head_dim = inner // heads
    state_dim = (xbc_in.shape[1] - inner) // 2
    classes = level_table.shape[0]
    levels = level_table.shape[1]
    groups = group_class.shape[0]
    group_len = length // groups
    edge_part = shifted(xbc_in[length - taps + 1 :], "seq", 1)
    window = jnp.concatenate([edge_part, xbc_in], axis=0)
    preact = conv_forward(window, conv_weight, conv_bias, length)
    x_act, b_key, c_query = split_act(preact, heads, head_dim, state_dim)
    log_decay = -decay_rate[None, :] * jax.nn.softplus(dt_raw)
    grad_out = cotangent.reshape(length, heads, head_dim)
    picked = (group_class[:, None] == jnp.arange(classes, dtype=jnp.int32)[None, :]).astype(
        jnp.float32
    )
    weight_rows = exact("gk,klh->glh", picked, level_table)
    x_groups = x_act.reshape(groups, group_len, heads, head_dim)
    c_groups = c_query.reshape(groups, group_len, state_dim)
    grad_groups = grad_out.reshape(groups, group_len, heads, head_dim)
    y_inner, states, cumuls, grad_inner, level_zero = jax.vmap(local_group)(
        x_groups,
        b_key.reshape(groups, group_len, state_dim),
        c_groups,
        log_decay.reshape(groups, group_len, heads),
        grad_groups,
        weight_rows[:, 0],
    )
    totals = cumuls[:, -1]
    dev_decay = jnp.sum(totals, axis=0)
    later = dev_decay[None, :] - jnp.cumsum(totals, axis=0)
    dev_state = exact("gh,ghnp->hnp", jnp.exp(later), states)
    devices = lax.axis_size("seq")
    depth = devices.bit_length() - 1
    myself = lax.axis_index("seq")
    block, block_decay = (dev_state, dev_decay)
    leading = jnp.zeros_like(dev_decay)
    found_all = []
    for bit_pos in range(depth):
        other, other_decay = from_partner((block, block_decay), "seq", bit_pos)
        upper = jnp.zeros_like(dev_decay) + (jnp.right_shift(myself, bit_pos) & 1).astype(
            jnp.float32
        )
        block, block_decay, leading, found = combine(
            block, block_decay, other, other_decay, leading, upper
        )
        found_all.append(found)
    cross = jnp.stack(found_all, axis=0)
    low_levels = groups.bit_length() - 1
    local_ids = jnp.arange(groups, dtype=jnp.int32)
    differ = jnp.bitwise_xor(local_ids[:, None], local_ids[None, :])
    lower = local_ids[:, None] > local_ids[None, :]
    slot_of = jnp.zeros((groups, groups), jnp.int32)
    onehot = (
        (slot_of[:, :, None] == jnp.arange(low_levels, dtype=jnp.int32)[None, None, :])
        & lower[:, :, None]
    ).astype(jnp.float32)
    before = jnp.cumsum(totals, axis=0) - totals
    gap = before[:, None, :] - before[None, :, :] - totals[None, :, :]
    below = lower[:, :, None]
    fade_pairs = jnp.where(below, jnp.exp(jnp.where(below, gap, 0.0)), 0.0)
    local_weight = exact("cds,csh->cdh", onehot, weight_rows[:, 1 : 1 + low_levels]) * fade_pairs
    lead_fade = jnp.exp(before)
    cross_weight = weight_rows[:, 1 + low_levels : 1 + low_levels + depth] * lead_fade[:, None, :]
    mixed = (
        exact("cdh,dhnp->chnp", local_weight, states) + exact("clh,lhnp->chnp", cross_weight, cross)
    ).astype(jnp.bfloat16)
    scaled = jnp.exp(cumuls) / state_dim
    query_faded = (c_groups[:, :, None, :] * scaled[:, :, :, None]).astype(jnp.bfloat16)
    y_cross = contract("cthn,chnp->cthp", query_faded, mixed)
    backed = contract("chnp,cthp->cthn", mixed, grad_groups)
    grad_cross = jnp.sum(backed * scaled[:, :, :, None], axis=2)
    gram = contract("cthn,cthp->chnp", query_faded, grad_groups)
    inner_pairs = exact("dhnp,chnp->cdh", states, gram)
    level_local = exact("cds,cdh->csh", onehot, fade_pairs * inner_pairs)
    level_cross = lead_fade[:, None, :] * exact("lhnp,chnp->clh", cross, gram)
    level_rest = jnp.concatenate(
        [
            level_local,
            level_cross,
            jnp.zeros((groups, levels - 1 - low_levels - depth, heads), jnp.float32),
        ],
        axis=1,
    )
    grads = exact("ck,clh->klh", picked, level_rest)
    ssm_out = (
        (y_inner + y_cross + skip[None, None, :, None] * x_groups)
        .astype(jnp.bfloat16)
        .reshape(length, inner)
    )
    grad_query = (grad_inner + grad_cross).reshape(length, state_dim)
    after_rows = shifted(grad_query[: taps - 1], "seq", -1)
    extended = jnp.concatenate([grad_query, after_rows], axis=0)
    query_taps = conv_weight[:, inner + state_dim :]
    grad_c_in = jnp.zeros((length, state_dim), jnp.float32)
    for offset in range(taps):
        lagged = taps - 1 - offset
        grad_c_in = grad_c_in + query_taps[offset][None, :] * extended[lagged : lagged + length]
    grad_first = exact("gk,gh->kh", picked, level_zero)
    local_grads = jnp.concatenate([grad_first[:, None, :], grads], axis=1)
    summed = lax.psum(local_grads, "seq")
    level_update = level_table + summed / math.sqrt(length * devices)
    return (ssm_out, grad_c_in, level_update)


def solution(mesh):
    placed = (
        P(("grp", "seq"), None),
        P(),
        P(),
        P(("grp", "seq"), None),
        P(),
        P(),
        P(),
        P(("grp", "seq")),
        P(("grp", "seq"), None),
    )
    return jax.shard_map(
        local,
        mesh=mesh,
        in_specs=placed,
        out_specs=(P(("grp", "seq"), None), P(("grp", "seq"), None), P("grp", None, None)),
        check_vma=False,
    )
```

profile of v0, /device:TPU:0, one launch (start us, length us, event | category | flops | bytes accessed | tf_op | source)
XLA Modules:
  0.0 356.1 jit_solution(6967669314118187644)
XLA Ops:
  1.5 4.8 %collective-permute-start = (bf16[3,4352]{1,0:T(4,128)(2,1)S(1)}, bf16[3,4352]{1,0:T(4,128)(2,1)S(1)}, u32[]{:S(2)}, u32[]{:S(2)}) collective-permute-start(bf16[3,4352]{1,0:T(4,128)(2,1)S(1)} %slice.77), channel_id=1, source_target_pairs={{0,4},{4,8},{8,12},{12,16},{16,20},{20,24},{24,28},{1,5},{5,9},{9,... | collective-permute-start | bytes 78344 | tf_op jit(solution)/shard_map/ppermute | solution.py:12
  9.6 4.4 %fusion.89 = (bf16[128,4352]{1,0:T(8,128)(2,1)}, f32[128,4352]{1,0:T(8,128)S(1)}) fusion(f32[4352]{0:T(1024)S(1)} %get-tuple-element.6, bf16[128,4352]{1,0:T(8,128)(2,1)} %param.9, f32[4352]{0:T(1024)S(1)} %get-tuple-element.7, bf16[3,4352]{1,0:T(4,128)(2,1)S(1)} %collective-permute-done, f32[4352]{0:T(1024)S(1)} %get-tuple-element.8, ...), kind=kLoop, calls=%fused_computation.134 | loop fusion | flops 12255232 | bytes 4569600 | tf_op jit(solution)/shard_map/convert.2
  14.5 2.3 reshape_reshape.6
  16.8 3.0 copy.63
  20.6 4.4 %fusion.8 = (f32[64,128,64]{1,2,0:T(8,128)S(1)}, f32[2,64,64,128]{3,2,1,0:T(8,128)}) fusion(f32[64,2]{0,1:T(2,128)S(1)} %get-tuple-element.32, bf16[2,64,128,1]{2,1,3,0:T(8,128)(2,1)S(1)} %bitcast.113, bf16[2,64,64,64]{1,3,2,0:T(8,128)(2,1)} %copy.63, f32[2,64,64]{1,2,0:T(8,128)S(1)} %copy.66), kind=kOutput, calls=%fused_computation.15 | convolution fusion | flops 137363456 | bytes 7406080 | tf_op jit(solution)/shard_map/vmap(sn,shp->hnp)/dot_general | solution.py:22
  27.0 45.2 %collective-permute-done.2 = f32[64]{0:T(128)S(1)} collective-permute-done((f32[64]{0:T(128)S(1)}, f32[64]{0:T(128)S(1)}, u32[]{:S(2)}, u32[]{:S(2)}) %collective-permute-start.2) | collective-permute-done | bytes 288 | tf_op jit(solution)/shard_map/ppermute | solution.py:18
  75.8 4.3 %broadcast_multiply_fusion.2 = (f32[64,128,64]{1,2,0:T(8,128)}, f32[64,128,64]{1,2,0:T(8,128)}) fusion(f32[64,128,64]{1,2,0:T(8,128)} %collective-permute-done.1, f32[]{:T(128)S(6)} %convert_element_type.69, f32[64,128,64]{1,2,0:T(8,128)S(1)} %get-tuple-element.39, f32[64]{0:T(128)S(1)} %get-tuple-element.37, f32[]{:T(128)S(6)} %sub.93, ...), kind=kLoop, calls=%fused_computation.60 | loop fusion | flops 4194304 | bytes 8389128 | tf_op jit(solution)/shard_map/mul | solution.py:73
  81.8 2.3 reshape_reshape.7
  84.2 2.9 copy.84
  88.8 36.6 %collective-permute-done.3 = f32[64,128,64]{1,2,0:T(8,128)} collective-permute-done((f32[64,128,64]{1,2,0:T(8,128)}, f32[64,128,64]{1,2,0:T(8,128)}, u32[]{:S(2)}, u32[]{:S(2)}) %collective-permute-start.3) | collective-permute-done | bytes 2097184 | tf_op jit(solution)/shard_map/ppermute | solution.py:18
  125.4 5.1 %broadcast_multiply_fusion.1 = (f32[64,128,64]{1,2,0:T(8,128)}, f32[64,128,64]{1,2,0:T(8,128)}) fusion(f32[64,128,64]{1,2,0:T(8,128)} %collective-permute-done.3, f32[64]{0:T(128)S(1)} %get-tuple-element.34, f32[64,128,64]{1,2,0:T(8,128)} %get-tuple-element.16, f32[64]{0:T(128)S(1)} %get-tuple-element.36, f32[]{:T(128)S(6)} %sub.94, ...), kind=kLoop, calls=%fused_computation.59 | loop fusion | flops 4194304 | bytes 8389384 | tf_op jit(solution)/shard_map/mul | solution.py:73
  130.5 2.5 collective-permute-start.5
  133.0 3.7 %fusion.7 = (f32[2,64]{1,0:T(2,128)S(1)}, f32[2,64,64]{1,2,0:T(8,128)S(1)}) fusion(f32[2,64,64]{1,2,0:T(8,128)S(1)} %fusion.91, f32[2,64,64]{2,1,0:T(8,128)S(1)} %copy.60, pred[64,64]{0,1:T(8,128)(4,1)S(1)} %iota_compare_fusion, f32[2,64]{1,0:T(2,128)S(1)} %get-tuple-element.28, bf16[2,64,64,64]{1,3,2,0:T(8,128)(2,1)S(1)} %copy-done, ...), kind=kOutput, calls=%fused_computation.13 | convolution fusion | flops 72343424 | bytes 2200576 | tf_op jit(solution)/shard_map/vmap(thp,shp->hts)/dot_general | solution.py:22
  137.1 2.9 fusion.17
  139.9 55.9 %fusion.44 = f32[2,2,64]{1,0,2:T(2,128)S(1)} fusion(f32[2,64,128,64]{2,3,1,0:T(8,128)S(1)} %bitcast.104, f32[2,64,128,64]{2,3,1,0:T(8,128)S(1)} %fusion.17, f32[2,64]{0,1:T(8,128)S(1)} %copy.71, f32[2,64]{0,1:T(8,128)S(1)} %copy.70, f32[2,64]{0,1:T(8,128)S(1)} %copy.69, pred[2,2]{1,0:T(4,128)(4,1)S(1)} %get-tuple-element.41), kind=kOutput, calls=%fused_computation.57 | convolution fusion | flops 25167104 | bytes 8391172 | tf_op jit(solution)/shard_map/dhnp,chnp->cdh/dot_general | solution.py:26
  196.0 17.9 %fusion.14 = f32[64,128,64,2]{1,3,2,0:T(2,128)} fusion(f32[2,64,128,64]{2,3,1,0:T(8,128)S(1)} %bitcast.105, f32[2,64]{0,1:T(8,128)S(1)} %copy.67, f32[2,2]{1,0:T(2,128)S(1)} %get-tuple-element.42, pred[2,2]{1,0:T(4,128)(4,1)S(1)} %get-tuple-element.41, f32[2,64]{0,1:T(8,128)S(1)} %copy.71, f32[2,64]{0,1:T(8,128)S(1)} %copy.70, f32[2,64]{0,1:T(8,128)S(1)} %copy.69), kind=kOutput, calls=%fused_computation.25 | convolution fusion | flops 25167360 | bytes 8390676 | tf_op jit(solution)/shard_map/cdh,dhnp->chnp/dot_general | solution.py:26
  213.9 6.9 %collective-permute-done.5 = f32[64,128,64]{1,2,0:T(8,128)} collective-permute-done((f32[64,128,64]{1,2,0:T(8,128)}, f32[64,128,64]{1,2,0:T(8,128)}, u32[]{:S(2)}, u32[]{:S(2)}) %collective-permute-start.5) | collective-permute-done | bytes 2097184 | tf_op jit(solution)/shard_map/ppermute | solution.py:18
  224.1 51.6 %fusion.39 = f32[64,2,3]{2,1,0:T(2,128)S(1)} fusion(f32[1,64,128,64]{2,0,3,1:T(1,128)S(1)} %bitcast.110, f32[1,64,128,64]{2,0,3,1:T(1,128)S(1)} %bitcast.109, f32[1,64,128,64]{2,0,3,1:T(1,128)S(1)} %bitcast.107, f32[2,64,128,64]{2,3,1,0:T(8,128)S(1)} %fusion.17), kind=kOutput, calls=%fused_computation.51 | convolution fusion | flops 40894464 | bytes 10487296 | tf_op jit(solution)/shard_map/lhnp,chnp->clh/dot_general | solution.py:26
  275.9 23.9 %fusion.16 = bf16[2,64,128,64]{2,0,3,1:T(2,128)(2,1)S(1)} fusion(f32[64,128,64,2]{1,3,2,0:T(2,128)} %fusion.14, f32[2,3,64,1]{1,0,3,2:T(2,128)S(1)} %copy.98, f32[1,64,128,64]{2,0,3,1:T(1,128)} %bitcast.111, f32[1,64,128,64]{2,0,3,1:T(1,128)} %bitcast.108, f32[1,64,128,64]{2,0,3,1:T(1,128)} %bitcast.106), kind=kOutput, calls=%fused_computation.27 | convolution fusion | flops 42991616 | bytes 12584448 | tf_op jit(solution)/shard_map/clh,lhnp->chnp/dot_general | solution.py:26
  301.8 3.4 fusion.18
  305.6 36.6 %psum.7 = f32[8,12,64]{2,0,1:T(8,128)S(1)} all-reduce(f32[8,12,64]{2,0,1:T(8,128)S(1)} %pad_maximum_fusion.11), channel_id=1, replica_groups=mesh['seq'=8,'grp'=4] {'seq'}, use_global_device_ids=true, to_apply=%region_6.7 | all-reduce | flops 6144 | bytes 49152 | tf_op jit(solution)/shard_map/psum | solution.py:186
  343.6 5.2 %fusion.4 = bf16[2,64,64,64]{1,3,2,0:T(8,128)(2,1)} fusion(bf16[2,64,64,64]{1,3,2,0:T(8,128)(2,1)S(1)} %copy-done, f32[2,64,64,64]{3,2,1,0:T(8,128)} %fusion.18, f32[64]{0:T(128)S(1)} %copy-done.10, f32[2,64]{1,0:T(2,128)S(1)} %broadcast_multiply_fusion.3, f32[2,64,64]{1,2,0:T(8,128)S(1)} %fusion.91, f32[2,64,64]{2,1,0:T(8,128)S(1)} %copy.60, ...), kind=kOutput, calls=%fused_computation.7 | convolution fusion | flops 72876032 | bytes 4264704 | tf_op jit(solution)/shard_map/vmap(hts,shp->thp)/dot_general | solution.py:22
  349.4 3.3 copy.78
  352.8 2.5 reshape.98
  (78 shorter events, 23.4 us)
Async XLA Ops:
  1.5 8.0 %collective-permute-start = (bf16[3,4352]{1,0:T(4,128)(2,1)S(1)}, bf16[3,4352]{1,0:T(4,128)(2,1)S(1)}, u32[]{:S(2)}, u32[]{:S(2)}) collective-permute-start(bf16[3,4352]{1,0:T(4,128)(2,1)S(1)} %slice.77), channel_id=1, source_target_pairs={{0,4},{4,8},{8,12},{12,16},{16,20},{20,24},{24,28},{1,5},{5,9},{9,... | collective-permute-start | bytes 78344 | tf_op jit(solution)/shard_map/ppermute | solution.py:12
  25.0 50.8 %collective-permute-start.1 = (f32[64,128,64]{1,2,0:T(8,128)S(1)}, f32[64,128,64]{1,2,0:T(8,128)}, u32[]{:S(2)}, u32[]{:S(2)}) collective-permute-start(f32[64,128,64]{1,2,0:T(8,128)S(1)} %get-tuple-element.39), channel_id=1, source_target_pairs={{0,4},{4,0},{8,12},{12,8},{16,20},{20,16},{24,28},{28,24},{1,5},{5... | collective-permute-start | bytes 6291464 | tf_op jit(solution)/shard_map/ppermute | solution.py:18
  26.5 45.6 %collective-permute-start.2 = (f32[64]{0:T(128)S(1)}, f32[64]{0:T(128)S(1)}, u32[]{:S(2)}, u32[]{:S(2)}) collective-permute-start(f32[64]{0:T(128)S(1)} %get-tuple-element.25), channel_id=1, source_target_pairs={{0,4},{4,0},{8,12},{12,8},{16,20},{20,16},{24,28},{28,24},{1,5},{5... | collective-permute-start | bytes 776 | tf_op jit(solution)/shard_map/ppermute | solution.py:18
  72.2 3.5 collective-permute-start.4
  75.8 6.1 %copy-start.7 = (bf16[128,4096]{1,0:T(8,128)(2,1)S(1)}, bf16[128,4096]{1,0:T(8,128)(2,1)}, u32[]{:S(2)}) copy-start(bf16[128,4096]{1,0:T(8,128)(2,1)} %param.17) | copy-start | bytes 3145732
  80.1 45.3 %collective-permute-start.3 = (f32[64,128,64]{1,2,0:T(8,128)}, f32[64,128,64]{1,2,0:T(8,128)}, u32[]{:S(2)}, u32[]{:S(2)}) collective-permute-start(f32[64,128,64]{1,2,0:T(8,128)} %get-tuple-element.16), channel_id=1, source_target_pairs={{0,8},{4,12},{8,0},{12,4},{16,24},{20,28},{24,16},{28,20},{1,9},{5... | collective-permute-start | bytes 6291464 | tf_op jit(solution)/shard_map/ppermute | solution.py:18
  84.1 3.2 copy-start.8
  84.2 3.2 copy-start.9
  125.4 7.5 %copy-start = (bf16[2,64,64,64]{1,3,2,0:T(8,128)(2,1)S(1)}, bf16[2,64,64,64]{1,3,2,0:T(8,128)(2,1)}, u32[]{:S(2)}) copy-start(bf16[2,64,64,64]{1,3,2,0:T(8,128)(2,1)} %copy.63) | copy-start | bytes 3145732
  125.4 7.5 %copy-start.1 = (bf16[2,64,64,64]{1,3,2,0:T(8,128)(2,1)S(1)}, bf16[2,64,64,64]{1,3,2,0:T(8,128)(2,1)}, u32[]{:S(2)}) copy-start(bf16[2,64,64,64]{1,3,2,0:T(8,128)(2,1)} %copy.84) | copy-start | bytes 3145732
  130.5 90.3 %collective-permute-start.5 = (f32[64,128,64]{1,2,0:T(8,128)}, f32[64,128,64]{1,2,0:T(8,128)}, u32[]{:S(2)}, u32[]{:S(2)}) collective-permute-start(f32[64,128,64]{1,2,0:T(8,128)} %get-tuple-element.18), channel_id=1, source_target_pairs={{0,16},{4,20},{8,24},{12,28},{16,0},{20,4},{24,8},{28,12},{1,17},{... | collective-permute-start | bytes 6291464 | tf_op jit(solution)/shard_map/ppermute | solution.py:18
  137.0 2.9 copy-start.3
  220.7 3.3 copy-start.4
  220.7 3.3 copy-start.5
  222.7 1.4 copy-start.6
  275.9 23.9 %copy-start.2 = (bf16[2,64,64,64]{1,3,2,0:T(8,128)(2,1)S(1)}, bf16[2,64,64,64]{1,3,2,0:T(8,128)(2,1)}, u32[]{:S(2)}) copy-start(bf16[2,64,64,64]{1,3,2,0:T(8,128)(2,1)} %copy.84) | copy-start | bytes 3145732
  301.8 41.7 %copy-start.10 = (f32[64]{0:T(128)S(1)}, f32[64]{0:T(128)}, u32[]{:S(2)}) copy-start(f32[64]{0:T(128)} %param.14) | copy-start | bytes 772
  342.3 13.0 %collective-permute-start.6 = (f32[3,128]{1,0:T(4,128)S(1)}, f32[3,128]{1,0:T(4,128)S(1)}, u32[]{:S(2)}, u32[]{:S(2)}) collective-permute-start(f32[3,128]{1,0:T(4,128)S(1)} %slice.111), channel_id=1, source_target_pairs={{4,0},{8,4},{12,8},{16,12},{20,16},{24,20},{28,24},{5,1},{9,5},{13... | collective-permute-start | bytes 4616 | tf_op jit(solution)/shard_map/ppermute | solution.py:12
where the time goes:
time: 363 us; the launch traced here: 356 us
  matrix products  172 us (47%)
  waiting for transfers between devices  90.6 us (25%)
  blocking collectives  36.6 us (10%)
  local copies, waits for them, and re-layouts  22.6 us (6%)
  other arithmetic  19.3 us (5%)
  starting transfers between devices  13.8 us (4%)
    dot_general x8, matrix products, exact(): return jnp.einsum(form, left, right, precision=lax.Precision.HIGHEST)  150 us
    ppermute x5, waiting for transfers between devices, from_partner(): return lax.ppermute(value, axis, pairs)  90.6 us
    psum x1, blocking collectives, local(): summed = lax.psum(local_grads, 'seq')  36.6 us
    dot_general x6, matrix products, contract(): return jnp.einsum(form, left, right, preferred_element_type=jnp.float32)  21.7 us
    mul x4, other arithmetic, combine(): found = grown * jnp.exp(leading)[..., None, None] * other  11.3 us
    ppermute x5, starting transfers between devices, from_partner(): return lax.ppermute(value, axis, pairs)  7.65 us
  transfers between devices with their start and end apart: 7, of which 4 were waited for; matrix products, arithmetic and copies ran while one was open for 29% of the time, Pallas kernels for 0%

commit v1 on v0

--- a/solution.py
+++ b/solution.py
@@ -16,6 +16,19 @@
     mask = 2**distance
     pairs = [(source, source ^ mask) for source in range(lax.axis_size(axis))]
     return lax.ppermute(value, axis, pairs)
+
+
+def upward(value, axis, distance):
+    mask = 2**distance
+    count = lax.axis_size(axis)
+    pairs = [(source, source | mask) for source in range(count) if not source & mask]
+    return lax.ppermute(value, axis, pairs)
+
+
+def all_sum(value, axis):
+    for distance in range(lax.axis_size(axis).bit_length() - 1):
+        value = value + from_partner(value, axis, distance)
+    return value
 
 
 def contract(form, left, right):
@@ -114,7 +127,7 @@
     totals = cumuls[:, -1]
     dev_decay = jnp.sum(totals, axis=0)
     later = dev_decay[None, :] - jnp.cumsum(totals, axis=0)
-    dev_state = exact("gh,ghnp->hnp", jnp.exp(later), states)
+    dev_state = jnp.sum(jnp.exp(later)[:, :, None, None] * states, axis=0)
     devices = lax.axis_size("seq")
     depth = devices.bit_length() - 1
     myself = lax.axis_index("seq")
@@ -122,7 +135,12 @@
     leading = jnp.zeros_like(dev_decay)
     found_all = []
     for bit_pos in range(depth):
-        other, other_decay = from_partner((block, block_decay), "seq", bit_pos)
+        if bit_pos == depth - 1:
+            sent = upward(block.astype(jnp.bfloat16), "seq", bit_pos)
+            other, other_decay = (sent.astype(jnp.float32), jnp.zeros_like(block_decay))
+        else:
+            sent, other_decay = from_partner((block.astype(jnp.bfloat16), block_decay), "seq", bit_pos)
+            other = sent.astype(jnp.float32)
         upper = jnp.zeros_like(dev_decay) + (jnp.right_shift(myself, bit_pos) & 1).astype(
             jnp.float32
         )
@@ -147,18 +165,18 @@
     local_weight = exact("cds,csh->cdh", onehot, weight_rows[:, 1 : 1 + low_levels]) * fade_pairs
     lead_fade = jnp.exp(before)
     cross_weight = weight_rows[:, 1 + low_levels : 1 + low_levels + depth] * lead_fade[:, None, :]
-    mixed = (
-        exact("cdh,dhnp->chnp", local_weight, states) + exact("clh,lhnp->chnp", cross_weight, cross)
-    ).astype(jnp.bfloat16)
+    terms = [local_weight[:, d, :, None, None] * states[d][None] for d in range(groups)]
+    terms += [cross_weight[:, l, :, None, None] * cross[l][None] for l in range(depth)]
+    mixed = sum(terms[1:], terms[0]).astype(jnp.bfloat16)
     scaled = jnp.exp(cumuls) / state_dim
     query_faded = (c_groups[:, :, None, :] * scaled[:, :, :, None]).astype(jnp.bfloat16)
     y_cross = contract("cthn,chnp->cthp", query_faded, mixed)
     backed = contract("chnp,cthp->cthn", mixed, grad_groups)
     grad_cross = jnp.sum(backed * scaled[:, :, :, None], axis=2)
     gram = contract("cthn,cthp->chnp", query_faded, grad_groups)
-    inner_pairs = exact("dhnp,chnp->cdh", states, gram)
+    inner_pairs = jnp.sum(states[None] * gram[:, None], axis=(3, 4))
     level_local = exact("cds,cdh->csh", onehot, fade_pairs * inner_pairs)
-    level_cross = lead_fade[:, None, :] * exact("lhnp,chnp->clh", cross, gram)
+    level_cross = lead_fade[:, None, :] * jnp.sum(cross[None] * gram[:, None], axis=(3, 4))
     level_rest = jnp.concatenate(
         [
             level_local,
@@ -183,7 +201,7 @@
         grad_c_in = grad_c_in + query_taps[offset][None, :] * extended[lagged : lagged + length]
     grad_first = exact("gk,gh->kh", picked, level_zero)
     local_grads = jnp.concatenate([grad_first[:, None, :], grads], axis=1)
-    summed = lax.psum(local_grads, "seq")
+    summed = all_sum(local_grads, "seq")
     level_update = level_table + summed / math.sqrt(length * devices)
     return (ssm_out, grad_c_in, level_update)
 

time: 363 us -> 165 us (0.45); the launches traced: 356 us -> 164 us
  matrix products: 172 us -> 23.2 us
  waiting for transfers between devices: 90.6 us -> 39.4 us
  blocking collectives: 36.6 us -> 0 us
  starting transfers between devices: 13.8 us -> 44.7 us
  other arithmetic: 19.3 us -> 27 us
  local copies, waits for them, and re-layouts: 22.6 us -> 28.8 us
    dot_general x8 -> x4, matrix products: 150 us -> 2.44 us  [exact(): return jnp.einsum(form, left, right, precision=lax.Precision.HIGHEST)]
    ppermute x5 -> x7, waiting for transfers between devices: 90.6 us -> 25.7 us  [from_partner(): return lax.ppermute(value, axis, pairs)]
    psum x1 -> x0, blocking collectives: 36.6 us -> none  [local(): summed = lax.psum(local_grads, 'seq')]
    ppermute x5 -> x7, starting transfers between devices: 7.65 us -> 33.9 us  [from_partner(): return lax.ppermute(value, axis, pairs)]
    ppermute x0 -> x1, waiting for transfers between devices: none -> 13.6 us  [upward(): return lax.ppermute(value, axis, pairs)]
    mul x4 -> x1, other arithmetic: 11.3 us -> 0.59 us  [combine(): found = grown * jnp.exp(leading)[..., None, None] * other]
    convert_element_type x0 -> x3, other arithmetic: none -> 7.81 us  [the longest x1 4.99 us: local(): mixed = sum(terms[1:], terms[0]).astype(jnp.bfloat16)]
    another operation x1 -> x4, other arithmetic: 4.42 us -> 10.9 us  [the longest x3 6.49 us: local(): cross = jnp.stack(found_all, axis=0)]
  transfers between devices with their start and end apart: 7 -> 10, of which waited for: 4 -> 5; matrix products, arithmetic and copies ran while one was open for 29% -> 41% of each run, Pallas kernels for 0% -> 0%
where the time goes in v1:
time: 165 us; the launch traced here: 164 us
  starting transfers between devices  44.7 us (27%)
  waiting for transfers between devices  39.4 us (24%)
  local copies, waits for them, and re-layouts  28.8 us (17%)
  other arithmetic  27 us (16%)
  matrix products  23.2 us (14%)
    ppermute x7, starting transfers between devices, from_partner(): return lax.ppermute(value, axis, pairs)  33.9 us
    ppermute x7, waiting for transfers between devices, from_partner(): return lax.ppermute(value, axis, pairs)  25.7 us
    dot_general x6, matrix products, contract(): return jnp.einsum(form, left, right, preferred_element_type=jnp.float32)  20.5 us
    ppermute x1, waiting for transfers between devices, upward(): return lax.ppermute(value, axis, pairs)  13.6 us
    another operation x2, local copies, waits for them, and re-layouts, local(): grad_groups = grad_out.reshape(groups, group_len, heads, head_dim)  8.45 us
    another operation x3, other arithmetic, local(): cross = jnp.stack(found_all, axis=0)  6.49 us
    ppermute x2, starting transfers between devices, shifted(): lax.ppermute(value, axis, [(source, source + steps) for source in range(l...  6.14 us
    another operation x2, local copies, waits for them, and re-layouts, local(): x_groups = x_act.reshape(groups, group_len, heads, head_dim)  5.27 us
  transfers between devices with their start and end apart: 10, of which 5 were waited for; matrix products, arithmetic and copies ran while one was open for 41% of the time, Pallas kernels for 0%

profile of v1, /device:TPU:0, one launch (start us, length us, event | category | flops | bytes accessed | tf_op | source)
XLA Modules:
  0.0 164.1 jit_solution(8814437175388361331)
XLA Ops:
  1.5 4.8 %collective-permute-start = (bf16[3,4352]{1,0:T(4,128)(2,1)S(1)}, bf16[3,4352]{1,0:T(4,128)(2,1)S(1)}, u32[]{:S(2)}, u32[]{:S(2)}) collective-permute-start(bf16[3,4352]{1,0:T(4,128)(2,1)S(1)} %slice.98), channel_id=1, source_target_pairs={{0,4},{4,8},{8,12},{12,16},{16,20},{20,24},{24,28},{1,5},{5,9},{9,... | collective-permute-start | bytes 78344 | tf_op jit(solution)/shard_map/ppermute | solution.py:12
  14.8 4.4 %fusion.70 = (bf16[128,4352]{1,0:T(8,128)(2,1)}, f32[128,4352]{1,0:T(8,128)S(1)}) fusion(f32[4352]{0:T(1024)S(1)} %get-tuple-element.6, bf16[128,4352]{1,0:T(8,128)(2,1)} %param.9, f32[4352]{0:T(1024)S(1)} %get-tuple-element.7, bf16[3,4352]{1,0:T(4,128)(2,1)S(1)} %collective-permute-done, f32[4352]{0:T(1024)S(1)} %get-tuple-element.8, ...), kind=kLoop, calls=%fused_computation.136 | loop fusion | flops 12255232 | bytes 4569600 | tf_op jit(solution)/shard_map/convert.2
  19.8 2.3 %reshape_reshape.6 = bf16[2,64,64,64]{3,2,1,0:T(8,128)(2,1)S(1)} reshape(bf16[128,4096]{1,0:T(8,128)(2,1)S(1)} %multiply_convert_fusion.5) | data formatting | bytes 2097152 | tf_op jit(solution)/shard_map/reshape;reshape | solution.py:116
  22.0 3.0 %copy.71 = bf16[2,64,64,64]{1,3,2,0:T(8,128)(2,1)} copy(bf16[2,64,64,64]{3,2,1,0:T(8,128)(2,1)S(1)} %reshape_reshape.6) | data formatting | bytes 2097152 | tf_op jit(solution)/shard_map/reshape;reshape | solution.py:116
  25.8 4.4 %multiply_reduce_fusion.2 = (f32[64,128,64]{1,2,0:T(8,128)S(1)}, f32[2,64,128,64]{2,3,1,0:T(8,128)}) fusion(f32[2,64]{1,0:T(2,128)S(1)} %get-tuple-element.45, bf16[2,64,128,1]{2,1,3,0:T(8,128)(2,1)S(1)} %bitcast.90, bf16[2,64,64,64]{1,3,2,0:T(8,128)(2,1)} %copy.71, f32[2,64,64]{1,2,0:T(8,128)S(1)} %copy.75), kind=kOutput, calls=%fused_computation.16 | convolution fusion | flops 137363456 | bytes 7406080 | tf_op jit(solution)/shard_map/vmap(sn,shp->hnp)/dot_general | solution.py:35
  32.6 4.2 %reshape_reshape.7 = bf16[2,64,64,64]{3,2,1,0:T(8,128)(2,1)} reshape(bf16[128,4096]{1,0:T(8,128)(2,1)} %param.17) | data formatting | bytes 2097152 | tf_op jit(solution)/shard_map/reshape;reshape | solution.py:118
  36.8 4.2 %copy.82 = bf16[2,64,64,64]{1,3,2,0:T(8,128)(2,1)} copy(bf16[2,64,64,64]{3,2,1,0:T(8,128)(2,1)} %reshape_reshape.7) | data formatting | bytes 2097152 | tf_op jit(solution)/shard_map/reshape;reshape | solution.py:118
  45.4 10.6 %collective-permute-done.1 = bf16[64,128,64]{1,2,0:T(8,128)(2,1)S(1)} collective-permute-done((bf16[64,128,64]{1,2,0:T(8,128)(2,1)}, bf16[64,128,64]{1,2,0:T(8,128)(2,1)S(1)}, u32[]{:S(2)}, u32[]{:S(2)}) %collective-permute-start.1) | collective-permute-done | bytes 1048608 | tf_op jit(solution)/shard_map/ppermute | solution.py:18
  59.2 4.4 %fusion.5 = (f32[2,64]{1,0:T(2,128)}, f32[2,64,64]{1,2,0:T(8,128)}) fusion(f32[2,64,64]{1,2,0:T(8,128)S(1)} %fusion.74, f32[2,64,64]{2,1,0:T(8,128)S(1)} %copy.68, pred[64,64]{0,1:T(8,128)(4,1)S(1)} %iota_compare_fusion, f32[2,64]{1,0:T(2,128)S(1)} %copy-done.18, bf16[2,64,64,64]{1,3,2,0:T(8,128)(2,1)S(1)} %copy-done.1, ...), kind=kOutput, calls=%fused_computation.13 | convolution fusion | flops 72343424 | bytes 2200576 | tf_op jit(solution)/shard_map/vmap(thp,shp->hts)/dot_general | solution.py:35
  65.5 2.9 %fusion.7 = f32[2,64,128,64]{2,3,1,0:T(8,128)S(1)} fusion(bf16[2,64,64,64]{1,3,2,0:T(8,128)(2,1)} %copy.82, f32[2,64,64]{1,2,0:T(8,128)S(1)} %copy.76, f32[2,64,128]{2,1,0:T(8,128)S(1)} %convert_element_type.94), kind=kOutput, calls=%fused_computation.26 | convolution fusion | flops 136314880 | bytes 5341184 | tf_op jit(solution)/shard_map/cthn,cthp->chnp/dot_general | solution.py:35
  69.3 12.1 %collective-permute-done.3 = bf16[64,128,64]{1,2,0:T(8,128)(2,1)} collective-permute-done((bf16[64,128,64]{1,2,0:T(8,128)(2,1)}, bf16[64,128,64]{1,2,0:T(8,128)(2,1)}, u32[]{:S(2)}, u32[]{:S(2)}) %collective-permute-start.3) | collective-permute-done | bytes 1048608 | tf_op jit(solution)/shard_map/ppermute | solution.py:18
  81.4 3.9 %fusion.33 = (f32[1,64,128,64]{2,3,1,0:T(8,128)S(1)}, bf16[64,128,64]{1,2,0:T(8,128)(2,1)S(1)}, f32[64,128,64]{1,2,0:T(8,128)}, f32[1,64,128,64]{2,3,1,0:T(8,128)S(1)}, f32[64,128,64]{1,2,0:T(8,128)}) fusion(bf16[64,128,64]{1,2,0:T(8,128)(2,1)S(1)} %collective-permute-done.1, f32[]{:T(128)S(6)} %convert_element_type.84, f32[64]{0:T(128)S(1)} %copy-done.11, ...), kind=kLoop, calls=%fused_computation.62 | loop fusion | flops 9961472 | bytes 13632784 | tf_op jit(solution)/shard_map/stack | solution.py:151
  85.3 4.7 %collective-permute-start.5 = (bf16[64,128,64]{1,2,0:T(8,128)(2,1)S(1)}, bf16[64,128,64]{1,2,0:T(8,128)(2,1)S(1)}, u32[]{:S(2)}, u32[]{:S(2)}) collective-permute-start(bf16[64,128,64]{1,2,0:T(8,128)(2,1)S(1)} %get-tuple-element.24), channel_id=1, source_target_pairs={{0,16},{4,20},{8,24},{12,28},{1,17},{5,21},{9,25},{13,29},{2,18},{... | collective-permute-start | bytes 3145736 | tf_op jit(solution)/shard_map/ppermute | solution.py:25
  90.2 2.2 %slice_bitcast_fusion.1 = (f32[64,128,64]{1,2,0:T(8,128)}, f32[64,128,64]{1,2,0:T(8,128)}) fusion(f32[2,64,128,64]{2,3,1,0:T(8,128)S(1)} %copy-done), kind=kLoop, calls=%fused_computation.41 | loop fusion | bytes 8388608 | tf_op jit(solution)/shard_map/mul | solution.py:168
  92.6 3.6 %fusion.9 = f32[2,64,64,64]{3,2,1,0:T(8,128)} fusion(bf16[2,64,64,64]{1,3,2,0:T(8,128)(2,1)S(1)} %copy-done.2, f32[2,64]{1,0:T(2,128)S(1)} %copy-done.17, f32[2,64,64]{1,2,0:T(8,128)S(1)} %fusion.74, f32[2,64,64]{2,1,0:T(8,128)S(1)} %copy.68, pred[64,64]{0,1:T(8,128)(4,1)S(1)} %iota_compare_fusion), kind=kOutput, calls=%fused_computation.30 | convolution fusion | flops 70254592 | bytes 3215872 | tf_op jit(solution)/shard_map/vmap(hts,shp->thp)/dot_general | solution.py:35
  96.2 13.6 %collective-permute-done.5 = bf16[64,128,64]{1,2,0:T(8,128)(2,1)S(1)} collective-permute-done((bf16[64,128,64]{1,2,0:T(8,128)(2,1)S(1)}, bf16[64,128,64]{1,2,0:T(8,128)(2,1)S(1)}, u32[]{:S(2)}, u32[]{:S(2)}) %collective-permute-start.5) | collective-permute-done | bytes 1048608 | tf_op jit(solution)/shard_map/ppermute | solution.py:25
  115.3 5.0 %add_convert_fusion = bf16[2,64,128,64]{2,3,1,0:T(8,128)(2,1)S(1)} fusion(f32[64,128,64]{1,2,0:T(8,128)} %get-tuple-element.22, f32[2,64]{1,0:T(2,128)S(1)} %get-tuple-element.38, f32[64,128,64]{1,2,0:T(8,128)} %get-tuple-element.25, f32[2,64]{1,0:T(2,128)S(1)} %get-tuple-element.39, f32[64,128,64]{1,2,0:T(8,128)} %get-tuple-element.27, ...), kind=kLoop, calls=%fused_computation.15 | loop fusion | flops 10485760 | bytes 12585472 | tf_op jit(solution)/shard_map/convert_element_type | solution.py:170
  120.3 2.0 %fusion.3 = f32[2,64,128]{2,1,0:T(8,128)S(1)} fusion(bf16[2,64,64,64]{1,3,2,0:T(8,128)(2,1)S(1)} %copy-done.5, bf16[2,64,128,64]{2,3,1,0:T(8,128)(2,1)S(1)} %add_convert_fusion, f32[2,64,64]{1,2,0:T(8,128)S(1)} %copy.76), kind=kOutput, calls=%fused_computation.9 | convolution fusion | flops 136298496 | bytes 3244032 | tf_op jit(solution)/shard_map/chnp,cthp->cthn/dot_general | solution.py:35
  123.7 24.6 %collective-permute-start.8 = (f32[8,12,64]{2,0,1:T(8,128)S(1)}, f32[8,12,64]{2,0,1:T(8,128)S(1)}, u32[]{:S(2)}, u32[]{:S(2)}) collective-permute-start(f32[8,12,64]{2,0,1:T(8,128)S(1)} %fusion.64), channel_id=1, source_target_pairs={{0,8},{4,12},{8,0},{12,4},{16,24},{20,28},{24,16},{28,20},{1,9},{5... | collective-permute-start | bytes 73736 | tf_op jit(solution)/shard_map/ppermute | solution.py:18
  148.3 3.2 %fusion.2 = bf16[2,64,64,64]{1,3,2,0:T(8,128)(2,1)} fusion(bf16[2,64,64,64]{1,3,2,0:T(8,128)(2,1)S(1)} %copy-done.3, f32[2,64,64,64]{3,2,1,0:T(8,128)S(1)} %copy-done.6, f32[64]{0:T(128)S(1)} %copy-done.9, bf16[2,64,128,64]{2,3,1,0:T(8,128)(2,1)S(1)} %add_convert_fusion, f32[2,64,64]{1,2,0:T(8,128)S(1)} %copy.76, f32[2,64,128]{2,1,0:T(8,128)S(1)} %convert_element_type.94), kind=kOutput, calls=%fused_computation.7 | convolution fusion | flops 138936320 | bytes 6390016 | tf_op jit(solution)/shard_map/cthn,chnp->cthp/dot_general | solution.py:35
  151.6 3.3 %copy.77 = bf16[2,64,64,64]{3,2,1,0:T(8,128)(2,1)S(1)} copy(bf16[2,64,64,64]{1,3,2,0:T(8,128)(2,1)} %fusion.2) | data formatting | bytes 2097152 | tf_op jit(solution)/shard_map/convert_element_type | solution.py:191
  154.9 2.5 %reshape.123 = bf16[128,4096]{1,0:T(8,128)(2,1)} reshape(bf16[2,64,64,64]{3,2,1,0:T(8,128)(2,1)S(1)} %copy.77) | data formatting | bytes 2097152 | tf_op jit(solution)/shard_map/reshape | solution.py:192
  157.4 3.4 %collective-permute-start.9 = (f32[8,12,64]{2,0,1:T(8,128)S(1)}, f32[8,12,64]{2,0,1:T(8,128)S(1)}, u32[]{:S(2)}, u32[]{:S(2)}) collective-permute-start(f32[8,12,64]{2,0,1:T(8,128)S(1)} %add.127), channel_id=1, source_target_pairs={{0,16},{4,20},{8,24},{12,28},{16,0},{20,4},{24,8},{28,12},{1,17},{... | collective-permute-start | bytes 73736 | tf_op jit(solution)/shard_map/ppermute | solution.py:18
  161.6 1.9 %collective-permute-done.9 = f32[8,12,64]{2,0,1:T(8,128)S(1)} collective-permute-done((f32[8,12,64]{2,0,1:T(8,128)S(1)}, f32[8,12,64]{2,0,1:T(8,128)S(1)}, u32[]{:S(2)}, u32[]{:S(2)}) %collective-permute-start.9) | collective-permute-done | bytes 24608 | tf_op jit(solution)/shard_map/ppermute | solution.py:18
  (110 shorter events, 31.8 us)
Async XLA Ops:
  1.5 13.3 %collective-permute-start = (bf16[3,4352]{1,0:T(4,128)(2,1)S(1)}, bf16[3,4352]{1,0:T(4,128)(2,1)S(1)}, u32[]{:S(2)}, u32[]{:S(2)}) collective-permute-start(bf16[3,4352]{1,0:T(4,128)(2,1)S(1)} %slice.98), channel_id=1, source_target_pairs={{0,4},{4,8},{8,12},{12,16},{16,20},{20,24},{24,28},{1,5},{5,9},{9,... | collective-permute-start | bytes 78344 | tf_op jit(solution)/shard_map/ppermute | solution.py:12
  8.2 32.9 %collective-permute-start.2 = (f32[64]{0:T(128)S(1)}, f32[64]{0:T(128)S(1)}, u32[]{:S(2)}, u32[]{:S(2)}) collective-permute-start(f32[64]{0:T(128)S(1)} %get-tuple-element.34), channel_id=1, source_target_pairs={{0,4},{4,0},{8,12},{12,8},{16,20},{20,16},{24,28},{28,24},{1,5},{5... | collective-permute-start | bytes 776 | tf_op jit(solution)/shard_map/ppermute | solution.py:18
  9.8 9.4 %copy-start.19 = (pred[2,2]{1,0:T(4,128)(4,1)}, pred[2,2]{1,0:T(4,128)(4,1)S(1)}, u32[]{:S(2)}) copy-start(pred[2,2]{1,0:T(4,128)(4,1)S(1)} %get-tuple-element.53) | copy-start | bytes 16
  10.9 8.3 %copy-start.8 = (f32[2,12,64]{2,0,1:T(2,128)}, f32[2,12,64]{2,0,1:T(2,128)S(1)}, u32[]{:S(2)}) copy-start(f32[2,12,64]{2,0,1:T(2,128)S(1)} %fusion.53) | copy-start | bytes 18436
  31.4 24.5 %collective-permute-start.1 = (bf16[64,128,64]{1,2,0:T(8,128)(2,1)}, bf16[64,128,64]{1,2,0:T(8,128)(2,1)S(1)}, u32[]{:S(2)}, u32[]{:S(2)}) collective-permute-start(bf16[64,128,64]{1,2,0:T(8,128)(2,1)} %convert_element_type.85), channel_id=1, source_target_pairs={{0,4},{4,0},{8,12},{12,8},{16,20},{20,16},{24,28},{28,24},{1,5},{5... | collective-permute-start | bytes 3145736 | tf_op jit(solution)/shard_map/ppermute | solution.py:18
  41.0 3.6 %collective-permute-start.4 = (f32[64]{0:T(128)S(1)}, f32[64]{0:T(128)S(1)}, u32[]{:S(2)}, u32[]{:S(2)}) collective-permute-start(f32[64]{0:T(128)S(1)} %get-tuple-element.12), channel_id=1, source_target_pairs={{0,8},{4,12},{8,0},{12,4},{16,24},{20,28},{24,16},{28,20},{1,9},{5... | collective-permute-start | bytes 776 | tf_op jit(solution)/shard_map/ppermute | solution.py:18
  57.6 23.7 %collective-permute-start.3 = (bf16[64,128,64]{1,2,0:T(8,128)(2,1)}, bf16[64,128,64]{1,2,0:T(8,128)(2,1)}, u32[]{:S(2)}, u32[]{:S(2)}) collective-permute-start(bf16[64,128,64]{1,2,0:T(8,128)(2,1)} %fusion.67), channel_id=1, source_target_pairs={{0,8},{4,12},{8,0},{12,4},{16,24},{20,28},{24,16},{28,20},{1,9},{5... | collective-permute-start | bytes 3145736 | tf_op jit(solution)/shard_map/ppermute | solution.py:18
  68.4 13.0 %copy-start.10 = (f32[64]{0:T(128)S(1)}, f32[64]{0:T(128)}, u32[]{:S(2)}) copy-start(f32[64]{0:T(128)} %get-tuple-element.46) | copy-start | bytes 772
  68.4 13.0 %copy-start.11 = (f32[64]{0:T(128)S(1)}, f32[64]{0:T(128)}, u32[]{:S(2)}) copy-start(f32[64]{0:T(128)} %get-tuple-element.48) | copy-start | bytes 772
  81.4 8.6 %copy-start.20 = (pred[2,2]{1,0:T(4,128)(4,1)S(1)}, pred[2,2]{1,0:T(4,128)(4,1)}, u32[]{:S(2)}) copy-start(pred[2,2]{1,0:T(4,128)(4,1)} %copy-done.19) | copy-start | bytes 16
  81.4 8.6 %copy-start.23 = (pred[2,2,1]{1,0,2:T(4,128)(4,1)S(1)}, pred[2,2,1]{1,0,2:T(4,128)(4,1)}, u32[]{:S(2)}) copy-start(pred[2,2,1]{1,0,2:T(4,128)(4,1)} %fusion.59) | copy-start | bytes 16
  85.3 24.5 %collective-permute-start.5 = (bf16[64,128,64]{1,2,0:T(8,128)(2,1)S(1)}, bf16[64,128,64]{1,2,0:T(8,128)(2,1)S(1)}, u32[]{:S(2)}, u32[]{:S(2)}) collective-permute-start(bf16[64,128,64]{1,2,0:T(8,128)(2,1)S(1)} %get-tuple-element.24), channel_id=1, source_target_pairs={{0,16},{4,20},{8,24},{12,28},{1,17},{5,21},{9,25},{13,29},{2,18},{... | collective-permute-start | bytes 3145736 | tf_op jit(solution)/shard_map/ppermute | solution.py:25
  92.6 17.2 %copy-start.16 = (f32[64]{0:T(128)S(1)}, f32[64]{0:T(128)}, u32[]{:S(2)}) copy-start(f32[64]{0:T(128)} %get-tuple-element.47) | copy-start | bytes 772
  114.7 9.0 %collective-permute-start.7 = (f32[8,12,64]{2,0,1:T(8,128)S(1)}, f32[8,12,64]{2,0,1:T(8,128)S(1)}, u32[]{:S(2)}, u32[]{:S(2)}) collective-permute-start(f32[8,12,64]{2,0,1:T(8,128)S(1)} %pad_maximum_fusion.3), channel_id=1, source_target_pairs={{0,4},{4,0},{8,12},{12,8},{16,20},{20,16},{24,28},{28,24},{1,5},{5... | collective-permute-start | bytes 73736 | tf_op jit(solution)/shard_map/ppermute | solution.py:18
  115.3 33.1 %copy-start.6 = (f32[2,64,64,64]{3,2,1,0:T(8,128)S(1)}, f32[2,64,64,64]{3,2,1,0:T(8,128)}, u32[]{:S(2)}) copy-start(f32[2,64,64,64]{3,2,1,0:T(8,128)} %fusion.9) | copy-start | bytes 6291460
  120.3 28.1 %copy-start.3 = (bf16[2,64,64,64]{1,3,2,0:T(8,128)(2,1)S(1)}, bf16[2,64,64,64]{1,3,2,0:T(8,128)(2,1)}, u32[]{:S(2)}) copy-start(bf16[2,64,64,64]{1,3,2,0:T(8,128)(2,1)} %copy.71) | copy-start | bytes 3145732
  120.3 28.0 %copy-start.9 = (f32[64]{0:T(128)S(1)}, f32[64]{0:T(128)}, u32[]{:S(2)}) copy-start(f32[64]{0:T(128)} %param.14) | copy-start | bytes 772
  122.4 38.5 %collective-permute-start.6 = (f32[3,128]{1,0:T(4,128)S(1)}, f32[3,128]{1,0:T(4,128)S(1)}, u32[]{:S(2)}, u32[]{:S(2)}) collective-permute-start(f32[3,128]{1,0:T(4,128)S(1)} %slice.146), channel_id=1, source_target_pairs={{4,0},{8,4},{12,8},{16,12},{20,16},{24,20},{28,24},{5,1},{9,5},{13... | collective-permute-start | bytes 4616 | tf_op jit(solution)/shard_map/ppermute | solution.py:12
  123.7 33.7 %collective-permute-start.8 = (f32[8,12,64]{2,0,1:T(8,128)S(1)}, f32[8,12,64]{2,0,1:T(8,128)S(1)}, u32[]{:S(2)}, u32[]{:S(2)}) collective-permute-start(f32[8,12,64]{2,0,1:T(8,128)S(1)} %fusion.64), channel_id=1, source_target_pairs={{0,8},{4,12},{8,0},{12,4},{16,24},{20,28},{24,16},{28,20},{1,9},{5... | collective-permute-start | bytes 73736 | tf_op jit(solution)/shard_map/ppermute | solution.py:18
  154.9 6.0 %copy-start.12 = (f32[128]{0:T(128)S(1)}, f32[128]{0:T(128)}, u32[]{:S(2)}) copy-start(f32[128]{0:T(128)} %get-tuple-element.28) | copy-start | bytes 1540
  154.9 6.0 %copy-start.13 = (f32[128]{0:T(128)S(1)}, f32[128]{0:T(128)}, u32[]{:S(2)}) copy-start(f32[128]{0:T(128)} %get-tuple-element.29) | copy-start | bytes 1540
  154.9 6.0 %copy-start.14 = (f32[128]{0:T(128)S(1)}, f32[128]{0:T(128)}, u32[]{:S(2)}) copy-start(f32[128]{0:T(128)} %get-tuple-element.30) | copy-start | bytes 1540
  154.9 8.5 %copy-start.7 = (f32[8,12,64]{2,0,1:T(8,128)S(1)}, f32[8,12,64]{2,0,1:T(8,128)}, u32[]{:S(2)}) copy-start(f32[8,12,64]{2,0,1:T(8,128)} %param.15) | copy-start | bytes 73732
  157.4 6.0 %collective-permute-start.9 = (f32[8,12,64]{2,0,1:T(8,128)S(1)}, f32[8,12,64]{2,0,1:T(8,128)S(1)}, u32[]{:S(2)}, u32[]{:S(2)}) collective-permute-start(f32[8,12,64]{2,0,1:T(8,128)S(1)} %add.127), channel_id=1, source_target_pairs={{0,16},{4,20},{8,24},{12,28},{16,0},{20,4},{24,8},{28,12},{1,17},{... | collective-permute-start | bytes 73736 | tf_op jit(solution)/shard_map/ppermute | solution.py:18
  (10 other events, 32.3 us)

commit v2 on v1

--- a/solution.py
+++ b/solution.py
@@ -70,24 +70,30 @@
     basic = fading * scores[None] / state_dim
     intra = (weight_zero[:, None, None] * basic).astype(jnp.bfloat16)
     y_inner = contract("hts,shp->thp", intra, x_part)
-    x_faded = (x_part * jnp.exp(cumul[-1][None, :] - cumul)[:, :, None]).astype(jnp.bfloat16)
-    group_state = contract("sn,shp->hnp", b_part, x_faded)
     products = contract("thp,shp->hts", grad_part, x_part)
     grad_weight = (
         jnp.sum(weight_zero[:, None, None] * fading * products, axis=0) / state_dim
     ).astype(jnp.bfloat16)
     grad_inner = jnp.dot(grad_weight, b_part, preferred_element_type=jnp.float32)
     level_zero = jnp.sum(basic * products, axis=(1, 2))
-    return (y_inner, group_state, cumul, grad_inner, level_zero)
-
-
-def combine(block, block_decay, other, other_decay, leading, upper):
-    grown = upper[..., None, None]
-    found = grown * jnp.exp(leading)[..., None, None] * other
-    joined = grown * (other * jnp.exp(block_decay)[..., None, None] + block) + (1.0 - grown) * (
-        block * jnp.exp(other_decay)[..., None, None] + other
+    return (y_inner, cumul, grad_inner, level_zero)
+
+
+def combine(block, block_decay, other, other_decay, leading, upper, head_dim):
+    grown = upper
+    found = grown * lanes(jnp.exp(leading), head_dim) * other
+    joined = grown * (other * lanes(jnp.exp(block_decay), head_dim) + block) + (1.0 - grown) * (
+        block * lanes(jnp.exp(other_decay), head_dim) + other
     )
     return (joined, block_decay + other_decay, leading + upper * other_decay, found)
+
+
+def lanes(per_head, head_dim):
+    return jnp.repeat(per_head, head_dim, axis=-1)
+
+
+def per_head(value, head_dim):
+    return jnp.sum(value.reshape(value.shape[:-1] + (-1, head_dim)), axis=-1)
 
 
 def local(
@@ -116,7 +122,7 @@
     x_groups = x_act.reshape(groups, group_len, heads, head_dim)
     c_groups = c_query.reshape(groups, group_len, state_dim)
     grad_groups = grad_out.reshape(groups, group_len, heads, head_dim)
-    y_inner, states, cumuls, grad_inner, level_zero = jax.vmap(local_group)(
+    y_inner, cumuls, grad_inner, level_zero = jax.vmap(local_group)(
         x_groups,
         b_key.reshape(groups, group_len, state_dim),
         c_groups,
@@ -124,10 +130,16 @@
         grad_groups,
         weight_rows[:, 0],
     )
+    x_flat = x_act.reshape(groups, group_len, inner)
+    b_groups = b_key.reshape(groups, group_len, state_dim)
+    g_flat = cotangent.reshape(groups, group_len, inner)
+    ending = lanes(jnp.exp(cumuls[:, -1:, :] - cumuls), head_dim)
+    x_faded = (x_flat * ending).astype(jnp.bfloat16)
+    states = contract("gtn,gtq->gnq", b_groups, x_faded)
     totals = cumuls[:, -1]
     dev_decay = jnp.sum(totals, axis=0)
     later = dev_decay[None, :] - jnp.cumsum(totals, axis=0)
-    dev_state = jnp.sum(jnp.exp(later)[:, :, None, None] * states, axis=0)
+    dev_state = jnp.sum(lanes(jnp.exp(later), head_dim)[:, None, :] * states, axis=0)
     devices = lax.axis_size("seq")
     depth = devices.bit_length() - 1
     myself = lax.axis_index("seq")
@@ -141,11 +153,9 @@
         else:
             sent, other_decay = from_partner((block.astype(jnp.bfloat16), block_decay), "seq", bit_pos)
             other = sent.astype(jnp.float32)
-        upper = jnp.zeros_like(dev_decay) + (jnp.right_shift(myself, bit_pos) & 1).astype(
-            jnp.float32
-        )
+        upper = (jnp.right_shift(myself, bit_pos) & 1).astype(jnp.float32)
         block, block_decay, leading, found = combine(
-            block, block_decay, other, other_decay, leading, upper
+            block, block_decay, other, other_decay, leading, upper, head_dim
         )
         found_all.append(found)
     cross = jnp.stack(found_all, axis=0)
@@ -165,18 +175,22 @@
     local_weight = exact("cds,csh->cdh", onehot, weight_rows[:, 1 : 1 + low_levels]) * fade_pairs
     lead_fade = jnp.exp(before)
     cross_weight = weight_rows[:, 1 + low_levels : 1 + low_levels + depth] * lead_fade[:, None, :]
-    terms = [local_weight[:, d, :, None, None] * states[d][None] for d in range(groups)]
-    terms += [cross_weight[:, l, :, None, None] * cross[l][None] for l in range(depth)]
+    terms = [lanes(local_weight[:, d], head_dim)[:, None, :] * states[d][None] for d in range(groups)]
+    terms += [lanes(cross_weight[:, l], head_dim)[:, None, :] * cross[l][None] for l in range(depth)]
     mixed = sum(terms[1:], terms[0]).astype(jnp.bfloat16)
-    scaled = jnp.exp(cumuls) / state_dim
-    query_faded = (c_groups[:, :, None, :] * scaled[:, :, :, None]).astype(jnp.bfloat16)
-    y_cross = contract("cthn,chnp->cthp", query_faded, mixed)
-    backed = contract("chnp,cthp->cthn", mixed, grad_groups)
-    grad_cross = jnp.sum(backed * scaled[:, :, :, None], axis=2)
-    gram = contract("cthn,cthp->chnp", query_faded, grad_groups)
-    inner_pairs = jnp.sum(states[None] * gram[:, None], axis=(3, 4))
+    scaled = lanes(jnp.exp(cumuls) / state_dim, head_dim)
+    y_cross = scaled * contract("ctn,cnq->ctq", c_groups, mixed)
+    grad_scaled = scaled * g_flat
+    grad_cross = exact("ctq,cnq->ctn", grad_scaled, mixed.astype(jnp.float32))
+    gram = exact("ctn,ctq->cnq", c_groups.astype(jnp.float32), grad_scaled)
+    inner_pairs = jnp.stack(
+        [jnp.stack([per_head(jnp.sum(states[d] * gram[c], axis=0), head_dim) for d in range(groups)]) for c in range(groups)]
+    )
+    cross_pairs = jnp.stack(
+        [jnp.stack([per_head(jnp.sum(cross[l] * gram[c], axis=0), head_dim) for l in range(depth)]) for c in range(groups)]
+    )
     level_local = exact("cds,cdh->csh", onehot, fade_pairs * inner_pairs)
-    level_cross = lead_fade[:, None, :] * jnp.sum(cross[None] * gram[:, None], axis=(3, 4))
+    level_cross = lead_fade[:, None, :] * cross_pairs
     level_rest = jnp.concatenate(
         [
             level_local,
@@ -187,7 +201,7 @@
     )
     grads = exact("ck,clh->klh", picked, level_rest)
     ssm_out = (
-        (y_inner + y_cross + skip[None, None, :, None] * x_groups)
+        (y_inner.reshape(groups, group_len, inner) + y_cross + lanes(skip, head_dim) * x_flat)
         .astype(jnp.bfloat16)
         .reshape(length, inner)
     )

time: 165 us -> 182 us (1.10)
  local copies, waits for them, and re-layouts: 28.8 us -> 38.7 us
  matrix products: 23.2 us -> 30.1 us
  other arithmetic: 27 us -> 30.5 us
  waiting for transfers between devices: 39.4 us -> 37.2 us
    reshape x1 -> x13, local copies, waits for them, and re-layouts: 2.47 us -> 13.6 us  [the longest x2 8.38 us: lanes(): return jnp.repeat(per_head, head_dim, axis=-1)]
    another operation x4, other arithmetic: 10.9 us -> 3.4 us  [the longest x3 6.49 us: local(): cross = jnp.stack(found_all, axis=0)]
    dot_general x4 -> x6, matrix products: 2.44 us -> 8.73 us  [exact(): return jnp.einsum(form, left, right, precision=lax.Precision.HIGHEST)]
    ppermute x7, waiting for transfers between devices: 25.7 us -> 19.7 us  [from_partner(): return lax.ppermute(value, axis, pairs)]
    broadcast_in_dim x0 -> x15, local copies, waits for them, and re-layouts: none -> 6.02 us  [lanes(): return jnp.repeat(per_head, head_dim, axis=-1)]
    another operation x2 -> x1, local copies, waits for them, and re-layouts: 8.45 us -> 3.28 us  [local(): grad_groups = grad_out.reshape(groups, group_len, heads, head_dim)]
    reduce_sum x2 -> x11, other arithmetic: 2.21 us -> 6.57 us  [the longest x1 5.42 us: local(): jnp.sum(states[d] * gram[c], axis=0)]
    ppermute x1, waiting for transfers between devices: 13.6 us -> 17.5 us  [upward(): return lax.ppermute(value, axis, pairs)]
  transfers between devices with their start and end apart: 10 -> 10, of which waited for: 5 -> 5; matrix products, arithmetic and copies ran while one was open for 41% -> 43% of each run, Pallas kernels for 0% -> 0%
where the time goes in v2:
time: 182 us; the launch traced here: 181 us
  starting transfers between devices  43.3 us (24%)
  local copies, waits for them, and re-layouts  38.7 us (21%)
  waiting for transfers between devices  37.2 us (20%)
  other arithmetic  30.5 us (17%)
  matrix products  30.1 us (17%)
    ppermute x7, starting transfers between devices, from_partner(): return lax.ppermute(value, axis, pairs)  33.5 us
    dot_general x4, matrix products, contract(): return jnp.einsum(form, left, right, preferred_element_type=jnp.float32)  21.1 us
    ppermute x7, waiting for transfers between devices, from_partner(): return lax.ppermute(value, axis, pairs)  19.7 us
    ppermute x1, waiting for transfers between devices, upward(): return lax.ppermute(value, axis, pairs)  17.5 us
    dot_general x6, matrix products, exact(): return jnp.einsum(form, left, right, precision=lax.Precision.HIGHEST)  8.73 us
    reshape x2, local copies, waits for them, and re-layouts, lanes(): return jnp.repeat(per_head, head_dim, axis=-1)  8.38 us
    ppermute x2, starting transfers between devices, shifted(): lax.ppermute(value, axis, [(source, source + steps) for source in range(l...  6.14 us
    broadcast_in_dim x15, local copies, waits for them, and re-layouts, lanes(): return jnp.repeat(per_head, head_dim, axis=-1)  6.02 us
  transfers between devices with their start and end apart: 10, of which 5 were waited for; matrix products, arithmetic and copies ran while one was open for 43% of the time, Pallas kernels for 0%

profile of v2, /device:TPU:0, one launch (start us, length us, event | category | flops | bytes accessed | tf_op | source)
XLA Modules:
  0.0 181.0 jit_solution(6148734934060888890)
XLA Ops:
  1.5 4.8 %collective-permute-start = (bf16[3,4352]{1,0:T(4,128)(2,1)S(1)}, bf16[3,4352]{1,0:T(4,128)(2,1)S(1)}, u32[]{:S(2)}, u32[]{:S(2)}) collective-permute-start(bf16[3,4352]{1,0:T(4,128)(2,1)S(1)} %slice.116), channel_id=1, source_target_pairs={{0,4},{4,8},{8,12},{12,16},{16,20},{20,24},{24,28},{1,5},{5,9},{9,... | collective-permute-start | bytes 78344 | tf_op jit(solution)/shard_map/ppermute | solution.py:12
  15.9 2.6 %broadcast_in_dim.115 = f32[2,64,64,64]{3,2,1,0:T(8,128)} broadcast(f32[2,64,64]{2,1,0:T(8,128)S(1)} %get-tuple-element.43), dimensions={0,1,2} | broadcast | bytes 2129920 | tf_op jit(solution)/shard_map/broadcast_in_dim | solution.py:92
  18.5 4.8 %reshape.149 = f32[2,64,4096]{2,1,0:T(8,128)} reshape(f32[2,64,64,64]{3,2,1,0:T(8,128)} %broadcast_in_dim.115) | data formatting | bytes 4194304 | tf_op jit(solution)/shard_map/reshape | solution.py:92
  23.2 2.5 %broadcast_in_dim.111 = f32[2,64,64,64]{3,2,1,0:T(8,128)} broadcast(f32[2,64,64]{2,1,0:T(8,128)S(1)} %get-tuple-element.44), dimensions={0,1,2} | broadcast | bytes 2129920 | tf_op jit(solution)/shard_map/broadcast_in_dim | solution.py:92
  25.8 3.6 %reshape.147 = f32[2,64,4096]{2,1,0:T(8,128)S(1)} reshape(f32[2,64,64,64]{3,2,1,0:T(8,128)} %broadcast_in_dim.111) | data formatting | bytes 4194304 | tf_op jit(solution)/shard_map/reshape | solution.py:92
  30.1 3.3 %reshape_reshape.8 = bf16[2,64,64,64]{3,2,1,0:T(8,128)(2,1)} reshape(bf16[128,4096]{1,0:T(8,128)(2,1)S(1)} %copy-done.3) | data formatting | bytes 2097152 | tf_op jit(solution)/shard_map/reshape;reshape | solution.py:124
  37.1 3.4 %fusion.71 = (bf16[128,4352]{1,0:T(8,128)(2,1)S(1)}, f32[128,4352]{1,0:T(8,128)S(1)}) fusion(f32[4352]{0:T(1024)S(1)} %get-tuple-element.20, bf16[128,4352]{1,0:T(8,128)(2,1)} %param.9, f32[4352]{0:T(1024)S(1)} %get-tuple-element.21, bf16[3,4352]{1,0:T(4,128)(2,1)S(1)} %collective-permute-done, f32[4352]{0:T(1024)S(1)} %get-tuple-element.22, ...), kind=kLoop, calls=%fused_computation.149 | loop fusion | flops 12255232 | bytes 4569600 | tf_op jit(solution)/shard_map/convert.4
  42.1 3.0 %multiply_reduce_fusion = (f32[128,4096]{1,0:T(8,128)S(1)}, f32[2,128,4096]{2,1,0:T(8,128)}) fusion(f32[2,4096]{1,0:T(2,128)S(1)} %mul.453, bf16[2,64,128]{2,1,0:T(8,128)(2,1)S(1)} %bitcast.134, f32[2,64,4096]{2,1,0:T(8,128)S(1)} %copy-done.6, bf16[2,64,4096]{2,1,0:T(8,128)(2,1)S(1)} %bitcast.124), kind=kOutput, calls=%fused_computation.9 | convolution fusion | flops 137363456 | bytes 9502720 | tf_op jit(solution)/shard_map/gtn,gtq->gnq/dot_general | solution.py:35
  49.1 3.3 %reshape_reshape.7 = bf16[2,64,64,64]{3,2,1,0:T(8,128)(2,1)} reshape(bf16[128,4096]{1,0:T(8,128)(2,1)S(1)} %multiply_convert_fusion.2) | data formatting | bytes 2097152 | tf_op jit(solution)/shard_map/reshape;reshape | solution.py:122
  52.5 8.5 %fusion.4 = (f32[2,64]{1,0:T(2,128)S(1)}, f32[2,64,64]{1,2,0:T(8,128)}) fusion(f32[2,64,64]{1,2,0:T(8,128)S(1)} %fusion.75, f32[2,64,64]{2,1,0:T(8,128)S(1)} %copy-done.8, pred[64,64]{0,1:T(8,128)(4,1)S(1)} %iota_compare_fusion, f32[2,64]{1,0:T(2,128)S(1)} %copy-done.23, bf16[2,64,64,64]{3,2,1,0:T(8,128)(2,1)} %reshape_reshape.8, ...), kind=kOutput, calls=%fused_computation.7 | convolution fusion | flops 72343424 | bytes 2200576 | tf_op jit(solution)/shard_map/vmap(thp,shp->hts)/dot_general | solution.py:35
  62.0 9.8 %collective-permute-done.1 = bf16[128,4096]{1,0:T(8,128)(2,1)} collective-permute-done((bf16[128,4096]{1,0:T(8,128)(2,1)}, bf16[128,4096]{1,0:T(8,128)(2,1)}, u32[]{:S(2)}, u32[]{:S(2)}) %collective-permute-start.1) | collective-permute-done | bytes 1048608 | tf_op jit(solution)/shard_map/ppermute | solution.py:18
  71.8 3.4 %fusion.34 = bf16[128,4096]{1,0:T(8,128)(2,1)} fusion(f32[128,4096]{1,0:T(8,128)} %copy-done.1, f32[4096]{0:T(1024)S(1)} %mul.472, f32[]{:T(128)S(6)} %sub.84, f32[4096]{0:T(1024)S(1)} %mul.467, bf16[128,4096]{1,0:T(8,128)(2,1)} %collective-permute-done.1, f32[]{:T(128)S(6)} %convert_element_type.85), kind=kLoop, calls=%fused_computation.70 | loop fusion | flops 4718592 | bytes 4227080 | tf_op jit(solution)/shard_map/convert_element_type | solution.py:154
  75.7 7.9 %fusion.6 = f32[2,64,64,64]{3,2,1,0:T(8,128)} fusion(f32[2,64]{1,0:T(2,128)S(1)} %copy-done.22, f32[2,64,64]{1,2,0:T(8,128)S(1)} %copy-done.11, f32[2,64,64]{2,1,0:T(8,128)S(1)} %copy-done.9, pred[64,64]{0,1:T(8,128)(4,1)S(1)} %iota_compare_fusion, bf16[2,64,64,64]{3,2,1,0:T(8,128)(2,1)S(1)} %copy-done.7), kind=kOutput, calls=%fused_computation.22 | convolution fusion | flops 70254592 | bytes 3215872 | tf_op jit(solution)/shard_map/vmap(hts,shp->thp)/dot_general | solution.py:35
  83.6 3.8 %copy.40 = f32[2,64,4096]{2,1,0:T(8,128)} copy(f32[2,64,4096]{1,2,0:T(8,128)} %bitcast.128) | data formatting | bytes 4194304 | tf_op jit(solution)/shard_map/reshape | solution.py:204
  87.7 3.2 %fusion.27 = f32[2,128,4096]{2,1,0:T(8,128)S(1)} fusion(bf16[2,64,128]{2,1,0:T(8,128)(2,1)S(1)} %bitcast.132, f32[2,64,4096]{2,1,0:T(8,128)S(1)} %reshape.147, bf16[2,64,4096]{2,1,0:T(8,128)(2,1)} %bitcast.126), kind=kOutput, calls=%fused_computation.62 | convolution fusion | flops 806354944 | bytes 7372800 | tf_op jit(solution)/shard_map/ctn,ctq->cnq/dot_general | solution.py:39
  91.0 7.7 %collective-permute-done.3 = bf16[128,4096]{1,0:T(8,128)(2,1)} collective-permute-done((bf16[128,4096]{1,0:T(8,128)(2,1)}, bf16[128,4096]{1,0:T(8,128)(2,1)}, u32[]{:S(2)}, u32[]{:S(2)}) %collective-permute-start.3) | collective-permute-done | bytes 1048608 | tf_op jit(solution)/shard_map/ppermute | solution.py:18
  98.7 2.7 %fusion.15 = bf16[128,4096]{1,0:T(8,128)(2,1)S(1)} fusion(bf16[128,4096]{1,0:T(8,128)(2,1)} %collective-permute-done.3, f32[4096]{0:T(1024)S(1)} %mul.492, f32[]{:T(128)S(6)} %sub.85, f32[4096]{0:T(1024)S(1)} %mul.487, f32[]{:T(128)S(6)} %convert_element_type.88, f32[128,4096]{1,0:T(8,128)S(1)} %copy-done.2, f32[4096]{0:T(1024)S(1)} %mul.472, f32[]{:T(128)S(6)} %sub.84, ...), kind=kLoop, calls=%fused_computation.31 | loop fusion | flops 8912896 | bytes 5308432 | tf_op jit(solution)/shard_map/convert_element_type | solution.py:151
  101.3 3.6 %collective-permute-start.5 = (bf16[128,4096]{1,0:T(8,128)(2,1)S(1)}, bf16[128,4096]{1,0:T(8,128)(2,1)S(1)}, u32[]{:S(2)}, u32[]{:S(2)}) collective-permute-start(bf16[128,4096]{1,0:T(8,128)(2,1)S(1)} %fusion.15), channel_id=1, source_target_pairs={{0,16},{4,20},{8,24},{12,28},{1,17},{5,21},{9,25},{13,29},{2,18},{... | collective-permute-start | bytes 3145736 | tf_op jit(solution)/shard_map/ppermute | solution.py:25
  105.0 2.5 %slice_bitcast_fusion.3 = (f32[128,4096]{1,0:T(8,128)}, f32[128,4096]{1,0:T(8,128)}) fusion(f32[2,128,4096]{2,1,0:T(8,128)S(1)} %copy-done), kind=kLoop, calls=%fused_computation.36 | loop fusion | bytes 8388608 | tf_op jit(solution)/shard_map/mul | solution.py:178
  107.4 17.5 %collective-permute-done.5 = bf16[128,4096]{1,0:T(8,128)(2,1)S(1)} collective-permute-done((bf16[128,4096]{1,0:T(8,128)(2,1)S(1)}, bf16[128,4096]{1,0:T(8,128)(2,1)S(1)}, u32[]{:S(2)}, u32[]{:S(2)}) %collective-permute-start.5) | collective-permute-done | bytes 1048608 | tf_op jit(solution)/shard_map/ppermute | solution.py:25
  124.9 5.4 %multiply_reduce_fusion.10 = (f32[4096]{0:T(1024)}, f32[4096]{0:T(1024)S(1)}, f32[4096]{0:T(1024)S(1)}, f32[4096]{0:T(1024)S(1)}, f32[4096]{0:T(1024)S(1)}, /*in...) fusion(f32[2,128,4096]{2,1,0:T(8,128)S(1)} %fusion.27, ...), kind=kLoop, calls=%fused_computation.49 | loop fusion | flops 13590528 | bytes 18022404 | tf_op jit(solution)/shard_map/reduce_sum | solution.py:187
  138.0 4.8 %add_convert_fusion = bf16[2,128,4096]{2,1,0:T(8,128)(2,1)S(1)} fusion(f32[128,4096]{1,0:T(8,128)} %get-tuple-element.35, f32[2,4096]{1,0:T(2,128)S(1)} %mul.479, f32[128,4096]{1,0:T(8,128)} %get-tuple-element.36, f32[2,4096]{1,0:T(2,128)S(1)} %mul.459, f32[128,4096]{1,0:T(8,128)} %get-tuple-element.37, f32[2,4096]{1,0:T(2,128)S(1)} %mul.450, ...), kind=kLoop, calls=%fused_computation.8 | loop fusion | flops 10485760 | bytes 12746752 | tf_op jit(solution)/shard_map/convert_element_type | solution.py:180
  147.3 23.6 %collective-permute-start.8 = (f32[8,12,64]{2,0,1:T(8,128)S(1)}, f32[8,12,64]{2,0,1:T(8,128)S(1)}, u32[]{:S(2)}, u32[]{:S(2)}) collective-permute-start(f32[8,12,64]{2,0,1:T(8,128)S(1)} %fusion.68), channel_id=1, source_target_pairs={{0,8},{4,12},{8,0},{12,4},{16,24},{20,28},{24,16},{28,20},{1,9},{5... | collective-permute-start | bytes 73736 | tf_op jit(solution)/shard_map/ppermute | solution.py:18
  173.0 4.7 %collective-permute-start.9 = (f32[8,12,64]{2,0,1:T(8,128)S(1)}, f32[8,12,64]{2,0,1:T(8,128)S(1)}, u32[]{:S(2)}, u32[]{:S(2)}) collective-permute-start(f32[8,12,64]{2,0,1:T(8,128)S(1)} %add.117), channel_id=1, source_target_pairs={{0,16},{4,20},{8,24},{12,28},{16,0},{20,4},{24,8},{28,12},{1,17},{... | collective-permute-start | bytes 73736 | tf_op jit(solution)/shard_map/ppermute | solution.py:18
  (162 shorter events, 39.5 us)
Async XLA Ops:
  1.5 35.6 %collective-permute-start = (bf16[3,4352]{1,0:T(4,128)(2,1)S(1)}, bf16[3,4352]{1,0:T(4,128)(2,1)S(1)}, u32[]{:S(2)}, u32[]{:S(2)}) collective-permute-start(bf16[3,4352]{1,0:T(4,128)(2,1)S(1)} %slice.116), channel_id=1, source_target_pairs={{0,4},{4,8},{8,12},{12,16},{16,20},{20,24},{24,28},{1,5},{5,9},{9,... | collective-permute-start | bytes 78344 | tf_op jit(solution)/shard_map/ppermute | solution.py:12
  8.7 24.7 %copy-start.14 = (f32[2,1,64]{2,1,0:T(1,128)}, f32[2,1,64]{2,1,0:T(1,128)S(1)}, u32[]{:S(2)}) copy-start(f32[2,1,64]{2,1,0:T(1,128)S(1)} %get-tuple-element.24) | copy-start | bytes 1540
  8.7 26.0 %collective-permute-start.2 = (f32[64]{0:T(128)S(1)}, f32[64]{0:T(128)S(1)}, u32[]{:S(2)}, u32[]{:S(2)}) collective-permute-start(f32[64]{0:T(128)S(1)} %get-tuple-element.42), channel_id=1, source_target_pairs={{0,4},{4,0},{8,12},{12,8},{16,20},{20,16},{24,28},{28,24},{1,5},{5... | collective-permute-start | bytes 776 | tf_op jit(solution)/shard_map/ppermute | solution.py:18
  10.3 23.1 %copy-start.16 = (f32[2,64]{1,0:T(2,128)}, f32[2,64]{1,0:T(2,128)S(1)}, u32[]{:S(2)}) copy-start(f32[2,64]{1,0:T(2,128)S(1)} %get-tuple-element.54) | copy-start | bytes 1540
  10.4 23.1 %copy-start.25 = (pred[2,2]{1,0:T(4,128)(4,1)}, pred[2,2]{1,0:T(4,128)(4,1)S(1)}, u32[]{:S(2)}) copy-start(pred[2,2]{1,0:T(4,128)(4,1)S(1)} %get-tuple-element.63) | copy-start | bytes 16
  35.2 12.7 %collective-permute-start.4 = (f32[64]{0:T(128)}, f32[64]{0:T(128)}, u32[]{:S(2)}, u32[]{:S(2)}) collective-permute-start(f32[64]{0:T(128)} %get-tuple-element.26), channel_id=1, source_target_pairs={{0,8},{4,12},{8,0},{12,4},{16,24},{20,28},{24,16},{28,20},{1,9},{5... | collective-permute-start | bytes 776 | tf_op jit(solution)/shard_map/ppermute | solution.py:18
  47.4 24.4 %collective-permute-start.1 = (bf16[128,4096]{1,0:T(8,128)(2,1)}, bf16[128,4096]{1,0:T(8,128)(2,1)}, u32[]{:S(2)}, u32[]{:S(2)}) collective-permute-start(bf16[128,4096]{1,0:T(8,128)(2,1)} %convert_element_type.86), channel_id=1, source_target_pairs={{0,4},{4,0},{8,12},{12,8},{16,20},{20,16},{24,28},{28,24},{1,5},{5... | collective-permute-start | bytes 3145736 | tf_op jit(solution)/shard_map/ppermute | solution.py:18
  61.9 13.7 %copy-start.7 = (bf16[2,64,64,64]{3,2,1,0:T(8,128)(2,1)S(1)}, bf16[2,64,64,64]{3,2,1,0:T(8,128)(2,1)}, u32[]{:S(2)}) copy-start(bf16[2,64,64,64]{3,2,1,0:T(8,128)(2,1)} %reshape_reshape.7) | copy-start | bytes 3145732
  61.9 13.7 %copy-start.9 = (f32[2,64,64]{2,1,0:T(8,128)S(1)}, f32[2,64,64]{2,1,0:T(8,128)}, u32[]{:S(2)}) copy-start(f32[2,64,64]{2,1,0:T(8,128)} %copy.34) | copy-start | bytes 98308
  62.0 13.7 %copy-start.11 = (f32[2,64,64]{1,2,0:T(8,128)S(1)}, f32[2,64,64]{1,2,0:T(8,128)}, u32[]{:S(2)}) copy-start(f32[2,64,64]{1,2,0:T(8,128)} %copy-done.10) | copy-start | bytes 98308
  75.2 23.4 %collective-permute-start.3 = (bf16[128,4096]{1,0:T(8,128)(2,1)}, bf16[128,4096]{1,0:T(8,128)(2,1)}, u32[]{:S(2)}, u32[]{:S(2)}) collective-permute-start(bf16[128,4096]{1,0:T(8,128)(2,1)} %fusion.34), channel_id=1, source_target_pairs={{0,8},{4,12},{8,0},{12,4},{16,24},{20,28},{24,16},{28,20},{1,9},{5... | collective-permute-start | bytes 3145736 | tf_op jit(solution)/shard_map/ppermute | solution.py:18
  91.0 14.0 %copy-start = (f32[2,128,4096]{2,1,0:T(8,128)S(1)}, f32[2,128,4096]{2,1,0:T(8,128)}, u32[]{:S(2)}) copy-start(f32[2,128,4096]{2,1,0:T(8,128)} %get-tuple-element.62) | copy-start | bytes 12582916
  101.3 23.6 %collective-permute-start.5 = (bf16[128,4096]{1,0:T(8,128)(2,1)S(1)}, bf16[128,4096]{1,0:T(8,128)(2,1)S(1)}, u32[]{:S(2)}, u32[]{:S(2)}) collective-permute-start(bf16[128,4096]{1,0:T(8,128)(2,1)S(1)} %fusion.15), channel_id=1, source_target_pairs={{0,16},{4,20},{8,24},{12,28},{1,17},{5,21},{9,25},{13,29},{2,18},{... | collective-permute-start | bytes 3145736 | tf_op jit(solution)/shard_map/ppermute | solution.py:25
  107.4 25.6 %copy-start.15 = (f32[2,1,64]{2,1,0:T(1,128)S(1)}, f32[2,1,64]{2,1,0:T(1,128)}, u32[]{:S(2)}) copy-start(f32[2,1,64]{2,1,0:T(1,128)} %copy-done.14) | copy-start | bytes 1540
  136.3 10.2 %collective-permute-start.7 = (f32[8,12,64]{2,0,1:T(8,128)}, f32[8,12,64]{2,0,1:T(8,128)}, u32[]{:S(2)}, u32[]{:S(2)}) collective-permute-start(f32[8,12,64]{2,0,1:T(8,128)} %pad_maximum_fusion.2), channel_id=1, source_target_pairs={{0,4},{4,0},{8,12},{12,8},{16,20},{20,16},{24,28},{28,24},{1,5},{5... | collective-permute-start | bytes 73736 | tf_op jit(solution)/shard_map/ppermute | solution.py:18
  142.8 28.1 %copy-start.5 = (f32[2,64,4096]{2,1,0:T(8,128)S(1)}, f32[2,64,4096]{2,1,0:T(8,128)}, u32[]{:S(2)}) copy-start(f32[2,64,4096]{2,1,0:T(8,128)} %copy.40) | copy-start | bytes 6291460
  145.2 32.5 %collective-permute-start.6 = (f32[3,128]{1,0:T(4,128)S(1)}, f32[3,128]{1,0:T(4,128)S(1)}, u32[]{:S(2)}, u32[]{:S(2)}) collective-permute-start(f32[3,128]{1,0:T(4,128)S(1)} %slice.166), channel_id=1, source_target_pairs={{4,0},{8,4},{12,8},{16,12},{20,16},{24,20},{28,24},{5,1},{9,5},{13... | collective-permute-start | bytes 4616 | tf_op jit(solution)/shard_map/ppermute | solution.py:12
  147.3 30.4 %copy-start.18 = (f32[128]{0:T(128)S(1)}, f32[128]{0:T(128)}, u32[]{:S(2)}) copy-start(f32[128]{0:T(128)} %get-tuple-element.38) | copy-start | bytes 1540
  147.3 30.4 %copy-start.19 = (f32[128]{0:T(128)S(1)}, f32[128]{0:T(128)}, u32[]{:S(2)}) copy-start(f32[128]{0:T(128)} %get-tuple-element.39) | copy-start | bytes 1540
  147.3 30.4 %copy-start.20 = (f32[128]{0:T(128)S(1)}, f32[128]{0:T(128)}, u32[]{:S(2)}) copy-start(f32[128]{0:T(128)} %get-tuple-element.40) | copy-start | bytes 1540
  147.3 30.4 %copy-start.21 = (f32[128]{0:T(128)S(1)}, f32[128]{0:T(128)}, u32[]{:S(2)}) copy-start(f32[128]{0:T(128)} %get-tuple-element.41) | copy-start | bytes 1540
  147.3 33.0 %copy-start.12 = (f32[8,12,64]{2,0,1:T(8,128)S(1)}, f32[8,12,64]{2,0,1:T(8,128)}, u32[]{:S(2)}) copy-start(f32[8,12,64]{2,0,1:T(8,128)} %param.15) | copy-start | bytes 73732
  147.3 25.6 %collective-permute-start.8 = (f32[8,12,64]{2,0,1:T(8,128)S(1)}, f32[8,12,64]{2,0,1:T(8,128)S(1)}, u32[]{:S(2)}, u32[]{:S(2)}) collective-permute-start(f32[8,12,64]{2,0,1:T(8,128)S(1)} %fusion.68), channel_id=1, source_target_pairs={{0,8},{4,12},{8,0},{12,4},{16,24},{20,28},{24,16},{28,20},{1,9},{5... | collective-permute-start | bytes 73736 | tf_op jit(solution)/shard_map/ppermute | solution.py:18
  173.0 7.3 %collective-permute-start.9 = (f32[8,12,64]{2,0,1:T(8,128)S(1)}, f32[8,12,64]{2,0,1:T(8,128)S(1)}, u32[]{:S(2)}, u32[]{:S(2)}) collective-permute-start(f32[8,12,64]{2,0,1:T(8,128)S(1)} %add.117), channel_id=1, source_target_pairs={{0,16},{4,20},{8,24},{12,28},{16,0},{20,4},{24,8},{28,12},{1,17},{... | collective-permute-start | bytes 73736 | tf_op jit(solution)/shard_map/ppermute | solution.py:18
  (13 other events, 75.2 us)

commit v3 on v1

--- a/solution.py
+++ b/solution.py
@@ -170,9 +170,6 @@
     mixed = sum(terms[1:], terms[0]).astype(jnp.bfloat16)
     scaled = jnp.exp(cumuls) / state_dim
     query_faded = (c_groups[:, :, None, :] * scaled[:, :, :, None]).astype(jnp.bfloat16)
-    y_cross = contract("cthn,chnp->cthp", query_faded, mixed)
-    backed = contract("chnp,cthp->cthn", mixed, grad_groups)
-    grad_cross = jnp.sum(backed * scaled[:, :, :, None], axis=2)
     gram = contract("cthn,cthp->chnp", query_faded, grad_groups)
     inner_pairs = jnp.sum(states[None] * gram[:, None], axis=(3, 4))
     level_local = exact("cds,cdh->csh", onehot, fade_pairs * inner_pairs)
@@ -186,6 +183,13 @@
         axis=1,
     )
     grads = exact("ck,clh->klh", picked, level_rest)
+    grad_first = exact("gk,gh->kh", picked, level_zero)
+    local_grads = jnp.concatenate([grad_first[:, None, :], grads], axis=1)
+    summed = all_sum(local_grads, "seq")
+    summed, mixed, y_inner, x_groups = lax.optimization_barrier((summed, mixed, y_inner, x_groups))
+    y_cross = contract("cthn,chnp->cthp", query_faded, mixed)
+    backed = contract("chnp,cthp->cthn", mixed, grad_groups)
+    grad_cross = jnp.sum(backed * scaled[:, :, :, None], axis=2)
     ssm_out = (
         (y_inner + y_cross + skip[None, None, :, None] * x_groups)
         .astype(jnp.bfloat16)
@@ -199,9 +203,6 @@
     for offset in range(taps):
         lagged = taps - 1 - offset
         grad_c_in = grad_c_in + query_taps[offset][None, :] * extended[lagged : lagged + length]
-    grad_first = exact("gk,gh->kh", picked, level_zero)
-    local_grads = jnp.concatenate([grad_first[:, None, :], grads], axis=1)
-    summed = all_sum(local_grads, "seq")
     level_update = level_table + summed / math.sqrt(length * devices)
     return (ssm_out, grad_c_in, level_update)
 

time: 165 us -> 178 us (1.079)
  other arithmetic: 27 us -> 36.5 us
  waiting for transfers between devices: 39.4 us -> 43.9 us
    convert_element_type x0 -> x2, other arithmetic: none -> 6.76 us  [the longest x1 5.39 us: local(): ssm_out = (y_inner + y_cross + skip[None, None, :, None] * x_groups).asty...]
    mul x1 -> x3, other arithmetic: 0.59 us -> 5.74 us  [combine(): found = grown * jnp.exp(leading)[..., None, None] * other]
    another operation x2 -> x1, local copies, waits for them, and re-layouts: 8.45 us -> 4.24 us  [local(): grad_groups = grad_out.reshape(groups, group_len, heads, head_dim)]
    another operation x3 -> x1, other arithmetic: 6.49 us -> 3.23 us  [local(): cross = jnp.stack(found_all, axis=0)]
    ppermute x7, waiting for transfers between devices: 25.7 us -> 28.8 us  [from_partner(): return lax.ppermute(value, axis, pairs)]
    optimization_barrier x0 -> x1, local copies, waits for them, and re-layouts: none -> 2.94 us  [local(): lax.optimization_barrier((summed, mixed, y_inner, x_groups))]
    reduce_sum x1, other arithmetic: 1.29 us -> 4.14 us  [local(): jnp.sum(cross[None] * gram[:, None], axis=(3, 4))]
    dot_general x6, matrix products: 20.5 us -> 22.8 us  [contract(): return jnp.einsum(form, left, right, preferred_element_type=jnp.float32)]
  transfers between devices with their start and end apart: 10 -> 10, of which waited for: 5 -> 6; matrix products, arithmetic and copies ran while one was open for 41% -> 37% of each run, Pallas kernels for 0% -> 0%
where the time goes in v3:
time: 178 us; the launch traced here: 177 us
  waiting for transfers between devices  43.9 us (25%)
  starting transfers between devices  43.6 us (24%)
  other arithmetic  36.5 us (21%)
  local copies, waits for them, and re-layouts  27.3 us (15%)
  matrix products  24.8 us (14%)
    ppermute x7, starting transfers between devices, from_partner(): return lax.ppermute(value, axis, pairs)  32.8 us
    ppermute x7, waiting for transfers between devices, from_partner(): return lax.ppermute(value, axis, pairs)  28.8 us
    dot_general x6, matrix products, contract(): return jnp.einsum(form, left, right, preferred_element_type=jnp.float32)  22.8 us
    ppermute x1, waiting for transfers between devices, upward(): return lax.ppermute(value, axis, pairs)  15.1 us
    another operation x2, local copies, waits for them, and re-layouts, local(): x_groups = x_act.reshape(groups, group_len, heads, head_dim)  6.49 us
    ppermute x2, starting transfers between devices, shifted(): lax.ppermute(value, axis, [(source, source + steps) for source in range(l...  6.14 us
    mul x3, other arithmetic, combine(): found = grown * jnp.exp(leading)[..., None, None] * other  5.74 us
    convert_element_type x1, other arithmetic, local(): ssm_out = (y_inner + y_cross + skip[None, None, :, None] * x_groups).asty...  5.39 us
  transfers between devices with their start and end apart: 10, of which 6 were waited for; matrix products, arithmetic and copies ran while one was open for 37% of the time, Pallas kernels for 0%

profile of v3, /device:TPU:0, one launch (start us, length us, event | category | flops | bytes accessed | tf_op | source)
XLA Modules:
  0.0 177.1 jit_solution(1777768759396642152)
XLA Ops:
  1.5 4.8 %collective-permute-start = (bf16[3,4352]{1,0:T(4,128)(2,1)S(1)}, bf16[3,4352]{1,0:T(4,128)(2,1)S(1)}, u32[]{:S(2)}, u32[]{:S(2)}) collective-permute-start(bf16[3,4352]{1,0:T(4,128)(2,1)S(1)} %slice.98), channel_id=1, source_target_pairs={{0,4},{4,8},{8,12},{12,16},{16,20},{20,24},{24,28},{1,5},{5,9},{9,... | collective-permute-start | bytes 78344 | tf_op jit(solution)/shard_map/ppermute | solution.py:12
  13.1 4.4 %fusion.71 = (bf16[128,4352]{1,0:T(8,128)(2,1)}, f32[128,4352]{1,0:T(8,128)S(1)}) fusion(f32[4352]{0:T(1024)S(1)} %get-tuple-element.14, bf16[128,4352]{1,0:T(8,128)(2,1)} %param.9, f32[4352]{0:T(1024)S(1)} %get-tuple-element.15, bf16[3,4352]{1,0:T(4,128)(2,1)S(1)} %collective-permute-done, f32[4352]{0:T(1024)S(1)} %get-tuple-element.16, ...), kind=kLoop, calls=%fused_computation.139 | loop fusion | flops 12255232 | bytes 4569600 | tf_op jit(solution)/shard_map/convert.2
  18.0 2.3 %reshape_reshape.6 = bf16[2,64,64,64]{3,2,1,0:T(8,128)(2,1)S(1)} reshape(bf16[128,4096]{1,0:T(8,128)(2,1)S(1)} %multiply_convert_fusion.6) | data formatting | bytes 2097152 | tf_op jit(solution)/shard_map/reshape;reshape | solution.py:116
  22.6 4.1 %multiply_reduce_fusion.2 = (f32[64,128,64]{1,2,0:T(8,128)S(1)}, f32[2,64,128,64]{2,3,1,0:T(8,128)}) fusion(f32[2,64]{1,0:T(2,128)S(1)} %get-tuple-element.53, bf16[2,64,128,1]{2,1,3,0:T(8,128)(2,1)S(1)} %bitcast.93, bf16[2,64,64,64]{3,2,1,0:T(8,128)(2,1)S(1)} %multiply_convert_fusion.2), kind=kOutput, calls=%fused_computation.14 | convolution fusion | flops 135790592 | bytes 7373312 | tf_op jit(solution)/shard_map/vmap(sn,shp->hnp)/dot_general | solution.py:35
  28.4 4.2 %reshape_reshape.7 = bf16[2,64,64,64]{3,2,1,0:T(8,128)(2,1)} reshape(bf16[128,4096]{1,0:T(8,128)(2,1)} %param.17) | data formatting | bytes 2097152 | tf_op jit(solution)/shard_map/reshape;reshape | solution.py:118
  36.3 4.2 %copy.78 = bf16[2,64,64,64]{1,3,2,0:T(8,128)(2,1)} copy(bf16[2,64,64,64]{3,2,1,0:T(8,128)(2,1)} %copy-done.1) | data formatting | bytes 2097152 | tf_op jit(solution)/shard_map/reshape;reshape | solution.py:116
  40.6 11.9 %collective-permute-done.1 = bf16[64,128,64]{1,2,0:T(8,128)(2,1)} collective-permute-done((bf16[64,128,64]{1,2,0:T(8,128)(2,1)}, bf16[64,128,64]{1,2,0:T(8,128)(2,1)}, u32[]{:S(2)}, u32[]{:S(2)}) %collective-permute-start.1) | collective-permute-done | bytes 1048608 | tf_op jit(solution)/shard_map/ppermute | solution.py:18
  56.2 7.0 %fusion.4 = (f32[2,64,64]{1,2,0:T(8,128)S(1)}, f32[2,64]{1,0:T(2,128)S(1)}) fusion(f32[2,64]{1,0:T(2,128)S(1)} %get-tuple-element.44, f32[2,64,64]{2,1,0:T(8,128)S(1)} %copy.68, pred[64,64]{0,1:T(8,128)(4,1)S(1)} %iota_compare_fusion, f32[2,64,64]{1,2,0:T(8,128)S(1)} %fusion.75, bf16[2,64,64,64]{1,3,2,0:T(8,128)(2,1)S(1)} %copy-done.6, ...), kind=kOutput, calls=%fused_computation.11 | convolution fusion | flops 72343424 | bytes 2200576 | tf_op jit(solution)/shard_map/vmap(thp,shp->hts)/dot_general | solution.py:35
  63.4 2.8 %fusion.7 = f32[2,64,128,64]{2,3,1,0:T(8,128)S(1)} fusion(f32[2,64,64]{1,2,0:T(8,128)S(1)} %copy.75, f32[2,64,128]{2,1,0:T(8,128)S(1)} %convert_element_type.85, bf16[2,64,64,64]{3,2,1,0:T(8,128)(2,1)S(1)} %copy-done.3), kind=kOutput, calls=%fused_computation.26 | convolution fusion | flops 136314880 | bytes 5341184 | tf_op jit(solution)/shard_map/cthn,cthp->chnp/dot_general | solution.py:35
  66.3 11.8 %collective-permute-done.3 = bf16[64,128,64]{1,2,0:T(8,128)(2,1)S(1)} collective-permute-done((bf16[64,128,64]{1,2,0:T(8,128)(2,1)S(1)}, bf16[64,128,64]{1,2,0:T(8,128)(2,1)S(1)}, u32[]{:S(2)}, u32[]{:S(2)}) %collective-permute-start.3) | collective-permute-done | bytes 1048608 | tf_op jit(solution)/shard_map/ppermute | solution.py:18
  78.0 4.1 %convert_multiply_fusion.3 = (f32[64,128,64]{1,2,0:T(8,128)}, bf16[64,128,64]{1,2,0:T(8,128)(2,1)S(1)}, f32[1,64,128,64]{2,3,1,0:T(8,128)S(1)}, f32[64,128,64]{1,2,0:T(8,128)}, f32[1,64,128,64]{2,3,1,0:T(8,128)S(1)}) fusion(bf16[64,128,64]{1,2,0:T(8,128)(2,1)} %collective-permute-done.1, f32[]{:T(128)S(6)} %convert_element_type.87, ...), kind=kLoop, calls=%fused_computation.24 | loop fusion | flops 9961472 | bytes 13632784 | tf_op jit(solution)/shard_map/mul | solution.py:86
  82.1 4.7 %collective-permute-start.5 = (bf16[64,128,64]{1,2,0:T(8,128)(2,1)S(1)}, bf16[64,128,64]{1,2,0:T(8,128)(2,1)S(1)}, u32[]{:S(2)}, u32[]{:S(2)}) collective-permute-start(bf16[64,128,64]{1,2,0:T(8,128)(2,1)S(1)} %get-tuple-element.32), channel_id=1, source_target_pairs={{0,16},{4,20},{8,24},{12,28},{1,17},{5,21},{9,25},{13,29},{2,18},{... | collective-permute-start | bytes 3145736 | tf_op jit(solution)/shard_map/ppermute | solution.py:25
  88.0 3.6 %convolution_bitcast_fusion = f32[2,64,64,64]{1,3,2,0:T(8,128)} fusion(bf16[2,64,64,64]{1,3,2,0:T(8,128)(2,1)S(1)} %copy-done.6, f32[2,64]{1,0:T(2,128)S(1)} %broadcast_multiply_fusion, f32[2,64,64]{1,2,0:T(8,128)S(1)} %fusion.75, f32[2,64,64]{2,1,0:T(8,128)S(1)} %copy.68, pred[64,64]{0,1:T(8,128)(4,1)S(1)} %iota_compare_fusion), kind=kOutput, calls=%fused_computation.28 | convolution fusion | flops 70254592 | bytes 3215872 | tf_op jit(solution)/shard_map/vmap(hts,shp->thp)/dot_general | solution.py:35
  91.6 15.1 %collective-permute-done.5 = bf16[64,128,64]{1,2,0:T(8,128)(2,1)S(1)} collective-permute-done((bf16[64,128,64]{1,2,0:T(8,128)(2,1)S(1)}, bf16[64,128,64]{1,2,0:T(8,128)(2,1)S(1)}, u32[]{:S(2)}, u32[]{:S(2)}) %collective-permute-start.5) | collective-permute-done | bytes 1048608 | tf_op jit(solution)/shard_map/ppermute | solution.py:25
  108.3 3.2 %pad_maximum_fusion = f32[3,64,128,64]{2,3,1,0:T(8,128)} fusion(f32[1,64,128,64]{2,3,1,0:T(8,128)S(1)} %get-tuple-element.30, f32[1,64,128,64]{2,3,1,0:T(8,128)S(1)} %get-tuple-element.33, f32[1,64,128,64]{2,3,1,0:T(8,128)S(1)} %get-tuple-element.35), kind=kLoop, calls=%fused_computation.2 | loop fusion | flops 3145728 | bytes 12582912 | tf_op jit(solution)/shard_map/stack | solution.py:151
  111.5 4.1 %multiply_reduce_fusion = f32[2,3,64]{2,1,0:T(4,128)S(1)} fusion(f32[2,64,128,64]{2,3,1,0:T(8,128)S(1)} %fusion.7, f32[3,64,128,64]{2,3,1,0:T(8,128)} %pad_maximum_fusion), kind=kLoop, calls=%fused_computation | loop fusion | flops 6291072 | bytes 10487296 | tf_op jit(solution)/shard_map/reduce_sum | solution.py:176
  120.2 23.4 %collective-permute-start.7 = (f32[8,12,64]{2,0,1:T(8,128)S(1)}, f32[8,12,64]{2,0,1:T(8,128)S(1)}, u32[]{:S(2)}, u32[]{:S(2)}) collective-permute-start(f32[8,12,64]{2,0,1:T(8,128)S(1)} %fusion.65), channel_id=1, source_target_pairs={{0,8},{4,12},{8,0},{12,4},{16,24},{20,28},{24,16},{28,20},{1,9},{5... | collective-permute-start | bytes 73736 | tf_op jit(solution)/shard_map/ppermute | solution.py:18
  145.7 3.4 %collective-permute-start.8 = (f32[8,12,64]{2,0,1:T(8,128)S(1)}, f32[8,12,64]{2,0,1:T(8,128)S(1)}, u32[]{:S(2)}, u32[]{:S(2)}) collective-permute-start(f32[8,12,64]{2,0,1:T(8,128)S(1)} %add.113), channel_id=1, source_target_pairs={{0,16},{4,20},{8,24},{12,28},{16,0},{20,4},{24,8},{28,12},{1,17},{... | collective-permute-start | bytes 73736 | tf_op jit(solution)/shard_map/ppermute | solution.py:18
  149.1 4.4 %add_convert_fusion = bf16[2,64,128,64]{2,3,1,0:T(8,128)(2,1)S(1)} fusion(f32[64,128,64]{1,2,0:T(8,128)} %get-tuple-element.29, f32[2,64]{1,0:T(2,128)S(1)} %get-tuple-element.46, f32[64,128,64]{1,2,0:T(8,128)} %get-tuple-element.34, f32[2,64]{1,0:T(2,128)S(1)} %get-tuple-element.47, f32[64,128,64]{1,2,0:T(8,128)S(1)} %copy-done.5, ...), kind=kLoop, calls=%fused_computation.13 | loop fusion | flops 10485760 | bytes 12585472 | tf_op jit(solution)/shard_map/convert_element_type | solution.py:170
  155.5 3.4 %fusion.6 = f32[2,64,64,64]{3,2,1,0:T(8,128)} fusion(bf16[2,64,128,64]{2,3,1,0:T(8,128)(2,1)S(1)} %add_convert_fusion, f32[2,64,64]{1,2,0:T(8,128)S(1)} %copy.75, f32[2,64,128]{2,1,0:T(8,128)S(1)} %convert_element_type.85), kind=kOutput, calls=%fused_computation.25 | convolution fusion | flops 136314880 | bytes 4292608 | tf_op jit(solution)/shard_map/cthn,chnp->cthp/dot_general | solution.py:35
  160.4 2.9 %copy.80 = bf16[2,64,64,64]{1,3,2,0:T(8,128)(2,1)} copy(bf16[2,64,64,64]{3,2,1,0:T(8,128)(2,1)S(1)} %copy-done.2) | data formatting | bytes 2097152 | tf_op jit(solution)/shard_map/optimization_barrier | solution.py:189
  163.3 5.4 %fusion.2 = bf16[2,64,64,64]{1,3,2,0:T(8,128)(2,1)S(1)} fusion(f32[2,64,64,64]{1,3,2,0:T(8,128)} %convolution_bitcast_fusion, f32[2,64,64,64]{3,2,1,0:T(8,128)} %fusion.6, bf16[2,64,64,64]{1,3,2,0:T(8,128)(2,1)} %copy.80, f32[64]{0:T(128)S(1)} %copy-done.8), kind=kLoop, calls=%fused_computation.7 | loop fusion | flops 2621440 | bytes 6291712 | tf_op jit(solution)/shard_map/convert_element_type | solution.py:195
  169.3 2.9 %copy.81 = bf16[2,64,64,64]{3,2,1,0:T(8,128)(2,1)} copy(bf16[2,64,64,64]{1,3,2,0:T(8,128)(2,1)S(1)} %fusion.2) | data formatting | bytes 2097152 | tf_op jit(solution)/shard_map/convert_element_type | solution.py:195
  172.3 4.1 %reshape.123 = bf16[128,4096]{1,0:T(8,128)(2,1)} reshape(bf16[2,64,64,64]{3,2,1,0:T(8,128)(2,1)} %copy.81) | data formatting | bytes 2097152 | tf_op jit(solution)/shard_map/reshape | solution.py:196
  (84 shorter events, 33.8 us)
Async XLA Ops:
  1.5 11.5 %collective-permute-start = (bf16[3,4352]{1,0:T(4,128)(2,1)S(1)}, bf16[3,4352]{1,0:T(4,128)(2,1)S(1)}, u32[]{:S(2)}, u32[]{:S(2)}) collective-permute-start(bf16[3,4352]{1,0:T(4,128)(2,1)S(1)} %slice.98), channel_id=1, source_target_pairs={{0,4},{4,8},{8,12},{12,16},{16,20},{20,24},{24,28},{1,5},{5,9},{9,... | collective-permute-start | bytes 78344 | tf_op jit(solution)/shard_map/ppermute | solution.py:12
  8.2 24.5 %collective-permute-start.2 = (f32[64]{0:T(128)S(1)}, f32[64]{0:T(128)S(1)}, u32[]{:S(2)}, u32[]{:S(2)}) collective-permute-start(f32[64]{0:T(128)S(1)} %get-tuple-element.40), channel_id=1, source_target_pairs={{0,4},{4,0},{8,12},{12,8},{16,20},{20,16},{24,28},{28,24},{1,5},{5... | collective-permute-start | bytes 776 | tf_op jit(solution)/shard_map/ppermute | solution.py:18
  20.3 2.2 %copy-start.1 = (bf16[2,64,64,64]{3,2,1,0:T(8,128)(2,1)}, bf16[2,64,64,64]{3,2,1,0:T(8,128)(2,1)S(1)}, u32[]{:S(2)}) copy-start(bf16[2,64,64,64]{3,2,1,0:T(8,128)(2,1)S(1)} %reshape_reshape.6) | copy-start | bytes 3145732
  27.8 24.7 %collective-permute-start.1 = (bf16[64,128,64]{1,2,0:T(8,128)(2,1)}, bf16[64,128,64]{1,2,0:T(8,128)(2,1)}, u32[]{:S(2)}, u32[]{:S(2)}) collective-permute-start(bf16[64,128,64]{1,2,0:T(8,128)(2,1)} %convert_element_type.88), channel_id=1, source_target_pairs={{0,4},{4,0},{8,12},{12,8},{16,20},{20,16},{24,28},{28,24},{1,5},{5... | collective-permute-start | bytes 3145736 | tf_op jit(solution)/shard_map/ppermute | solution.py:18
  32.7 3.6 %collective-permute-start.4 = (f32[64]{0:T(128)S(1)}, f32[64]{0:T(128)S(1)}, u32[]{:S(2)}, u32[]{:S(2)}) collective-permute-start(f32[64]{0:T(128)S(1)} %get-tuple-element.20), channel_id=1, source_target_pairs={{0,8},{4,12},{8,0},{12,4},{16,24},{20,28},{24,16},{28,20},{1,9},{5... | collective-permute-start | bytes 776 | tf_op jit(solution)/shard_map/ppermute | solution.py:18
  52.5 3.7 %copy-start.3 = (bf16[2,64,64,64]{3,2,1,0:T(8,128)(2,1)S(1)}, bf16[2,64,64,64]{3,2,1,0:T(8,128)(2,1)}, u32[]{:S(2)}) copy-start(bf16[2,64,64,64]{3,2,1,0:T(8,128)(2,1)} %reshape_reshape.7) | copy-start | bytes 3145732
  52.5 3.7 %copy-start.6 = (bf16[2,64,64,64]{1,3,2,0:T(8,128)(2,1)S(1)}, bf16[2,64,64,64]{1,3,2,0:T(8,128)(2,1)}, u32[]{:S(2)}) copy-start(bf16[2,64,64,64]{1,3,2,0:T(8,128)(2,1)} %copy.78) | copy-start | bytes 3145732
  54.6 23.5 %collective-permute-start.3 = (bf16[64,128,64]{1,2,0:T(8,128)(2,1)S(1)}, bf16[64,128,64]{1,2,0:T(8,128)(2,1)S(1)}, u32[]{:S(2)}, u32[]{:S(2)}) collective-permute-start(bf16[64,128,64]{1,2,0:T(8,128)(2,1)S(1)} %fusion.68), channel_id=1, source_target_pairs={{0,8},{4,12},{8,0},{12,4},{16,24},{20,28},{24,16},{28,20},{1,9},{5... | collective-permute-start | bytes 3145736 | tf_op jit(solution)/shard_map/ppermute | solution.py:18
  56.2 7.0 %copy-start.9 = (s32[2]{0:T(128)S(1)}, s32[2]{0:T(128)}, u32[]{:S(2)}) copy-start(s32[2]{0:T(128)} %param.16) | copy-start | bytes 28
  78.0 8.8 %copy-start = (f32[2,64,128,64]{2,3,1,0:T(8,128)S(1)}, f32[2,64,128,64]{2,3,1,0:T(8,128)}, u32[]{:S(2)}) copy-start(f32[2,64,128,64]{2,3,1,0:T(8,128)} %get-tuple-element.60) | copy-start | bytes 12582916
  82.1 24.5 %collective-permute-start.5 = (bf16[64,128,64]{1,2,0:T(8,128)(2,1)S(1)}, bf16[64,128,64]{1,2,0:T(8,128)(2,1)S(1)}, u32[]{:S(2)}, u32[]{:S(2)}) collective-permute-start(bf16[64,128,64]{1,2,0:T(8,128)(2,1)S(1)} %get-tuple-element.32), channel_id=1, source_target_pairs={{0,16},{4,20},{8,24},{12,28},{1,17},{5,21},{9,25},{13,29},{2,18},{... | collective-permute-start | bytes 3145736 | tf_op jit(solution)/shard_map/ppermute | solution.py:25
  116.0 33.1 %copy-start.5 = (f32[64,128,64]{1,2,0:T(8,128)S(1)}, f32[64,128,64]{1,2,0:T(8,128)}, u32[]{:S(2)}) copy-start(f32[64,128,64]{1,2,0:T(8,128)} %get-tuple-element.31) | copy-start | bytes 6291460
  116.0 4.2 %collective-permute-start.6 = (f32[8,12,64]{2,0,1:T(8,128)S(1)}, f32[8,12,64]{2,0,1:T(8,128)S(1)}, u32[]{:S(2)}, u32[]{:S(2)}) collective-permute-start(f32[8,12,64]{2,0,1:T(8,128)S(1)} %pad_maximum_fusion.3), channel_id=1, source_target_pairs={{0,4},{4,0},{8,12},{12,8},{16,20},{20,16},{24,28},{28,24},{1,5},{5... | collective-permute-start | bytes 73736 | tf_op jit(solution)/shard_map/ppermute | solution.py:18
  120.2 25.5 %collective-permute-start.7 = (f32[8,12,64]{2,0,1:T(8,128)S(1)}, f32[8,12,64]{2,0,1:T(8,128)S(1)}, u32[]{:S(2)}, u32[]{:S(2)}) collective-permute-start(f32[8,12,64]{2,0,1:T(8,128)S(1)} %fusion.65), channel_id=1, source_target_pairs={{0,8},{4,12},{8,0},{12,4},{16,24},{20,28},{24,16},{28,20},{1,9},{5... | collective-permute-start | bytes 73736 | tf_op jit(solution)/shard_map/ppermute | solution.py:18
  145.7 7.8 %collective-permute-start.8 = (f32[8,12,64]{2,0,1:T(8,128)S(1)}, f32[8,12,64]{2,0,1:T(8,128)S(1)}, u32[]{:S(2)}, u32[]{:S(2)}) collective-permute-start(f32[8,12,64]{2,0,1:T(8,128)S(1)} %add.113), channel_id=1, source_target_pairs={{0,16},{4,20},{8,24},{12,28},{16,0},{20,4},{24,8},{28,12},{1,17},{... | collective-permute-start | bytes 73736 | tf_op jit(solution)/shard_map/ppermute | solution.py:18
  149.1 4.4 %copy-start.4 = (bf16[2,64,64,64]{3,2,1,0:T(8,128)(2,1)S(1)}, bf16[2,64,64,64]{3,2,1,0:T(8,128)(2,1)}, u32[]{:S(2)}) copy-start(bf16[2,64,64,64]{3,2,1,0:T(8,128)(2,1)} %reshape_reshape.7) | copy-start | bytes 3145732
  155.5 4.9 %copy-start.2 = (bf16[2,64,64,64]{3,2,1,0:T(8,128)(2,1)S(1)}, bf16[2,64,64,64]{3,2,1,0:T(8,128)(2,1)}, u32[]{:S(2)}) copy-start(bf16[2,64,64,64]{3,2,1,0:T(8,128)(2,1)} %copy-done.1) | copy-start | bytes 3145732
  159.0 4.3 %copy-start.8 = (f32[64]{0:T(128)S(1)}, f32[64]{0:T(128)}, u32[]{:S(2)}) copy-start(f32[64]{0:T(128)} %param.14) | copy-start | bytes 772
  159.1 17.4 %collective-permute-start.9 = (f32[3,128]{1,0:T(4,128)S(1)}, f32[3,128]{1,0:T(4,128)S(1)}, u32[]{:S(2)}, u32[]{:S(2)}) collective-permute-start(f32[3,128]{1,0:T(4,128)S(1)} %slice.146), channel_id=1, source_target_pairs={{4,0},{8,4},{12,8},{16,12},{20,16},{24,20},{28,24},{5,1},{9,5},{13... | collective-permute-start | bytes 4616 | tf_op jit(solution)/shard_map/ppermute | solution.py:12
  163.3 5.4 %copy-start.7 = (f32[8,12,64]{2,0,1:T(8,128)S(1)}, f32[8,12,64]{2,0,1:T(8,128)}, u32[]{:S(2)}) copy-start(f32[8,12,64]{2,0,1:T(8,128)} %param.15) | copy-start | bytes 73732

commit v4 on v1

--- a/solution.py
+++ b/solution.py
@@ -201,6 +201,7 @@
         grad_c_in = grad_c_in + query_taps[offset][None, :] * extended[lagged : lagged + length]
     grad_first = exact("gk,gh->kh", picked, level_zero)
     local_grads = jnp.concatenate([grad_first[:, None, :], grads], axis=1)
+    local_grads, ssm_out, grad_c_in = lax.optimization_barrier((local_grads, ssm_out, grad_c_in))
     summed = all_sum(local_grads, "seq")
     level_update = level_table + summed / math.sqrt(length * devices)
     return (ssm_out, grad_c_in, level_update)

time: 165 us -> 172 us (1.042)
  matrix products: 23.2 us -> 27.8 us
  waiting for transfers between devices: 39.4 us -> 43.8 us
  local copies, waits for them, and re-layouts: 28.8 us -> 24.6 us
  starting transfers between devices: 44.7 us -> 46.5 us
    mul x1 -> x3, other arithmetic: 0.59 us -> 6.18 us  [combine(): found = grown * jnp.exp(leading)[..., None, None] * other]
    another operation x3 -> x1, other arithmetic: 6.49 us -> 0.93 us  [local(): cross = jnp.stack(found_all, axis=0)]
    dot_general x6, matrix products: 20.5 us -> 25.1 us  [contract(): return jnp.einsum(form, left, right, preferred_element_type=jnp.float32)]
    ppermute x7, waiting for transfers between devices: 25.7 us -> 30 us  [from_partner(): return lax.ppermute(value, axis, pairs)]
    another operation x2 -> x1, local copies, waits for them, and re-layouts: 8.45 us -> 4.27 us  [local(): grad_groups = grad_out.reshape(groups, group_len, heads, head_dim)]
    ppermute x7, starting transfers between devices: 33.9 us -> 35.9 us  [from_partner(): return lax.ppermute(value, axis, pairs)]
  transfers between devices with their start and end apart: 10 -> 10, of which waited for: 5 -> 7; matrix products, arithmetic and copies ran while one was open for 41% -> 35% of each run, Pallas kernels for 0% -> 0%
where the time goes in v4:
time: 172 us; the launch traced here: 171 us
  starting transfers between devices  46.5 us (27%)
  waiting for transfers between devices  43.8 us (25%)
  matrix products  27.8 us (16%)
  other arithmetic  27 us (16%)
  local copies, waits for them, and re-layouts  24.6 us (14%)
    ppermute x7, starting transfers between devices, from_partner(): return lax.ppermute(value, axis, pairs)  35.9 us
    ppermute x7, waiting for transfers between devices, from_partner(): return lax.ppermute(value, axis, pairs)  30 us
    dot_general x6, matrix products, contract(): return jnp.einsum(form, left, right, preferred_element_type=jnp.float32)  25.1 us
    ppermute x1, waiting for transfers between devices, upward(): return lax.ppermute(value, axis, pairs)  13.8 us
    mul x3, other arithmetic, combine(): found = grown * jnp.exp(leading)[..., None, None] * other  6.18 us
    ppermute x2, starting transfers between devices, shifted(): lax.ppermute(value, axis, [(source, source + steps) for source in range(l...  6.14 us
    another operation x2, local copies, waits for them, and re-layouts, local(): x_groups = x_act.reshape(groups, group_len, heads, head_dim)  5.27 us
    convert_element_type x1, other arithmetic, local(): mixed = sum(terms[1:], terms[0]).astype(jnp.bfloat16)  4.98 us
  transfers between devices with their start and end apart: 10, of which 7 were waited for; matrix products, arithmetic and copies ran while one was open for 35% of the time, Pallas kernels for 0%

profile of v4, /device:TPU:0, one launch (start us, length us, event | category | flops | bytes accessed | tf_op | source)
XLA Modules:
  0.0 170.9 jit_solution(1255186373421627415)
XLA Ops:
  1.5 4.8 %collective-permute-start = (bf16[3,4352]{1,0:T(4,128)(2,1)S(1)}, bf16[3,4352]{1,0:T(4,128)(2,1)S(1)}, u32[]{:S(2)}, u32[]{:S(2)}) collective-permute-start(bf16[3,4352]{1,0:T(4,128)(2,1)S(1)} %slice.98), channel_id=1, source_target_pairs={{0,4},{4,8},{8,12},{12,16},{16,20},{20,24},{24,28},{1,5},{5,9},{9,... | collective-permute-start | bytes 78344 | tf_op jit(solution)/shard_map/ppermute | solution.py:12
  14.8 4.4 %fusion.73 = (bf16[128,4352]{1,0:T(8,128)(2,1)}, f32[128,4352]{1,0:T(8,128)S(1)}) fusion(f32[4352]{0:T(1024)S(1)} %get-tuple-element.12, bf16[128,4352]{1,0:T(8,128)(2,1)} %param.9, f32[4352]{0:T(1024)S(1)} %get-tuple-element.13, bf16[3,4352]{1,0:T(4,128)(2,1)S(1)} %collective-permute-done, f32[4352]{0:T(1024)S(1)} %get-tuple-element.14, ...), kind=kLoop, calls=%fused_computation.139 | loop fusion | flops 12255232 | bytes 4569600 | tf_op jit(solution)/shard_map/convert.2
  19.8 2.3 %reshape_reshape.6 = bf16[2,64,64,64]{3,2,1,0:T(8,128)(2,1)S(1)} reshape(bf16[128,4096]{1,0:T(8,128)(2,1)S(1)} %multiply_convert_fusion.5) | data formatting | bytes 2097152 | tf_op jit(solution)/shard_map/reshape;reshape | solution.py:116
  22.0 3.0 %copy.74 = bf16[2,64,64,64]{1,3,2,0:T(8,128)(2,1)} copy(bf16[2,64,64,64]{3,2,1,0:T(8,128)(2,1)S(1)} %reshape_reshape.6) | data formatting | bytes 2097152 | tf_op jit(solution)/shard_map/reshape;reshape | solution.py:116
  25.8 4.4 %multiply_reduce_fusion.2 = (f32[64,128,64]{1,2,0:T(8,128)S(1)}, f32[2,64,128,64]{2,3,1,0:T(8,128)}) fusion(f32[2,64]{1,0:T(2,128)S(1)} %get-tuple-element.51, bf16[2,64,128,1]{2,1,3,0:T(8,128)(2,1)S(1)} %bitcast.87, bf16[2,64,64,64]{1,3,2,0:T(8,128)(2,1)} %copy.74, f32[2,64,64]{1,2,0:T(8,128)S(1)} %copy.75), kind=kOutput, calls=%fused_computation.16 | convolution fusion | flops 137363456 | bytes 7406080 | tf_op jit(solution)/shard_map/vmap(sn,shp->hnp)/dot_general | solution.py:35
  32.6 4.3 %reshape_reshape.7 = bf16[2,64,64,64]{3,2,1,0:T(8,128)(2,1)} reshape(bf16[128,4096]{1,0:T(8,128)(2,1)} %param.17) | data formatting | bytes 2097152 | tf_op jit(solution)/shard_map/reshape;reshape | solution.py:118
  41.2 14.8 %collective-permute-done.1 = bf16[64,128,64]{1,2,0:T(8,128)(2,1)S(1)} collective-permute-done((bf16[64,128,64]{1,2,0:T(8,128)(2,1)}, bf16[64,128,64]{1,2,0:T(8,128)(2,1)S(1)}, u32[]{:S(2)}, u32[]{:S(2)}) %collective-permute-start.1) | collective-permute-done | bytes 1048608 | tf_op jit(solution)/shard_map/ppermute | solution.py:18
  59.2 7.6 %fusion.5 = (f32[2,64,64]{1,2,0:T(8,128)}, f32[2,64]{1,0:T(2,128)}) fusion(f32[2,64]{1,0:T(2,128)S(1)} %copy-done.18, f32[2,64,64]{2,1,0:T(8,128)S(1)} %copy.68, pred[64,64]{0,1:T(8,128)(4,1)S(1)} %iota_compare_fusion, f32[2,64,64]{1,2,0:T(8,128)S(1)} %fusion.77, bf16[2,64,64,64]{1,3,2,0:T(8,128)(2,1)S(1)} %copy-done.1, ...), kind=kOutput, calls=%fused_computation.13 | convolution fusion | flops 72343424 | bytes 2200576 | tf_op jit(solution)/shard_map/vmap(thp,shp->hts)/dot_general | solution.py:35
  68.7 4.4 %fusion.8 = f32[2,64,128,64]{2,3,1,0:T(8,128)S(1)} fusion(f32[2,64,64]{1,2,0:T(8,128)S(1)} %copy.76, f32[2,64,128]{2,1,0:T(8,128)S(1)} %convert_element_type.83, bf16[2,64,64,64]{3,2,1,0:T(8,128)(2,1)} %reshape_reshape.7), kind=kOutput, calls=%fused_computation.27 | convolution fusion | flops 136314880 | bytes 5341184 | tf_op jit(solution)/shard_map/cthn,cthp->chnp/dot_general | solution.py:35
  74.1 7.3 %collective-permute-done.3 = bf16[64,128,64]{1,2,0:T(8,128)(2,1)} collective-permute-done((bf16[64,128,64]{1,2,0:T(8,128)(2,1)}, bf16[64,128,64]{1,2,0:T(8,128)(2,1)}, u32[]{:S(2)}, u32[]{:S(2)}) %collective-permute-start.3) | collective-permute-done | bytes 1048608 | tf_op jit(solution)/shard_map/ppermute | solution.py:18
  81.4 3.9 %convert_multiply_fusion.5 = (f32[64,128,64]{1,2,0:T(8,128)}, bf16[64,128,64]{1,2,0:T(8,128)(2,1)S(1)}, f32[1,64,128,64]{2,3,1,0:T(8,128)S(1)}, f32[64,128,64]{1,2,0:T(8,128)}, f32[1,64,128,64]{2,3,1,0:T(8,128)S(1)}) fusion(bf16[64,128,64]{1,2,0:T(8,128)(2,1)S(1)} %collective-permute-done.1, f32[]{:T(128)S(6)} %convert_element_type.85, f32[64]{0:T(128)S(1)} %copy-done.11, ...), kind=kLoop, calls=%fused_computation.25 | loop fusion | flops 9961472 | bytes 13632784 | tf_op jit(solution)/shard_map/mul | solution.py:86
  85.3 4.5 %collective-permute-start.5 = (bf16[64,128,64]{1,2,0:T(8,128)(2,1)S(1)}, bf16[64,128,64]{1,2,0:T(8,128)(2,1)S(1)}, u32[]{:S(2)}, u32[]{:S(2)}) collective-permute-start(bf16[64,128,64]{1,2,0:T(8,128)(2,1)S(1)} %get-tuple-element.30), channel_id=1, source_target_pairs={{0,16},{4,20},{8,24},{12,28},{1,17},{5,21},{9,25},{13,29},{2,18},{... | collective-permute-start | bytes 3145736 | tf_op jit(solution)/shard_map/ppermute | solution.py:25
  90.1 2.2 %slice_bitcast_fusion.1 = (f32[64,128,64]{1,2,0:T(8,128)}, f32[64,128,64]{1,2,0:T(8,128)}) fusion(f32[2,64,128,64]{2,3,1,0:T(8,128)S(1)} %copy-done), kind=kLoop, calls=%fused_computation.41 | loop fusion | bytes 8388608 | tf_op jit(solution)/shard_map/mul | solution.py:168
  92.4 3.6 %fusion.9 = f32[2,64,64,64]{3,2,1,0:T(8,128)} fusion(bf16[2,64,64,64]{1,3,2,0:T(8,128)(2,1)S(1)} %copy-done.2, f32[2,64]{1,0:T(2,128)S(1)} %copy-done.17, f32[2,64,64]{1,2,0:T(8,128)S(1)} %fusion.77, f32[2,64,64]{2,1,0:T(8,128)S(1)} %copy.68, pred[64,64]{0,1:T(8,128)(4,1)S(1)} %iota_compare_fusion), kind=kOutput, calls=%fused_computation.30 | convolution fusion | flops 70254592 | bytes 3215872 | tf_op jit(solution)/shard_map/vmap(hts,shp->thp)/dot_general | solution.py:35
  96.0 13.8 %collective-permute-done.5 = bf16[64,128,64]{1,2,0:T(8,128)(2,1)S(1)} collective-permute-done((bf16[64,128,64]{1,2,0:T(8,128)(2,1)S(1)}, bf16[64,128,64]{1,2,0:T(8,128)(2,1)S(1)}, u32[]{:S(2)}, u32[]{:S(2)}) %collective-permute-start.5) | collective-permute-done | bytes 1048608 | tf_op jit(solution)/shard_map/ppermute | solution.py:25
  114.4 5.0 %add_convert_fusion = bf16[2,64,128,64]{2,3,1,0:T(8,128)(2,1)S(1)} fusion(f32[64,128,64]{1,2,0:T(8,128)} %get-tuple-element.27, f32[2,64]{1,0:T(2,128)S(1)} %get-tuple-element.44, f32[64,128,64]{1,2,0:T(8,128)} %get-tuple-element.32, f32[2,64]{1,0:T(2,128)S(1)} %get-tuple-element.45, f32[64,128,64]{1,2,0:T(8,128)} %get-tuple-element.29, ...), kind=kLoop, calls=%fused_computation.14 | loop fusion | flops 10485760 | bytes 12585472 | tf_op jit(solution)/shard_map/convert_element_type | solution.py:170
  122.9 3.2 %fusion.2 = bf16[2,64,64,64]{1,3,2,0:T(8,128)(2,1)} fusion(bf16[2,64,64,64]{1,3,2,0:T(8,128)(2,1)S(1)} %copy-done.3, f32[2,64,64,64]{3,2,1,0:T(8,128)S(1)} %copy-done.6, f32[64]{0:T(128)S(1)} %copy-done.9, bf16[2,64,128,64]{2,3,1,0:T(8,128)(2,1)S(1)} %add_convert_fusion, f32[2,64,64]{1,2,0:T(8,128)S(1)} %copy.76, f32[2,64,128]{2,1,0:T(8,128)S(1)} %convert_element_type.83), kind=kOutput, calls=%fused_computation.7 | convolution fusion | flops 138936320 | bytes 6390016 | tf_op jit(solution)/shard_map/cthn,chnp->cthp/dot_general | solution.py:35
  126.4 3.3 %copy.81 = bf16[2,64,64,64]{3,2,1,0:T(8,128)(2,1)S(1)} copy(bf16[2,64,64,64]{1,3,2,0:T(8,128)(2,1)} %fusion.2) | data formatting | bytes 2097152 | tf_op jit(solution)/shard_map/convert_element_type | solution.py:191
  129.8 2.5 %reshape.123 = bf16[128,4096]{1,0:T(8,128)(2,1)} reshape(bf16[2,64,64,64]{3,2,1,0:T(8,128)(2,1)S(1)} %copy.81) | data formatting | bytes 2097152 | tf_op jit(solution)/shard_map/reshape | solution.py:192
  132.9 17.6 %collective-permute-start.7 = (f32[8,12,64]{2,0,1:T(8,128)S(1)}, f32[8,12,64]{2,0,1:T(8,128)S(1)}, u32[]{:S(2)}, u32[]{:S(2)}) collective-permute-start(f32[8,12,64]{2,0,1:T(8,128)S(1)} %pad_maximum_fusion.3), channel_id=1, source_target_pairs={{0,4},{4,0},{8,12},{12,8},{16,20},{20,16},{24,28},{28,24},{1,5},{5... | collective-permute-start | bytes 73736 | tf_op jit(solution)/shard_map/ppermute | solution.py:18
  152.6 8.4 %collective-permute-start.8 = (f32[8,12,64]{2,0,1:T(8,128)S(1)}, f32[8,12,64]{2,0,1:T(8,128)S(1)}, u32[]{:S(2)}, u32[]{:S(2)}) collective-permute-start(f32[8,12,64]{2,0,1:T(8,128)S(1)} %add.126), channel_id=1, source_target_pairs={{0,8},{4,12},{8,0},{12,4},{16,24},{20,28},{24,16},{28,20},{1,9},{5... | collective-permute-start | bytes 73736 | tf_op jit(solution)/shard_map/ppermute | solution.py:18
  161.1 2.1 %collective-permute-done.8 = f32[8,12,64]{2,0,1:T(8,128)S(1)} collective-permute-done((f32[8,12,64]{2,0,1:T(8,128)S(1)}, f32[8,12,64]{2,0,1:T(8,128)S(1)}, u32[]{:S(2)}, u32[]{:S(2)}) %collective-permute-start.8) | collective-permute-done | bytes 24608 | tf_op jit(solution)/shard_map/ppermute | solution.py:18
  163.1 4.5 %collective-permute-start.9 = (f32[8,12,64]{2,0,1:T(8,128)S(1)}, f32[8,12,64]{2,0,1:T(8,128)S(1)}, u32[]{:S(2)}, u32[]{:S(2)}) collective-permute-start(f32[8,12,64]{2,0,1:T(8,128)S(1)} %add.127), channel_id=1, source_target_pairs={{0,16},{4,20},{8,24},{12,28},{16,0},{20,4},{24,8},{28,12},{1,17},{... | collective-permute-start | bytes 73736 | tf_op jit(solution)/shard_map/ppermute | solution.py:18
  167.6 2.6 %collective-permute-done.9 = f32[8,12,64]{2,0,1:T(8,128)S(1)} collective-permute-done((f32[8,12,64]{2,0,1:T(8,128)S(1)}, f32[8,12,64]{2,0,1:T(8,128)S(1)}, u32[]{:S(2)}, u32[]{:S(2)}) %collective-permute-start.9) | collective-permute-done | bytes 24608 | tf_op jit(solution)/shard_map/ppermute | solution.py:18
  (109 shorter events, 35.3 us)
Async XLA Ops:
  1.5 13.3 %collective-permute-start = (bf16[3,4352]{1,0:T(4,128)(2,1)S(1)}, bf16[3,4352]{1,0:T(4,128)(2,1)S(1)}, u32[]{:S(2)}, u32[]{:S(2)}) collective-permute-start(bf16[3,4352]{1,0:T(4,128)(2,1)S(1)} %slice.98), channel_id=1, source_target_pairs={{0,4},{4,8},{8,12},{12,16},{16,20},{20,24},{24,28},{1,5},{5,9},{9,... | collective-permute-start | bytes 78344 | tf_op jit(solution)/shard_map/ppermute | solution.py:12
  8.2 28.7 %collective-permute-start.2 = (f32[64]{0:T(128)S(1)}, f32[64]{0:T(128)S(1)}, u32[]{:S(2)}, u32[]{:S(2)}) collective-permute-start(f32[64]{0:T(128)S(1)} %get-tuple-element.38), channel_id=1, source_target_pairs={{0,4},{4,0},{8,12},{12,8},{16,20},{20,16},{24,28},{28,24},{1,5},{5... | collective-permute-start | bytes 776 | tf_op jit(solution)/shard_map/ppermute | solution.py:18
  9.8 9.4 %copy-start.19 = (pred[2,2]{1,0:T(4,128)(4,1)}, pred[2,2]{1,0:T(4,128)(4,1)S(1)}, u32[]{:S(2)}) copy-start(pred[2,2]{1,0:T(4,128)(4,1)S(1)} %get-tuple-element.59) | copy-start | bytes 16
  10.9 8.3 %copy-start.8 = (f32[2,12,64]{2,0,1:T(2,128)}, f32[2,12,64]{2,0,1:T(2,128)S(1)}, u32[]{:S(2)}) copy-start(f32[2,12,64]{2,0,1:T(2,128)S(1)} %fusion.56) | copy-start | bytes 18436
  31.4 24.5 %collective-permute-start.1 = (bf16[64,128,64]{1,2,0:T(8,128)(2,1)}, bf16[64,128,64]{1,2,0:T(8,128)(2,1)S(1)}, u32[]{:S(2)}, u32[]{:S(2)}) collective-permute-start(bf16[64,128,64]{1,2,0:T(8,128)(2,1)} %convert_element_type.86), channel_id=1, source_target_pairs={{0,4},{4,0},{8,12},{12,8},{16,20},{20,16},{24,28},{28,24},{1,5},{5... | collective-permute-start | bytes 3145736 | tf_op jit(solution)/shard_map/ppermute | solution.py:18
  36.9 3.6 %collective-permute-start.4 = (f32[64]{0:T(128)S(1)}, f32[64]{0:T(128)S(1)}, u32[]{:S(2)}, u32[]{:S(2)}) collective-permute-start(f32[64]{0:T(128)S(1)} %get-tuple-element.18), channel_id=1, source_target_pairs={{0,8},{4,12},{8,0},{12,4},{16,24},{20,28},{24,16},{28,20},{1,9},{5... | collective-permute-start | bytes 776 | tf_op jit(solution)/shard_map/ppermute | solution.py:18
  57.6 23.7 %collective-permute-start.3 = (bf16[64,128,64]{1,2,0:T(8,128)(2,1)}, bf16[64,128,64]{1,2,0:T(8,128)(2,1)}, u32[]{:S(2)}, u32[]{:S(2)}) collective-permute-start(bf16[64,128,64]{1,2,0:T(8,128)(2,1)} %fusion.70), channel_id=1, source_target_pairs={{0,8},{4,12},{8,0},{12,4},{16,24},{20,28},{24,16},{28,20},{1,9},{5... | collective-permute-start | bytes 3145736 | tf_op jit(solution)/shard_map/ppermute | solution.py:18
  68.7 4.4 %copy-start = (f32[2,64,128,64]{2,3,1,0:T(8,128)S(1)}, f32[2,64,128,64]{2,3,1,0:T(8,128)}, u32[]{:S(2)}) copy-start(f32[2,64,128,64]{2,3,1,0:T(8,128)} %get-tuple-element.58) | copy-start | bytes 12582916
  73.1 8.2 %copy-start.10 = (f32[64]{0:T(128)S(1)}, f32[64]{0:T(128)}, u32[]{:S(2)}) copy-start(f32[64]{0:T(128)} %get-tuple-element.52) | copy-start | bytes 772
  73.1 8.2 %copy-start.11 = (f32[64]{0:T(128)S(1)}, f32[64]{0:T(128)}, u32[]{:S(2)}) copy-start(f32[64]{0:T(128)} %get-tuple-element.54) | copy-start | bytes 772
  81.4 8.5 %copy-start.20 = (pred[2,2]{1,0:T(4,128)(4,1)S(1)}, pred[2,2]{1,0:T(4,128)(4,1)}, u32[]{:S(2)}) copy-start(pred[2,2]{1,0:T(4,128)(4,1)} %copy-done.19) | copy-start | bytes 16
  81.4 8.5 %copy-start.23 = (pred[2,2,1]{1,0,2:T(4,128)(4,1)S(1)}, pred[2,2,1]{1,0,2:T(4,128)(4,1)}, u32[]{:S(2)}) copy-start(pred[2,2,1]{1,0,2:T(4,128)(4,1)} %fusion.64) | copy-start | bytes 16
  85.3 24.5 %collective-permute-start.5 = (bf16[64,128,64]{1,2,0:T(8,128)(2,1)S(1)}, bf16[64,128,64]{1,2,0:T(8,128)(2,1)S(1)}, u32[]{:S(2)}, u32[]{:S(2)}) collective-permute-start(bf16[64,128,64]{1,2,0:T(8,128)(2,1)S(1)} %get-tuple-element.30), channel_id=1, source_target_pairs={{0,16},{4,20},{8,24},{12,28},{1,17},{5,21},{9,25},{13,29},{2,18},{... | collective-permute-start | bytes 3145736 | tf_op jit(solution)/shard_map/ppermute | solution.py:25
  92.4 17.4 %copy-start.16 = (f32[64]{0:T(128)S(1)}, f32[64]{0:T(128)}, u32[]{:S(2)}) copy-start(f32[64]{0:T(128)} %get-tuple-element.53) | copy-start | bytes 772
  114.4 5.0 %copy-start.5 = (bf16[2,64,64,64]{3,2,1,0:T(8,128)(2,1)S(1)}, bf16[2,64,64,64]{3,2,1,0:T(8,128)(2,1)}, u32[]{:S(2)}) copy-start(bf16[2,64,64,64]{3,2,1,0:T(8,128)(2,1)} %reshape_reshape.7) | copy-start | bytes 3145732
  119.4 3.5 %copy-start.3 = (bf16[2,64,64,64]{1,3,2,0:T(8,128)(2,1)S(1)}, bf16[2,64,64,64]{1,3,2,0:T(8,128)(2,1)}, u32[]{:S(2)}) copy-start(bf16[2,64,64,64]{1,3,2,0:T(8,128)(2,1)} %copy.74) | copy-start | bytes 3145732
  119.4 3.5 %copy-start.6 = (f32[2,64,64,64]{3,2,1,0:T(8,128)S(1)}, f32[2,64,64,64]{3,2,1,0:T(8,128)}, u32[]{:S(2)}) copy-start(f32[2,64,64,64]{3,2,1,0:T(8,128)} %fusion.9) | copy-start | bytes 6291460
  121.6 4.5 %copy-start.21 = (s32[2]{0:T(128)S(1)}, s32[2]{0:T(128)}, u32[]{:S(2)}) copy-start(s32[2]{0:T(128)} %param.16) | copy-start | bytes 28
  121.6 4.5 %copy-start.22 = (f32[11]{0:T(128)S(1)}, f32[11]{0:T(128)}, u32[]{:S(2)}) copy-start(f32[11]{0:T(128)} %pad.6.clone) | copy-start | bytes 136
  121.6 10.7 %collective-permute-start.6 = (f32[3,128]{1,0:T(4,128)S(1)}, f32[3,128]{1,0:T(4,128)S(1)}, u32[]{:S(2)}, u32[]{:S(2)}) collective-permute-start(f32[3,128]{1,0:T(4,128)S(1)} %slice.146), channel_id=1, source_target_pairs={{4,0},{8,4},{12,8},{16,12},{20,16},{24,20},{28,24},{5,1},{9,5},{13... | collective-permute-start | bytes 4616 | tf_op jit(solution)/shard_map/ppermute | solution.py:12
  129.7 40.5 %copy-start.7 = (f32[8,12,64]{2,0,1:T(8,128)S(1)}, f32[8,12,64]{2,0,1:T(8,128)}, u32[]{:S(2)}) copy-start(f32[8,12,64]{2,0,1:T(8,128)} %param.15) | copy-start | bytes 73732
  132.9 19.7 %collective-permute-start.7 = (f32[8,12,64]{2,0,1:T(8,128)S(1)}, f32[8,12,64]{2,0,1:T(8,128)S(1)}, u32[]{:S(2)}, u32[]{:S(2)}) collective-permute-start(f32[8,12,64]{2,0,1:T(8,128)S(1)} %pad_maximum_fusion.3), channel_id=1, source_target_pairs={{0,4},{4,0},{8,12},{12,8},{16,20},{20,16},{24,28},{28,24},{1,5},{5... | collective-permute-start | bytes 73736 | tf_op jit(solution)/shard_map/ppermute | solution.py:18
  152.6 10.5 %collective-permute-start.8 = (f32[8,12,64]{2,0,1:T(8,128)S(1)}, f32[8,12,64]{2,0,1:T(8,128)S(1)}, u32[]{:S(2)}, u32[]{:S(2)}) collective-permute-start(f32[8,12,64]{2,0,1:T(8,128)S(1)} %add.126), channel_id=1, source_target_pairs={{0,8},{4,12},{8,0},{12,4},{16,24},{20,28},{24,16},{28,20},{1,9},{5... | collective-permute-start | bytes 73736 | tf_op jit(solution)/shard_map/ppermute | solution.py:18
  163.1 7.1 %collective-permute-start.9 = (f32[8,12,64]{2,0,1:T(8,128)S(1)}, f32[8,12,64]{2,0,1:T(8,128)S(1)}, u32[]{:S(2)}, u32[]{:S(2)}) collective-permute-start(f32[8,12,64]{2,0,1:T(8,128)S(1)} %add.127), channel_id=1, source_target_pairs={{0,16},{4,20},{8,24},{12,28},{16,0},{20,4},{24,8},{28,12},{1,17},{... | collective-permute-start | bytes 73736 | tf_op jit(solution)/shard_map/ppermute | solution.py:18
  (10 other events, 28.0 us)

commit v5 on v1

--- a/solution.py
+++ b/solution.py
@@ -90,6 +90,37 @@
     return (joined, block_decay + other_decay, leading + upper * other_decay, found)
 
 
+def relay(value, axis, bit_pos):
+    half = 2**bit_pos
+    step = half // 2
+    first = lax.ppermute(value, axis, [(source, source + step) for source in range(half - step, half)])
+    second = lax.ppermute(first, axis, [(source, source + step) for source in range(half, half + step)])
+    return first + second
+
+
+def exchange(block, block_decay, depth, myself):
+    leading = jnp.zeros_like(block_decay)
+    found_all = []
+    for bit_pos in range(depth):
+        if bit_pos == depth - 1:
+            if bit_pos == 0:
+                sent = upward(block.astype(jnp.bfloat16), "seq", bit_pos)
+            else:
+                sent = relay(block.astype(jnp.bfloat16), "seq", bit_pos)
+            other, other_decay = (sent.astype(jnp.float32), jnp.zeros_like(block_decay))
+        else:
+            sent, other_decay = from_partner((block.astype(jnp.bfloat16), block_decay), "seq", bit_pos)
+            other = sent.astype(jnp.float32)
+        upper = jnp.zeros_like(block_decay) + (jnp.right_shift(myself, bit_pos) & 1).astype(
+            jnp.float32
+        )
+        block, block_decay, leading, found = combine(
+            block, block_decay, other, other_decay, leading, upper
+        )
+        found_all.append(found)
+    return jnp.stack(found_all, axis=0)
+
+
 def local(
     xbc_in, conv_weight, conv_bias, dt_raw, decay_rate, skip, level_table, group_class, cotangent
 ):
@@ -131,24 +162,13 @@
     devices = lax.axis_size("seq")
     depth = devices.bit_length() - 1
     myself = lax.axis_index("seq")
-    block, block_decay = (dev_state, dev_decay)
-    leading = jnp.zeros_like(dev_decay)
-    found_all = []
-    for bit_pos in range(depth):
-        if bit_pos == depth - 1:
-            sent = upward(block.astype(jnp.bfloat16), "seq", bit_pos)
-            other, other_decay = (sent.astype(jnp.float32), jnp.zeros_like(block_decay))
-        else:
-            sent, other_decay = from_partner((block.astype(jnp.bfloat16), block_decay), "seq", bit_pos)
-            other = sent.astype(jnp.float32)
-        upper = jnp.zeros_like(dev_decay) + (jnp.right_shift(myself, bit_pos) & 1).astype(
-            jnp.float32
-        )
-        block, block_decay, leading, found = combine(
-            block, block_decay, other, other_decay, leading, upper
-        )
-        found_all.append(found)
-    cross = jnp.stack(found_all, axis=0)
+    chunks = 2 if heads % 2 == 0 else 1
+    width = heads // chunks
+    pieces = [
+        exchange(dev_state[k * width : (k + 1) * width], dev_decay[k * width : (k + 1) * width], depth, myself)
+        for k in range(chunks)
+    ]
+    cross = jnp.concatenate(pieces, axis=1)
     low_levels = groups.bit_length() - 1
     local_ids = jnp.arange(groups, dtype=jnp.int32)
     differ = jnp.bitwise_xor(local_ids[:, None], local_ids[None, :])

time: 165 us -> 141 us (0.85)
  waiting for transfers between devices: 39.4 us -> 22.5 us
  matrix products: 23.2 us -> 14.9 us
  starting transfers between devices: 44.7 us -> 47.7 us
  other arithmetic: 27 us -> 24.1 us
    ppermute x1 -> x4, waiting for transfers between devices: 13.6 us -> 0.01 us  [the longest x2 0.01 us: relay(): lax.ppermute(first, axis, [(source, source + step) for source in range(ha...]
    dot_general x6, matrix products: 20.5 us -> 12.9 us  [contract(): return jnp.einsum(form, left, right, preferred_element_type=jnp.float32)]
    ppermute x7 -> x11, starting transfers between devices: 33.9 us -> 39.6 us  [from_partner(): return lax.ppermute(value, axis, pairs)]
    another operation x4, other arithmetic: 10.9 us -> 5.56 us  [the longest x3 6.49 us: local(): cross = jnp.stack(found_all, axis=0)]
    convert_element_type x1, other arithmetic: 4.99 us -> 1.7 us  [local(): mixed = sum(terms[1:], terms[0]).astype(jnp.bfloat16)]
    ppermute x7 -> x11, waiting for transfers between devices: 25.7 us -> 22.5 us  [from_partner(): return lax.ppermute(value, axis, pairs)]
    concatenate x0 -> x1, other arithmetic: none -> 2.67 us  [local(): cross = jnp.concatenate(pieces, axis=1)]
    another operation x2, local copies, waits for them, and re-layouts: 8.45 us -> 6.22 us  [local(): grad_groups = grad_out.reshape(groups, group_len, heads, head_dim)]
  transfers between devices with their start and end apart: 10 -> 17, of which waited for: 5 -> 8; matrix products, arithmetic and copies ran while one was open for 41% -> 35% of each run, Pallas kernels for 0% -> 0%
where the time goes in v5:
time: 141 us; the launch traced here: 140 us
  starting transfers between devices  47.7 us (34%)
  local copies, waits for them, and re-layouts  29.4 us (21%)
  other arithmetic  24.1 us (17%)
  waiting for transfers between devices  22.5 us (16%)
  matrix products  14.9 us (11%)
    ppermute x11, starting transfers between devices, from_partner(): return lax.ppermute(value, axis, pairs)  39.6 us
    ppermute x11, waiting for transfers between devices, from_partner(): return lax.ppermute(value, axis, pairs)  22.5 us
    dot_general x6, matrix products, contract(): return jnp.einsum(form, left, right, preferred_element_type=jnp.float32)  12.9 us
    another operation x2, local copies, waits for them, and re-layouts, local(): x_groups = x_act.reshape(groups, group_len, heads, head_dim)  6.58 us
    another operation x2, local copies, waits for them, and re-layouts, local(): grad_groups = grad_out.reshape(groups, group_len, heads, head_dim)  6.22 us
    ppermute x2, starting transfers between devices, shifted(): lax.ppermute(value, axis, [(source, source + steps) for source in range(l...  5.19 us
    another operation x1, other arithmetic  3.46 us
    convert_element_type x1, local copies, waits for them, and re-layouts, local(): ssm_out = (y_inner + y_cross + skip[None, None, :, None] * x_groups).asty...  3.31 us
  transfers between devices with their start and end apart: 17, of which 8 were waited for; matrix products, arithmetic and copies ran while one was open for 35% of the time, Pallas kernels for 0%

profile of v5, /device:TPU:0, one launch (start us, length us, event | category | flops | bytes accessed | tf_op | source)
XLA Modules:
  0.0 139.9 jit_solution(17578909569985097479)
XLA Ops:
  3.5 2.9 %collective-permute-start.2 = (f32[32]{0:T(128)}, f32[32]{0:T(128)}, u32[]{:S(2)}, u32[]{:S(2)}) collective-permute-start(f32[32]{0:T(128)} %get-tuple-element.61), channel_id=1, source_target_pairs={{0,4},{4,0},{8,12},{12,8},{16,20},{20,16},{24,28},{28,24},{1,5},{5... | collective-permute-start | bytes 392 | tf_op jit(solution)/shard_map/ppermute | solution.py:18
  7.4 3.9 %collective-permute-start = (bf16[3,4352]{1,0:T(4,128)(2,1)S(1)}, bf16[3,4352]{1,0:T(4,128)(2,1)S(1)}, u32[]{:S(2)}, u32[]{:S(2)}) collective-permute-start(bf16[3,4352]{1,0:T(4,128)(2,1)S(1)} %slice.119), channel_id=1, source_target_pairs={{0,4},{4,8},{8,12},{12,16},{16,20},{20,24},{24,28},{1,5},{5,9},{9,... | collective-permute-start | bytes 78344 | tf_op jit(solution)/shard_map/ppermute | solution.py:12
  18.1 3.3 %reshape_reshape.7 = bf16[2,64,64,64]{3,2,1,0:T(8,128)(2,1)S(1)} reshape(bf16[128,4096]{1,0:T(8,128)(2,1)} %param.17) | data formatting | bytes 2097152 | tf_op jit(solution)/shard_map/reshape;reshape | solution.py:149
  21.4 3.0 %copy.82 = bf16[2,64,64,64]{1,3,2,0:T(8,128)(2,1)} copy(bf16[2,64,64,64]{3,2,1,0:T(8,128)(2,1)S(1)} %reshape_reshape.7) | data formatting | bytes 2097152 | tf_op jit(solution)/shard_map/reshape;reshape | solution.py:149
  25.1 3.5 %fusion.81 = (bf16[128,4352]{1,0:T(8,128)(2,1)S(1)}, f32[128,4352]{1,0:T(8,128)S(1)}) fusion(f32[4352]{0:T(1024)S(1)} %get-tuple-element.6, bf16[128,4352]{1,0:T(8,128)(2,1)} %param.9, f32[4352]{0:T(1024)S(1)} %get-tuple-element.7, bf16[3,4352]{1,0:T(4,128)(2,1)S(1)} %collective-permute-done, f32[4352]{0:T(1024)S(1)} %get-tuple-element.8, ...), kind=kLoop, calls=%fused_computation.165 | loop fusion | flops 12255232 | bytes 4569600 | tf_op jit(solution)/shard_map/convert.2
  29.1 3.2 %reshape_reshape.6 = bf16[2,64,64,64]{3,2,1,0:T(8,128)(2,1)} reshape(bf16[128,4096]{1,0:T(8,128)(2,1)S(1)} %multiply_convert_fusion.5) | data formatting | bytes 2097152 | tf_op jit(solution)/shard_map/reshape;reshape | solution.py:147
  32.3 3.3 %copy.71 = bf16[2,64,64,64]{1,3,2,0:T(8,128)(2,1)S(1)} copy(bf16[2,64,64,64]{3,2,1,0:T(8,128)(2,1)} %reshape_reshape.6) | data formatting | bytes 2097152 | tf_op jit(solution)/shard_map/reshape;reshape | solution.py:147
  36.6 1.6 %collective-permute-start.1 = (bf16[32,128,64]{1,2,0:T(8,128)(2,1)S(1)}, bf16[32,128,64]{1,2,0:T(8,128)(2,1)S(1)}, u32[]{:S(2)}, u32[]{:S(2)}) collective-permute-start(bf16[32,128,64]{1,2,0:T(8,128)(2,1)S(1)} %get-tuple-element.24), channel_id=1, source_target_pairs={{0,4},{4,0},{8,12},{12,8},{16,20},{20,16},{24,28},{28,24},{1,5},{5... | collective-permute-start | bytes 1572872 | tf_op jit(solution)/shard_map/ppermute | solution.py:18
  45.3 6.3 %collective-permute-done.1 = bf16[32,128,64]{1,2,0:T(8,128)(2,1)S(1)} collective-permute-done((bf16[32,128,64]{1,2,0:T(8,128)(2,1)S(1)}, bf16[32,128,64]{1,2,0:T(8,128)(2,1)S(1)}, u32[]{:S(2)}, u32[]{:S(2)}) %collective-permute-start.1) | collective-permute-done | bytes 524320 | tf_op jit(solution)/shard_map/ppermute | solution.py:18
  52.0 1.6 %collective-permute-start.3 = (bf16[32,128,64]{1,2,0:T(8,128)(2,1)S(1)}, bf16[32,128,64]{1,2,0:T(8,128)(2,1)S(1)}, u32[]{:S(2)}, u32[]{:S(2)}) collective-permute-start(bf16[32,128,64]{1,2,0:T(8,128)(2,1)S(1)} %fusion.77), channel_id=1, source_target_pairs={{0,8},{4,12},{8,0},{12,4},{16,24},{20,28},{24,16},{28,20},{1,9},{5... | collective-permute-start | bytes 1572872 | tf_op jit(solution)/shard_map/ppermute | solution.py:18
  55.2 5.5 %collective-permute-done.7 = bf16[32,128,64]{1,2,0:T(8,128)(2,1)S(1)} collective-permute-done((bf16[32,128,64]{1,2,0:T(8,128)(2,1)S(1)}, bf16[32,128,64]{1,2,0:T(8,128)(2,1)S(1)}, u32[]{:S(2)}, u32[]{:S(2)}) %collective-permute-start.7) | collective-permute-done | bytes 524320 | tf_op jit(solution)/shard_map/ppermute | solution.py:18
  61.9 2.6 %fusion.32 = (bf16[32,128,64]{1,2,0:T(8,128)(2,1)S(1)}, bf16[32,128,64]{1,2,0:T(8,128)(2,1)S(1)}, f32[1,32,128,64]{2,3,1,0:T(8,128)}, f32[1,32,128,64]{2,3,1,0:T(8,128)}, f32[1,32,128,64]{2,3,1,0:T(8,128)}) fusion(bf16[32,128,64]{1,2,0:T(8,128)(2,1)S(1)} %collective-permute-done.3, f32[32]{0:T(128)S(1)} %get-tuple-element.53, f32[]{:T(128)S(6)} %sub.97, ...), kind=kLoop, calls=%fused_computation.69 | loop fusion | flops 7602176 | bytes 7865232 | tf_op jit(solution)/shard_map/convert_element_type | solution.py:109
  66.1 3.8 %fusion.5 = (f32[2,64]{1,0:T(2,128)S(1)}, f32[2,64,64]{1,2,0:T(8,128)S(1)}) fusion(f32[2,64,64]{1,2,0:T(8,128)S(1)} %fusion.87, f32[2,64,64]{2,1,0:T(8,128)S(1)} %copy.68, pred[64,64]{0,1:T(8,128)(4,1)S(1)} %iota_compare_fusion, f32[2,64]{1,0:T(2,128)S(1)} %copy-done.23, bf16[2,64,64,64]{1,3,2,0:T(8,128)(2,1)S(1)} %copy.71, ...), kind=kOutput, calls=%fused_computation.13 | convolution fusion | flops 72343424 | bytes 2200576 | tf_op jit(solution)/shard_map/vmap(thp,shp->hts)/dot_general | solution.py:35
  70.6 4.7 %collective-permute-done.9 = bf16[32,128,64]{1,2,0:T(8,128)(2,1)S(1)} collective-permute-done((bf16[32,128,64]{1,2,0:T(8,128)(2,1)S(1)}, bf16[32,128,64]{1,2,0:T(8,128)(2,1)S(1)}, u32[]{:S(2)}, u32[]{:S(2)}) %collective-permute-start.9) | collective-permute-done | bytes 524320 | tf_op jit(solution)/shard_map/ppermute | solution.py:18
  75.3 1.7 %fusion.39 = (f32[1,32,128,64]{2,3,1,0:T(8,128)}, bf16[32,128,64]{1,2,0:T(8,128)(2,1)S(1)}) fusion(bf16[32,128,64]{1,2,0:T(8,128)(2,1)S(1)} %collective-permute-done.9, f32[32]{0:T(128)S(1)} %get-tuple-element.59, f32[32]{0:T(128)S(1)} %get-tuple-element.64, f32[]{:T(128)S(6)} %sub.97, f32[32]{0:T(128)S(1)} %get-tuple-element.60, f32[]{:T(128)S(6)} %sub.96, ...), kind=kLoop, calls=%fused_computation.76 | loop fusion | flops 4718592 | bytes 3670672 | tf_op jit(solution)/shard_map/stack | solution.py:121
  79.6 2.3 %slice_bitcast_fusion.4 = (f32[64,128,64]{1,2,0:T(8,128)}, f32[64,128,64]{1,2,0:T(8,128)}) fusion(f32[2,64,128,64]{2,3,1,0:T(8,128)S(1)} %get-tuple-element.66), kind=kLoop, calls=%fused_computation.28 | loop fusion | bytes 8388608 | tf_op jit(solution)/shard_map/mul | solution.py:188
  83.6 2.7 %maximum_maximum_fusion = f32[3,64,128,64]{2,3,1,0:T(8,128)S(1)} fusion(f32[1,32,128,64]{2,3,1,0:T(8,128)S(1)} %multiply_bitcast_fusion, f32[1,32,128,64]{2,3,1,0:T(8,128)} %get-tuple-element.31, f32[1,32,128,64]{2,3,1,0:T(8,128)} %get-tuple-element.28, f32[1,32,128,64]{2,3,1,0:T(8,128)S(1)} %multiply_bitcast_fusion.1, ...), kind=kLoop, calls=%fused_computation.2 | loop fusion | flops 7864320 | bytes 12582912 | tf_op jit(solution)/shard_map/concatenate | solution.py:171
  90.6 1.7 %add_convert_fusion = bf16[2,64,128,64]{2,3,1,0:T(8,128)(2,1)S(1)} fusion(f32[64,128,64]{1,2,0:T(8,128)S(1)} %get-tuple-element.18, f32[2,64]{1,0:T(2,128)S(1)} %get-tuple-element.43, f32[64,128,64]{1,2,0:T(8,128)S(1)} %get-tuple-element.19, f32[2,64]{1,0:T(2,128)S(1)} %get-tuple-element.44, f32[64,128,64]{1,2,0:T(8,128)S(1)} %get-tuple-element.17, ...), kind=kLoop, calls=%fused_computation.15 | loop fusion | flops 10485760 | bytes 12585472 | tf_op jit(solution)/shard_map/convert_element_type | solution.py:190
  92.3 2.0 %fusion.3 = f32[2,64,128]{2,1,0:T(8,128)S(1)} fusion(bf16[2,64,64,64]{1,3,2,0:T(8,128)(2,1)S(1)} %copy-done.5, bf16[2,64,128,64]{2,3,1,0:T(8,128)(2,1)S(1)} %add_convert_fusion, f32[2,64,64]{1,2,0:T(8,128)S(1)} %copy.76), kind=kOutput, calls=%fused_computation.9 | convolution fusion | flops 136298496 | bytes 3244032 | tf_op jit(solution)/shard_map/chnp,cthp->cthn/dot_general | solution.py:35
  100.3 12.3 %collective-permute-start.15 = (f32[8,12,64]{2,0,1:T(8,128)S(1)}, f32[8,12,64]{2,0,1:T(8,128)S(1)}, u32[]{:S(2)}, u32[]{:S(2)}) collective-permute-start(f32[8,12,64]{2,0,1:T(8,128)S(1)} %fusion.75), channel_id=1, source_target_pairs={{0,8},{4,12},{8,0},{12,4},{16,24},{20,28},{24,16},{28,20},{1,9},{5... | collective-permute-start | bytes 73736 | tf_op jit(solution)/shard_map/ppermute | solution.py:18
  112.7 3.4 %fusion.2 = bf16[2,64,64,64]{1,3,2,0:T(8,128)(2,1)} fusion(bf16[2,64,64,64]{1,3,2,0:T(8,128)(2,1)S(1)} %copy-done.3, f32[2,64,64,64]{3,2,1,0:T(8,128)S(1)} %fusion.8, f32[64]{0:T(128)S(1)} %copy-done.27, f32[2,64]{1,0:T(2,128)S(1)} %copy-done.22, f32[2,64,64]{1,2,0:T(8,128)S(1)} %fusion.87, f32[2,64,64]{2,1,0:T(8,128)S(1)} %copy.68, ...), kind=kOutput, calls=%fused_computation.7 | convolution fusion | flops 72876032 | bytes 4264704 | tf_op jit(solution)/shard_map/vmap(hts,shp->thp)/dot_general | solution.py:35
  116.1 3.3 %copy.77 = bf16[2,64,64,64]{3,2,1,0:T(8,128)(2,1)S(1)} copy(bf16[2,64,64,64]{1,3,2,0:T(8,128)(2,1)} %fusion.2) | data formatting | bytes 2097152 | tf_op jit(solution)/shard_map/convert_element_type | solution.py:211
  119.4 2.5 %reshape.126 = bf16[128,4096]{1,0:T(8,128)(2,1)} reshape(bf16[2,64,64,64]{3,2,1,0:T(8,128)(2,1)S(1)} %copy.77) | data formatting | bytes 2097152 | tf_op jit(solution)/shard_map/reshape | solution.py:212
  121.9 15.3 %collective-permute-start.16 = (f32[8,12,64]{2,0,1:T(8,128)S(1)}, f32[8,12,64]{2,0,1:T(8,128)S(1)}, u32[]{:S(2)}, u32[]{:S(2)}) collective-permute-start(f32[8,12,64]{2,0,1:T(8,128)S(1)} %add.170), channel_id=1, source_target_pairs={{0,16},{4,20},{8,24},{12,28},{16,0},{20,4},{24,8},{28,12},{1,17},{... | collective-permute-start | bytes 73736 | tf_op jit(solution)/shard_map/ppermute | solution.py:18
  (141 shorter events, 42.2 us)
Async XLA Ops:
  2.9 21.4 %copy-start.13 = (f32[2,1,64]{2,1,0:T(1,128)}, f32[2,1,64]{2,1,0:T(1,128)S(1)}, u32[]{:S(2)}) copy-start(f32[2,1,64]{2,1,0:T(1,128)S(1)} %get-tuple-element.10) | copy-start | bytes 1540
  3.5 34.8 %collective-permute-start.2 = (f32[32]{0:T(128)}, f32[32]{0:T(128)}, u32[]{:S(2)}, u32[]{:S(2)}) collective-permute-start(f32[32]{0:T(128)} %get-tuple-element.61), channel_id=1, source_target_pairs={{0,4},{4,0},{8,12},{12,8},{16,20},{20,16},{24,28},{28,24},{1,5},{5... | collective-permute-start | bytes 392 | tf_op jit(solution)/shard_map/ppermute | solution.py:18
  6.4 31.8 %collective-permute-start.8 = (f32[32]{0:T(128)}, f32[32]{0:T(128)}, u32[]{:S(2)}, u32[]{:S(2)}) collective-permute-start(f32[32]{0:T(128)} %get-tuple-element.62), channel_id=1, source_target_pairs={{0,4},{4,0},{8,12},{12,8},{16,20},{20,16},{24,28},{28,24},{1,5},{5... | collective-permute-start | bytes 392 | tf_op jit(solution)/shard_map/ppermute | solution.py:18
  7.4 17.7 %collective-permute-start = (bf16[3,4352]{1,0:T(4,128)(2,1)S(1)}, bf16[3,4352]{1,0:T(4,128)(2,1)S(1)}, u32[]{:S(2)}, u32[]{:S(2)}) collective-permute-start(bf16[3,4352]{1,0:T(4,128)(2,1)S(1)} %slice.119), channel_id=1, source_target_pairs={{0,4},{4,8},{8,12},{12,16},{16,20},{20,24},{24,28},{1,5},{5,9},{9,... | collective-permute-start | bytes 78344 | tf_op jit(solution)/shard_map/ppermute | solution.py:12
  35.7 30.4 %copy-start.2 = (bf16[2,64,64,64]{1,3,2,0:T(8,128)(2,1)}, bf16[2,64,64,64]{1,3,2,0:T(8,128)(2,1)S(1)}, u32[]{:S(2)}) copy-start(bf16[2,64,64,64]{1,3,2,0:T(8,128)(2,1)S(1)} %copy.71) | copy-start | bytes 3145732
  36.6 14.9 %collective-permute-start.1 = (bf16[32,128,64]{1,2,0:T(8,128)(2,1)S(1)}, bf16[32,128,64]{1,2,0:T(8,128)(2,1)S(1)}, u32[]{:S(2)}, u32[]{:S(2)}) collective-permute-start(bf16[32,128,64]{1,2,0:T(8,128)(2,1)S(1)} %get-tuple-element.24), channel_id=1, source_target_pairs={{0,4},{4,0},{8,12},{12,8},{16,20},{20,16},{24,28},{28,24},{1,5},{5... | collective-permute-start | bytes 1572872 | tf_op jit(solution)/shard_map/ppermute | solution.py:18
  39.0 3.5 %collective-permute-start.10 = (f32[32]{0:T(128)S(1)}, f32[32]{0:T(128)S(1)}, u32[]{:S(2)}, u32[]{:S(2)}) collective-permute-start(f32[32]{0:T(128)S(1)} %get-tuple-element.58), channel_id=1, source_target_pairs={{0,8},{4,12},{8,0},{12,4},{16,24},{20,28},{24,16},{28,20},{1,9},{5... | collective-permute-start | bytes 392 | tf_op jit(solution)/shard_map/ppermute | solution.py:18
  40.6 3.5 %collective-permute-start.4 = (f32[32]{0:T(128)S(1)}, f32[32]{0:T(128)S(1)}, u32[]{:S(2)}, u32[]{:S(2)}) collective-permute-start(f32[32]{0:T(128)S(1)} %get-tuple-element.12), channel_id=1, source_target_pairs={{0,8},{4,12},{8,0},{12,4},{16,24},{20,28},{24,16},{28,20},{1,9},{5... | collective-permute-start | bytes 392 | tf_op jit(solution)/shard_map/ppermute | solution.py:18
  44.8 15.9 %collective-permute-start.7 = (bf16[32,128,64]{1,2,0:T(8,128)(2,1)S(1)}, bf16[32,128,64]{1,2,0:T(8,128)(2,1)S(1)}, u32[]{:S(2)}, u32[]{:S(2)}) collective-permute-start(bf16[32,128,64]{1,2,0:T(8,128)(2,1)S(1)} %get-tuple-element.25), channel_id=1, source_target_pairs={{0,4},{4,0},{8,12},{12,8},{16,20},{20,16},{24,28},{28,24},{1,5},{5... | collective-permute-start | bytes 1572872 | tf_op jit(solution)/shard_map/ppermute | solution.py:18
  52.0 9.9 %collective-permute-start.3 = (bf16[32,128,64]{1,2,0:T(8,128)(2,1)S(1)}, bf16[32,128,64]{1,2,0:T(8,128)(2,1)S(1)}, u32[]{:S(2)}, u32[]{:S(2)}) collective-permute-start(bf16[32,128,64]{1,2,0:T(8,128)(2,1)S(1)} %fusion.77), channel_id=1, source_target_pairs={{0,8},{4,12},{8,0},{12,4},{16,24},{20,28},{24,16},{28,20},{1,9},{5... | collective-permute-start | bytes 1572872 | tf_op jit(solution)/shard_map/ppermute | solution.py:18
  55.2 22.7 %copy-start = (f32[2,64,128,64]{2,3,1,0:T(8,128)}, f32[2,64,128,64]{2,3,1,0:T(8,128)S(1)}, u32[]{:S(2)}) copy-start(f32[2,64,128,64]{2,3,1,0:T(8,128)S(1)} %fusion.7) | copy-start | bytes 12582916
  64.5 10.8 %collective-permute-start.9 = (bf16[32,128,64]{1,2,0:T(8,128)(2,1)S(1)}, bf16[32,128,64]{1,2,0:T(8,128)(2,1)S(1)}, u32[]{:S(2)}, u32[]{:S(2)}) collective-permute-start(bf16[32,128,64]{1,2,0:T(8,128)(2,1)S(1)} %get-tuple-element.23), channel_id=1, source_target_pairs={{0,8},{4,12},{8,0},{12,4},{16,24},{20,28},{24,16},{28,20},{1,9},{5... | collective-permute-start | bytes 1572872 | tf_op jit(solution)/shard_map/ppermute | solution.py:18
  69.9 9.0 %collective-permute-start.5 = (bf16[32,128,64]{1,2,0:T(8,128)(2,1)S(1)}, bf16[32,128,64]{1,2,0:T(8,128)(2,1)S(1)}, u32[]{:S(2)}, u32[]{:S(2)}) collective-permute-start(bf16[32,128,64]{1,2,0:T(8,128)(2,1)S(1)} %get-tuple-element.22), channel_id=1, source_target_pairs={{8,16},{12,20},{9,17},{13,21},{10,18},{14,22},{11,19},{15,23}} | collective-permute-start | bytes 1572872 | tf_op jit(solution)/shard_map/ppermute | solution.py:96
  77.0 4.9 %collective-permute-start.11 = (bf16[32,128,64]{1,2,0:T(8,128)(2,1)S(1)}, bf16[32,128,64]{1,2,0:T(8,128)(2,1)S(1)}, u32[]{:S(2)}, u32[]{:S(2)}) collective-permute-start(bf16[32,128,64]{1,2,0:T(8,128)(2,1)S(1)} %get-tuple-element.32), channel_id=1, source_target_pairs={{8,16},{12,20},{9,17},{13,21},{10,18},{14,22},{11,19},{15,23}} | collective-permute-start | bytes 1572872 | tf_op jit(solution)/shard_map/ppermute | solution.py:96
  78.9 4.3 %collective-permute-start.6 = (bf16[32,128,64]{1,2,0:T(8,128)(2,1)S(1)}, bf16[32,128,64]{1,2,0:T(8,128)(2,1)S(1)}, u32[]{:S(2)}, u32[]{:S(2)}) collective-permute-start(bf16[32,128,64]{1,2,0:T(8,128)(2,1)S(1)} %collective-permute-done.5), channel_id=1, source_target_pairs={{16,24},{20,28},{17,25},{21,29},{18,26},{22,30},{19,27},{23,31}} | collective-permute-start | bytes 1572872 | tf_op jit(solution)/shard_map/ppermute | solution.py:97
  81.9 1.5 %collective-permute-start.12 = (bf16[32,128,64]{1,2,0:T(8,128)(2,1)S(1)}, bf16[32,128,64]{1,2,0:T(8,128)(2,1)S(1)}, u32[]{:S(2)}, u32[]{:S(2)}) collective-permute-start(bf16[32,128,64]{1,2,0:T(8,128)(2,1)S(1)} %collective-permute-done.11), channel_id=1, source_target_pairs={{16,24},{20,28},{17,25},{21,29},{18,26},{22,30},{19,27},{23,31}} | collective-permute-start | bytes 1572872 | tf_op jit(solution)/shard_map/ppermute | solution.py:97
  94.3 18.4 %copy-start.3 = (bf16[2,64,64,64]{1,3,2,0:T(8,128)(2,1)S(1)}, bf16[2,64,64,64]{1,3,2,0:T(8,128)(2,1)}, u32[]{:S(2)}) copy-start(bf16[2,64,64,64]{1,3,2,0:T(8,128)(2,1)} %copy-done.2) | copy-start | bytes 3145732
  94.3 18.4 %copy-start.22 = (f32[2,64]{1,0:T(2,128)S(1)}, f32[2,64]{1,0:T(2,128)}, u32[]{:S(2)}) copy-start(f32[2,64]{1,0:T(2,128)} %broadcast_multiply_fusion) | copy-start | bytes 1540
  94.3 18.4 %copy-start.27 = (f32[64]{0:T(128)S(1)}, f32[64]{0:T(128)}, u32[]{:S(2)}) copy-start(f32[64]{0:T(128)} %param.14) | copy-start | bytes 772
  96.2 4.2 %collective-permute-start.14 = (f32[8,12,64]{2,0,1:T(8,128)S(1)}, f32[8,12,64]{2,0,1:T(8,128)S(1)}, u32[]{:S(2)}, u32[]{:S(2)}) collective-permute-start(f32[8,12,64]{2,0,1:T(8,128)S(1)} %pad_maximum_fusion.2), channel_id=1, source_target_pairs={{0,4},{4,0},{8,12},{12,8},{16,20},{20,16},{24,28},{28,24},{1,5},{5... | collective-permute-start | bytes 73736 | tf_op jit(solution)/shard_map/ppermute | solution.py:18
  97.9 39.3 %collective-permute-start.13 = (f32[3,128]{1,0:T(4,128)S(1)}, f32[3,128]{1,0:T(4,128)S(1)}, u32[]{:S(2)}, u32[]{:S(2)}) collective-permute-start(f32[3,128]{1,0:T(4,128)S(1)} %slice.179), channel_id=1, source_target_pairs={{4,0},{8,4},{12,8},{16,12},{20,16},{24,20},{28,24},{5,1},{9,5},{13... | collective-permute-start | bytes 4616 | tf_op jit(solution)/shard_map/ppermute | solution.py:12
  100.3 21.6 %collective-permute-start.15 = (f32[8,12,64]{2,0,1:T(8,128)S(1)}, f32[8,12,64]{2,0,1:T(8,128)S(1)}, u32[]{:S(2)}, u32[]{:S(2)}) collective-permute-start(f32[8,12,64]{2,0,1:T(8,128)S(1)} %fusion.75), channel_id=1, source_target_pairs={{0,8},{4,12},{8,0},{12,4},{16,24},{20,28},{24,16},{28,20},{1,9},{5... | collective-permute-start | bytes 73736 | tf_op jit(solution)/shard_map/ppermute | solution.py:18
  119.4 19.9 %copy-start.8 = (f32[8,12,64]{2,0,1:T(8,128)S(1)}, f32[8,12,64]{2,0,1:T(8,128)}, u32[]{:S(2)}) copy-start(f32[8,12,64]{2,0,1:T(8,128)} %param.15) | copy-start | bytes 73732
  121.9 17.4 %collective-permute-start.16 = (f32[8,12,64]{2,0,1:T(8,128)S(1)}, f32[8,12,64]{2,0,1:T(8,128)S(1)}, u32[]{:S(2)}, u32[]{:S(2)}) collective-permute-start(f32[8,12,64]{2,0,1:T(8,128)S(1)} %add.170), channel_id=1, source_target_pairs={{0,16},{4,20},{8,24},{12,28},{16,0},{20,4},{24,8},{28,12},{1,17},{... | collective-permute-start | bytes 73736 | tf_op jit(solution)/shard_map/ppermute | solution.py:18
  (23 other events, 165.9 us)

commit v6 on v5

--- a/solution.py
+++ b/solution.py
@@ -162,7 +162,7 @@
     devices = lax.axis_size("seq")
     depth = devices.bit_length() - 1
     myself = lax.axis_index("seq")
-    chunks = 2 if heads % 2 == 0 else 1
+    chunks = 4 if heads % 4 == 0 else 1
     width = heads // chunks
     pieces = [
         exchange(dev_state[k * width : (k + 1) * width], dev_decay[k * width : (k + 1) * width], depth, myself)

time: 141 us -> 145 us (1.028)
  waiting for transfers between devices: 22.5 us -> 15.1 us
  other arithmetic: 24.1 us -> 30 us
  local copies, waits for them, and re-layouts: 29.4 us -> 31.8 us
  matrix products: 14.9 us -> 17.3 us
    ppermute x11 -> x19, waiting for transfers between devices: 22.5 us -> 15.1 us  [from_partner(): return lax.ppermute(value, axis, pairs)]
    ppermute x11 -> x19, starting transfers between devices: 39.6 us -> 35.6 us  [from_partner(): return lax.ppermute(value, axis, pairs)]
    mul x2 -> x4, other arithmetic: 1.35 us -> 4.87 us  [combine(): found = grown * jnp.exp(leading)[..., None, None] * other]
    dot_general x6, matrix products: 12.9 us -> 15.3 us  [contract(): return jnp.einsum(form, left, right, preferred_element_type=jnp.float32)]
    concatenate x1, other arithmetic: 2.67 us -> 0.8 us  [local(): cross = jnp.concatenate(pieces, axis=1)]
    ppermute x2 -> x4, starting transfers between devices: 1.56 us -> 3.39 us  [relay(): lax.ppermute(value, axis, [(source, source + step) for source in range(ha...]
    ppermute x2 -> x4, starting transfers between devices: 1.38 us -> 2.84 us  [relay(): lax.ppermute(first, axis, [(source, source + step) for source in range(ha...]
    convert_element_type x1 -> x2, other arithmetic: 2.61 us -> 3.59 us  [exchange(): sent = relay(block.astype(jnp.bfloat16), 'seq', bit_pos)]
  transfers between devices with their start and end apart: 17 -> 29, of which waited for: 8 -> 7; matrix products, arithmetic and copies ran while one was open for 35% -> 36% of each run, Pallas kernels for 0% -> 0%
where the time goes in v6:
time: 145 us; the launch traced here: 144 us
  starting transfers between devices  47.6 us (33%)
  local copies, waits for them, and re-layouts  31.8 us (22%)
  other arithmetic  30 us (21%)
  matrix products  17.3 us (12%)
  waiting for transfers between devices  15.1 us (10%)
  between operations  1.81 us (1%)
    ppermute x19, starting transfers between devices, from_partner(): return lax.ppermute(value, axis, pairs)  35.6 us
    dot_general x6, matrix products, contract(): return jnp.einsum(form, left, right, preferred_element_type=jnp.float32)  15.3 us
    ppermute x19, waiting for transfers between devices, from_partner(): return lax.ppermute(value, axis, pairs)  15.1 us
    another operation x2, local copies, waits for them, and re-layouts, local(): grad_groups = grad_out.reshape(groups, group_len, heads, head_dim)  6.2 us
    ppermute x2, starting transfers between devices, shifted(): lax.ppermute(value, axis, [(source, source + steps) for source in range(l...  5.78 us
    another operation x2, local copies, waits for them, and re-layouts, local(): x_groups = x_act.reshape(groups, group_len, heads, head_dim)  5.28 us
    mul x4, other arithmetic, combine(): found = grown * jnp.exp(leading)[..., None, None] * other  4.87 us
    convert_element_type x2, other arithmetic, exchange(): sent = relay(block.astype(jnp.bfloat16), 'seq', bit_pos)  3.59 us
  transfers between devices with their start and end apart: 29, of which 7 were waited for; matrix products, arithmetic and copies ran while one was open for 36% of the time, Pallas kernels for 0%

profile of v6, /device:TPU:0, one launch (start us, length us, event | category | flops | bytes accessed | tf_op | source)
XLA Modules:
  0.0 143.6 jit_solution(12781001000442414626)
XLA Ops:
  3.6 2.9 %collective-permute-start.14 = (f32[16]{0:T(128)}, f32[16]{0:T(128)}, u32[]{:S(2)}, u32[]{:S(2)}) collective-permute-start(f32[16]{0:T(128)} %get-tuple-element.85), channel_id=1, source_target_pairs={{0,4},{4,0},{8,12},{12,8},{16,20},{20,16},{24,28},{28,24},{1,5},{5... | collective-permute-start | bytes 200 | tf_op jit(solution)/shard_map/ppermute | solution.py:18
  6.6 2.0 %collective-permute-start.20 = (f32[16]{0:T(128)}, f32[16]{0:T(128)}, u32[]{:S(2)}, u32[]{:S(2)}) collective-permute-start(f32[16]{0:T(128)} %get-tuple-element.84), channel_id=1, source_target_pairs={{0,4},{4,0},{8,12},{12,8},{16,20},{20,16},{24,28},{28,24},{1,5},{5... | collective-permute-start | bytes 200 | tf_op jit(solution)/shard_map/ppermute | solution.py:18
  10.2 4.5 %collective-permute-start = (bf16[3,4352]{1,0:T(4,128)(2,1)}, bf16[3,4352]{1,0:T(4,128)(2,1)}, u32[]{:S(2)}, u32[]{:S(2)}) collective-permute-start(bf16[3,4352]{1,0:T(4,128)(2,1)} %slice.131), channel_id=1, source_target_pairs={{0,4},{4,8},{8,12},{12,16},{16,20},{20,24},{24,28},{1,5},{5,9},{9,... | collective-permute-start | bytes 78344 | tf_op jit(solution)/shard_map/ppermute | solution.py:12
  22.1 3.3 %reshape_reshape.7 = bf16[2,64,64,64]{3,2,1,0:T(8,128)(2,1)S(1)} reshape(bf16[128,4096]{1,0:T(8,128)(2,1)} %param.17) | data formatting | bytes 2097152 | tf_op jit(solution)/shard_map/reshape;reshape | solution.py:149
  25.5 2.9 %copy.82 = bf16[2,64,64,64]{1,3,2,0:T(8,128)(2,1)} copy(bf16[2,64,64,64]{3,2,1,0:T(8,128)(2,1)S(1)} %reshape_reshape.7) | data formatting | bytes 2097152 | tf_op jit(solution)/shard_map/reshape;reshape | solution.py:149
  40.8 3.0 %fusion.107 = (bf16[128,4352]{1,0:T(8,128)(2,1)}, f32[128,4352]{1,0:T(8,128)S(1)}) fusion(f32[4352]{0:T(1024)S(1)} %get-tuple-element.6, bf16[128,4352]{1,0:T(8,128)(2,1)S(1)} %copy-done.11, f32[4352]{0:T(1024)S(1)} %get-tuple-element.7, bf16[3,4352]{1,0:T(4,128)(2,1)} %collective-permute-done, f32[4352]{0:T(1024)S(1)} %get-tuple-element.8, ...), kind=kLoop, calls=%fused_computation.215 | loop fusion | flops 12255232 | bytes 4569600 | tf_op jit(solution)/shard_map/convert.2
  44.4 2.3 %reshape_reshape.6 = bf16[2,64,64,64]{3,2,1,0:T(8,128)(2,1)S(1)} reshape(bf16[128,4096]{1,0:T(8,128)(2,1)S(1)} %multiply_convert_fusion.5) | data formatting | bytes 2097152 | tf_op jit(solution)/shard_map/reshape;reshape | solution.py:147
  46.7 3.0 %copy.71 = bf16[2,64,64,64]{1,3,2,0:T(8,128)(2,1)} copy(bf16[2,64,64,64]{3,2,1,0:T(8,128)(2,1)S(1)} %reshape_reshape.6) | data formatting | bytes 2097152 | tf_op jit(solution)/shard_map/reshape;reshape | solution.py:147
  50.5 2.6 %multiply_reduce_fusion.2 = (f32[64,128,64]{1,2,0:T(8,128)S(1)}, f32[2,64,128,64]{2,3,1,0:T(8,128)S(1)}) fusion(f32[2,64]{1,0:T(2,128)S(1)} %copy-done.34, bf16[2,64,128,1]{2,1,3,0:T(8,128)(2,1)S(1)} %bitcast.114, bf16[2,64,64,64]{1,3,2,0:T(8,128)(2,1)} %copy.71, f32[2,64,64]{1,2,0:T(8,128)S(1)} %copy.75), kind=kOutput, calls=%fused_computation.16 | convolution fusion | flops 137363456 | bytes 7406080 | tf_op jit(solution)/shard_map/vmap(sn,shp->hnp)/dot_general | solution.py:35
  57.6 4.4 %fusion.5 = (f32[2,64]{1,0:T(2,128)S(1)}, f32[2,64,64]{1,2,0:T(8,128)}) fusion(f32[2,64,64]{1,2,0:T(8,128)S(1)} %fusion.113, f32[2,64,64]{2,1,0:T(8,128)S(1)} %copy-done.14, pred[64,64]{0,1:T(8,128)(4,1)S(1)} %copy-done.24, f32[2,64]{1,0:T(2,128)S(1)} %copy-done.64, bf16[2,64,64,64]{1,3,2,0:T(8,128)(2,1)S(1)} %copy-done.4, ...), kind=kOutput, calls=%fused_computation.13 | convolution fusion | flops 72343424 | bytes 2200576 | tf_op jit(solution)/shard_map/vmap(thp,shp->hts)/dot_general | solution.py:35
  65.8 2.5 %collective-permute-done.1 = bf16[16,128,64]{1,2,0:T(8,128)(2,1)S(1)} collective-permute-done((bf16[16,128,64]{1,2,0:T(8,128)(2,1)S(1)}, bf16[16,128,64]{1,2,0:T(8,128)(2,1)S(1)}, u32[]{:S(2)}, u32[]{:S(2)}) %collective-permute-start.1) | collective-permute-done | bytes 262176 | tf_op jit(solution)/shard_map/ppermute | solution.py:18
  68.3 2.3 %collective-permute-done.21 = bf16[16,128,64]{1,2,0:T(8,128)(2,1)S(1)} collective-permute-done((bf16[16,128,64]{1,2,0:T(8,128)(2,1)S(1)}, bf16[16,128,64]{1,2,0:T(8,128)(2,1)S(1)}, u32[]{:S(2)}, u32[]{:S(2)}) %collective-permute-start.21) | collective-permute-done | bytes 262176 | tf_op jit(solution)/shard_map/ppermute | solution.py:18
  73.2 2.4 %slice_bitcast_fusion.4 = (f32[64,128,64]{1,2,0:T(8,128)}, f32[64,128,64]{1,2,0:T(8,128)}) fusion(f32[2,64,128,64]{2,3,1,0:T(8,128)S(1)} %get-tuple-element.94), kind=kLoop, calls=%fused_computation.28 | loop fusion | bytes 8388608 | tf_op jit(solution)/shard_map/mul | solution.py:188
  80.5 3.5 %collective-permute-start.15 = (bf16[16,128,64]{1,2,0:T(8,128)(2,1)}, bf16[16,128,64]{1,2,0:T(8,128)(2,1)}, u32[]{:S(2)}, u32[]{:S(2)}) collective-permute-start(bf16[16,128,64]{1,2,0:T(8,128)(2,1)} %get-tuple-element.28), channel_id=1, source_target_pairs={{0,8},{4,12},{8,0},{12,4},{16,24},{20,28},{24,16},{28,20},{1,9},{5... | collective-permute-start | bytes 786440 | tf_op jit(solution)/shard_map/ppermute | solution.py:18
  86.6 2.1 %collective-permute-done.15 = bf16[16,128,64]{1,2,0:T(8,128)(2,1)} collective-permute-done((bf16[16,128,64]{1,2,0:T(8,128)(2,1)}, bf16[16,128,64]{1,2,0:T(8,128)(2,1)}, u32[]{:S(2)}, u32[]{:S(2)}) %collective-permute-start.15) | collective-permute-done | bytes 262176 | tf_op jit(solution)/shard_map/ppermute | solution.py:18
  88.7 2.8 %collective-permute-done.9 = bf16[16,128,64]{1,2,0:T(8,128)(2,1)} collective-permute-done((bf16[16,128,64]{1,2,0:T(8,128)(2,1)}, bf16[16,128,64]{1,2,0:T(8,128)(2,1)}, u32[]{:S(2)}, u32[]{:S(2)}) %collective-permute-start.9) | collective-permute-done | bytes 262176 | tf_op jit(solution)/shard_map/ppermute | solution.py:18
  91.5 1.9 %fusion.43 = (bf16[16,128,64]{1,2,0:T(8,128)(2,1)S(1)}, bf16[16,128,64]{1,2,0:T(8,128)(2,1)S(1)}, f32[1,16,128,64]{2,3,1,0:T(8,128)S(1)}, f32[1,16,128,64]{2,3,1,0:T(8,128)S(1)}) fusion(bf16[16,128,64]{1,2,0:T(8,128)(2,1)} %collective-permute-done.9, f32[16]{0:T(128)S(1)} %copy-done.49, f32[16]{0:T(128)S(1)} %copy-done.45, f32[]{:T(128)S(6)} %sub.101, ...), kind=kLoop, calls=%fused_computation.92 | loop fusion | flops 4718592 | bytes 3670608 | tf_op jit(solution)/shard_map/convert_element_type | solution.py:109
  107.1 2.0 %fusion.3 = f32[2,64,128]{2,1,0:T(8,128)S(1)} fusion(bf16[2,64,64,64]{1,3,2,0:T(8,128)(2,1)S(1)} %copy-done.3, bf16[2,64,128,64]{2,3,1,0:T(8,128)(2,1)S(1)} %add_convert_fusion, f32[2,64,64]{1,2,0:T(8,128)S(1)} %copy.76), kind=kOutput, calls=%fused_computation.9 | convolution fusion | flops 136298496 | bytes 3244032 | tf_op jit(solution)/shard_map/chnp,cthp->cthn/dot_general | solution.py:35
  112.8 2.4 %collective-permute-done.26 = f32[8,12,64]{2,0,1:T(8,128)S(1)} collective-permute-done((f32[8,12,64]{2,0,1:T(8,128)S(1)}, f32[8,12,64]{2,0,1:T(8,128)S(1)}, u32[]{:S(2)}, u32[]{:S(2)}) %collective-permute-start.26) | collective-permute-done | bytes 24608 | tf_op jit(solution)/shard_map/ppermute | solution.py:18
  115.2 6.9 %collective-permute-start.27 = (f32[8,12,64]{2,0,1:T(8,128)S(1)}, f32[8,12,64]{2,0,1:T(8,128)S(1)}, u32[]{:S(2)}, u32[]{:S(2)}) collective-permute-start(f32[8,12,64]{2,0,1:T(8,128)S(1)} %fusion.97), channel_id=1, source_target_pairs={{0,8},{4,12},{8,0},{12,4},{16,24},{20,28},{24,16},{28,20},{1,9},{5... | collective-permute-start | bytes 73736 | tf_op jit(solution)/shard_map/ppermute | solution.py:18
  122.1 3.4 %fusion.2 = bf16[2,64,64,64]{1,3,2,0:T(8,128)(2,1)} fusion(bf16[2,64,64,64]{1,3,2,0:T(8,128)(2,1)S(1)} %copy-done.5, f32[2,64,64,64]{3,2,1,0:T(8,128)S(1)} %fusion.8, f32[64]{0:T(128)S(1)} %copy-done.69, f32[2,64]{1,0:T(2,128)S(1)} %copy-done.63, f32[2,64,64]{1,2,0:T(8,128)S(1)} %copy-done.17, f32[2,64,64]{2,1,0:T(8,128)S(1)} %copy-done.15, ...), kind=kOutput, calls=%fused_computation.7 | convolution fusion | flops 72876032 | bytes 4264704 | tf_op jit(solution)/shard_map/vmap(hts,shp->thp)/dot_general | solution.py:35
  125.5 3.3 %copy.77 = bf16[2,64,64,64]{3,2,1,0:T(8,128)(2,1)S(1)} copy(bf16[2,64,64,64]{1,3,2,0:T(8,128)(2,1)} %fusion.2) | data formatting | bytes 2097152 | tf_op jit(solution)/shard_map/convert_element_type | solution.py:211
  128.9 2.5 %reshape.142 = bf16[128,4096]{1,0:T(8,128)(2,1)} reshape(bf16[2,64,64,64]{3,2,1,0:T(8,128)(2,1)S(1)} %copy.77) | data formatting | bytes 2097152 | tf_op jit(solution)/shard_map/reshape | solution.py:212
  131.3 9.6 %collective-permute-start.28 = (f32[8,12,64]{2,0,1:T(8,128)S(1)}, f32[8,12,64]{2,0,1:T(8,128)S(1)}, u32[]{:S(2)}, u32[]{:S(2)}) collective-permute-start(f32[8,12,64]{2,0,1:T(8,128)S(1)} %add.248), channel_id=1, source_target_pairs={{0,16},{4,20},{8,24},{12,28},{16,0},{20,4},{24,8},{28,12},{1,17},{... | collective-permute-start | bytes 73736 | tf_op jit(solution)/shard_map/ppermute | solution.py:18
  (256 shorter events, 63.6 us)
Async XLA Ops:
  3.6 26.8 %collective-permute-start.14 = (f32[16]{0:T(128)}, f32[16]{0:T(128)}, u32[]{:S(2)}, u32[]{:S(2)}) collective-permute-start(f32[16]{0:T(128)} %get-tuple-element.85), channel_id=1, source_target_pairs={{0,4},{4,0},{8,12},{12,8},{16,20},{20,16},{24,28},{28,24},{1,5},{5... | collective-permute-start | bytes 200 | tf_op jit(solution)/shard_map/ppermute | solution.py:18
  6.6 23.9 %collective-permute-start.2 = (f32[16]{0:T(128)}, f32[16]{0:T(128)}, u32[]{:S(2)}, u32[]{:S(2)}) collective-permute-start(f32[16]{0:T(128)} %get-tuple-element.83), channel_id=1, source_target_pairs={{0,4},{4,0},{8,12},{12,8},{16,20},{20,16},{24,28},{28,24},{1,5},{5... | collective-permute-start | bytes 200 | tf_op jit(solution)/shard_map/ppermute | solution.py:18
  6.6 23.8 %collective-permute-start.20 = (f32[16]{0:T(128)}, f32[16]{0:T(128)}, u32[]{:S(2)}, u32[]{:S(2)}) collective-permute-start(f32[16]{0:T(128)} %get-tuple-element.84), channel_id=1, source_target_pairs={{0,4},{4,0},{8,12},{12,8},{16,20},{20,16},{24,28},{28,24},{1,5},{5... | collective-permute-start | bytes 200 | tf_op jit(solution)/shard_map/ppermute | solution.py:18
  8.6 21.8 %collective-permute-start.8 = (f32[16]{0:T(128)}, f32[16]{0:T(128)}, u32[]{:S(2)}, u32[]{:S(2)}) collective-permute-start(f32[16]{0:T(128)} %get-tuple-element.86), channel_id=1, source_target_pairs={{0,4},{4,0},{8,12},{12,8},{16,20},{20,16},{24,28},{28,24},{1,5},{5... | collective-permute-start | bytes 200 | tf_op jit(solution)/shard_map/ppermute | solution.py:18
  10.2 30.7 %collective-permute-start = (bf16[3,4352]{1,0:T(4,128)(2,1)}, bf16[3,4352]{1,0:T(4,128)(2,1)}, u32[]{:S(2)}, u32[]{:S(2)}) collective-permute-start(bf16[3,4352]{1,0:T(4,128)(2,1)} %slice.131), channel_id=1, source_target_pairs={{0,4},{4,8},{8,12},{12,16},{16,20},{20,24},{24,28},{1,5},{5,9},{9,... | collective-permute-start | bytes 78344 | tf_op jit(solution)/shard_map/ppermute | solution.py:12
  32.9 4.2 %collective-permute-start.22 = (f32[16]{0:T(128)S(1)}, f32[16]{0:T(128)S(1)}, u32[]{:S(2)}, u32[]{:S(2)}) collective-permute-start(f32[16]{0:T(128)S(1)} %get-tuple-element.80), channel_id=1, source_target_pairs={{0,8},{4,12},{8,0},{12,4},{16,24},{20,28},{24,16},{28,20},{1,9},{5... | collective-permute-start | bytes 200 | tf_op jit(solution)/shard_map/ppermute | solution.py:18
  33.9 4.4 %collective-permute-start.10 = (f32[16]{0:T(128)S(1)}, f32[16]{0:T(128)S(1)}, u32[]{:S(2)}, u32[]{:S(2)}) collective-permute-start(f32[16]{0:T(128)S(1)} %get-tuple-element.70), channel_id=1, source_target_pairs={{0,8},{4,12},{8,0},{12,4},{16,24},{20,28},{24,16},{28,20},{1,9},{5... | collective-permute-start | bytes 200 | tf_op jit(solution)/shard_map/ppermute | solution.py:18
  34.9 4.7 %collective-permute-start.16 = (f32[16]{0:T(128)S(1)}, f32[16]{0:T(128)S(1)}, u32[]{:S(2)}, u32[]{:S(2)}) collective-permute-start(f32[16]{0:T(128)S(1)} %get-tuple-element.75), channel_id=1, source_target_pairs={{0,8},{4,12},{8,0},{12,4},{16,24},{20,28},{24,16},{28,20},{1,9},{5... | collective-permute-start | bytes 200 | tf_op jit(solution)/shard_map/ppermute | solution.py:18
  53.3 10.2 %collective-permute-start.19 = (bf16[16,128,64]{1,2,0:T(8,128)(2,1)S(1)}, bf16[16,128,64]{1,2,0:T(8,128)(2,1)S(1)}, u32[]{:S(2)}, u32[]{:S(2)}) collective-permute-start(bf16[16,128,64]{1,2,0:T(8,128)(2,1)S(1)} %get-tuple-element.32), channel_id=1, source_target_pairs={{0,4},{4,0},{8,12},{12,8},{16,20},{20,16},{24,28},{28,24},{1,5},{5... | collective-permute-start | bytes 786440 | tf_op jit(solution)/shard_map/ppermute | solution.py:18
  54.3 13.9 %collective-permute-start.1 = (bf16[16,128,64]{1,2,0:T(8,128)(2,1)S(1)}, bf16[16,128,64]{1,2,0:T(8,128)(2,1)S(1)}, u32[]{:S(2)}, u32[]{:S(2)}) collective-permute-start(bf16[16,128,64]{1,2,0:T(8,128)(2,1)S(1)} %get-tuple-element.31), channel_id=1, source_target_pairs={{0,4},{4,0},{8,12},{12,8},{16,20},{20,16},{24,28},{28,24},{1,5},{5... | collective-permute-start | bytes 786440 | tf_op jit(solution)/shard_map/ppermute | solution.py:18
  55.4 21.6 %collective-permute-start.13 = (bf16[16,128,64]{1,2,0:T(8,128)(2,1)S(1)}, bf16[16,128,64]{1,2,0:T(8,128)(2,1)S(1)}, u32[]{:S(2)}, u32[]{:S(2)}) collective-permute-start(bf16[16,128,64]{1,2,0:T(8,128)(2,1)S(1)} %get-tuple-element.33), channel_id=1, source_target_pairs={{0,4},{4,0},{8,12},{12,8},{16,20},{20,16},{24,28},{28,24},{1,5},{5... | collective-permute-start | bytes 786440 | tf_op jit(solution)/shard_map/ppermute | solution.py:18
  56.4 20.6 %collective-permute-start.7 = (bf16[16,128,64]{1,2,0:T(8,128)(2,1)S(1)}, bf16[16,128,64]{1,2,0:T(8,128)(2,1)S(1)}, u32[]{:S(2)}, u32[]{:S(2)}) collective-permute-start(bf16[16,128,64]{1,2,0:T(8,128)(2,1)S(1)} %get-tuple-element.34), channel_id=1, source_target_pairs={{0,4},{4,0},{8,12},{12,8},{16,20},{20,16},{24,28},{28,24},{1,5},{5... | collective-permute-start | bytes 786440 | tf_op jit(solution)/shard_map/ppermute | solution.py:18
  63.8 6.8 %collective-permute-start.21 = (bf16[16,128,64]{1,2,0:T(8,128)(2,1)S(1)}, bf16[16,128,64]{1,2,0:T(8,128)(2,1)S(1)}, u32[]{:S(2)}, u32[]{:S(2)}) collective-permute-start(bf16[16,128,64]{1,2,0:T(8,128)(2,1)S(1)} %fusion.98), channel_id=1, source_target_pairs={{0,8},{4,12},{8,0},{12,4},{16,24},{20,28},{24,16},{28,20},{1,9},{5... | collective-permute-start | bytes 786440 | tf_op jit(solution)/shard_map/ppermute | solution.py:18
  72.1 6.4 %collective-permute-start.3 = (bf16[16,128,64]{1,2,0:T(8,128)(2,1)S(1)}, bf16[16,128,64]{1,2,0:T(8,128)(2,1)S(1)}, u32[]{:S(2)}, u32[]{:S(2)}) collective-permute-start(bf16[16,128,64]{1,2,0:T(8,128)(2,1)S(1)} %get-tuple-element.29), channel_id=1, source_target_pairs={{0,8},{4,12},{8,0},{12,4},{16,24},{20,28},{24,16},{28,20},{1,9},{5... | collective-permute-start | bytes 786440 | tf_op jit(solution)/shard_map/ppermute | solution.py:18
  75.6 10.3 %collective-permute-start.23 = (bf16[16,128,64]{1,2,0:T(8,128)(2,1)}, bf16[16,128,64]{1,2,0:T(8,128)(2,1)}, u32[]{:S(2)}, u32[]{:S(2)}) collective-permute-start(bf16[16,128,64]{1,2,0:T(8,128)(2,1)} %get-tuple-element.30), channel_id=1, source_target_pairs={{8,16},{12,20},{9,17},{13,21},{10,18},{14,22},{11,19},{15,23}} | collective-permute-start | bytes 786440 | tf_op jit(solution)/shard_map/ppermute | solution.py:96
  80.5 8.2 %collective-permute-start.15 = (bf16[16,128,64]{1,2,0:T(8,128)(2,1)}, bf16[16,128,64]{1,2,0:T(8,128)(2,1)}, u32[]{:S(2)}, u32[]{:S(2)}) collective-permute-start(bf16[16,128,64]{1,2,0:T(8,128)(2,1)} %get-tuple-element.28), channel_id=1, source_target_pairs={{0,8},{4,12},{8,0},{12,4},{16,24},{20,28},{24,16},{28,20},{1,9},{5... | collective-permute-start | bytes 786440 | tf_op jit(solution)/shard_map/ppermute | solution.py:18
  84.0 7.5 %collective-permute-start.9 = (bf16[16,128,64]{1,2,0:T(8,128)(2,1)}, bf16[16,128,64]{1,2,0:T(8,128)(2,1)}, u32[]{:S(2)}, u32[]{:S(2)}) collective-permute-start(bf16[16,128,64]{1,2,0:T(8,128)(2,1)} %get-tuple-element.27), channel_id=1, source_target_pairs={{0,8},{4,12},{8,0},{12,4},{16,24},{20,28},{24,16},{28,20},{1,9},{5... | collective-permute-start | bytes 786440 | tf_op jit(solution)/shard_map/ppermute | solution.py:18
  85.2 9.7 %collective-permute-start.5 = (bf16[16,128,64]{1,2,0:T(8,128)(2,1)}, bf16[16,128,64]{1,2,0:T(8,128)(2,1)S(1)}, u32[]{:S(2)}, u32[]{:S(2)}) collective-permute-start(bf16[16,128,64]{1,2,0:T(8,128)(2,1)} %get-tuple-element.26), channel_id=1, source_target_pairs={{8,16},{12,20},{9,17},{13,21},{10,18},{14,22},{11,19},{15,23}} | collective-permute-start | bytes 786440 | tf_op jit(solution)/shard_map/ppermute | solution.py:96
  85.9 9.7 %collective-permute-start.24 = (bf16[16,128,64]{1,2,0:T(8,128)(2,1)}, bf16[16,128,64]{1,2,0:T(8,128)(2,1)S(1)}, u32[]{:S(2)}, u32[]{:S(2)}) collective-permute-start(bf16[16,128,64]{1,2,0:T(8,128)(2,1)} %collective-permute-done.23), channel_id=1, source_target_pairs={{16,24},{20,28},{17,25},{21,29},{18,26},{22,30},{19,27},{23,31}} | collective-permute-start | bytes 786440 | tf_op jit(solution)/shard_map/ppermute | solution.py:97
  94.2 4.4 %collective-permute-start.17 = (bf16[16,128,64]{1,2,0:T(8,128)(2,1)S(1)}, bf16[16,128,64]{1,2,0:T(8,128)(2,1)S(1)}, u32[]{:S(2)}, u32[]{:S(2)}) collective-permute-start(bf16[16,128,64]{1,2,0:T(8,128)(2,1)S(1)} %get-tuple-element.36), channel_id=1, source_target_pairs={{8,16},{12,20},{9,17},{13,21},{10,18},{14,22},{11,19},{15,23}} | collective-permute-start | bytes 786440 | tf_op jit(solution)/shard_map/ppermute | solution.py:96
  94.9 4.4 %collective-permute-start.6 = (bf16[16,128,64]{1,2,0:T(8,128)(2,1)S(1)}, bf16[16,128,64]{1,2,0:T(8,128)(2,1)S(1)}, u32[]{:S(2)}, u32[]{:S(2)}) collective-permute-start(bf16[16,128,64]{1,2,0:T(8,128)(2,1)S(1)} %collective-permute-done.5), channel_id=1, source_target_pairs={{16,24},{20,28},{17,25},{21,29},{18,26},{22,30},{19,27},{23,31}} | collective-permute-start | bytes 786440 | tf_op jit(solution)/shard_map/ppermute | solution.py:97
  111.5 29.4 %collective-permute-start.25 = (f32[3,128]{1,0:T(4,128)S(1)}, f32[3,128]{1,0:T(4,128)S(1)}, u32[]{:S(2)}, u32[]{:S(2)}) collective-permute-start(f32[3,128]{1,0:T(4,128)S(1)} %slice.197), channel_id=1, source_target_pairs={{4,0},{8,4},{12,8},{16,12},{20,16},{24,20},{28,24},{5,1},{9,5},{13... | collective-permute-start | bytes 4616 | tf_op jit(solution)/shard_map/ppermute | solution.py:12
  115.2 16.1 %collective-permute-start.27 = (f32[8,12,64]{2,0,1:T(8,128)S(1)}, f32[8,12,64]{2,0,1:T(8,128)S(1)}, u32[]{:S(2)}, u32[]{:S(2)}) collective-permute-start(f32[8,12,64]{2,0,1:T(8,128)S(1)} %fusion.97), channel_id=1, source_target_pairs={{0,8},{4,12},{8,0},{12,4},{16,24},{20,28},{24,16},{28,20},{1,9},{5... | collective-permute-start | bytes 73736 | tf_op jit(solution)/shard_map/ppermute | solution.py:18
  131.3 11.6 %collective-permute-start.28 = (f32[8,12,64]{2,0,1:T(8,128)S(1)}, f32[8,12,64]{2,0,1:T(8,128)S(1)}, u32[]{:S(2)}, u32[]{:S(2)}) collective-permute-start(f32[8,12,64]{2,0,1:T(8,128)S(1)} %add.248), channel_id=1, source_target_pairs={{0,16},{4,20},{8,24},{12,28},{16,0},{20,4},{24,8},{28,12},{1,17},{... | collective-permute-start | bytes 73736 | tf_op jit(solution)/shard_map/ppermute | solution.py:18
  (77 other events, 493.4 us)

commit v7 on v5

--- a/solution.py
+++ b/solution.py
@@ -58,10 +58,16 @@
     return (x_act, b_key, c_query)
 
 
-def local_group(x_part, b_part, c_part, decay_part, grad_part, weight_zero):
+def group_state_of(x_part, b_part, decay_part):
+    cumul = jnp.cumsum(decay_part, axis=0)
+    x_faded = (x_part * jnp.exp(cumul[-1][None, :] - cumul)[:, :, None]).astype(jnp.bfloat16)
+    group_state = contract("sn,shp->hnp", b_part, x_faded)
+    return (group_state, cumul)
+
+
+def local_group(x_part, b_part, c_part, cumul, grad_part, weight_zero):
     length = x_part.shape[0]
     state_dim = b_part.shape[1]
-    cumul = jnp.cumsum(decay_part, axis=0)
     scores = jnp.dot(c_part, b_part.T, preferred_element_type=jnp.float32)
     causal = (jnp.arange(length)[:, None] >= jnp.arange(length)[None, :])[None]
     across = jnp.transpose(cumul)
@@ -70,15 +76,13 @@
     basic = fading * scores[None] / state_dim
     intra = (weight_zero[:, None, None] * basic).astype(jnp.bfloat16)
     y_inner = contract("hts,shp->thp", intra, x_part)
-    x_faded = (x_part * jnp.exp(cumul[-1][None, :] - cumul)[:, :, None]).astype(jnp.bfloat16)
-    group_state = contract("sn,shp->hnp", b_part, x_faded)
     products = contract("thp,shp->hts", grad_part, x_part)
     grad_weight = (
         jnp.sum(weight_zero[:, None, None] * fading * products, axis=0) / state_dim
     ).astype(jnp.bfloat16)
     grad_inner = jnp.dot(grad_weight, b_part, preferred_element_type=jnp.float32)
     level_zero = jnp.sum(basic * products, axis=(1, 2))
-    return (y_inner, group_state, cumul, grad_inner, level_zero)
+    return (y_inner, grad_inner, level_zero)
 
 
 def combine(block, block_decay, other, other_decay, leading, upper):
@@ -101,6 +105,7 @@
 def exchange(block, block_decay, depth, myself):
     leading = jnp.zeros_like(block_decay)
     found_all = []
+    first = None
     for bit_pos in range(depth):
         if bit_pos == depth - 1:
             if bit_pos == 0:
@@ -111,6 +116,7 @@
         else:
             sent, other_decay = from_partner((block.astype(jnp.bfloat16), block_decay), "seq", bit_pos)
             other = sent.astype(jnp.float32)
+        first = sent if first is None else first
         upper = jnp.zeros_like(block_decay) + (jnp.right_shift(myself, bit_pos) & 1).astype(
             jnp.float32
         )
@@ -118,7 +124,8 @@
             block, block_decay, other, other_decay, leading, upper
         )
         found_all.append(found)
-    return jnp.stack(found_all, axis=0)
+    first = block if first is None else first
+    return (jnp.stack(found_all, axis=0), first)
 
 
 def local(
@@ -147,13 +154,9 @@
     x_groups = x_act.reshape(groups, group_len, heads, head_dim)
     c_groups = c_query.reshape(groups, group_len, state_dim)
     grad_groups = grad_out.reshape(groups, group_len, heads, head_dim)
-    y_inner, states, cumuls, grad_inner, level_zero = jax.vmap(local_group)(
-        x_groups,
-        b_key.reshape(groups, group_len, state_dim),
-        c_groups,
-        log_decay.reshape(groups, group_len, heads),
-        grad_groups,
-        weight_rows[:, 0],
+    b_groups = b_key.reshape(groups, group_len, state_dim)
+    states, cumuls = jax.vmap(group_state_of)(
+        x_groups, b_groups, log_decay.reshape(groups, group_len, heads)
     )
     totals = cumuls[:, -1]
     dev_decay = jnp.sum(totals, axis=0)
@@ -168,7 +171,12 @@
         exchange(dev_state[k * width : (k + 1) * width], dev_decay[k * width : (k + 1) * width], depth, myself)
         for k in range(chunks)
     ]
-    cross = jnp.concatenate(pieces, axis=1)
+    cross = jnp.concatenate([piece for piece, _ in pieces], axis=1)
+    late_cotangent = lax.optimization_barrier((cotangent, pieces[0][1]))[0]
+    grad_groups = late_cotangent.reshape(groups, group_len, heads, head_dim)
+    y_inner, grad_inner, level_zero = jax.vmap(local_group)(
+        x_groups, b_groups, c_groups, cumuls, grad_groups, weight_rows[:, 0]
+    )
     low_levels = groups.bit_length() - 1
     local_ids = jnp.arange(groups, dtype=jnp.int32)
     differ = jnp.bitwise_xor(local_ids[:, None], local_ids[None, :])

time: 141 us -> 133 us (0.943)
  waiting for transfers between devices: 22.5 us -> 16.7 us
  other arithmetic: 24.1 us -> 20.1 us
  matrix products: 14.9 us -> 16.7 us
    reshape x0 -> x2, local copies, waits for them, and re-layouts: none -> 8.43 us  [local(): grad_groups = late_cotangent.reshape(groups, group_len, heads, head_dim)]
    another operation x2 -> x0, local copies, waits for them, and re-layouts: 6.22 us -> none  [local(): grad_groups = grad_out.reshape(groups, group_len, heads, head_dim)]
    ppermute x11, waiting for transfers between devices: 22.5 us -> 16.7 us  [from_partner(): return lax.ppermute(value, axis, pairs)]
    dot_general x6, matrix products: 12.9 us -> 14.7 us  [contract(): return jnp.einsum(form, left, right, preferred_element_type=jnp.float32)]
    concatenate x1, other arithmetic: 2.67 us -> 1.22 us  [local(): cross = jnp.concatenate([piece for piece, _ in pieces], axis=1)]
  transfers between devices with their start and end apart: 17 -> 17, of which waited for: 8 -> 6; matrix products, arithmetic and copies ran while one was open for 35% -> 39% of each run, Pallas kernels for 0% -> 0%
where the time goes in v7:
time: 133 us; the launch traced here: 132 us
  starting transfers between devices  48 us (36%)
  local copies, waits for them, and re-layouts  29.5 us (22%)
  other arithmetic  20.1 us (15%)
  matrix products  16.7 us (13%)
  waiting for transfers between devices  16.7 us (13%)
    ppermute x11, starting transfers between devices, from_partner(): return lax.ppermute(value, axis, pairs)  39.8 us
    ppermute x11, waiting for transfers between devices, from_partner(): return lax.ppermute(value, axis, pairs)  16.7 us
    dot_general x6, matrix products, contract(): return jnp.einsum(form, left, right, preferred_element_type=jnp.float32)  14.7 us
    reshape x2, local copies, waits for them, and re-layouts, local(): grad_groups = late_cotangent.reshape(groups, group_len, heads, head_dim)  8.43 us
    another operation x2, local copies, waits for them, and re-layouts, local(): x_groups = x_act.reshape(groups, group_len, heads, head_dim)  5.25 us
    ppermute x2, starting transfers between devices, shifted(): lax.ppermute(value, axis, [(source, source + steps) for source in range(l...  5.15 us
    another operation x1, other arithmetic  3.46 us
    convert_element_type x1, local copies, waits for them, and re-layouts, local(): ssm_out = (y_inner + y_cross + skip[None, None, :, None] * x_groups).asty...  3.31 us
  transfers between devices with their start and end apart: 17, of which 6 were waited for; matrix products, arithmetic and copies ran while one was open for 39% of the time, Pallas kernels for 0%

profile of v7, /device:TPU:0, one launch (start us, length us, event | category | flops | bytes accessed | tf_op | source)
XLA Modules:
  0.0 132.3 jit_solution(5894084104324564830)
XLA Ops:
  2.5 2.9 %collective-permute-start.2 = (f32[32]{0:T(128)S(1)}, f32[32]{0:T(128)S(1)}, u32[]{:S(2)}, u32[]{:S(2)}) collective-permute-start(f32[32]{0:T(128)S(1)} %get-tuple-element.63), channel_id=1, source_target_pairs={{0,4},{4,0},{8,12},{12,8},{16,20},{20,16},{24,28},{28,24},{1,5},{5... | collective-permute-start | bytes 392 | tf_op jit(solution)/shard_map/ppermute | solution.py:18
  6.4 3.9 %collective-permute-start = (bf16[3,4352]{1,0:T(4,128)(2,1)S(1)}, bf16[3,4352]{1,0:T(4,128)(2,1)S(1)}, u32[]{:S(2)}, u32[]{:S(2)}) collective-permute-start(bf16[3,4352]{1,0:T(4,128)(2,1)S(1)} %slice.119), channel_id=1, source_target_pairs={{0,4},{4,8},{8,12},{12,16},{16,20},{20,24},{24,28},{1,5},{5,9},{9,... | collective-permute-start | bytes 78344 | tf_op jit(solution)/shard_map/ppermute | solution.py:12
  16.7 3.5 %fusion.79 = (bf16[128,4352]{1,0:T(8,128)(2,1)S(1)}, f32[128,4352]{1,0:T(8,128)S(1)}) fusion(f32[4352]{0:T(1024)S(1)} %get-tuple-element.8, bf16[128,4352]{1,0:T(8,128)(2,1)} %param.9, f32[4352]{0:T(1024)S(1)} %get-tuple-element.9, bf16[3,4352]{1,0:T(4,128)(2,1)S(1)} %collective-permute-done, f32[4352]{0:T(1024)S(1)} %get-tuple-element.10, ...), kind=kLoop, calls=%fused_computation.163 | loop fusion | flops 12255232 | bytes 4569600 | tf_op jit(solution)/shard_map/convert.2
  20.7 2.3 %reshape_reshape.3 = bf16[2,64,64,64]{3,2,1,0:T(8,128)(2,1)S(1)} reshape(bf16[128,4096]{1,0:T(8,128)(2,1)S(1)} %multiply_convert_fusion.5) | data formatting | bytes 2097152 | tf_op jit(solution)/shard_map/reshape;reshape | solution.py:154
  23.0 3.0 %copy.46 = bf16[2,64,64,64]{1,3,2,0:T(8,128)(2,1)} copy(bf16[2,64,64,64]{3,2,1,0:T(8,128)(2,1)S(1)} %reshape_reshape.3) | data formatting | bytes 2097152 | tf_op jit(solution)/shard_map/reshape;reshape | solution.py:154
  26.0 2.5 %multiply_reduce_fusion.4 = (f32[64,128,64]{1,2,0:T(8,128)S(1)}, f32[2,64,128,64]{2,3,1,0:T(8,128)S(1)}) fusion(f32[2,64]{1,0:T(2,128)S(1)} %get-tuple-element.52, bf16[2,64,128,1]{2,1,3,0:T(8,128)(2,1)S(1)} %bitcast.95, bf16[2,64,64,64]{1,3,2,0:T(8,128)(2,1)} %copy.46, f32[2,64,64]{1,2,0:T(8,128)S(1)} %copy.49), kind=kOutput, calls=%fused_computation.14 | convolution fusion | flops 137363456 | bytes 7406080 | tf_op jit(solution)/shard_map/vmap(sn,shp->hnp)/dot_general | solution.py:35
  29.6 1.5 %collective-permute-start.1 = (bf16[32,128,64]{1,2,0:T(8,128)(2,1)S(1)}, bf16[32,128,64]{1,2,0:T(8,128)(2,1)S(1)}, u32[]{:S(2)}, u32[]{:S(2)}) collective-permute-start(bf16[32,128,64]{1,2,0:T(8,128)(2,1)S(1)} %get-tuple-element.26), channel_id=1, source_target_pairs={{0,4},{4,0},{8,12},{12,8},{16,20},{20,16},{24,28},{28,24},{1,5},{5... | collective-permute-start | bytes 1572872 | tf_op jit(solution)/shard_map/ppermute | solution.py:18
  31.2 1.6 %collective-permute-start.10 = (f32[32]{0:T(128)S(1)}, f32[32]{0:T(128)S(1)}, u32[]{:S(2)}, u32[]{:S(2)}) collective-permute-start(f32[32]{0:T(128)S(1)} %get-tuple-element.60), channel_id=1, source_target_pairs={{0,8},{4,12},{8,0},{12,4},{16,24},{20,28},{24,16},{28,20},{1,9},{5... | collective-permute-start | bytes 392 | tf_op jit(solution)/shard_map/ppermute | solution.py:18
  37.4 7.1 %collective-permute-done.1 = bf16[32,128,64]{1,2,0:T(8,128)(2,1)S(1)} collective-permute-done((bf16[32,128,64]{1,2,0:T(8,128)(2,1)S(1)}, bf16[32,128,64]{1,2,0:T(8,128)(2,1)S(1)}, u32[]{:S(2)}, u32[]{:S(2)}) %collective-permute-start.1) | collective-permute-done | bytes 524320 | tf_op jit(solution)/shard_map/ppermute | solution.py:18
  45.7 1.6 %collective-permute-start.3 = (bf16[32,128,64]{1,2,0:T(8,128)(2,1)}, bf16[32,128,64]{1,2,0:T(8,128)(2,1)}, u32[]{:S(2)}, u32[]{:S(2)}) collective-permute-start(bf16[32,128,64]{1,2,0:T(8,128)(2,1)} %fusion.75), channel_id=1, source_target_pairs={{0,8},{4,12},{8,0},{12,4},{16,24},{20,28},{24,16},{28,20},{1,9},{5... | collective-permute-start | bytes 1572872 | tf_op jit(solution)/shard_map/ppermute | solution.py:18
  47.4 2.4 %slice_bitcast_fusion.4 = (f32[64,128,64]{1,2,0:T(8,128)}, f32[64,128,64]{1,2,0:T(8,128)}) fusion(f32[2,64,128,64]{2,3,1,0:T(8,128)S(1)} %get-tuple-element.68), kind=kLoop, calls=%fused_computation.26 | loop fusion | bytes 8388608 | tf_op jit(solution)/shard_map/mul | solution.py:196
  49.8 4.2 %reshape.130 = bf16[2,64,64,64]{3,2,1,0:T(8,128)(2,1)} reshape(bf16[128,4096]{1,0:T(8,128)(2,1)} %param.17) | data formatting | bytes 2097152 | tf_op jit(solution)/shard_map/reshape | solution.py:176
  54.0 4.2 %copy.55 = bf16[2,64,64,64]{1,3,2,0:T(8,128)(2,1)} copy(bf16[2,64,64,64]{3,2,1,0:T(8,128)(2,1)} %reshape.130) | data formatting | bytes 2097152 | tf_op jit(solution)/shard_map/reshape | solution.py:176
  58.2 2.3 %fusion.30 = (bf16[32,128,64]{1,2,0:T(8,128)(2,1)S(1)}, bf16[32,128,64]{1,2,0:T(8,128)(2,1)S(1)}, f32[1,32,128,64]{2,3,1,0:T(8,128)S(1)}, f32[1,32,128,64]{2,3,1,0:T(8,128)S(1)}, f32[1,32,128,64]{2,3,1,0:T(8,128)S(1)}) fusion(bf16[32,128,64]{1,2,0:T(8,128)(2,1)} %collective-permute-done.3, f32[32]{0:T(128)S(1)} %get-tuple-element.55, f32[]{:T(128)S(6)} %sub.97, ...), kind=kLoop, calls=%fused_computation.67 | loop fusion | flops 7602176 | bytes 7865232 | tf_op jit(solution)/shard_map/convert_element_type | solution.py:114
  61.0 3.7 %multiply_reduce_fusion.2 = (f32[2,64]{1,0:T(2,128)S(1)}, f32[2,64,64]{2,1,0:T(8,128)S(1)}) fusion(f32[2,64,64]{2,1,0:T(8,128)S(1)} %fusion.85, f32[2,64,64]{2,1,0:T(8,128)S(1)} %copy.44, pred[64,64]{1,0:T(8,128)(4,1)S(1)} %iota_compare_fusion, f32[2,64]{1,0:T(2,128)S(1)} %copy-done.18, bf16[2,64,64,64]{1,3,2,0:T(8,128)(2,1)S(1)} %copy-done.4, ...), kind=kOutput, calls=%fused_computation.10 | convolution fusion | flops 72343424 | bytes 2200576 | tf_op jit(solution)/shard_map/vmap(thp,shp->hts)/dot_general | solution.py:35
  65.5 4.7 %collective-permute-done.9 = bf16[32,128,64]{1,2,0:T(8,128)(2,1)S(1)} collective-permute-done((bf16[32,128,64]{1,2,0:T(8,128)(2,1)S(1)}, bf16[32,128,64]{1,2,0:T(8,128)(2,1)S(1)}, u32[]{:S(2)}, u32[]{:S(2)}) %collective-permute-start.9) | collective-permute-done | bytes 524320 | tf_op jit(solution)/shard_map/ppermute | solution.py:18
  81.5 1.7 %add_convert_fusion = bf16[2,64,128,64]{2,3,1,0:T(8,128)(2,1)S(1)} fusion(f32[64,128,64]{1,2,0:T(8,128)S(1)} %get-tuple-element.20, f32[2,64]{1,0:T(2,128)S(1)} %get-tuple-element.45, f32[64,128,64]{1,2,0:T(8,128)S(1)} %get-tuple-element.21, f32[2,64]{1,0:T(2,128)S(1)} %get-tuple-element.46, f32[64,128,64]{1,2,0:T(8,128)S(1)} %get-tuple-element.19, ...), kind=kLoop, calls=%fused_computation.13 | loop fusion | flops 10485760 | bytes 12585472 | tf_op jit(solution)/shard_map/convert_element_type | solution.py:198
  83.2 2.0 %fusion.3 = f32[2,64,128]{2,1,0:T(8,128)S(1)} fusion(bf16[2,64,64,64]{1,3,2,0:T(8,128)(2,1)S(1)} %copy-done.5, bf16[2,64,128,64]{2,3,1,0:T(8,128)(2,1)S(1)} %add_convert_fusion, f32[2,64,64]{1,2,0:T(8,128)S(1)} %copy.50), kind=kOutput, calls=%fused_computation.9 | convolution fusion | flops 136298496 | bytes 3244032 | tf_op jit(solution)/shard_map/chnp,cthp->cthn/dot_general | solution.py:35
  87.1 1.6 %collective-permute-start.14 = (f32[8,12,64]{2,0,1:T(8,128)S(1)}, f32[8,12,64]{2,0,1:T(8,128)S(1)}, u32[]{:S(2)}, u32[]{:S(2)}) collective-permute-start(f32[8,12,64]{2,0,1:T(8,128)S(1)} %pad_maximum_fusion.2), channel_id=1, source_target_pairs={{0,4},{4,0},{8,12},{12,8},{16,20},{20,16},{24,28},{28,24},{1,5},{5... | collective-permute-start | bytes 73736 | tf_op jit(solution)/shard_map/ppermute | solution.py:18
  91.3 12.8 %collective-permute-start.15 = (f32[8,12,64]{2,0,1:T(8,128)S(1)}, f32[8,12,64]{2,0,1:T(8,128)S(1)}, u32[]{:S(2)}, u32[]{:S(2)}) collective-permute-start(f32[8,12,64]{2,0,1:T(8,128)S(1)} %fusion.73), channel_id=1, source_target_pairs={{0,8},{4,12},{8,0},{12,4},{16,24},{20,28},{24,16},{28,20},{1,9},{5... | collective-permute-start | bytes 73736 | tf_op jit(solution)/shard_map/ppermute | solution.py:18
  104.1 3.5 %fusion.2 = bf16[2,64,64,64]{1,3,2,0:T(8,128)(2,1)} fusion(bf16[2,64,64,64]{1,3,2,0:T(8,128)(2,1)S(1)} %copy-done.3, f32[2,64,64,64]{3,2,1,0:T(8,128)S(1)} %fusion.6, f32[64]{0:T(128)S(1)} %copy-done.22, f32[2,64]{1,0:T(2,128)S(1)} %copy-done.17, f32[2,64,64]{2,1,0:T(8,128)S(1)} %fusion.85, f32[2,64,64]{2,1,0:T(8,128)S(1)} %copy.44, ...), kind=kOutput, calls=%fused_computation.7 | convolution fusion | flops 72876032 | bytes 4264704 | tf_op jit(solution)/shard_map/vmap(hts,shp->thp)/dot_general | solution.py:35
  107.5 3.3 %copy.51 = bf16[2,64,64,64]{3,2,1,0:T(8,128)(2,1)S(1)} copy(bf16[2,64,64,64]{1,3,2,0:T(8,128)(2,1)} %fusion.2) | data formatting | bytes 2097152 | tf_op jit(solution)/shard_map/convert_element_type | solution.py:219
  110.9 2.5 %reshape.129 = bf16[128,4096]{1,0:T(8,128)(2,1)} reshape(bf16[2,64,64,64]{3,2,1,0:T(8,128)(2,1)S(1)} %copy.51) | data formatting | bytes 2097152 | tf_op jit(solution)/shard_map/reshape | solution.py:220
  113.4 16.2 %collective-permute-start.16 = (f32[8,12,64]{2,0,1:T(8,128)S(1)}, f32[8,12,64]{2,0,1:T(8,128)S(1)}, u32[]{:S(2)}, u32[]{:S(2)}) collective-permute-start(f32[8,12,64]{2,0,1:T(8,128)S(1)} %add.170), channel_id=1, source_target_pairs={{0,16},{4,20},{8,24},{12,28},{16,0},{20,4},{24,8},{28,12},{1,17},{... | collective-permute-start | bytes 73736 | tf_op jit(solution)/shard_map/ppermute | solution.py:18
  (130 shorter events, 36.2 us)
Async XLA Ops:
  2.5 28.7 %collective-permute-start.2 = (f32[32]{0:T(128)S(1)}, f32[32]{0:T(128)S(1)}, u32[]{:S(2)}, u32[]{:S(2)}) collective-permute-start(f32[32]{0:T(128)S(1)} %get-tuple-element.63), channel_id=1, source_target_pairs={{0,4},{4,0},{8,12},{12,8},{16,20},{20,16},{24,28},{28,24},{1,5},{5... | collective-permute-start | bytes 392 | tf_op jit(solution)/shard_map/ppermute | solution.py:18
  5.4 25.8 %collective-permute-start.8 = (f32[32]{0:T(128)S(1)}, f32[32]{0:T(128)S(1)}, u32[]{:S(2)}, u32[]{:S(2)}) collective-permute-start(f32[32]{0:T(128)S(1)} %get-tuple-element.64), channel_id=1, source_target_pairs={{0,4},{4,0},{8,12},{12,8},{16,20},{20,16},{24,28},{28,24},{1,5},{5... | collective-permute-start | bytes 392 | tf_op jit(solution)/shard_map/ppermute | solution.py:18
  6.4 10.3 %collective-permute-start = (bf16[3,4352]{1,0:T(4,128)(2,1)S(1)}, bf16[3,4352]{1,0:T(4,128)(2,1)S(1)}, u32[]{:S(2)}, u32[]{:S(2)}) collective-permute-start(bf16[3,4352]{1,0:T(4,128)(2,1)S(1)} %slice.119), channel_id=1, source_target_pairs={{0,4},{4,8},{8,12},{12,16},{16,20},{20,24},{24,28},{1,5},{5,9},{9,... | collective-permute-start | bytes 78344 | tf_op jit(solution)/shard_map/ppermute | solution.py:12
  28.5 18.9 %copy-start = (f32[2,64,128,64]{2,3,1,0:T(8,128)}, f32[2,64,128,64]{2,3,1,0:T(8,128)S(1)}, u32[]{:S(2)}) copy-start(f32[2,64,128,64]{2,3,1,0:T(8,128)S(1)} %get-tuple-element.68) | copy-start | bytes 12582916
  29.6 14.9 %collective-permute-start.1 = (bf16[32,128,64]{1,2,0:T(8,128)(2,1)S(1)}, bf16[32,128,64]{1,2,0:T(8,128)(2,1)S(1)}, u32[]{:S(2)}, u32[]{:S(2)}) collective-permute-start(bf16[32,128,64]{1,2,0:T(8,128)(2,1)S(1)} %get-tuple-element.26), channel_id=1, source_target_pairs={{0,4},{4,0},{8,12},{12,8},{16,20},{20,16},{24,28},{28,24},{1,5},{5... | collective-permute-start | bytes 1572872 | tf_op jit(solution)/shard_map/ppermute | solution.py:18
  31.2 3.6 %collective-permute-start.10 = (f32[32]{0:T(128)S(1)}, f32[32]{0:T(128)S(1)}, u32[]{:S(2)}, u32[]{:S(2)}) collective-permute-start(f32[32]{0:T(128)S(1)} %get-tuple-element.60), channel_id=1, source_target_pairs={{0,8},{4,12},{8,0},{12,4},{16,24},{20,28},{24,16},{28,20},{1,9},{5... | collective-permute-start | bytes 392 | tf_op jit(solution)/shard_map/ppermute | solution.py:18
  32.8 3.5 %collective-permute-start.4 = (f32[32]{0:T(128)S(1)}, f32[32]{0:T(128)S(1)}, u32[]{:S(2)}, u32[]{:S(2)}) collective-permute-start(f32[32]{0:T(128)S(1)} %get-tuple-element.14), channel_id=1, source_target_pairs={{0,8},{4,12},{8,0},{12,4},{16,24},{20,28},{24,16},{28,20},{1,9},{5... | collective-permute-start | bytes 392 | tf_op jit(solution)/shard_map/ppermute | solution.py:18
  36.9 21.3 %collective-permute-start.7 = (bf16[32,128,64]{1,2,0:T(8,128)(2,1)}, bf16[32,128,64]{1,2,0:T(8,128)(2,1)S(1)}, u32[]{:S(2)}, u32[]{:S(2)}) collective-permute-start(bf16[32,128,64]{1,2,0:T(8,128)(2,1)} %get-tuple-element.27), channel_id=1, source_target_pairs={{0,4},{4,0},{8,12},{12,8},{16,20},{20,16},{24,28},{28,24},{1,5},{5... | collective-permute-start | bytes 1572872 | tf_op jit(solution)/shard_map/ppermute | solution.py:18
  45.7 12.5 %collective-permute-start.3 = (bf16[32,128,64]{1,2,0:T(8,128)(2,1)}, bf16[32,128,64]{1,2,0:T(8,128)(2,1)}, u32[]{:S(2)}, u32[]{:S(2)}) collective-permute-start(bf16[32,128,64]{1,2,0:T(8,128)(2,1)} %fusion.75), channel_id=1, source_target_pairs={{0,8},{4,12},{8,0},{12,4},{16,24},{20,28},{24,16},{28,20},{1,9},{5... | collective-permute-start | bytes 1572872 | tf_op jit(solution)/shard_map/ppermute | solution.py:18
  60.5 9.6 %collective-permute-start.9 = (bf16[32,128,64]{1,2,0:T(8,128)(2,1)S(1)}, bf16[32,128,64]{1,2,0:T(8,128)(2,1)S(1)}, u32[]{:S(2)}, u32[]{:S(2)}) collective-permute-start(bf16[32,128,64]{1,2,0:T(8,128)(2,1)S(1)} %get-tuple-element.25), channel_id=1, source_target_pairs={{0,8},{4,12},{8,0},{12,4},{16,24},{20,28},{24,16},{28,20},{1,9},{5... | collective-permute-start | bytes 1572872 | tf_op jit(solution)/shard_map/ppermute | solution.py:18
  64.8 8.5 %collective-permute-start.5 = (bf16[32,128,64]{1,2,0:T(8,128)(2,1)S(1)}, bf16[32,128,64]{1,2,0:T(8,128)(2,1)S(1)}, u32[]{:S(2)}, u32[]{:S(2)}) collective-permute-start(bf16[32,128,64]{1,2,0:T(8,128)(2,1)S(1)} %get-tuple-element.24), channel_id=1, source_target_pairs={{8,16},{12,20},{9,17},{13,21},{10,18},{14,22},{11,19},{15,23}} | collective-permute-start | bytes 1572872 | tf_op jit(solution)/shard_map/ppermute | solution.py:100
  70.9 4.2 %collective-permute-start.11 = (bf16[32,128,64]{1,2,0:T(8,128)(2,1)S(1)}, bf16[32,128,64]{1,2,0:T(8,128)(2,1)S(1)}, u32[]{:S(2)}, u32[]{:S(2)}) collective-permute-start(bf16[32,128,64]{1,2,0:T(8,128)(2,1)S(1)} %get-tuple-element.34), channel_id=1, source_target_pairs={{8,16},{12,20},{9,17},{13,21},{10,18},{14,22},{11,19},{15,23}} | collective-permute-start | bytes 1572872 | tf_op jit(solution)/shard_map/ppermute | solution.py:100
  73.3 3.0 %collective-permute-start.6 = (bf16[32,128,64]{1,2,0:T(8,128)(2,1)S(1)}, bf16[32,128,64]{1,2,0:T(8,128)(2,1)S(1)}, u32[]{:S(2)}, u32[]{:S(2)}) collective-permute-start(bf16[32,128,64]{1,2,0:T(8,128)(2,1)S(1)} %collective-permute-done.5), channel_id=1, source_target_pairs={{16,24},{20,28},{17,25},{21,29},{18,26},{22,30},{19,27},{23,31}} | collective-permute-start | bytes 1572872 | tf_op jit(solution)/shard_map/ppermute | solution.py:101
  75.1 1.4 %collective-permute-start.12 = (bf16[32,128,64]{1,2,0:T(8,128)(2,1)S(1)}, bf16[32,128,64]{1,2,0:T(8,128)(2,1)S(1)}, u32[]{:S(2)}, u32[]{:S(2)}) collective-permute-start(bf16[32,128,64]{1,2,0:T(8,128)(2,1)S(1)} %collective-permute-done.11), channel_id=1, source_target_pairs={{16,24},{20,28},{17,25},{21,29},{18,26},{22,30},{19,27},{23,31}} | collective-permute-start | bytes 1572872 | tf_op jit(solution)/shard_map/ppermute | solution.py:101
  85.2 18.9 %copy-start.3 = (bf16[2,64,64,64]{1,3,2,0:T(8,128)(2,1)S(1)}, bf16[2,64,64,64]{1,3,2,0:T(8,128)(2,1)}, u32[]{:S(2)}) copy-start(bf16[2,64,64,64]{1,3,2,0:T(8,128)(2,1)} %copy.46) | copy-start | bytes 3145732
  85.2 18.9 %copy-start.17 = (f32[2,64]{1,0:T(2,128)S(1)}, f32[2,64]{1,0:T(2,128)}, u32[]{:S(2)}) copy-start(f32[2,64]{1,0:T(2,128)} %broadcast_multiply_fusion) | copy-start | bytes 1540
  85.2 18.8 %copy-start.22 = (f32[64]{0:T(128)S(1)}, f32[64]{0:T(128)}, u32[]{:S(2)}) copy-start(f32[64]{0:T(128)} %param.14) | copy-start | bytes 772
  87.1 4.2 %collective-permute-start.14 = (f32[8,12,64]{2,0,1:T(8,128)S(1)}, f32[8,12,64]{2,0,1:T(8,128)S(1)}, u32[]{:S(2)}, u32[]{:S(2)}) collective-permute-start(f32[8,12,64]{2,0,1:T(8,128)S(1)} %pad_maximum_fusion.2), channel_id=1, source_target_pairs={{0,4},{4,0},{8,12},{12,8},{16,20},{20,16},{24,28},{28,24},{1,5},{5... | collective-permute-start | bytes 73736 | tf_op jit(solution)/shard_map/ppermute | solution.py:18
  88.8 40.8 %collective-permute-start.13 = (f32[3,128]{1,0:T(4,128)S(1)}, f32[3,128]{1,0:T(4,128)S(1)}, u32[]{:S(2)}, u32[]{:S(2)}) collective-permute-start(f32[3,128]{1,0:T(4,128)S(1)} %slice.179), channel_id=1, source_target_pairs={{4,0},{8,4},{12,8},{16,12},{20,16},{24,20},{28,24},{5,1},{9,5},{13... | collective-permute-start | bytes 4616 | tf_op jit(solution)/shard_map/ppermute | solution.py:12
  91.3 22.1 %collective-permute-start.15 = (f32[8,12,64]{2,0,1:T(8,128)S(1)}, f32[8,12,64]{2,0,1:T(8,128)S(1)}, u32[]{:S(2)}, u32[]{:S(2)}) collective-permute-start(f32[8,12,64]{2,0,1:T(8,128)S(1)} %fusion.73), channel_id=1, source_target_pairs={{0,8},{4,12},{8,0},{12,4},{16,24},{20,28},{24,16},{28,20},{1,9},{5... | collective-permute-start | bytes 73736 | tf_op jit(solution)/shard_map/ppermute | solution.py:18
  110.9 18.7 %copy-start.13 = (f32[128]{0:T(128)S(1)}, f32[128]{0:T(128)}, u32[]{:S(2)}) copy-start(f32[128]{0:T(128)} %get-tuple-element.35) | copy-start | bytes 1540
  110.9 18.7 %copy-start.14 = (f32[128]{0:T(128)S(1)}, f32[128]{0:T(128)}, u32[]{:S(2)}) copy-start(f32[128]{0:T(128)} %get-tuple-element.36) | copy-start | bytes 1540
  110.9 20.8 %copy-start.8 = (f32[8,12,64]{2,0,1:T(8,128)S(1)}, f32[8,12,64]{2,0,1:T(8,128)}, u32[]{:S(2)}) copy-start(f32[8,12,64]{2,0,1:T(8,128)} %param.15) | copy-start | bytes 73732
  113.4 18.3 %collective-permute-start.16 = (f32[8,12,64]{2,0,1:T(8,128)S(1)}, f32[8,12,64]{2,0,1:T(8,128)S(1)}, u32[]{:S(2)}, u32[]{:S(2)}) collective-permute-start(f32[8,12,64]{2,0,1:T(8,128)S(1)} %add.170), channel_id=1, source_target_pairs={{0,16},{4,20},{8,24},{12,28},{16,0},{20,4},{24,8},{28,12},{1,17},{... | collective-permute-start | bytes 73736 | tf_op jit(solution)/shard_map/ppermute | solution.py:18
  (18 other events, 98.7 us)

commit v8 on v7

--- a/solution.py
+++ b/solution.py
@@ -56,6 +56,20 @@
     b_key = preact[:, inner : inner + state_dim].astype(jnp.bfloat16)
     c_query = preact[:, inner + state_dim :].astype(jnp.bfloat16)
     return (x_act, b_key, c_query)
+
+
+def lanes(per_head, head_dim):
+    return jnp.repeat(per_head, head_dim, axis=-1)
+
+
+def per_head(value, head_dim):
+    return jnp.sum(value.reshape(value.shape[:-1] + (-1, head_dim)), axis=-1)
+
+
+def spread(per_head_values, heads, head_dim):
+    places = jnp.arange(heads * head_dim, dtype=jnp.int32)[None, :] // head_dim
+    expand = (places == jnp.arange(heads, dtype=jnp.int32)[:, None]).astype(jnp.float32)
+    return exact("...h,hq->...q", per_head_values, expand)
 
 
 def group_state_of(x_part, b_part, decay_part):
@@ -86,10 +100,11 @@
 
 
 def combine(block, block_decay, other, other_decay, leading, upper):
-    grown = upper[..., None, None]
-    found = grown * jnp.exp(leading)[..., None, None] * other
-    joined = grown * (other * jnp.exp(block_decay)[..., None, None] + block) + (1.0 - grown) * (
-        block * jnp.exp(other_decay)[..., None, None] + other
+    head_dim = block.shape[-1] // block_decay.shape[-1]
+    grown = upper
+    found = grown * lanes(jnp.exp(leading), head_dim) * other
+    joined = grown * (other * lanes(jnp.exp(block_decay), head_dim) + block) + (1.0 - grown) * (
+        block * lanes(jnp.exp(other_decay), head_dim) + other
     )
     return (joined, block_decay + other_decay, leading + upper * other_decay, found)
 
@@ -117,9 +132,7 @@
             sent, other_decay = from_partner((block.astype(jnp.bfloat16), block_decay), "seq", bit_pos)
             other = sent.astype(jnp.float32)
         first = sent if first is None else first
-        upper = jnp.zeros_like(block_decay) + (jnp.right_shift(myself, bit_pos) & 1).astype(
-            jnp.float32
-        )
+        upper = (jnp.right_shift(myself, bit_pos) & 1).astype(jnp.float32)
         block, block_decay, leading, found = combine(
             block, block_decay, other, other_decay, leading, upper
         )
@@ -155,25 +168,33 @@
     c_groups = c_query.reshape(groups, group_len, state_dim)
     grad_groups = grad_out.reshape(groups, group_len, heads, head_dim)
     b_groups = b_key.reshape(groups, group_len, state_dim)
-    states, cumuls = jax.vmap(group_state_of)(
-        x_groups, b_groups, log_decay.reshape(groups, group_len, heads)
-    )
+    cumuls = jnp.cumsum(log_decay.reshape(groups, group_len, heads), axis=1)
+    x_flat = x_act.reshape(groups, group_len, inner)
+    ending = spread(jnp.exp(cumuls[:, -1:, :] - cumuls), heads, head_dim)
+    x_faded = (x_flat * ending).astype(jnp.bfloat16)
+    states = contract("gtn,gtq->gnq", b_groups, x_faded)
     totals = cumuls[:, -1]
     dev_decay = jnp.sum(totals, axis=0)
     later = dev_decay[None, :] - jnp.cumsum(totals, axis=0)
-    dev_state = jnp.sum(jnp.exp(later)[:, :, None, None] * states, axis=0)
+    dev_state = jnp.sum(lanes(jnp.exp(later), head_dim)[:, None, :] * states, axis=0)
     devices = lax.axis_size("seq")
     depth = devices.bit_length() - 1
     myself = lax.axis_index("seq")
     chunks = 2 if heads % 2 == 0 else 1
     width = heads // chunks
     pieces = [
-        exchange(dev_state[k * width : (k + 1) * width], dev_decay[k * width : (k + 1) * width], depth, myself)
+        exchange(
+            dev_state[:, k * width * head_dim : (k + 1) * width * head_dim],
+            dev_decay[k * width : (k + 1) * width],
+            depth,
+            myself,
+        )
         for k in range(chunks)
     ]
-    cross = jnp.concatenate([piece for piece, _ in pieces], axis=1)
+    cross = jnp.concatenate([piece for piece, _ in pieces], axis=2)
     late_cotangent = lax.optimization_barrier((cotangent, pieces[0][1]))[0]
     grad_groups = late_cotangent.reshape(groups, group_len, heads, head_dim)
+    g_flat = late_cotangent.reshape(groups, group_len, inner)
     y_inner, grad_inner, level_zero = jax.vmap(local_group)(
         x_groups, b_groups, c_groups, cumuls, grad_groups, weight_rows[:, 0]
     )
@@ -193,18 +214,22 @@
     local_weight = exact("cds,csh->cdh", onehot, weight_rows[:, 1 : 1 + low_levels]) * fade_pairs
     lead_fade = jnp.exp(before)
     cross_weight = weight_rows[:, 1 + low_levels : 1 + low_levels + depth] * lead_fade[:, None, :]
-    terms = [local_weight[:, d, :, None, None] * states[d][None] for d in range(groups)]
-    terms += [cross_weight[:, l, :, None, None] * cross[l][None] for l in range(depth)]
+    terms = [lanes(local_weight[:, d], head_dim)[:, None, :] * states[d][None] for d in range(groups)]
+    terms += [lanes(cross_weight[:, l], head_dim)[:, None, :] * cross[l][None] for l in range(depth)]
     mixed = sum(terms[1:], terms[0]).astype(jnp.bfloat16)
-    scaled = jnp.exp(cumuls) / state_dim
-    query_faded = (c_groups[:, :, None, :] * scaled[:, :, :, None]).astype(jnp.bfloat16)
-    y_cross = contract("cthn,chnp->cthp", query_faded, mixed)
-    backed = contract("chnp,cthp->cthn", mixed, grad_groups)
-    grad_cross = jnp.sum(backed * scaled[:, :, :, None], axis=2)
-    gram = contract("cthn,cthp->chnp", query_faded, grad_groups)
-    inner_pairs = jnp.sum(states[None] * gram[:, None], axis=(3, 4))
+    scaled = spread(jnp.exp(cumuls) / state_dim, heads, head_dim)
+    y_cross = scaled * contract("ctn,cnq->ctq", c_groups, mixed)
+    grad_scaled = scaled * g_flat
+    grad_cross = exact("ctq,cnq->ctn", grad_scaled, mixed.astype(jnp.float32))
+    gram = exact("ctn,ctq->cnq", c_groups.astype(jnp.float32), grad_scaled)
+    inner_pairs = jnp.stack(
+        [jnp.stack([per_head(jnp.sum(states[d] * gram[c], axis=0), head_dim) for d in range(groups)]) for c in range(groups)]
+    )
+    cross_pairs = jnp.stack(
+        [jnp.stack([per_head(jnp.sum(cross[l] * gram[c], axis=0), head_dim) for l in range(depth)]) for c in range(groups)]
+    )
     level_local = exact("cds,cdh->csh", onehot, fade_pairs * inner_pairs)
-    level_cross = lead_fade[:, None, :] * jnp.sum(cross[None] * gram[:, None], axis=(3, 4))
+    level_cross = lead_fade[:, None, :] * cross_pairs
     level_rest = jnp.concatenate(
         [
             level_local,
@@ -215,7 +240,7 @@
     )
     grads = exact("ck,clh->klh", picked, level_rest)
     ssm_out = (
-        (y_inner + y_cross + skip[None, None, :, None] * x_groups)
+        (y_inner.reshape(groups, group_len, inner) + y_cross + lanes(skip, head_dim) * x_flat)
         .astype(jnp.bfloat16)
         .reshape(length, inner)
     )

time: 133 us -> 157 us (1.18)
  matrix products: 16.7 us -> 28.2 us
  other arithmetic: 20.1 us -> 27.5 us
  local copies, waits for them, and re-layouts: 29.5 us -> 36.1 us
  waiting for transfers between devices: 16.7 us -> 12.2 us
  starting transfers between devices: 48 us -> 50.8 us
    mul x3 -> x21, local copies, waits for them, and re-layouts: 2.98 us -> 10.7 us  [the longest x4 3.6 us: local(): lanes(cross_weight[:, l], head_dim)[:, None, :] * cross[l][None]]
    dot_general x4 -> x8, matrix products: 1.75 us -> 9.37 us  [exact(): return jnp.einsum(form, left, right, precision=lax.Precision.HIGHEST)]
    broadcast_in_dim x0 -> x19, local copies, waits for them, and re-layouts: none -> 4.59 us  [lanes(): return jnp.repeat(per_head, head_dim, axis=-1)]
    ppermute x11, waiting for transfers between devices: 16.7 us -> 12.2 us  [from_partner(): return lax.ppermute(value, axis, pairs)]
    reshape x2 -> x1, local copies, waits for them, and re-layouts: 8.43 us -> 4.29 us  [local(): grad_groups = late_cotangent.reshape(groups, group_len, heads, head_dim)]
    dot_general x6 -> x4, matrix products: 14.7 us -> 18.6 us  [contract(): return jnp.einsum(form, left, right, preferred_element_type=jnp.float32)]
    convert_element_type x1 -> x0, local copies, waits for them, and re-layouts: 3.31 us -> none  [local(): ssm_out = (y_inner + y_cross + skip[None, None, :, None] * x_groups).asty...]
    convert_element_type x1, other arithmetic: 1.69 us -> 4.8 us  [local(): mixed = sum(terms[1:], terms[0]).astype(jnp.bfloat16)]
  transfers between devices with their start and end apart: 17 -> 17, of which waited for: 6 -> 3; matrix products, arithmetic and copies ran while one was open for 39% -> 43% of each run, Pallas kernels for 0% -> 0%
where the time goes in v8:
time: 157 us; the launch traced here: 156 us
  starting transfers between devices  50.8 us (32%)
  local copies, waits for them, and re-layouts  36.1 us (23%)
  matrix products  28.2 us (18%)
  other arithmetic  27.5 us (18%)
  waiting for transfers between devices  12.2 us (8%)
    ppermute x11, starting transfers between devices, from_partner(): return lax.ppermute(value, axis, pairs)  42.2 us
    dot_general x4, matrix products, contract(): return jnp.einsum(form, left, right, preferred_element_type=jnp.float32)  18.6 us
    ppermute x11, waiting for transfers between devices, from_partner(): return lax.ppermute(value, axis, pairs)  12.2 us
    dot_general x8, matrix products, exact(): return jnp.einsum(form, left, right, precision=lax.Precision.HIGHEST)  9.37 us
    ppermute x2, starting transfers between devices, shifted(): lax.ppermute(value, axis, [(source, source + steps) for source in range(l...  5.73 us
    convert_element_type x1, other arithmetic, local(): mixed = sum(terms[1:], terms[0]).astype(jnp.bfloat16)  4.8 us
    broadcast_in_dim x19, local copies, waits for them, and re-layouts, lanes(): return jnp.repeat(per_head, head_dim, axis=-1)  4.59 us
    reshape x1, local copies, waits for them, and re-layouts, local(): grad_groups = late_cotangent.reshape(groups, group_len, heads, head_dim)  4.29 us
  transfers between devices with their start and end apart: 17, of which 3 were waited for; matrix products, arithmetic and copies ran while one was open for 43% of the time, Pallas kernels for 0%

profile of v8, /device:TPU:0, one launch (start us, length us, event | category | flops | bytes accessed | tf_op | source)
XLA Modules:
  0.0 156.3 jit_solution(9876127050744589712)
XLA Ops:
  3.1 2.9 %collective-permute-start.2 = (f32[32]{0:T(128)S(1)}, f32[32]{0:T(128)S(1)}, u32[]{:S(2)}, u32[]{:S(2)}) collective-permute-start(f32[32]{0:T(128)S(1)} %get-tuple-element.77), channel_id=1, source_target_pairs={{0,4},{4,0},{8,12},{12,8},{16,20},{20,16},{24,28},{28,24},{1,5},{5... | collective-permute-start | bytes 392 | tf_op jit(solution)/shard_map/ppermute | solution.py:18
  6.2 1.5 slice.143
  7.7 4.4 %collective-permute-start = (bf16[3,4352]{1,0:T(4,128)(2,1)}, bf16[3,4352]{1,0:T(4,128)(2,1)}, u32[]{:S(2)}, u32[]{:S(2)}) collective-permute-start(bf16[3,4352]{1,0:T(4,128)(2,1)} %slice.143), channel_id=1, source_target_pairs={{0,4},{4,8},{8,12},{12,16},{16,20},{20,24},{24,28},{1,5},{5,9},{9,... | collective-permute-start | bytes 78344 | tf_op jit(solution)/shard_map/ppermute | solution.py:12
  15.5 1.4 slice_bitcast_fusion.15
  34.5 2.1 %fusion.98 = (bf16[128,4352]{1,0:T(8,128)(2,1)S(1)}, f32[128,4352]{1,0:T(8,128)S(1)}) fusion(f32[4352]{0:T(1024)S(1)} %get-tuple-element.18, bf16[128,4352]{1,0:T(8,128)(2,1)S(1)} %copy-done.10, f32[4352]{0:T(1024)S(1)} %get-tuple-element.19, bf16[3,4352]{1,0:T(4,128)(2,1)} %collective-permute-done, f32[4352]{0:T(1024)S(1)} %get-tuple-element.20, ...), kind=kLoop, calls=%fused_computation.197 | loop fusion | flops 12255232 | bytes 4569600 | tf_op jit(solution)/shard_map/convert.4
  42.3 2.3 %slice_bitcast_fusion.6 = (f32[128,4096]{1,0:T(8,128)}, f32[128,4096]{1,0:T(8,128)}) fusion(f32[2,128,4096]{2,1,0:T(8,128)S(1)} %get-tuple-element.82), kind=kLoop, calls=%fused_computation.23 | loop fusion | bytes 8388608 | tf_op jit(solution)/shard_map/mul | solution.py:217
  44.6 10.6 %collective-permute-done.1 = bf16[128,2048]{1,0:T(8,128)(2,1)S(1)} collective-permute-done((bf16[128,2048]{1,0:T(8,128)(2,1)S(1)}, bf16[128,2048]{1,0:T(8,128)(2,1)S(1)}, u32[]{:S(2)}, u32[]{:S(2)}) %collective-permute-start.1) | collective-permute-done | bytes 524320 | tf_op jit(solution)/shard_map/ppermute | solution.py:18
  57.4 3.3 %reshape_reshape.4 = bf16[2,64,64,64]{3,2,1,0:T(8,128)(2,1)} reshape(bf16[128,4096]{1,0:T(8,128)(2,1)S(1)} %multiply_convert_fusion.2) | data formatting | bytes 2097152 | tf_op jit(solution)/shard_map/reshape;reshape | solution.py:167
  60.8 5.8 %fusion.5 = f32[2,64,64,64]{3,2,1,0:T(8,128)} fusion(f32[2,64]{1,0:T(2,128)S(1)} %copy-done.32, f32[2,64,64]{2,1,0:T(8,128)S(1)} %fusion.104, f32[2,64,64]{2,1,0:T(8,128)S(1)} %copy-done.11, pred[64,64]{1,0:T(8,128)(4,1)S(1)} %copy-done.21, bf16[2,64,64,64]{3,2,1,0:T(8,128)(2,1)} %reshape_reshape.4), kind=kOutput, calls=%fused_computation.16 | convolution fusion | flops 70254592 | bytes 3215872 | tf_op jit(solution)/shard_map/vmap(hts,shp->thp)/dot_general | solution.py:35
  66.6 3.8 %copy.25 = f32[2,64,4096]{2,1,0:T(8,128)} copy(f32[2,64,4096]{1,2,0:T(8,128)} %bitcast.152) | data formatting | bytes 4194304 | tf_op jit(solution)/shard_map/reshape | solution.py:243
  70.4 4.3 %reshape.199 = bf16[2,64,64,64]{3,2,1,0:T(8,128)(2,1)} reshape(bf16[128,4096]{1,0:T(8,128)(2,1)} %param.17) | data formatting | bytes 2097152 | tf_op jit(solution)/shard_map/reshape | solution.py:196
  74.7 3.1 %fusion.30 = (bf16[128,2048]{1,0:T(8,128)(2,1)S(1)}, bf16[128,2048]{1,0:T(8,128)(2,1)S(1)}, f32[1,128,2048]{2,1,0:T(8,128)S(1)}, f32[1,128,2048]{2,1,0:T(8,128)S(1)}, f32[1,128,2048]{2,1,0:T(8,128)S(1)}) fusion(bf16[128,2048]{1,0:T(8,128)(2,1)} %collective-permute-done.3, f32[2048]{0:T(1024)S(1)} %copy-done.18, f32[]{:T(128)S(6)} %sub.98, ...), kind=kLoop, calls=%fused_computation.76 | loop fusion | flops 7602176 | bytes 7921680 | tf_op jit(solution)/shard_map/convert_element_type | solution.py:129
  79.0 10.2 %multiply_reduce_fusion = (f32[2,64]{1,0:T(2,128)S(1)}, f32[2,64,64]{2,1,0:T(8,128)S(1)}) fusion(f32[2,64,64]{2,1,0:T(8,128)S(1)} %fusion.104, f32[2,64,64]{2,1,0:T(8,128)S(1)} %copy-done.11, pred[64,64]{1,0:T(8,128)(4,1)S(1)} %copy-done.21, f32[2,64]{1,0:T(2,128)S(1)} %copy-done.33, bf16[2,64,64,64]{3,2,1,0:T(8,128)(2,1)S(1)} %copy-done.7, ...), kind=kOutput, calls=%fused_computation.7 | convolution fusion | flops 72343424 | bytes 2200576 | tf_op jit(solution)/shard_map/vmap(thp,shp->hts)/dot_general | solution.py:35
  90.0 1.7 %fusion.37 = (f32[1,128,2048]{2,1,0:T(8,128)S(1)}, bf16[128,2048]{1,0:T(8,128)(2,1)S(1)}) fusion(bf16[128,2048]{1,0:T(8,128)(2,1)S(1)} %collective-permute-done.9, f32[2048]{0:T(1024)S(1)} %copy-done.13, f32[2048]{0:T(1024)S(1)} %copy-done.16, f32[]{:T(128)S(6)} %sub.98, f32[2048]{0:T(1024)S(1)} %mul.615, f32[]{:T(128)S(6)} %sub.97, ...), kind=kLoop, calls=%fused_computation.83 | loop fusion | flops 4718592 | bytes 3710992 | tf_op jit(solution)/shard_map/stack | solution.py:141
  93.3 1.9 %fusion.16 = f32[2,128,4096]{2,1,0:T(8,128)S(1)} fusion(bf16[2,64,128]{2,1,0:T(8,128)(2,1)S(1)} %bitcast.156, f32[2,64,4096]{2,1,0:T(8,128)S(1)} %fusion.45, bf16[2,64,4096]{2,1,0:T(8,128)(2,1)S(1)} %bitcast.150), kind=kOutput, calls=%fused_computation.60 | convolution fusion | flops 806354944 | bytes 7372800 | tf_op jit(solution)/shard_map/ctn,ctq->cnq/dot_general | solution.py:39
  97.0 3.3 %slice_bitcast_fusion.4 = (f32[128,4096]{1,0:T(8,128)}, f32[128,4096]{1,0:T(8,128)}, f32[128,4096]{1,0:T(8,128)}) fusion(f32[3,128,4096]{2,1,0:T(8,128)S(1)} %maximum_maximum_fusion), kind=kLoop, calls=%fused_computation.21 | loop fusion | bytes 12582912 | tf_op jit(solution)/shard_map/mul | solution.py:218
  101.4 2.0 %multiply_reduce_fusion.12 = (f32[4096]{0:T(1024)S(1)}, f32[4096]{0:T(1024)S(1)}, f32[4096]{0:T(1024)S(1)}, f32[4096]{0:T(1024)S(1)}, f32[4096]{0:T(1024)S(1)}, ...) fusion(f32[2,128,4096]{2,1,0:T(8,128)S(1)} %fusion.16, ...), kind=kLoop, calls=%fused_computation.36 | loop fusion | flops 10444800 | bytes 14843904 | tf_op jit(solution)/shard_map/reduce_sum | solution.py:226
  110.2 4.8 %add_convert_fusion = bf16[2,128,4096]{2,1,0:T(8,128)(2,1)S(1)} fusion(f32[128,4096]{1,0:T(8,128)} %get-tuple-element.30, f32[2,4096]{1,0:T(2,128)S(1)} %mul.641, f32[128,4096]{1,0:T(8,128)} %get-tuple-element.31, f32[2,4096]{1,0:T(2,128)S(1)} %mul.636, f32[128,4096]{1,0:T(8,128)} %get-tuple-element.29, f32[2,4096]{1,0:T(2,128)S(1)} %mul.567, ...), kind=kLoop, calls=%fused_computation.9 | loop fusion | flops 10485760 | bytes 12746752 | tf_op jit(solution)/shard_map/convert_element_type | solution.py:219
  115.0 2.4 %fusion.18 = f32[2,64,128]{2,1,0:T(8,128)S(1)} fusion(f32[2,64,128]{2,1,0:T(8,128)S(1)} %fusion.63, bf16[2,128,4096]{2,1,0:T(8,128)(2,1)S(1)} %add_convert_fusion, f32[2,64,4096]{2,1,0:T(8,128)S(1)} %fusion.45, bf16[2,64,4096]{2,1,0:T(8,128)(2,1)S(1)} %bitcast.151), kind=kOutput, calls=%fused_computation.62 | convolution fusion | flops 806371328 | bytes 5373952 | tf_op jit(solution)/shard_map/ctq,cnq->ctn/dot_general | solution.py:39
  117.4 1.3 collective-permute-start.13
  119.5 16.7 %collective-permute-start.15 = (f32[8,12,64]{2,0,1:T(8,128)S(1)}, f32[8,12,64]{2,0,1:T(8,128)S(1)}, u32[]{:S(2)}, u32[]{:S(2)}) collective-permute-start(f32[8,12,64]{2,0,1:T(8,128)S(1)} %fusion.94), channel_id=1, source_target_pairs={{0,8},{4,12},{8,0},{12,4},{16,24},{20,28},{24,16},{28,20},{1,9},{5... | collective-permute-start | bytes 73736 | tf_op jit(solution)/shard_map/ppermute | solution.py:18
  136.3 1.8 %fusion.3 = bf16[2,64,4096]{2,1,0:T(8,128)(2,1)} fusion(f32[2,64,4096]{2,1,0:T(8,128)S(1)} %copy-done.6, f32[2,64,4096]{2,1,0:T(8,128)S(1)} %fusion.45, bf16[2,64,128]{2,1,0:T(8,128)(2,1)S(1)} %bitcast.157, bf16[2,128,4096]{2,1,0:T(8,128)(2,1)S(1)} %add_convert_fusion, bf16[2,64,4096]{2,1,0:T(8,128)(2,1)S(1)} %bitcast.149, f32[4096]{0:T(1024)S(1)} %mul.647), kind=kOutput, calls=%fused_computation.6 | convolution fusion | flops 137363456 | bytes 8437760 | tf_op jit(solution)/shard_map/ctn,cnq->ctq/dot_general | solution.py:35
  138.4 15.3 %collective-permute-start.16 = (f32[8,12,64]{2,0,1:T(8,128)S(1)}, f32[8,12,64]{2,0,1:T(8,128)S(1)}, u32[]{:S(2)}, u32[]{:S(2)}) collective-permute-start(f32[8,12,64]{2,0,1:T(8,128)S(1)} %add.163), channel_id=1, source_target_pairs={{0,16},{4,20},{8,24},{12,28},{16,0},{20,4},{24,8},{28,12},{1,17},{... | collective-permute-start | bytes 73736 | tf_op jit(solution)/shard_map/ppermute | solution.py:18
  154.3 1.4 collective-permute-done.16
  (212 shorter events, 46.6 us)
Async XLA Ops:
  0.6 33.8 %copy-start.10 = (bf16[128,4352]{1,0:T(8,128)(2,1)S(1)}, bf16[128,4352]{1,0:T(8,128)(2,1)}, u32[]{:S(2)}) copy-start(bf16[128,4352]{1,0:T(8,128)(2,1)} %param.9) | copy-start | bytes 3342340
  3.1 18.9 %collective-permute-start.2 = (f32[32]{0:T(128)S(1)}, f32[32]{0:T(128)S(1)}, u32[]{:S(2)}, u32[]{:S(2)}) collective-permute-start(f32[32]{0:T(128)S(1)} %get-tuple-element.77), channel_id=1, source_target_pairs={{0,4},{4,0},{8,12},{12,8},{16,20},{20,16},{24,28},{28,24},{1,5},{5... | collective-permute-start | bytes 392 | tf_op jit(solution)/shard_map/ppermute | solution.py:18
  6.1 15.9 %collective-permute-start.8 = (f32[32]{0:T(128)S(1)}, f32[32]{0:T(128)S(1)}, u32[]{:S(2)}, u32[]{:S(2)}) collective-permute-start(f32[32]{0:T(128)S(1)} %get-tuple-element.78), channel_id=1, source_target_pairs={{0,4},{4,0},{8,12},{12,8},{16,20},{20,16},{24,28},{28,24},{1,5},{5... | collective-permute-start | bytes 392 | tf_op jit(solution)/shard_map/ppermute | solution.py:18
  7.7 26.8 %collective-permute-start = (bf16[3,4352]{1,0:T(4,128)(2,1)}, bf16[3,4352]{1,0:T(4,128)(2,1)}, u32[]{:S(2)}, u32[]{:S(2)}) collective-permute-start(bf16[3,4352]{1,0:T(4,128)(2,1)} %slice.143), channel_id=1, source_target_pairs={{0,4},{4,8},{8,12},{12,16},{16,20},{20,24},{24,28},{1,5},{5,9},{9,... | collective-permute-start | bytes 78344 | tf_op jit(solution)/shard_map/ppermute | solution.py:12
  22.7 4.1 %collective-permute-start.4 = (f32[32]{0:T(128)}, f32[32]{0:T(128)}, u32[]{:S(2)}, u32[]{:S(2)}) collective-permute-start(f32[32]{0:T(128)} %get-tuple-element.24), channel_id=1, source_target_pairs={{0,8},{4,12},{8,0},{12,4},{16,24},{20,28},{24,16},{28,20},{1,9},{5... | collective-permute-start | bytes 392 | tf_op jit(solution)/shard_map/ppermute | solution.py:18
  23.7 4.3 %collective-permute-start.10 = (f32[32]{0:T(128)}, f32[32]{0:T(128)}, u32[]{:S(2)}, u32[]{:S(2)}) collective-permute-start(f32[32]{0:T(128)} %get-tuple-element.74), channel_id=1, source_target_pairs={{0,8},{4,12},{8,0},{12,4},{16,24},{20,28},{24,16},{28,20},{1,9},{5... | collective-permute-start | bytes 392 | tf_op jit(solution)/shard_map/ppermute | solution.py:18
  40.3 14.9 %collective-permute-start.1 = (bf16[128,2048]{1,0:T(8,128)(2,1)S(1)}, bf16[128,2048]{1,0:T(8,128)(2,1)S(1)}, u32[]{:S(2)}, u32[]{:S(2)}) collective-permute-start(bf16[128,2048]{1,0:T(8,128)(2,1)S(1)} %get-tuple-element.42), channel_id=1, source_target_pairs={{0,4},{4,0},{8,12},{12,8},{16,20},{20,16},{24,28},{28,24},{1,5},{5... | collective-permute-start | bytes 1572872 | tf_op jit(solution)/shard_map/ppermute | solution.py:18
  41.2 33.4 %collective-permute-start.7 = (bf16[128,2048]{1,0:T(8,128)(2,1)}, bf16[128,2048]{1,0:T(8,128)(2,1)}, u32[]{:S(2)}, u32[]{:S(2)}) collective-permute-start(bf16[128,2048]{1,0:T(8,128)(2,1)} %get-tuple-element.43), channel_id=1, source_target_pairs={{0,4},{4,0},{8,12},{12,8},{16,20},{20,16},{24,28},{28,24},{1,5},{5... | collective-permute-start | bytes 1572872 | tf_op jit(solution)/shard_map/ppermute | solution.py:18
  56.3 18.4 %collective-permute-start.3 = (bf16[128,2048]{1,0:T(8,128)(2,1)}, bf16[128,2048]{1,0:T(8,128)(2,1)}, u32[]{:S(2)}, u32[]{:S(2)}) collective-permute-start(bf16[128,2048]{1,0:T(8,128)(2,1)} %fusion.50), channel_id=1, source_target_pairs={{0,8},{4,12},{8,0},{12,4},{16,24},{20,28},{24,16},{28,20},{1,9},{5... | collective-permute-start | bytes 1572872 | tf_op jit(solution)/shard_map/ppermute | solution.py:18
  77.8 12.2 %collective-permute-start.9 = (bf16[128,2048]{1,0:T(8,128)(2,1)S(1)}, bf16[128,2048]{1,0:T(8,128)(2,1)S(1)}, u32[]{:S(2)}, u32[]{:S(2)}) collective-permute-start(bf16[128,2048]{1,0:T(8,128)(2,1)S(1)} %get-tuple-element.41), channel_id=1, source_target_pairs={{0,8},{4,12},{8,0},{12,4},{16,24},{20,28},{24,16},{28,20},{1,9},{5... | collective-permute-start | bytes 1572872 | tf_op jit(solution)/shard_map/ppermute | solution.py:18
  89.2 3.4 %collective-permute-start.5 = (bf16[128,2048]{1,0:T(8,128)(2,1)S(1)}, bf16[128,2048]{1,0:T(8,128)(2,1)S(1)}, u32[]{:S(2)}, u32[]{:S(2)}) collective-permute-start(bf16[128,2048]{1,0:T(8,128)(2,1)S(1)} %get-tuple-element.40), channel_id=1, source_target_pairs={{8,16},{12,20},{9,17},{13,21},{10,18},{14,22},{11,19},{15,23}} | collective-permute-start | bytes 1572872 | tf_op jit(solution)/shard_map/ppermute | solution.py:115
  91.7 3.5 %collective-permute-start.11 = (bf16[128,2048]{1,0:T(8,128)(2,1)S(1)}, bf16[128,2048]{1,0:T(8,128)(2,1)S(1)}, u32[]{:S(2)}, u32[]{:S(2)}) collective-permute-start(bf16[128,2048]{1,0:T(8,128)(2,1)S(1)} %get-tuple-element.50), channel_id=1, source_target_pairs={{8,16},{12,20},{9,17},{13,21},{10,18},{14,22},{11,19},{15,23}} | collective-permute-start | bytes 1572872 | tf_op jit(solution)/shard_map/ppermute | solution.py:115
  92.5 3.6 %collective-permute-start.6 = (bf16[128,2048]{1,0:T(8,128)(2,1)S(1)}, bf16[128,2048]{1,0:T(8,128)(2,1)S(1)}, u32[]{:S(2)}, u32[]{:S(2)}) collective-permute-start(bf16[128,2048]{1,0:T(8,128)(2,1)S(1)} %collective-permute-done.5), channel_id=1, source_target_pairs={{16,24},{20,28},{17,25},{21,29},{18,26},{22,30},{19,27},{23,31}} | collective-permute-start | bytes 1572872 | tf_op jit(solution)/shard_map/ppermute | solution.py:116
  95.2 1.1 collective-permute-start.12
  108.6 10.0 %collective-permute-start.14 = (f32[8,12,64]{2,0,1:T(8,128)}, f32[8,12,64]{2,0,1:T(8,128)}, u32[]{:S(2)}, u32[]{:S(2)}) collective-permute-start(f32[8,12,64]{2,0,1:T(8,128)} %pad_maximum_fusion.2), channel_id=1, source_target_pairs={{0,4},{4,0},{8,12},{12,8},{16,20},{20,16},{24,28},{28,24},{1,5},{5... | collective-permute-start | bytes 73736 | tf_op jit(solution)/shard_map/ppermute | solution.py:18
  115.0 21.3 %copy-start.6 = (f32[2,64,4096]{2,1,0:T(8,128)S(1)}, f32[2,64,4096]{2,1,0:T(8,128)}, u32[]{:S(2)}) copy-start(f32[2,64,4096]{2,1,0:T(8,128)} %copy.25) | copy-start | bytes 6291460
  117.4 36.2 %collective-permute-start.13 = (f32[3,128]{1,0:T(4,128)S(1)}, f32[3,128]{1,0:T(4,128)S(1)}, u32[]{:S(2)}, u32[]{:S(2)}) collective-permute-start(f32[3,128]{1,0:T(4,128)S(1)} %slice.205), channel_id=1, source_target_pairs={{4,0},{8,4},{12,8},{16,12},{20,16},{24,20},{28,24},{5,1},{9,5},{13... | collective-permute-start | bytes 4616 | tf_op jit(solution)/shard_map/ppermute | solution.py:12
  119.5 34.1 %copy-start.28 = (f32[128]{0:T(128)S(1)}, f32[128]{0:T(128)}, u32[]{:S(2)}) copy-start(f32[128]{0:T(128)} %get-tuple-element.51) | copy-start | bytes 1540
  119.5 34.1 %copy-start.29 = (f32[128]{0:T(128)S(1)}, f32[128]{0:T(128)}, u32[]{:S(2)}) copy-start(f32[128]{0:T(128)} %get-tuple-element.52) | copy-start | bytes 1540
  119.5 34.1 %copy-start.30 = (f32[128]{0:T(128)S(1)}, f32[128]{0:T(128)}, u32[]{:S(2)}) copy-start(f32[128]{0:T(128)} %get-tuple-element.53) | copy-start | bytes 1540
  119.5 34.1 %copy-start.31 = (f32[128]{0:T(128)S(1)}, f32[128]{0:T(128)}, u32[]{:S(2)}) copy-start(f32[128]{0:T(128)} %get-tuple-element.54) | copy-start | bytes 1540
  119.5 36.2 %copy-start.12 = (f32[8,12,64]{2,0,1:T(8,128)S(1)}, f32[8,12,64]{2,0,1:T(8,128)}, u32[]{:S(2)}) copy-start(f32[8,12,64]{2,0,1:T(8,128)} %param.15) | copy-start | bytes 73732
  119.5 18.8 %collective-permute-start.15 = (f32[8,12,64]{2,0,1:T(8,128)S(1)}, f32[8,12,64]{2,0,1:T(8,128)S(1)}, u32[]{:S(2)}, u32[]{:S(2)}) collective-permute-start(f32[8,12,64]{2,0,1:T(8,128)S(1)} %fusion.94), channel_id=1, source_target_pairs={{0,8},{4,12},{8,0},{12,4},{16,24},{20,28},{24,16},{28,20},{1,9},{5... | collective-permute-start | bytes 73736 | tf_op jit(solution)/shard_map/ppermute | solution.py:18
  138.4 17.3 %collective-permute-start.16 = (f32[8,12,64]{2,0,1:T(8,128)S(1)}, f32[8,12,64]{2,0,1:T(8,128)S(1)}, u32[]{:S(2)}, u32[]{:S(2)}) collective-permute-start(f32[8,12,64]{2,0,1:T(8,128)S(1)} %add.163), channel_id=1, source_target_pairs={{0,16},{4,20},{8,24},{12,28},{16,0},{20,4},{24,8},{28,12},{1,17},{... | collective-permute-start | bytes 73736 | tf_op jit(solution)/shard_map/ppermute | solution.py:18
  (30 other events, 173.0 us)

commit v9 on v7

--- a/solution.py
+++ b/solution.py
@@ -113,6 +113,9 @@
             else:
                 sent = relay(block.astype(jnp.bfloat16), "seq", bit_pos)
             other, other_decay = (sent.astype(jnp.float32), jnp.zeros_like(block_decay))
+        elif bit_pos == depth - 2:
+            sent, other_decay = upward((block.astype(jnp.bfloat16), block_decay), "seq", bit_pos)
+            other = sent.astype(jnp.float32)
         else:
             sent, other_decay = from_partner((block.astype(jnp.bfloat16), block_decay), "seq", bit_pos)
             other = sent.astype(jnp.float32)

time: 133 us -> 137 us (1.030)
  starting transfers between devices: 48 us -> 56.5 us
  waiting for transfers between devices: 16.7 us -> 12.2 us
    ppermute x0 -> x4, starting transfers between devices: none -> 10.4 us  [upward(): return lax.ppermute(value, axis, pairs)]
    ppermute x11 -> x7, waiting for transfers between devices: 16.7 us -> 8.64 us  [from_partner(): return lax.ppermute(value, axis, pairs)]
    ppermute x0 -> x4, waiting for transfers between devices: none -> 3.5 us  [upward(): return lax.ppermute(value, axis, pairs)]
    ppermute x11 -> x7, starting transfers between devices: 39.8 us -> 37.9 us  [from_partner(): return lax.ppermute(value, axis, pairs)]
  transfers between devices with their start and end apart: 17 -> 17, of which waited for: 6 -> 5; matrix products, arithmetic and copies ran while one was open for 39% -> 37% of each run, Pallas kernels for 0% -> 0%
where the time goes in v9:
time: 137 us; the launch traced here: 136 us
  starting transfers between devices  56.5 us (41%)
  local copies, waits for them, and re-layouts  29.5 us (22%)
  other arithmetic  20.1 us (15%)
  matrix products  16.7 us (12%)
  waiting for transfers between devices  12.2 us (9%)
    ppermute x7, starting transfers between devices, from_partner(): return lax.ppermute(value, axis, pairs)  37.9 us
    dot_general x6, matrix products, contract(): return jnp.einsum(form, left, right, preferred_element_type=jnp.float32)  14.7 us
    ppermute x4, starting transfers between devices, upward(): return lax.ppermute(value, axis, pairs)  10.4 us
    ppermute x7, waiting for transfers between devices, from_partner(): return lax.ppermute(value, axis, pairs)  8.64 us
    reshape x2, local copies, waits for them, and re-layouts, local(): grad_groups = late_cotangent.reshape(groups, group_len, heads, head_dim)  8.43 us
    another operation x2, local copies, waits for them, and re-layouts, local(): x_groups = x_act.reshape(groups, group_len, heads, head_dim)  5.25 us
    ppermute x2, starting transfers between devices, shifted(): lax.ppermute(value, axis, [(source, source + steps) for source in range(l...  5.15 us
    ppermute x4, waiting for transfers between devices, upward(): return lax.ppermute(value, axis, pairs)  3.5 us
  transfers between devices with their start and end apart: 17, of which 5 were waited for; matrix products, arithmetic and copies ran while one was open for 37% of the time, Pallas kernels for 0%

profile of v9, /device:TPU:0, one launch (start us, length us, event | category | flops | bytes accessed | tf_op | source)
XLA Modules:
  0.0 136.3 jit_solution(9127548588421904562)
XLA Ops:
  2.5 2.9 %collective-permute-start.2 = (f32[32]{0:T(128)S(1)}, f32[32]{0:T(128)S(1)}, u32[]{:S(2)}, u32[]{:S(2)}) collective-permute-start(f32[32]{0:T(128)S(1)} %get-tuple-element.63), channel_id=1, source_target_pairs={{0,4},{4,0},{8,12},{12,8},{16,20},{20,16},{24,28},{28,24},{1,5},{5... | collective-permute-start | bytes 392 | tf_op jit(solution)/shard_map/ppermute | solution.py:18
  6.4 3.9 %collective-permute-start = (bf16[3,4352]{1,0:T(4,128)(2,1)S(1)}, bf16[3,4352]{1,0:T(4,128)(2,1)S(1)}, u32[]{:S(2)}, u32[]{:S(2)}) collective-permute-start(bf16[3,4352]{1,0:T(4,128)(2,1)S(1)} %slice.119), channel_id=1, source_target_pairs={{0,4},{4,8},{8,12},{12,16},{16,20},{20,24},{24,28},{1,5},{5,9},{9,... | collective-permute-start | bytes 78344 | tf_op jit(solution)/shard_map/ppermute | solution.py:12
  16.7 3.5 %fusion.79 = (bf16[128,4352]{1,0:T(8,128)(2,1)S(1)}, f32[128,4352]{1,0:T(8,128)S(1)}) fusion(f32[4352]{0:T(1024)S(1)} %get-tuple-element.8, bf16[128,4352]{1,0:T(8,128)(2,1)} %param.9, f32[4352]{0:T(1024)S(1)} %get-tuple-element.9, bf16[3,4352]{1,0:T(4,128)(2,1)S(1)} %collective-permute-done, f32[4352]{0:T(1024)S(1)} %get-tuple-element.10, ...), kind=kLoop, calls=%fused_computation.163 | loop fusion | flops 12255232 | bytes 4569600 | tf_op jit(solution)/shard_map/convert.2
  20.7 2.3 %reshape_reshape.3 = bf16[2,64,64,64]{3,2,1,0:T(8,128)(2,1)S(1)} reshape(bf16[128,4096]{1,0:T(8,128)(2,1)S(1)} %multiply_convert_fusion.5) | data formatting | bytes 2097152 | tf_op jit(solution)/shard_map/reshape;reshape | solution.py:157
  23.0 3.0 %copy.46 = bf16[2,64,64,64]{1,3,2,0:T(8,128)(2,1)} copy(bf16[2,64,64,64]{3,2,1,0:T(8,128)(2,1)S(1)} %reshape_reshape.3) | data formatting | bytes 2097152 | tf_op jit(solution)/shard_map/reshape;reshape | solution.py:157
  26.0 2.5 %multiply_reduce_fusion.4 = (f32[64,128,64]{1,2,0:T(8,128)S(1)}, f32[2,64,128,64]{2,3,1,0:T(8,128)S(1)}) fusion(f32[2,64]{1,0:T(2,128)S(1)} %get-tuple-element.52, bf16[2,64,128,1]{2,1,3,0:T(8,128)(2,1)S(1)} %bitcast.95, bf16[2,64,64,64]{1,3,2,0:T(8,128)(2,1)} %copy.46, f32[2,64,64]{1,2,0:T(8,128)S(1)} %copy.49), kind=kOutput, calls=%fused_computation.14 | convolution fusion | flops 137363456 | bytes 7406080 | tf_op jit(solution)/shard_map/vmap(sn,shp->hnp)/dot_general | solution.py:35
  29.6 1.5 %collective-permute-start.1 = (bf16[32,128,64]{1,2,0:T(8,128)(2,1)S(1)}, bf16[32,128,64]{1,2,0:T(8,128)(2,1)S(1)}, u32[]{:S(2)}, u32[]{:S(2)}) collective-permute-start(bf16[32,128,64]{1,2,0:T(8,128)(2,1)S(1)} %get-tuple-element.26), channel_id=1, source_target_pairs={{0,4},{4,0},{8,12},{12,8},{16,20},{20,16},{24,28},{28,24},{1,5},{5... | collective-permute-start | bytes 1572872 | tf_op jit(solution)/shard_map/ppermute | solution.py:18
  31.2 3.5 %collective-permute-start.10 = (f32[32]{0:T(128)S(1)}, f32[32]{0:T(128)S(1)}, u32[]{:S(2)}, u32[]{:S(2)}) collective-permute-start(f32[32]{0:T(128)S(1)} %get-tuple-element.60), channel_id=1, source_target_pairs={{0,8},{4,12},{16,24},{20,28},{1,9},{5,13},{17,25},{21,29},{2,10},{... | collective-permute-start | bytes 392 | tf_op jit(solution)/shard_map/ppermute | solution.py:25
  38.3 6.1 %collective-permute-done.1 = bf16[32,128,64]{1,2,0:T(8,128)(2,1)S(1)} collective-permute-done((bf16[32,128,64]{1,2,0:T(8,128)(2,1)S(1)}, bf16[32,128,64]{1,2,0:T(8,128)(2,1)S(1)}, u32[]{:S(2)}, u32[]{:S(2)}) %collective-permute-start.1) | collective-permute-done | bytes 524320 | tf_op jit(solution)/shard_map/ppermute | solution.py:18
  45.7 4.3 %collective-permute-start.3 = (bf16[32,128,64]{1,2,0:T(8,128)(2,1)}, bf16[32,128,64]{1,2,0:T(8,128)(2,1)}, u32[]{:S(2)}, u32[]{:S(2)}) collective-permute-start(bf16[32,128,64]{1,2,0:T(8,128)(2,1)} %fusion.75), channel_id=1, source_target_pairs={{0,8},{4,12},{16,24},{20,28},{1,9},{5,13},{17,25},{21,29},{2,10},{... | collective-permute-start | bytes 1572872 | tf_op jit(solution)/shard_map/ppermute | solution.py:25
  50.1 2.4 %slice_bitcast_fusion.4 = (f32[64,128,64]{1,2,0:T(8,128)}, f32[64,128,64]{1,2,0:T(8,128)}) fusion(f32[2,64,128,64]{2,3,1,0:T(8,128)S(1)} %get-tuple-element.68), kind=kLoop, calls=%fused_computation.26 | loop fusion | bytes 8388608 | tf_op jit(solution)/shard_map/mul | solution.py:199
  52.5 4.2 %reshape.130 = bf16[2,64,64,64]{3,2,1,0:T(8,128)(2,1)} reshape(bf16[128,4096]{1,0:T(8,128)(2,1)} %param.17) | data formatting | bytes 2097152 | tf_op jit(solution)/shard_map/reshape | solution.py:179
  56.7 4.2 %copy.55 = bf16[2,64,64,64]{1,3,2,0:T(8,128)(2,1)} copy(bf16[2,64,64,64]{3,2,1,0:T(8,128)(2,1)} %reshape.130) | data formatting | bytes 2097152 | tf_op jit(solution)/shard_map/reshape | solution.py:179
  60.9 2.3 %fusion.30 = (bf16[32,128,64]{1,2,0:T(8,128)(2,1)S(1)}, bf16[32,128,64]{1,2,0:T(8,128)(2,1)S(1)}, f32[1,32,128,64]{2,3,1,0:T(8,128)S(1)}, f32[1,32,128,64]{2,3,1,0:T(8,128)S(1)}, f32[1,32,128,64]{2,3,1,0:T(8,128)S(1)}) fusion(bf16[32,128,64]{1,2,0:T(8,128)(2,1)} %collective-permute-done.3, f32[32]{0:T(128)S(1)} %get-tuple-element.55, f32[]{:T(128)S(6)} %sub.97, ...), kind=kLoop, calls=%fused_computation.67 | loop fusion | flops 7602176 | bytes 7865232 | tf_op jit(solution)/shard_map/convert_element_type | solution.py:114
  64.6 3.7 %multiply_reduce_fusion.2 = (f32[2,64]{1,0:T(2,128)S(1)}, f32[2,64,64]{2,1,0:T(8,128)S(1)}) fusion(f32[2,64,64]{2,1,0:T(8,128)S(1)} %fusion.85, f32[2,64,64]{2,1,0:T(8,128)S(1)} %copy.44, pred[64,64]{1,0:T(8,128)(4,1)S(1)} %iota_compare_fusion, f32[2,64]{1,0:T(2,128)S(1)} %copy-done.18, bf16[2,64,64,64]{1,3,2,0:T(8,128)(2,1)S(1)} %copy-done.4, ...), kind=kOutput, calls=%fused_computation.10 | convolution fusion | flops 72343424 | bytes 2200576 | tf_op jit(solution)/shard_map/vmap(thp,shp->hts)/dot_general | solution.py:35
  69.1 2.8 %collective-permute-done.9 = bf16[32,128,64]{1,2,0:T(8,128)(2,1)S(1)} collective-permute-done((bf16[32,128,64]{1,2,0:T(8,128)(2,1)S(1)}, bf16[32,128,64]{1,2,0:T(8,128)(2,1)S(1)}, u32[]{:S(2)}, u32[]{:S(2)}) %collective-permute-start.9) | collective-permute-done | bytes 524320 | tf_op jit(solution)/shard_map/ppermute | solution.py:25
  83.2 1.7 %add_convert_fusion = bf16[2,64,128,64]{2,3,1,0:T(8,128)(2,1)S(1)} fusion(f32[64,128,64]{1,2,0:T(8,128)S(1)} %get-tuple-element.20, f32[2,64]{1,0:T(2,128)S(1)} %get-tuple-element.45, f32[64,128,64]{1,2,0:T(8,128)S(1)} %get-tuple-element.21, f32[2,64]{1,0:T(2,128)S(1)} %get-tuple-element.46, f32[64,128,64]{1,2,0:T(8,128)S(1)} %get-tuple-element.19, ...), kind=kLoop, calls=%fused_computation.13 | loop fusion | flops 10485760 | bytes 12585472 | tf_op jit(solution)/shard_map/convert_element_type | solution.py:201
  84.9 2.0 %fusion.3 = f32[2,64,128]{2,1,0:T(8,128)S(1)} fusion(bf16[2,64,64,64]{1,3,2,0:T(8,128)(2,1)S(1)} %copy-done.5, bf16[2,64,128,64]{2,3,1,0:T(8,128)(2,1)S(1)} %add_convert_fusion, f32[2,64,64]{1,2,0:T(8,128)S(1)} %copy.50), kind=kOutput, calls=%fused_computation.9 | convolution fusion | flops 136298496 | bytes 3244032 | tf_op jit(solution)/shard_map/chnp,cthp->cthn/dot_general | solution.py:35
  88.8 1.6 %collective-permute-start.14 = (f32[8,12,64]{2,0,1:T(8,128)S(1)}, f32[8,12,64]{2,0,1:T(8,128)S(1)}, u32[]{:S(2)}, u32[]{:S(2)}) collective-permute-start(f32[8,12,64]{2,0,1:T(8,128)S(1)} %pad_maximum_fusion.2), channel_id=1, source_target_pairs={{0,4},{4,0},{8,12},{12,8},{16,20},{20,16},{24,28},{28,24},{1,5},{5... | collective-permute-start | bytes 73736 | tf_op jit(solution)/shard_map/ppermute | solution.py:18
  93.0 14.9 %collective-permute-start.15 = (f32[8,12,64]{2,0,1:T(8,128)S(1)}, f32[8,12,64]{2,0,1:T(8,128)S(1)}, u32[]{:S(2)}, u32[]{:S(2)}) collective-permute-start(f32[8,12,64]{2,0,1:T(8,128)S(1)} %fusion.73), channel_id=1, source_target_pairs={{0,8},{4,12},{8,0},{12,4},{16,24},{20,28},{24,16},{28,20},{1,9},{5... | collective-permute-start | bytes 73736 | tf_op jit(solution)/shard_map/ppermute | solution.py:18
  107.9 3.5 %fusion.2 = bf16[2,64,64,64]{1,3,2,0:T(8,128)(2,1)} fusion(bf16[2,64,64,64]{1,3,2,0:T(8,128)(2,1)S(1)} %copy-done.3, f32[2,64,64,64]{3,2,1,0:T(8,128)S(1)} %fusion.6, f32[64]{0:T(128)S(1)} %copy-done.22, f32[2,64]{1,0:T(2,128)S(1)} %copy-done.17, f32[2,64,64]{2,1,0:T(8,128)S(1)} %fusion.85, f32[2,64,64]{2,1,0:T(8,128)S(1)} %copy.44, ...), kind=kOutput, calls=%fused_computation.7 | convolution fusion | flops 72876032 | bytes 4264704 | tf_op jit(solution)/shard_map/vmap(hts,shp->thp)/dot_general | solution.py:35
  111.4 3.3 %copy.51 = bf16[2,64,64,64]{3,2,1,0:T(8,128)(2,1)S(1)} copy(bf16[2,64,64,64]{1,3,2,0:T(8,128)(2,1)} %fusion.2) | data formatting | bytes 2097152 | tf_op jit(solution)/shard_map/convert_element_type | solution.py:222
  114.7 2.5 %reshape.129 = bf16[128,4096]{1,0:T(8,128)(2,1)} reshape(bf16[2,64,64,64]{3,2,1,0:T(8,128)(2,1)S(1)} %copy.51) | data formatting | bytes 2097152 | tf_op jit(solution)/shard_map/reshape | solution.py:223
  117.2 16.3 %collective-permute-start.16 = (f32[8,12,64]{2,0,1:T(8,128)S(1)}, f32[8,12,64]{2,0,1:T(8,128)S(1)}, u32[]{:S(2)}, u32[]{:S(2)}) collective-permute-start(f32[8,12,64]{2,0,1:T(8,128)S(1)} %add.170), channel_id=1, source_target_pairs={{0,16},{4,20},{8,24},{12,28},{16,0},{20,4},{24,8},{28,12},{1,17},{... | collective-permute-start | bytes 73736 | tf_op jit(solution)/shard_map/ppermute | solution.py:18
  (130 shorter events, 36.1 us)
Async XLA Ops:
  2.5 28.7 %collective-permute-start.2 = (f32[32]{0:T(128)S(1)}, f32[32]{0:T(128)S(1)}, u32[]{:S(2)}, u32[]{:S(2)}) collective-permute-start(f32[32]{0:T(128)S(1)} %get-tuple-element.63), channel_id=1, source_target_pairs={{0,4},{4,0},{8,12},{12,8},{16,20},{20,16},{24,28},{28,24},{1,5},{5... | collective-permute-start | bytes 392 | tf_op jit(solution)/shard_map/ppermute | solution.py:18
  5.4 25.8 %collective-permute-start.8 = (f32[32]{0:T(128)S(1)}, f32[32]{0:T(128)S(1)}, u32[]{:S(2)}, u32[]{:S(2)}) collective-permute-start(f32[32]{0:T(128)S(1)} %get-tuple-element.64), channel_id=1, source_target_pairs={{0,4},{4,0},{8,12},{12,8},{16,20},{20,16},{24,28},{28,24},{1,5},{5... | collective-permute-start | bytes 392 | tf_op jit(solution)/shard_map/ppermute | solution.py:18
  6.4 10.3 %collective-permute-start = (bf16[3,4352]{1,0:T(4,128)(2,1)S(1)}, bf16[3,4352]{1,0:T(4,128)(2,1)S(1)}, u32[]{:S(2)}, u32[]{:S(2)}) collective-permute-start(bf16[3,4352]{1,0:T(4,128)(2,1)S(1)} %slice.119), channel_id=1, source_target_pairs={{0,4},{4,8},{8,12},{12,16},{16,20},{20,24},{24,28},{1,5},{5,9},{9,... | collective-permute-start | bytes 78344 | tf_op jit(solution)/shard_map/ppermute | solution.py:12
  28.5 21.6 %copy-start = (f32[2,64,128,64]{2,3,1,0:T(8,128)}, f32[2,64,128,64]{2,3,1,0:T(8,128)S(1)}, u32[]{:S(2)}) copy-start(f32[2,64,128,64]{2,3,1,0:T(8,128)S(1)} %get-tuple-element.68) | copy-start | bytes 12582916
  29.6 14.9 %collective-permute-start.1 = (bf16[32,128,64]{1,2,0:T(8,128)(2,1)S(1)}, bf16[32,128,64]{1,2,0:T(8,128)(2,1)S(1)}, u32[]{:S(2)}, u32[]{:S(2)}) collective-permute-start(bf16[32,128,64]{1,2,0:T(8,128)(2,1)S(1)} %get-tuple-element.26), channel_id=1, source_target_pairs={{0,4},{4,0},{8,12},{12,8},{16,20},{20,16},{24,28},{28,24},{1,5},{5... | collective-permute-start | bytes 1572872 | tf_op jit(solution)/shard_map/ppermute | solution.py:18
  31.2 4.8 %collective-permute-start.10 = (f32[32]{0:T(128)S(1)}, f32[32]{0:T(128)S(1)}, u32[]{:S(2)}, u32[]{:S(2)}) collective-permute-start(f32[32]{0:T(128)S(1)} %get-tuple-element.60), channel_id=1, source_target_pairs={{0,8},{4,12},{16,24},{20,28},{1,9},{5,13},{17,25},{21,29},{2,10},{... | collective-permute-start | bytes 392 | tf_op jit(solution)/shard_map/ppermute | solution.py:25
  34.7 2.6 %collective-permute-start.4 = (f32[32]{0:T(128)S(1)}, f32[32]{0:T(128)S(1)}, u32[]{:S(2)}, u32[]{:S(2)}) collective-permute-start(f32[32]{0:T(128)S(1)} %get-tuple-element.14), channel_id=1, source_target_pairs={{0,8},{4,12},{16,24},{20,28},{1,9},{5,13},{17,25},{21,29},{2,10},{... | collective-permute-start | bytes 392 | tf_op jit(solution)/shard_map/ppermute | solution.py:25
  37.8 23.0 %collective-permute-start.7 = (bf16[32,128,64]{1,2,0:T(8,128)(2,1)}, bf16[32,128,64]{1,2,0:T(8,128)(2,1)S(1)}, u32[]{:S(2)}, u32[]{:S(2)}) collective-permute-start(bf16[32,128,64]{1,2,0:T(8,128)(2,1)} %get-tuple-element.27), channel_id=1, source_target_pairs={{0,4},{4,0},{8,12},{12,8},{16,20},{20,16},{24,28},{28,24},{1,5},{5... | collective-permute-start | bytes 1572872 | tf_op jit(solution)/shard_map/ppermute | solution.py:18
  45.7 15.2 %collective-permute-start.3 = (bf16[32,128,64]{1,2,0:T(8,128)(2,1)}, bf16[32,128,64]{1,2,0:T(8,128)(2,1)}, u32[]{:S(2)}, u32[]{:S(2)}) collective-permute-start(bf16[32,128,64]{1,2,0:T(8,128)(2,1)} %fusion.75), channel_id=1, source_target_pairs={{0,8},{4,12},{16,24},{20,28},{1,9},{5,13},{17,25},{21,29},{2,10},{... | collective-permute-start | bytes 1572872 | tf_op jit(solution)/shard_map/ppermute | solution.py:25
  63.2 8.7 %collective-permute-start.9 = (bf16[32,128,64]{1,2,0:T(8,128)(2,1)S(1)}, bf16[32,128,64]{1,2,0:T(8,128)(2,1)S(1)}, u32[]{:S(2)}, u32[]{:S(2)}) collective-permute-start(bf16[32,128,64]{1,2,0:T(8,128)(2,1)S(1)} %get-tuple-element.25), channel_id=1, source_target_pairs={{0,8},{4,12},{16,24},{20,28},{1,9},{5,13},{17,25},{21,29},{2,10},{... | collective-permute-start | bytes 1572872 | tf_op jit(solution)/shard_map/ppermute | solution.py:25
  68.4 6.7 %collective-permute-start.5 = (bf16[32,128,64]{1,2,0:T(8,128)(2,1)S(1)}, bf16[32,128,64]{1,2,0:T(8,128)(2,1)S(1)}, u32[]{:S(2)}, u32[]{:S(2)}) collective-permute-start(bf16[32,128,64]{1,2,0:T(8,128)(2,1)S(1)} %get-tuple-element.24), channel_id=1, source_target_pairs={{8,16},{12,20},{9,17},{13,21},{10,18},{14,22},{11,19},{15,23}} | collective-permute-start | bytes 1572872 | tf_op jit(solution)/shard_map/ppermute | solution.py:100
  72.6 4.2 %collective-permute-start.11 = (bf16[32,128,64]{1,2,0:T(8,128)(2,1)S(1)}, bf16[32,128,64]{1,2,0:T(8,128)(2,1)S(1)}, u32[]{:S(2)}, u32[]{:S(2)}) collective-permute-start(bf16[32,128,64]{1,2,0:T(8,128)(2,1)S(1)} %get-tuple-element.34), channel_id=1, source_target_pairs={{8,16},{12,20},{9,17},{13,21},{10,18},{14,22},{11,19},{15,23}} | collective-permute-start | bytes 1572872 | tf_op jit(solution)/shard_map/ppermute | solution.py:100
  75.1 3.0 %collective-permute-start.6 = (bf16[32,128,64]{1,2,0:T(8,128)(2,1)S(1)}, bf16[32,128,64]{1,2,0:T(8,128)(2,1)S(1)}, u32[]{:S(2)}, u32[]{:S(2)}) collective-permute-start(bf16[32,128,64]{1,2,0:T(8,128)(2,1)S(1)} %collective-permute-done.5), channel_id=1, source_target_pairs={{16,24},{20,28},{17,25},{21,29},{18,26},{22,30},{19,27},{23,31}} | collective-permute-start | bytes 1572872 | tf_op jit(solution)/shard_map/ppermute | solution.py:101
  76.9 1.4 %collective-permute-start.12 = (bf16[32,128,64]{1,2,0:T(8,128)(2,1)S(1)}, bf16[32,128,64]{1,2,0:T(8,128)(2,1)S(1)}, u32[]{:S(2)}, u32[]{:S(2)}) collective-permute-start(bf16[32,128,64]{1,2,0:T(8,128)(2,1)S(1)} %collective-permute-done.11), channel_id=1, source_target_pairs={{16,24},{20,28},{17,25},{21,29},{18,26},{22,30},{19,27},{23,31}} | collective-permute-start | bytes 1572872 | tf_op jit(solution)/shard_map/ppermute | solution.py:101
  86.9 21.0 %copy-start.3 = (bf16[2,64,64,64]{1,3,2,0:T(8,128)(2,1)S(1)}, bf16[2,64,64,64]{1,3,2,0:T(8,128)(2,1)}, u32[]{:S(2)}) copy-start(bf16[2,64,64,64]{1,3,2,0:T(8,128)(2,1)} %copy.46) | copy-start | bytes 3145732
  86.9 21.0 %copy-start.17 = (f32[2,64]{1,0:T(2,128)S(1)}, f32[2,64]{1,0:T(2,128)}, u32[]{:S(2)}) copy-start(f32[2,64]{1,0:T(2,128)} %broadcast_multiply_fusion) | copy-start | bytes 1540
  86.9 20.9 %copy-start.22 = (f32[64]{0:T(128)S(1)}, f32[64]{0:T(128)}, u32[]{:S(2)}) copy-start(f32[64]{0:T(128)} %param.14) | copy-start | bytes 772
  88.8 4.2 %collective-permute-start.14 = (f32[8,12,64]{2,0,1:T(8,128)S(1)}, f32[8,12,64]{2,0,1:T(8,128)S(1)}, u32[]{:S(2)}, u32[]{:S(2)}) collective-permute-start(f32[8,12,64]{2,0,1:T(8,128)S(1)} %pad_maximum_fusion.2), channel_id=1, source_target_pairs={{0,4},{4,0},{8,12},{12,8},{16,20},{20,16},{24,28},{28,24},{1,5},{5... | collective-permute-start | bytes 73736 | tf_op jit(solution)/shard_map/ppermute | solution.py:18
  90.6 43.0 %collective-permute-start.13 = (f32[3,128]{1,0:T(4,128)S(1)}, f32[3,128]{1,0:T(4,128)S(1)}, u32[]{:S(2)}, u32[]{:S(2)}) collective-permute-start(f32[3,128]{1,0:T(4,128)S(1)} %slice.179), channel_id=1, source_target_pairs={{4,0},{8,4},{12,8},{16,12},{20,16},{24,20},{28,24},{5,1},{9,5},{13... | collective-permute-start | bytes 4616 | tf_op jit(solution)/shard_map/ppermute | solution.py:12
  93.0 24.2 %collective-permute-start.15 = (f32[8,12,64]{2,0,1:T(8,128)S(1)}, f32[8,12,64]{2,0,1:T(8,128)S(1)}, u32[]{:S(2)}, u32[]{:S(2)}) collective-permute-start(f32[8,12,64]{2,0,1:T(8,128)S(1)} %fusion.73), channel_id=1, source_target_pairs={{0,8},{4,12},{8,0},{12,4},{16,24},{20,28},{24,16},{28,20},{1,9},{5... | collective-permute-start | bytes 73736 | tf_op jit(solution)/shard_map/ppermute | solution.py:18
  114.7 18.9 %copy-start.13 = (f32[128]{0:T(128)S(1)}, f32[128]{0:T(128)}, u32[]{:S(2)}) copy-start(f32[128]{0:T(128)} %get-tuple-element.35) | copy-start | bytes 1540
  114.7 18.9 %copy-start.14 = (f32[128]{0:T(128)S(1)}, f32[128]{0:T(128)}, u32[]{:S(2)}) copy-start(f32[128]{0:T(128)} %get-tuple-element.36) | copy-start | bytes 1540
  114.7 20.9 %copy-start.8 = (f32[8,12,64]{2,0,1:T(8,128)S(1)}, f32[8,12,64]{2,0,1:T(8,128)}, u32[]{:S(2)}) copy-start(f32[8,12,64]{2,0,1:T(8,128)} %param.15) | copy-start | bytes 73732
  117.2 18.4 %collective-permute-start.16 = (f32[8,12,64]{2,0,1:T(8,128)S(1)}, f32[8,12,64]{2,0,1:T(8,128)S(1)}, u32[]{:S(2)}, u32[]{:S(2)}) collective-permute-start(f32[8,12,64]{2,0,1:T(8,128)S(1)} %add.170), channel_id=1, source_target_pairs={{0,16},{4,20},{8,24},{12,28},{16,0},{20,4},{24,8},{28,12},{1,17},{... | collective-permute-start | bytes 73736 | tf_op jit(solution)/shard_map/ppermute | solution.py:18
  (18 other events, 99.6 us)

commit v10 on v7

--- a/solution.py
+++ b/solution.py
@@ -116,7 +116,7 @@
         else:
             sent, other_decay = from_partner((block.astype(jnp.bfloat16), block_decay), "seq", bit_pos)
             other = sent.astype(jnp.float32)
-        first = sent if first is None else first
+        first = sent if bit_pos < max(depth - 1, 1) else first
         upper = jnp.zeros_like(block_decay) + (jnp.right_shift(myself, bit_pos) & 1).astype(
             jnp.float32
         )
@@ -172,7 +172,7 @@
         for k in range(chunks)
     ]
     cross = jnp.concatenate([piece for piece, _ in pieces], axis=1)
-    late_cotangent = lax.optimization_barrier((cotangent, pieces[0][1]))[0]
+    late_cotangent = lax.optimization_barrier((cotangent, pieces[-1][1]))[0]
     grad_groups = late_cotangent.reshape(groups, group_len, heads, head_dim)
     y_inner, grad_inner, level_zero = jax.vmap(local_group)(
         x_groups, b_groups, c_groups, cumuls, grad_groups, weight_rows[:, 0]

time: 133 us -> 141 us (1.060)
  waiting for transfers between devices: 16.7 us -> 24.5 us
  starting transfers between devices: 48 us -> 44.1 us
  matrix products: 16.7 us -> 19.8 us
    ppermute x11, waiting for transfers between devices: 16.7 us -> 24.4 us  [from_partner(): return lax.ppermute(value, axis, pairs)]
    ppermute x11, starting transfers between devices: 39.8 us -> 34.4 us  [from_partner(): return lax.ppermute(value, axis, pairs)]
    another operation x3, other arithmetic: 1.1 us -> 4.37 us  [exchange(): return (jnp.stack(found_all, axis=0), first)]
    dot_general x6, matrix products: 14.7 us -> 17.8 us  [contract(): return jnp.einsum(form, left, right, preferred_element_type=jnp.float32)]
    ppermute x2, starting transfers between devices: 1.52 us -> 3.05 us  [relay(): lax.ppermute(value, axis, [(source, source + step) for source in range(ha...]
where the time goes in v10:
time: 141 us
  starting transfers between devices  44.1 us (31%)
  local copies, waits for them, and re-layouts  29.5 us (21%)
  waiting for transfers between devices  24.5 us (17%)
  other arithmetic  21.4 us (15%)
  matrix products  19.8 us (14%)
    ppermute x11, starting transfers between devices, from_partner(): return lax.ppermute(value, axis, pairs)  34.4 us
    ppermute x11, waiting for transfers between devices, from_partner(): return lax.ppermute(value, axis, pairs)  24.4 us
    dot_general x6, matrix products, contract(): return jnp.einsum(form, left, right, preferred_element_type=jnp.float32)  17.8 us
    reshape x2, local copies, waits for them, and re-layouts, local(): grad_groups = late_cotangent.reshape(groups, group_len, heads, head_dim)  7.58 us
    another operation x2, local copies, waits for them, and re-layouts, local(): x_groups = x_act.reshape(groups, group_len, heads, head_dim)  5.27 us
    ppermute x2, starting transfers between devices, shifted(): lax.ppermute(value, axis, [(source, source + steps) for source in range(l...  5.15 us
    another operation x3, other arithmetic, exchange(): return (jnp.stack(found_all, axis=0), first)  4.37 us
    another operation x1, other arithmetic  3.62 us
  transfers between devices with their start and end apart: 17, of which 6 were waited for; matrix products, arithmetic and copies ran while one was open for 39% of the time, Pallas kernels for 0%

profile of v10, /device:TPU:0, one launch (start us, length us, event | category | flops | bytes accessed | tf_op | source)
XLA Modules:
  0.0 140.6 jit_solution(16621913842038721161)
XLA Ops:
  2.5 2.9 %collective-permute-start.2 = (f32[32]{0:T(128)S(1)}, f32[32]{0:T(128)S(1)}, u32[]{:S(2)}, u32[]{:S(2)}) collective-permute-start(f32[32]{0:T(128)S(1)} %get-tuple-element.63), channel_id=1, source_target_pairs={{0,4},{4,0},{8,12},{12,8},{16,20},{20,16},{24,28},{28,24},{1,5},{5... | collective-permute-start | bytes 392 | tf_op jit(solution)/shard_map/ppermute | solution.py:18
  6.4 3.9 %collective-permute-start = (bf16[3,4352]{1,0:T(4,128)(2,1)S(1)}, bf16[3,4352]{1,0:T(4,128)(2,1)S(1)}, u32[]{:S(2)}, u32[]{:S(2)}) collective-permute-start(bf16[3,4352]{1,0:T(4,128)(2,1)S(1)} %slice.119), channel_id=1, source_target_pairs={{0,4},{4,8},{8,12},{12,16},{16,20},{20,24},{24,28},{1,5},{5,9},{9,... | collective-permute-start | bytes 78344 | tf_op jit(solution)/shard_map/ppermute | solution.py:12
  15.4 3.6 %fusion.79 = (bf16[128,4352]{1,0:T(8,128)(2,1)S(1)}, f32[128,4352]{1,0:T(8,128)S(1)}) fusion(f32[4352]{0:T(1024)S(1)} %get-tuple-element.8, bf16[128,4352]{1,0:T(8,128)(2,1)} %param.9, f32[4352]{0:T(1024)S(1)} %get-tuple-element.9, bf16[3,4352]{1,0:T(4,128)(2,1)S(1)} %collective-permute-done, f32[4352]{0:T(1024)S(1)} %get-tuple-element.10, ...), kind=kLoop, calls=%fused_computation.163 | loop fusion | flops 12255232 | bytes 4569600 | tf_op jit(solution)/shard_map/convert.2
  19.6 2.3 %reshape_reshape.3 = bf16[2,64,64,64]{3,2,1,0:T(8,128)(2,1)S(1)} reshape(bf16[128,4096]{1,0:T(8,128)(2,1)S(1)} %multiply_convert_fusion.5) | data formatting | bytes 2097152 | tf_op jit(solution)/shard_map/reshape;reshape | solution.py:154
  21.9 3.0 %copy.46 = bf16[2,64,64,64]{1,3,2,0:T(8,128)(2,1)} copy(bf16[2,64,64,64]{3,2,1,0:T(8,128)(2,1)S(1)} %reshape_reshape.3) | data formatting | bytes 2097152 | tf_op jit(solution)/shard_map/reshape;reshape | solution.py:154
  24.9 4.4 %multiply_reduce_fusion.4 = (f32[64,128,64]{1,2,0:T(8,128)S(1)}, f32[2,64,128,64]{2,3,1,0:T(8,128)}) fusion(f32[2,64]{1,0:T(2,128)S(1)} %get-tuple-element.52, bf16[2,64,128,1]{2,1,3,0:T(8,128)(2,1)S(1)} %bitcast.95, bf16[2,64,64,64]{1,3,2,0:T(8,128)(2,1)} %copy.46, f32[2,64,64]{1,2,0:T(8,128)S(1)} %copy.49), kind=kOutput, calls=%fused_computation.14 | convolution fusion | flops 137363456 | bytes 7406080 | tf_op jit(solution)/shard_map/vmap(sn,shp->hnp)/dot_general | solution.py:35
  33.7 1.9 %collective-permute-done.4 = f32[32]{0:T(128)S(1)} collective-permute-done((f32[32]{0:T(128)S(1)}, f32[32]{0:T(128)S(1)}, u32[]{:S(2)}, u32[]{:S(2)}) %collective-permute-start.4) | collective-permute-done | bytes 160 | tf_op jit(solution)/shard_map/ppermute | solution.py:18
  36.2 9.0 %collective-permute-done.1 = bf16[32,128,64]{1,2,0:T(8,128)(2,1)S(1)} collective-permute-done((bf16[32,128,64]{1,2,0:T(8,128)(2,1)S(1)}, bf16[32,128,64]{1,2,0:T(8,128)(2,1)S(1)}, u32[]{:S(2)}, u32[]{:S(2)}) %collective-permute-start.1) | collective-permute-done | bytes 524320 | tf_op jit(solution)/shard_map/ppermute | solution.py:18
  45.5 1.6 %collective-permute-start.3 = (bf16[32,128,64]{1,2,0:T(8,128)(2,1)S(1)}, bf16[32,128,64]{1,2,0:T(8,128)(2,1)S(1)}, u32[]{:S(2)}, u32[]{:S(2)}) collective-permute-start(bf16[32,128,64]{1,2,0:T(8,128)(2,1)S(1)} %fusion.75), channel_id=1, source_target_pairs={{0,8},{4,12},{8,0},{12,4},{16,24},{20,28},{24,16},{28,20},{1,9},{5... | collective-permute-start | bytes 1572872 | tf_op jit(solution)/shard_map/ppermute | solution.py:18
  48.8 6.7 %collective-permute-done.10 = f32[32]{0:T(128)S(1)} collective-permute-done((f32[32]{0:T(128)S(1)}, f32[32]{0:T(128)S(1)}, u32[]{:S(2)}, u32[]{:S(2)}) %collective-permute-start.10) | collective-permute-done | bytes 160 | tf_op jit(solution)/shard_map/ppermute | solution.py:18
  56.3 2.9 %fusion.30 = (bf16[32,128,64]{1,2,0:T(8,128)(2,1)}, bf16[32,128,64]{1,2,0:T(8,128)(2,1)S(1)}, f32[1,32,128,64]{2,3,1,0:T(8,128)}, f32[1,32,128,64]{2,3,1,0:T(8,128)}, f32[1,32,128,64]{2,3,1,0:T(8,128)}) fusion(bf16[32,128,64]{1,2,0:T(8,128)(2,1)S(1)} %collective-permute-done.3, f32[32]{0:T(128)S(1)} %get-tuple-element.55, f32[]{:T(128)S(6)} %sub.97, ...), kind=kLoop, calls=%fused_computation.67 | loop fusion | flops 7602176 | bytes 7865232 | tf_op jit(solution)/shard_map/convert_element_type | solution.py:114
  60.8 2.4 %slice_bitcast_fusion.4 = (f32[64,128,64]{1,2,0:T(8,128)}, f32[64,128,64]{1,2,0:T(8,128)}) fusion(f32[2,64,128,64]{2,3,1,0:T(8,128)S(1)} %copy-done), kind=kLoop, calls=%fused_computation.26 | loop fusion | bytes 8388608 | tf_op jit(solution)/shard_map/mul | solution.py:196
  64.8 4.3 %collective-permute-done.9 = bf16[32,128,64]{1,2,0:T(8,128)(2,1)S(1)} collective-permute-done((bf16[32,128,64]{1,2,0:T(8,128)(2,1)S(1)}, bf16[32,128,64]{1,2,0:T(8,128)(2,1)S(1)}, u32[]{:S(2)}, u32[]{:S(2)}) %collective-permute-start.9) | collective-permute-done | bytes 524320 | tf_op jit(solution)/shard_map/ppermute | solution.py:18
  69.1 1.9 %fusion.37 = (f32[1,32,128,64]{2,3,1,0:T(8,128)}, bf16[32,128,64]{1,2,0:T(8,128)(2,1)}) fusion(bf16[32,128,64]{1,2,0:T(8,128)(2,1)S(1)} %collective-permute-done.9, f32[32]{0:T(128)S(1)} %get-tuple-element.61, f32[32]{0:T(128)S(1)} %get-tuple-element.66, f32[]{:T(128)S(6)} %sub.97, f32[32]{0:T(128)S(1)} %get-tuple-element.62, f32[]{:T(128)S(6)} %sub.96, ...), kind=kLoop, calls=%fused_computation.74 | loop fusion | flops 4718592 | bytes 3670672 | tf_op jit(solution)/shard_map/stack | solution.py:128
  72.5 3.2 %reshape.130 = bf16[2,64,64,64]{3,2,1,0:T(8,128)(2,1)} reshape(bf16[128,4096]{1,0:T(8,128)(2,1)S(1)} %copy-done.12) | data formatting | bytes 2097152 | tf_op jit(solution)/shard_map/reshape | solution.py:176
  75.8 4.3 %copy.55 = bf16[2,64,64,64]{1,3,2,0:T(8,128)(2,1)} copy(bf16[2,64,64,64]{3,2,1,0:T(8,128)(2,1)} %reshape.130) | data formatting | bytes 2097152 | tf_op jit(solution)/shard_map/reshape | solution.py:176
  80.1 4.9 %multiply_reduce_fusion.2 = (f32[2,64]{1,0:T(2,128)S(1)}, f32[2,64,64]{2,1,0:T(8,128)S(1)}) fusion(f32[2,64,64]{2,1,0:T(8,128)S(1)} %fusion.85, f32[2,64,64]{2,1,0:T(8,128)S(1)} %copy.44, pred[64,64]{1,0:T(8,128)(4,1)S(1)} %iota_compare_fusion, f32[2,64]{1,0:T(2,128)S(1)} %copy-done.20, bf16[2,64,64,64]{1,3,2,0:T(8,128)(2,1)} %copy.55, ...), kind=kOutput, calls=%fused_computation.10 | convolution fusion | flops 72343424 | bytes 2200576 | tf_op jit(solution)/shard_map/vmap(thp,shp->hts)/dot_general | solution.py:35
  96.3 1.7 %add_convert_fusion = bf16[2,64,128,64]{2,3,1,0:T(8,128)(2,1)S(1)} fusion(f32[64,128,64]{1,2,0:T(8,128)S(1)} %get-tuple-element.20, f32[2,64]{1,0:T(2,128)S(1)} %get-tuple-element.45, f32[64,128,64]{1,2,0:T(8,128)S(1)} %get-tuple-element.21, f32[2,64]{1,0:T(2,128)S(1)} %get-tuple-element.46, f32[64,128,64]{1,2,0:T(8,128)S(1)} %get-tuple-element.19, ...), kind=kLoop, calls=%fused_computation.13 | loop fusion | flops 10485760 | bytes 12585472 | tf_op jit(solution)/shard_map/convert_element_type | solution.py:198
  98.0 2.0 %fusion.3 = f32[2,64,128]{2,1,0:T(8,128)S(1)} fusion(bf16[2,64,64,64]{1,3,2,0:T(8,128)(2,1)S(1)} %copy-done.5, bf16[2,64,128,64]{2,3,1,0:T(8,128)(2,1)S(1)} %add_convert_fusion, f32[2,64,64]{1,2,0:T(8,128)S(1)} %copy.50), kind=kOutput, calls=%fused_computation.9 | convolution fusion | flops 136298496 | bytes 3244032 | tf_op jit(solution)/shard_map/chnp,cthp->cthn/dot_general | solution.py:35
  106.0 4.5 %collective-permute-start.15 = (f32[8,12,64]{2,0,1:T(8,128)S(1)}, f32[8,12,64]{2,0,1:T(8,128)S(1)}, u32[]{:S(2)}, u32[]{:S(2)}) collective-permute-start(f32[8,12,64]{2,0,1:T(8,128)S(1)} %fusion.73), channel_id=1, source_target_pairs={{0,8},{4,12},{8,0},{12,4},{16,24},{20,28},{24,16},{28,20},{1,9},{5... | collective-permute-start | bytes 73736 | tf_op jit(solution)/shard_map/ppermute | solution.py:18
  110.5 3.5 %fusion.2 = bf16[2,64,64,64]{1,3,2,0:T(8,128)(2,1)} fusion(bf16[2,64,64,64]{1,3,2,0:T(8,128)(2,1)S(1)} %copy-done.3, f32[2,64,64,64]{3,2,1,0:T(8,128)S(1)} %fusion.6, f32[64]{0:T(128)S(1)} %copy-done.24, f32[2,64]{1,0:T(2,128)S(1)} %copy-done.19, f32[2,64,64]{2,1,0:T(8,128)S(1)} %fusion.85, f32[2,64,64]{2,1,0:T(8,128)S(1)} %copy.44, ...), kind=kOutput, calls=%fused_computation.7 | convolution fusion | flops 72876032 | bytes 4264704 | tf_op jit(solution)/shard_map/vmap(hts,shp->thp)/dot_general | solution.py:35
  114.0 3.3 %copy.51 = bf16[2,64,64,64]{3,2,1,0:T(8,128)(2,1)S(1)} copy(bf16[2,64,64,64]{1,3,2,0:T(8,128)(2,1)} %fusion.2) | data formatting | bytes 2097152 | tf_op jit(solution)/shard_map/convert_element_type | solution.py:219
  117.4 2.5 %reshape.129 = bf16[128,4096]{1,0:T(8,128)(2,1)} reshape(bf16[2,64,64,64]{3,2,1,0:T(8,128)(2,1)S(1)} %copy.51) | data formatting | bytes 2097152 | tf_op jit(solution)/shard_map/reshape | solution.py:220
  119.9 18.0 %collective-permute-start.16 = (f32[8,12,64]{2,0,1:T(8,128)S(1)}, f32[8,12,64]{2,0,1:T(8,128)S(1)}, u32[]{:S(2)}, u32[]{:S(2)}) collective-permute-start(f32[8,12,64]{2,0,1:T(8,128)S(1)} %add.170), channel_id=1, source_target_pairs={{0,16},{4,20},{8,24},{12,28},{16,0},{20,4},{24,8},{28,12},{1,17},{... | collective-permute-start | bytes 73736 | tf_op jit(solution)/shard_map/ppermute | solution.py:18
  (134 shorter events, 40.6 us)
Async XLA Ops:
  2.5 29.5 %collective-permute-start.2 = (f32[32]{0:T(128)S(1)}, f32[32]{0:T(128)S(1)}, u32[]{:S(2)}, u32[]{:S(2)}) collective-permute-start(f32[32]{0:T(128)S(1)} %get-tuple-element.63), channel_id=1, source_target_pairs={{0,4},{4,0},{8,12},{12,8},{16,20},{20,16},{24,28},{28,24},{1,5},{5... | collective-permute-start | bytes 392 | tf_op jit(solution)/shard_map/ppermute | solution.py:18
  5.4 26.5 %collective-permute-start.8 = (f32[32]{0:T(128)S(1)}, f32[32]{0:T(128)S(1)}, u32[]{:S(2)}, u32[]{:S(2)}) collective-permute-start(f32[32]{0:T(128)S(1)} %get-tuple-element.64), channel_id=1, source_target_pairs={{0,4},{4,0},{8,12},{12,8},{16,20},{20,16},{24,28},{28,24},{1,5},{5... | collective-permute-start | bytes 392 | tf_op jit(solution)/shard_map/ppermute | solution.py:18
  6.4 9.0 %collective-permute-start = (bf16[3,4352]{1,0:T(4,128)(2,1)S(1)}, bf16[3,4352]{1,0:T(4,128)(2,1)S(1)}, u32[]{:S(2)}, u32[]{:S(2)}) collective-permute-start(bf16[3,4352]{1,0:T(4,128)(2,1)S(1)} %slice.119), channel_id=1, source_target_pairs={{0,4},{4,8},{8,12},{12,16},{16,20},{20,24},{24,28},{1,5},{5,9},{9,... | collective-permute-start | bytes 78344 | tf_op jit(solution)/shard_map/ppermute | solution.py:12
  30.3 14.9 %collective-permute-start.1 = (bf16[32,128,64]{1,2,0:T(8,128)(2,1)S(1)}, bf16[32,128,64]{1,2,0:T(8,128)(2,1)S(1)}, u32[]{:S(2)}, u32[]{:S(2)}) collective-permute-start(bf16[32,128,64]{1,2,0:T(8,128)(2,1)S(1)} %get-tuple-element.26), channel_id=1, source_target_pairs={{0,4},{4,0},{8,12},{12,8},{16,20},{20,16},{24,28},{28,24},{1,5},{5... | collective-permute-start | bytes 1572872 | tf_op jit(solution)/shard_map/ppermute | solution.py:18
  32.0 15.2 %copy-start.18 = (f32[32]{0:T(128)}, f32[32]{0:T(128)S(1)}, u32[]{:S(2)}) copy-start(f32[32]{0:T(128)S(1)} %collective-permute-done.8) | copy-start | bytes 388
  32.0 3.6 %collective-permute-start.4 = (f32[32]{0:T(128)S(1)}, f32[32]{0:T(128)S(1)}, u32[]{:S(2)}, u32[]{:S(2)}) collective-permute-start(f32[32]{0:T(128)S(1)} %get-tuple-element.14), channel_id=1, source_target_pairs={{0,8},{4,12},{8,0},{12,4},{16,24},{20,28},{24,16},{28,20},{1,9},{5... | collective-permute-start | bytes 392 | tf_op jit(solution)/shard_map/ppermute | solution.py:18
  35.6 20.6 %collective-permute-start.7 = (bf16[32,128,64]{1,2,0:T(8,128)(2,1)}, bf16[32,128,64]{1,2,0:T(8,128)(2,1)S(1)}, u32[]{:S(2)}, u32[]{:S(2)}) collective-permute-start(bf16[32,128,64]{1,2,0:T(8,128)(2,1)} %get-tuple-element.27), channel_id=1, source_target_pairs={{0,4},{4,0},{8,12},{12,8},{16,20},{20,16},{24,28},{28,24},{1,5},{5... | collective-permute-start | bytes 1572872 | tf_op jit(solution)/shard_map/ppermute | solution.py:18
  45.5 10.7 %collective-permute-start.3 = (bf16[32,128,64]{1,2,0:T(8,128)(2,1)S(1)}, bf16[32,128,64]{1,2,0:T(8,128)(2,1)S(1)}, u32[]{:S(2)}, u32[]{:S(2)}) collective-permute-start(bf16[32,128,64]{1,2,0:T(8,128)(2,1)S(1)} %fusion.75), channel_id=1, source_target_pairs={{0,8},{4,12},{8,0},{12,4},{16,24},{20,28},{24,16},{28,20},{1,9},{5... | collective-permute-start | bytes 1572872 | tf_op jit(solution)/shard_map/ppermute | solution.py:18
  47.8 7.8 %collective-permute-start.10 = (f32[32]{0:T(128)S(1)}, f32[32]{0:T(128)S(1)}, u32[]{:S(2)}, u32[]{:S(2)}) collective-permute-start(f32[32]{0:T(128)S(1)} %get-tuple-element.60), channel_id=1, source_target_pairs={{0,8},{4,12},{8,0},{12,4},{16,24},{20,28},{24,16},{28,20},{1,9},{5... | collective-permute-start | bytes 392 | tf_op jit(solution)/shard_map/ppermute | solution.py:18
  59.1 10.0 %collective-permute-start.9 = (bf16[32,128,64]{1,2,0:T(8,128)(2,1)S(1)}, bf16[32,128,64]{1,2,0:T(8,128)(2,1)S(1)}, u32[]{:S(2)}, u32[]{:S(2)}) collective-permute-start(bf16[32,128,64]{1,2,0:T(8,128)(2,1)S(1)} %get-tuple-element.25), channel_id=1, source_target_pairs={{0,8},{4,12},{8,0},{12,4},{16,24},{20,28},{24,16},{28,20},{1,9},{5... | collective-permute-start | bytes 1572872 | tf_op jit(solution)/shard_map/ppermute | solution.py:18
  63.2 23.4 %collective-permute-start.5 = (bf16[32,128,64]{1,2,0:T(8,128)(2,1)}, bf16[32,128,64]{1,2,0:T(8,128)(2,1)}, u32[]{:S(2)}, u32[]{:S(2)}) collective-permute-start(bf16[32,128,64]{1,2,0:T(8,128)(2,1)} %get-tuple-element.24), channel_id=1, source_target_pairs={{8,16},{12,20},{9,17},{13,21},{10,18},{14,22},{11,19},{15,23}} | collective-permute-start | bytes 1572872 | tf_op jit(solution)/shard_map/ppermute | solution.py:100
  71.0 17.2 %collective-permute-start.11 = (bf16[32,128,64]{1,2,0:T(8,128)(2,1)}, bf16[32,128,64]{1,2,0:T(8,128)(2,1)}, u32[]{:S(2)}, u32[]{:S(2)}) collective-permute-start(bf16[32,128,64]{1,2,0:T(8,128)(2,1)} %get-tuple-element.34), channel_id=1, source_target_pairs={{8,16},{12,20},{9,17},{13,21},{10,18},{14,22},{11,19},{15,23}} | collective-permute-start | bytes 1572872 | tf_op jit(solution)/shard_map/ppermute | solution.py:100
  86.6 3.0 %collective-permute-start.6 = (bf16[32,128,64]{1,2,0:T(8,128)(2,1)}, bf16[32,128,64]{1,2,0:T(8,128)(2,1)S(1)}, u32[]{:S(2)}, u32[]{:S(2)}) collective-permute-start(bf16[32,128,64]{1,2,0:T(8,128)(2,1)} %collective-permute-done.5), channel_id=1, source_target_pairs={{16,24},{20,28},{17,25},{21,29},{18,26},{22,30},{19,27},{23,31}} | collective-permute-start | bytes 1572872 | tf_op jit(solution)/shard_map/ppermute | solution.py:101
  88.3 2.6 %collective-permute-start.12 = (bf16[32,128,64]{1,2,0:T(8,128)(2,1)}, bf16[32,128,64]{1,2,0:T(8,128)(2,1)S(1)}, u32[]{:S(2)}, u32[]{:S(2)}) collective-permute-start(bf16[32,128,64]{1,2,0:T(8,128)(2,1)} %collective-permute-done.11), channel_id=1, source_target_pairs={{16,24},{20,28},{17,25},{21,29},{18,26},{22,30},{19,27},{23,31}} | collective-permute-start | bytes 1572872 | tf_op jit(solution)/shard_map/ppermute | solution.py:101
  100.0 10.5 %copy-start.3 = (bf16[2,64,64,64]{1,3,2,0:T(8,128)(2,1)S(1)}, bf16[2,64,64,64]{1,3,2,0:T(8,128)(2,1)}, u32[]{:S(2)}) copy-start(bf16[2,64,64,64]{1,3,2,0:T(8,128)(2,1)} %copy.46) | copy-start | bytes 3145732
  101.9 4.2 %collective-permute-start.14 = (f32[8,12,64]{2,0,1:T(8,128)S(1)}, f32[8,12,64]{2,0,1:T(8,128)S(1)}, u32[]{:S(2)}, u32[]{:S(2)}) collective-permute-start(f32[8,12,64]{2,0,1:T(8,128)S(1)} %pad_maximum_fusion.2), channel_id=1, source_target_pairs={{0,4},{4,0},{8,12},{12,8},{16,20},{20,16},{24,28},{28,24},{1,5},{5... | collective-permute-start | bytes 73736 | tf_op jit(solution)/shard_map/ppermute | solution.py:18
  103.6 34.3 %collective-permute-start.13 = (f32[3,128]{1,0:T(4,128)S(1)}, f32[3,128]{1,0:T(4,128)S(1)}, u32[]{:S(2)}, u32[]{:S(2)}) collective-permute-start(f32[3,128]{1,0:T(4,128)S(1)} %slice.179), channel_id=1, source_target_pairs={{4,0},{8,4},{12,8},{16,12},{20,16},{24,20},{28,24},{5,1},{9,5},{13... | collective-permute-start | bytes 4616 | tf_op jit(solution)/shard_map/ppermute | solution.py:12
  106.0 13.8 %collective-permute-start.15 = (f32[8,12,64]{2,0,1:T(8,128)S(1)}, f32[8,12,64]{2,0,1:T(8,128)S(1)}, u32[]{:S(2)}, u32[]{:S(2)}) collective-permute-start(f32[8,12,64]{2,0,1:T(8,128)S(1)} %fusion.73), channel_id=1, source_target_pairs={{0,8},{4,12},{8,0},{12,4},{16,24},{20,28},{24,16},{28,20},{1,9},{5... | collective-permute-start | bytes 73736 | tf_op jit(solution)/shard_map/ppermute | solution.py:18
  117.3 20.5 %copy-start.14 = (f32[128]{0:T(128)S(1)}, f32[128]{0:T(128)}, u32[]{:S(2)}) copy-start(f32[128]{0:T(128)} %get-tuple-element.35) | copy-start | bytes 1540
  117.4 20.5 %copy-start.15 = (f32[128]{0:T(128)S(1)}, f32[128]{0:T(128)}, u32[]{:S(2)}) copy-start(f32[128]{0:T(128)} %get-tuple-element.36) | copy-start | bytes 1540
  117.4 20.5 %copy-start.16 = (f32[128]{0:T(128)S(1)}, f32[128]{0:T(128)}, u32[]{:S(2)}) copy-start(f32[128]{0:T(128)} %get-tuple-element.37) | copy-start | bytes 1540
  117.4 20.5 %copy-start.17 = (f32[128]{0:T(128)S(1)}, f32[128]{0:T(128)}, u32[]{:S(2)}) copy-start(f32[128]{0:T(128)} %get-tuple-element.38) | copy-start | bytes 1540
  117.4 22.6 %copy-start.13 = (f32[8,12,64]{2,0,1:T(8,128)S(1)}, f32[8,12,64]{2,0,1:T(8,128)}, u32[]{:S(2)}) copy-start(f32[8,12,64]{2,0,1:T(8,128)} %param.15) | copy-start | bytes 73732
  119.9 20.1 %collective-permute-start.16 = (f32[8,12,64]{2,0,1:T(8,128)S(1)}, f32[8,12,64]{2,0,1:T(8,128)S(1)}, u32[]{:S(2)}, u32[]{:S(2)}) collective-permute-start(f32[8,12,64]{2,0,1:T(8,128)S(1)} %add.170), channel_id=1, source_target_pairs={{0,16},{4,20},{8,24},{12,28},{16,0},{20,4},{24,8},{28,12},{1,17},{... | collective-permute-start | bytes 73736 | tf_op jit(solution)/shard_map/ppermute | solution.py:18
  (20 other events, 86.4 us)

commit v11 on v7

--- a/solution.py
+++ b/solution.py
@@ -229,7 +229,7 @@
         grad_c_in = grad_c_in + query_taps[offset][None, :] * extended[lagged : lagged + length]
     grad_first = exact("gk,gh->kh", picked, level_zero)
     local_grads = jnp.concatenate([grad_first[:, None, :], grads], axis=1)
-    summed = all_sum(local_grads, "seq")
+    summed = lax.psum(local_grads, "seq")
     level_update = level_table + summed / math.sqrt(length * devices)
     return (ssm_out, grad_c_in, level_update)
 

time: 133 us -> 167 us (1.26)
  blocking collectives: 0 us -> 63.1 us
  starting transfers between devices: 48 us -> 17.4 us
  matrix products: 16.7 us -> 21 us
  waiting for transfers between devices: 16.7 us -> 14.3 us
    psum x0 -> x1, blocking collectives: none -> 63.1 us  [local(): summed = lax.psum(local_grads, 'seq')]
    ppermute x11 -> x8, starting transfers between devices: 39.8 us -> 9.17 us  [from_partner(): return lax.ppermute(value, axis, pairs)]
    dot_general x6, matrix products: 14.7 us -> 18.4 us  [contract(): return jnp.einsum(form, left, right, preferred_element_type=jnp.float32)]
    ppermute x11 -> x8, waiting for transfers between devices: 16.7 us -> 14.3 us  [from_partner(): return lax.ppermute(value, axis, pairs)]
  transfers between devices with their start and end apart: 17 -> 14, of which waited for: 6 -> 4; matrix products, arithmetic and copies ran while one was open for 39% -> 32% of each run, Pallas kernels for 0% -> 0%
where the time goes in v11:
time: 167 us
  blocking collectives  63.1 us (38%)
  local copies, waits for them, and re-layouts  29.5 us (18%)
  matrix products  21 us (13%)
  other arithmetic  20.1 us (12%)
  starting transfers between devices  17.4 us (10%)
  waiting for transfers between devices  14.3 us (9%)
    psum x1, blocking collectives, local(): summed = lax.psum(local_grads, 'seq')  63.1 us
    dot_general x6, matrix products, contract(): return jnp.einsum(form, left, right, preferred_element_type=jnp.float32)  18.4 us
    ppermute x8, waiting for transfers between devices, from_partner(): return lax.ppermute(value, axis, pairs)  14.3 us
    ppermute x8, starting transfers between devices, from_partner(): return lax.ppermute(value, axis, pairs)  9.17 us
    reshape x2, local copies, waits for them, and re-layouts, local(): grad_groups = late_cotangent.reshape(groups, group_len, heads, head_dim)  8.45 us
    another operation x2, local copies, waits for them, and re-layouts, local(): x_groups = x_act.reshape(groups, group_len, heads, head_dim)  5.23 us
    ppermute x2, starting transfers between devices, shifted(): lax.ppermute(value, axis, [(source, source + steps) for source in range(l...  5.15 us
    another operation x1, other arithmetic  3.46 us
  transfers between devices with their start and end apart: 14, of which 4 were waited for; matrix products, arithmetic and copies ran while one was open for 32% of the time, Pallas kernels for 0%

profile of v11, /device:TPU:0, one launch (start us, length us, event | category | flops | bytes accessed | tf_op | source)
XLA Modules:
  0.0 166.7 jit_solution(13036059599389641695)
XLA Ops:
  2.5 2.9 %collective-permute-start.2 = (f32[32]{0:T(128)S(1)}, f32[32]{0:T(128)S(1)}, u32[]{:S(2)}, u32[]{:S(2)}) collective-permute-start(f32[32]{0:T(128)S(1)} %get-tuple-element.63), channel_id=1, source_target_pairs={{0,4},{4,0},{8,12},{12,8},{16,20},{20,16},{24,28},{28,24},{1,5},{5... | collective-permute-start | bytes 392 | tf_op jit(solution)/shard_map/ppermute | solution.py:18
  6.4 3.9 %collective-permute-start = (bf16[3,4352]{1,0:T(4,128)(2,1)S(1)}, bf16[3,4352]{1,0:T(4,128)(2,1)S(1)}, u32[]{:S(2)}, u32[]{:S(2)}) collective-permute-start(bf16[3,4352]{1,0:T(4,128)(2,1)S(1)} %slice.119), channel_id=1, source_target_pairs={{0,4},{4,8},{8,12},{12,16},{16,20},{20,24},{24,28},{1,5},{5,9},{9,... | collective-permute-start | bytes 78344 | tf_op jit(solution)/shard_map/ppermute | solution.py:12
  16.8 3.5 %fusion.78 = (bf16[128,4352]{1,0:T(8,128)(2,1)S(1)}, f32[128,4352]{1,0:T(8,128)S(1)}) fusion(f32[4352]{0:T(1024)S(1)} %get-tuple-element.8, bf16[128,4352]{1,0:T(8,128)(2,1)} %param.9, f32[4352]{0:T(1024)S(1)} %get-tuple-element.9, bf16[3,4352]{1,0:T(4,128)(2,1)S(1)} %collective-permute-done, f32[4352]{0:T(1024)S(1)} %get-tuple-element.10, ...), kind=kLoop, calls=%fused_computation.162 | loop fusion | flops 12255232 | bytes 4569600 | tf_op jit(solution)/shard_map/convert.2
  20.8 2.3 %reshape_reshape.3 = bf16[2,64,64,64]{3,2,1,0:T(8,128)(2,1)S(1)} reshape(bf16[128,4096]{1,0:T(8,128)(2,1)S(1)} %multiply_convert_fusion.5) | data formatting | bytes 2097152 | tf_op jit(solution)/shard_map/reshape;reshape | solution.py:154
  23.1 2.9 %copy.46 = bf16[2,64,64,64]{1,3,2,0:T(8,128)(2,1)} copy(bf16[2,64,64,64]{3,2,1,0:T(8,128)(2,1)S(1)} %reshape_reshape.3) | data formatting | bytes 2097152 | tf_op jit(solution)/shard_map/reshape;reshape | solution.py:154
  26.1 2.5 %multiply_reduce_fusion.4 = (f32[64,128,64]{1,2,0:T(8,128)S(1)}, f32[2,64,128,64]{2,3,1,0:T(8,128)S(1)}) fusion(f32[2,64]{1,0:T(2,128)S(1)} %get-tuple-element.52, bf16[2,64,128,1]{2,1,3,0:T(8,128)(2,1)S(1)} %bitcast.95, bf16[2,64,64,64]{1,3,2,0:T(8,128)(2,1)} %copy.46, f32[2,64,64]{1,2,0:T(8,128)S(1)} %copy.49), kind=kOutput, calls=%fused_computation.14 | convolution fusion | flops 137363456 | bytes 7406080 | tf_op jit(solution)/shard_map/vmap(sn,shp->hnp)/dot_general | solution.py:35
  29.7 1.5 collective-permute-start.1
  31.3 1.6 collective-permute-start.10
  33.4 1.5 collective-permute-done.10
  37.5 7.1 %collective-permute-done.1 = bf16[32,128,64]{1,2,0:T(8,128)(2,1)S(1)} collective-permute-done((bf16[32,128,64]{1,2,0:T(8,128)(2,1)S(1)}, bf16[32,128,64]{1,2,0:T(8,128)(2,1)S(1)}, u32[]{:S(2)}, u32[]{:S(2)}) %collective-permute-start.1) | collective-permute-done | bytes 524320 | tf_op jit(solution)/shard_map/ppermute | solution.py:18
  45.7 1.6 collective-permute-start.3
  47.4 2.4 %slice_bitcast_fusion.4 = (f32[64,128,64]{1,2,0:T(8,128)}, f32[64,128,64]{1,2,0:T(8,128)}) fusion(f32[2,64,128,64]{2,3,1,0:T(8,128)S(1)} %get-tuple-element.68), kind=kLoop, calls=%fused_computation.26 | loop fusion | bytes 8388608 | tf_op jit(solution)/shard_map/mul | solution.py:196
  49.8 4.3 %reshape.130 = bf16[2,64,64,64]{3,2,1,0:T(8,128)(2,1)} reshape(bf16[128,4096]{1,0:T(8,128)(2,1)} %param.17) | data formatting | bytes 2097152 | tf_op jit(solution)/shard_map/reshape | solution.py:176
  54.1 4.2 %copy.55 = bf16[2,64,64,64]{1,3,2,0:T(8,128)(2,1)} copy(bf16[2,64,64,64]{3,2,1,0:T(8,128)(2,1)} %reshape.130) | data formatting | bytes 2097152 | tf_op jit(solution)/shard_map/reshape | solution.py:176
  58.3 2.3 %fusion.30 = (bf16[32,128,64]{1,2,0:T(8,128)(2,1)S(1)}, bf16[32,128,64]{1,2,0:T(8,128)(2,1)S(1)}, f32[1,32,128,64]{2,3,1,0:T(8,128)S(1)}, f32[1,32,128,64]{2,3,1,0:T(8,128)S(1)}, f32[1,32,128,64]{2,3,1,0:T(8,128)S(1)}) fusion(bf16[32,128,64]{1,2,0:T(8,128)(2,1)} %collective-permute-done.3, f32[32]{0:T(128)S(1)} %get-tuple-element.55, f32[]{:T(128)S(6)} %sub.97, ...), kind=kLoop, calls=%fused_computation.67 | loop fusion | flops 7602176 | bytes 7865232 | tf_op jit(solution)/shard_map/convert_element_type | solution.py:114
  61.1 3.7 %multiply_reduce_fusion.2 = (f32[2,64]{1,0:T(2,128)S(1)}, f32[2,64,64]{2,1,0:T(8,128)S(1)}) fusion(f32[2,64,64]{2,1,0:T(8,128)S(1)} %fusion.84, f32[2,64,64]{2,1,0:T(8,128)S(1)} %copy.44, pred[64,64]{1,0:T(8,128)(4,1)S(1)} %iota_compare_fusion, f32[2,64]{1,0:T(2,128)S(1)} %copy-done.18, bf16[2,64,64,64]{1,3,2,0:T(8,128)(2,1)S(1)} %copy-done.4, ...), kind=kOutput, calls=%fused_computation.10 | convolution fusion | flops 72343424 | bytes 2200576 | tf_op jit(solution)/shard_map/vmap(thp,shp->hts)/dot_general | solution.py:35
  65.6 4.7 %collective-permute-done.9 = bf16[32,128,64]{1,2,0:T(8,128)(2,1)S(1)} collective-permute-done((bf16[32,128,64]{1,2,0:T(8,128)(2,1)S(1)}, bf16[32,128,64]{1,2,0:T(8,128)(2,1)S(1)}, u32[]{:S(2)}, u32[]{:S(2)}) %collective-permute-start.9) | collective-permute-done | bytes 524320 | tf_op jit(solution)/shard_map/ppermute | solution.py:18
  82.1 1.7 %add_convert_fusion = bf16[2,64,128,64]{2,3,1,0:T(8,128)(2,1)S(1)} fusion(f32[64,128,64]{1,2,0:T(8,128)S(1)} %get-tuple-element.20, f32[2,64]{1,0:T(2,128)S(1)} %get-tuple-element.45, f32[64,128,64]{1,2,0:T(8,128)S(1)} %get-tuple-element.21, f32[2,64]{1,0:T(2,128)S(1)} %get-tuple-element.46, f32[64,128,64]{1,2,0:T(8,128)S(1)} %get-tuple-element.19, ...), kind=kLoop, calls=%fused_computation.13 | loop fusion | flops 10485760 | bytes 12585472 | tf_op jit(solution)/shard_map/convert_element_type | solution.py:198
  83.8 2.0 %fusion.3 = f32[2,64,128]{2,1,0:T(8,128)S(1)} fusion(bf16[2,64,64,64]{1,3,2,0:T(8,128)(2,1)S(1)} %copy-done.5, bf16[2,64,128,64]{2,3,1,0:T(8,128)(2,1)S(1)} %add_convert_fusion, f32[2,64,64]{1,2,0:T(8,128)S(1)} %copy.50), kind=kOutput, calls=%fused_computation.9 | convolution fusion | flops 136298496 | bytes 3244032 | tf_op jit(solution)/shard_map/chnp,cthp->cthn/dot_general | solution.py:35
  85.9 3.4 %fusion.6 = f32[2,64,64,64]{3,2,1,0:T(8,128)} fusion(bf16[2,64,128,64]{2,3,1,0:T(8,128)(2,1)S(1)} %add_convert_fusion, f32[2,64,64]{1,2,0:T(8,128)S(1)} %copy.50, f32[2,64,128]{2,1,0:T(8,128)S(1)} %convert_element_type.121), kind=kOutput, calls=%fused_computation.19 | convolution fusion | flops 136314880 | bytes 4292608 | tf_op jit(solution)/shard_map/cthn,chnp->cthp/dot_general | solution.py:35
  91.0 63.1 %psum.7 = f32[8,12,64]{2,0,1:T(8,128)S(1)} all-reduce(f32[8,12,64]{2,0,1:T(8,128)S(1)} %pad_maximum_fusion.2), channel_id=1, replica_groups=mesh['seq'=8,'grp'=4] {'seq'}, use_global_device_ids=true, to_apply=%region_9.10 | all-reduce | flops 6144 | bytes 49152 | tf_op jit(solution)/shard_map/psum | solution.py:232
  154.2 5.4 %fusion.2 = bf16[2,64,64,64]{1,3,2,0:T(8,128)(2,1)} fusion(bf16[2,64,64,64]{1,3,2,0:T(8,128)(2,1)S(1)} %copy-done.3, f32[2,64,64,64]{3,2,1,0:T(8,128)} %fusion.6, f32[64]{0:T(128)S(1)} %copy-done.22, f32[2,64]{1,0:T(2,128)S(1)} %copy-done.17, f32[2,64,64]{2,1,0:T(8,128)S(1)} %fusion.84, f32[2,64,64]{2,1,0:T(8,128)S(1)} %copy.44, ...), kind=kOutput, calls=%fused_computation.7 | convolution fusion | flops 72876032 | bytes 4264704 | tf_op jit(solution)/shard_map/vmap(hts,shp->thp)/dot_general | solution.py:35
  160.2 3.3 %copy.51 = bf16[2,64,64,64]{3,2,1,0:T(8,128)(2,1)S(1)} copy(bf16[2,64,64,64]{1,3,2,0:T(8,128)(2,1)} %fusion.2) | data formatting | bytes 2097152 | tf_op jit(solution)/shard_map/convert_element_type | solution.py:219
  163.5 2.5 %reshape.129 = bf16[128,4096]{1,0:T(8,128)(2,1)} reshape(bf16[2,64,64,64]{3,2,1,0:T(8,128)(2,1)S(1)} %copy.51) | data formatting | bytes 2097152 | tf_op jit(solution)/shard_map/reshape | solution.py:220
  (125 shorter events, 31.4 us)
Async XLA Ops:
  2.5 28.8 %collective-permute-start.2 = (f32[32]{0:T(128)S(1)}, f32[32]{0:T(128)S(1)}, u32[]{:S(2)}, u32[]{:S(2)}) collective-permute-start(f32[32]{0:T(128)S(1)} %get-tuple-element.63), channel_id=1, source_target_pairs={{0,4},{4,0},{8,12},{12,8},{16,20},{20,16},{24,28},{28,24},{1,5},{5... | collective-permute-start | bytes 392 | tf_op jit(solution)/shard_map/ppermute | solution.py:18
  5.4 25.8 %collective-permute-start.8 = (f32[32]{0:T(128)S(1)}, f32[32]{0:T(128)S(1)}, u32[]{:S(2)}, u32[]{:S(2)}) collective-permute-start(f32[32]{0:T(128)S(1)} %get-tuple-element.64), channel_id=1, source_target_pairs={{0,4},{4,0},{8,12},{12,8},{16,20},{20,16},{24,28},{28,24},{1,5},{5... | collective-permute-start | bytes 392 | tf_op jit(solution)/shard_map/ppermute | solution.py:18
  6.4 10.4 %collective-permute-start = (bf16[3,4352]{1,0:T(4,128)(2,1)S(1)}, bf16[3,4352]{1,0:T(4,128)(2,1)S(1)}, u32[]{:S(2)}, u32[]{:S(2)}) collective-permute-start(bf16[3,4352]{1,0:T(4,128)(2,1)S(1)} %slice.119), channel_id=1, source_target_pairs={{0,4},{4,8},{8,12},{12,16},{16,20},{20,24},{24,28},{1,5},{5,9},{9,... | collective-permute-start | bytes 78344 | tf_op jit(solution)/shard_map/ppermute | solution.py:12
  10.3 5.7 %copy-start.19 = (pred[2,2]{1,0:T(4,128)(4,1)}, pred[2,2]{1,0:T(4,128)(4,1)S(1)}, u32[]{:S(2)}) copy-start(pred[2,2]{1,0:T(4,128)(4,1)S(1)} %get-tuple-element.69) | copy-start | bytes 16
  28.6 18.9 %copy-start = (f32[2,64,128,64]{2,3,1,0:T(8,128)}, f32[2,64,128,64]{2,3,1,0:T(8,128)S(1)}, u32[]{:S(2)}) copy-start(f32[2,64,128,64]{2,3,1,0:T(8,128)S(1)} %get-tuple-element.68) | copy-start | bytes 12582916
  29.7 14.9 %collective-permute-start.1 = (bf16[32,128,64]{1,2,0:T(8,128)(2,1)S(1)}, bf16[32,128,64]{1,2,0:T(8,128)(2,1)S(1)}, u32[]{:S(2)}, u32[]{:S(2)}) collective-permute-start(bf16[32,128,64]{1,2,0:T(8,128)(2,1)S(1)} %get-tuple-element.26), channel_id=1, source_target_pairs={{0,4},{4,0},{8,12},{12,8},{16,20},{20,16},{24,28},{28,24},{1,5},{5... | collective-permute-start | bytes 1572872 | tf_op jit(solution)/shard_map/ppermute | solution.py:18
  31.3 3.6 %collective-permute-start.10 = (f32[32]{0:T(128)S(1)}, f32[32]{0:T(128)S(1)}, u32[]{:S(2)}, u32[]{:S(2)}) collective-permute-start(f32[32]{0:T(128)S(1)} %get-tuple-element.60), channel_id=1, source_target_pairs={{0,8},{4,12},{8,0},{12,4},{16,24},{20,28},{24,16},{28,20},{1,9},{5... | collective-permute-start | bytes 392 | tf_op jit(solution)/shard_map/ppermute | solution.py:18
  32.9 3.5 %collective-permute-start.4 = (f32[32]{0:T(128)S(1)}, f32[32]{0:T(128)S(1)}, u32[]{:S(2)}, u32[]{:S(2)}) collective-permute-start(f32[32]{0:T(128)S(1)} %get-tuple-element.14), channel_id=1, source_target_pairs={{0,8},{4,12},{8,0},{12,4},{16,24},{20,28},{24,16},{28,20},{1,9},{5... | collective-permute-start | bytes 392 | tf_op jit(solution)/shard_map/ppermute | solution.py:18
  37.0 21.3 %collective-permute-start.7 = (bf16[32,128,64]{1,2,0:T(8,128)(2,1)}, bf16[32,128,64]{1,2,0:T(8,128)(2,1)S(1)}, u32[]{:S(2)}, u32[]{:S(2)}) collective-permute-start(bf16[32,128,64]{1,2,0:T(8,128)(2,1)} %get-tuple-element.27), channel_id=1, source_target_pairs={{0,4},{4,0},{8,12},{12,8},{16,20},{20,16},{24,28},{28,24},{1,5},{5... | collective-permute-start | bytes 1572872 | tf_op jit(solution)/shard_map/ppermute | solution.py:18
  45.7 12.5 %collective-permute-start.3 = (bf16[32,128,64]{1,2,0:T(8,128)(2,1)}, bf16[32,128,64]{1,2,0:T(8,128)(2,1)}, u32[]{:S(2)}, u32[]{:S(2)}) collective-permute-start(bf16[32,128,64]{1,2,0:T(8,128)(2,1)} %fusion.74), channel_id=1, source_target_pairs={{0,8},{4,12},{8,0},{12,4},{16,24},{20,28},{24,16},{28,20},{1,9},{5... | collective-permute-start | bytes 1572872 | tf_op jit(solution)/shard_map/ppermute | solution.py:18
  60.6 9.6 %collective-permute-start.9 = (bf16[32,128,64]{1,2,0:T(8,128)(2,1)S(1)}, bf16[32,128,64]{1,2,0:T(8,128)(2,1)S(1)}, u32[]{:S(2)}, u32[]{:S(2)}) collective-permute-start(bf16[32,128,64]{1,2,0:T(8,128)(2,1)S(1)} %get-tuple-element.25), channel_id=1, source_target_pairs={{0,8},{4,12},{8,0},{12,4},{16,24},{20,28},{24,16},{28,20},{1,9},{5... | collective-permute-start | bytes 1572872 | tf_op jit(solution)/shard_map/ppermute | solution.py:18
  61.1 9.1 %copy-start.12 = (f32[32]{0:T(128)S(1)}, f32[32]{0:T(128)}, u32[]{:S(2)}) copy-start(f32[32]{0:T(128)} %get-tuple-element.66) | copy-start | bytes 388
  64.9 8.5 %collective-permute-start.5 = (bf16[32,128,64]{1,2,0:T(8,128)(2,1)S(1)}, bf16[32,128,64]{1,2,0:T(8,128)(2,1)S(1)}, u32[]{:S(2)}, u32[]{:S(2)}) collective-permute-start(bf16[32,128,64]{1,2,0:T(8,128)(2,1)S(1)} %get-tuple-element.24), channel_id=1, source_target_pairs={{8,16},{12,20},{9,17},{13,21},{10,18},{14,22},{11,19},{15,23}} | collective-permute-start | bytes 1572872 | tf_op jit(solution)/shard_map/ppermute | solution.py:100
  71.0 4.2 %collective-permute-start.11 = (bf16[32,128,64]{1,2,0:T(8,128)(2,1)S(1)}, bf16[32,128,64]{1,2,0:T(8,128)(2,1)S(1)}, u32[]{:S(2)}, u32[]{:S(2)}) collective-permute-start(bf16[32,128,64]{1,2,0:T(8,128)(2,1)S(1)} %get-tuple-element.34), channel_id=1, source_target_pairs={{8,16},{12,20},{9,17},{13,21},{10,18},{14,22},{11,19},{15,23}} | collective-permute-start | bytes 1572872 | tf_op jit(solution)/shard_map/ppermute | solution.py:100
  73.4 3.8 %copy-start.10 = (f32[32]{0:T(128)S(1)}, f32[32]{0:T(128)}, u32[]{:S(2)}) copy-start(f32[32]{0:T(128)} %get-tuple-element.65) | copy-start | bytes 388
  73.4 3.6 %collective-permute-start.6 = (bf16[32,128,64]{1,2,0:T(8,128)(2,1)S(1)}, bf16[32,128,64]{1,2,0:T(8,128)(2,1)S(1)}, u32[]{:S(2)}, u32[]{:S(2)}) collective-permute-start(bf16[32,128,64]{1,2,0:T(8,128)(2,1)S(1)} %collective-permute-done.5), channel_id=1, source_target_pairs={{16,24},{20,28},{17,25},{21,29},{18,26},{22,30},{19,27},{23,31}} | collective-permute-start | bytes 1572872 | tf_op jit(solution)/shard_map/ppermute | solution.py:101
  75.2 1.9 %collective-permute-start.12 = (bf16[32,128,64]{1,2,0:T(8,128)(2,1)S(1)}, bf16[32,128,64]{1,2,0:T(8,128)(2,1)S(1)}, u32[]{:S(2)}, u32[]{:S(2)}) collective-permute-start(bf16[32,128,64]{1,2,0:T(8,128)(2,1)S(1)} %collective-permute-done.11), channel_id=1, source_target_pairs={{16,24},{20,28},{17,25},{21,29},{18,26},{22,30},{19,27},{23,31}} | collective-permute-start | bytes 1572872 | tf_op jit(solution)/shard_map/ppermute | solution.py:101
  85.8 4.8 %copy-start.23 = (f32[11]{0:T(128)S(1)}, f32[11]{0:T(128)}, u32[]{:S(2)}) copy-start(f32[11]{0:T(128)} %pad.4.clone) | copy-start | bytes 136
  85.8 4.8 %copy-start.24 = (f32[2,1,64]{2,1,0:T(1,128)S(1)}, f32[2,1,64]{2,1,0:T(1,128)}, u32[]{:S(2)}) copy-start(f32[2,1,64]{2,1,0:T(1,128)} %fusion.59) | copy-start | bytes 1540
  85.8 68.3 %copy-start.3 = (bf16[2,64,64,64]{1,3,2,0:T(8,128)(2,1)S(1)}, bf16[2,64,64,64]{1,3,2,0:T(8,128)(2,1)}, u32[]{:S(2)}) copy-start(bf16[2,64,64,64]{1,3,2,0:T(8,128)(2,1)} %copy.46) | copy-start | bytes 3145732
  85.9 68.3 %copy-start.17 = (f32[2,64]{1,0:T(2,128)S(1)}, f32[2,64]{1,0:T(2,128)}, u32[]{:S(2)}) copy-start(f32[2,64]{1,0:T(2,128)} %broadcast_multiply_fusion) | copy-start | bytes 1540
  85.9 68.3 %copy-start.22 = (f32[64]{0:T(128)S(1)}, f32[64]{0:T(128)}, u32[]{:S(2)}) copy-start(f32[64]{0:T(128)} %param.14) | copy-start | bytes 772
  89.4 76.6 %collective-permute-start.13 = (f32[3,128]{1,0:T(4,128)S(1)}, f32[3,128]{1,0:T(4,128)S(1)}, u32[]{:S(2)}, u32[]{:S(2)}) collective-permute-start(f32[3,128]{1,0:T(4,128)S(1)} %slice.179), channel_id=1, source_target_pairs={{4,0},{8,4},{12,8},{16,12},{20,16},{24,20},{28,24},{5,1},{9,5},{13... | collective-permute-start | bytes 4616 | tf_op jit(solution)/shard_map/ppermute | solution.py:12
  154.2 5.4 %copy-start.8 = (f32[8,12,64]{2,0,1:T(8,128)S(1)}, f32[8,12,64]{2,0,1:T(8,128)}, u32[]{:S(2)}) copy-start(f32[8,12,64]{2,0,1:T(8,128)} %param.15) | copy-start | bytes 73732
  (16 other events, 39.9 us)

commit v12 on v7

--- a/solution.py
+++ b/solution.py
@@ -97,9 +97,15 @@
 def relay(value, axis, bit_pos):
     half = 2**bit_pos
     step = half // 2
-    first = lax.ppermute(value, axis, [(source, source + step) for source in range(half - step, half)])
-    second = lax.ppermute(first, axis, [(source, source + step) for source in range(half, half + step)])
-    return first + second
+    parts = 2 if value.shape[0] % 2 == 0 else 1
+    size = value.shape[0] // parts
+    received = []
+    for index in range(parts):
+        piece = value[index * size : (index + 1) * size]
+        first = lax.ppermute(piece, axis, [(source, source + step) for source in range(half - step, half)])
+        second = lax.ppermute(first, axis, [(source, source + step) for source in range(half, half + step)])
+        received.append(first + second)
+    return jnp.concatenate(received, axis=0)
 
 
 def exchange(block, block_decay, depth, myself):

time: 133 us -> 132 us (level)
  starting transfers between devices: 48 us -> 43.4 us
  waiting for transfers between devices: 16.7 us -> 19.4 us
    ppermute x11, starting transfers between devices: 39.8 us -> 32.5 us  [from_partner(): return lax.ppermute(value, axis, pairs)]
    ppermute x11, waiting for transfers between devices: 16.7 us -> 19.3 us  [from_partner(): return lax.ppermute(value, axis, pairs)]
    reshape x2, local copies, waits for them, and re-layouts: 8.43 us -> 6.6 us  [local(): grad_groups = late_cotangent.reshape(groups, group_len, heads, head_dim)]
    dot_general x6, matrix products: 14.7 us -> 13 us  [contract(): return jnp.einsum(form, left, right, preferred_element_type=jnp.float32)]
    unnamed x50 -> x70, local copies, waits for them, and re-layouts: 0.75 us -> 2.23 us
    another operation x2, local copies, waits for them, and re-layouts: 5.25 us -> 6.58 us  [local(): x_groups = x_act.reshape(groups, group_len, heads, head_dim)]
    ppermute x2 -> x4, starting transfers between devices: 1.52 us -> 2.84 us  [relay(): lax.ppermute(piece, axis, [(source, source + step) for source in range(ha...]
    ppermute x2 -> x4, starting transfers between devices: 1.57 us -> 2.88 us  [relay(): lax.ppermute(first, axis, [(source, source + step) for source in range(ha...]
  transfers between devices with their start and end apart: 17 -> 21, of which waited for: 6 -> 6; matrix products, arithmetic and copies ran while one was open for 39% -> 29% of each run, Pallas kernels for 0% -> 0%
where the time goes in v12:
time: 132 us; the launch traced here: 131 us
  starting transfers between devices  43.4 us (33%)
  local copies, waits for them, and re-layouts  30.6 us (23%)
  other arithmetic  20.9 us (16%)
  waiting for transfers between devices  19.4 us (15%)
  matrix products  15.6 us (12%)
  between operations  1.45 us (1%)
    ppermute x11, starting transfers between devices, from_partner(): return lax.ppermute(value, axis, pairs)  32.5 us
    ppermute x11, waiting for transfers between devices, from_partner(): return lax.ppermute(value, axis, pairs)  19.3 us
    dot_general x6, matrix products, contract(): return jnp.einsum(form, left, right, preferred_element_type=jnp.float32)  13 us
    reshape x2, local copies, waits for them, and re-layouts, local(): grad_groups = late_cotangent.reshape(groups, group_len, heads, head_dim)  6.6 us
    another operation x2, local copies, waits for them, and re-layouts, local(): x_groups = x_act.reshape(groups, group_len, heads, head_dim)  6.58 us
    ppermute x2, starting transfers between devices, shifted(): lax.ppermute(value, axis, [(source, source + steps) for source in range(l...  5.15 us
    another operation x1, other arithmetic  3.47 us
    convert_element_type x1, local copies, waits for them, and re-layouts, local(): ssm_out = (y_inner + y_cross + skip[None, None, :, None] * x_groups).asty...  3.31 us
  transfers between devices with their start and end apart: 21, of which 6 were waited for; matrix products, arithmetic and copies ran while one was open for 29% of the time, Pallas kernels for 0%

profile of v12, /device:TPU:0, one launch (start us, length us, event | category | flops | bytes accessed | tf_op | source)
XLA Modules:
  0.0 131.2 jit_solution(13879291612327492550)
XLA Ops:
  2.5 2.9 %collective-permute-start.2 = (f32[32]{0:T(128)S(1)}, f32[32]{0:T(128)S(1)}, u32[]{:S(2)}, u32[]{:S(2)}) collective-permute-start(f32[32]{0:T(128)S(1)} %get-tuple-element.67), channel_id=1, source_target_pairs={{0,4},{4,0},{8,12},{12,8},{16,20},{20,16},{24,28},{28,24},{1,5},{5... | collective-permute-start | bytes 392 | tf_op jit(solution)/shard_map/ppermute | solution.py:18
  6.4 3.9 %collective-permute-start = (bf16[3,4352]{1,0:T(4,128)(2,1)S(1)}, bf16[3,4352]{1,0:T(4,128)(2,1)S(1)}, u32[]{:S(2)}, u32[]{:S(2)}) collective-permute-start(bf16[3,4352]{1,0:T(4,128)(2,1)S(1)} %slice.131), channel_id=1, source_target_pairs={{0,4},{4,8},{8,12},{12,16},{16,20},{20,24},{24,28},{1,5},{5,9},{9,... | collective-permute-start | bytes 78344 | tf_op jit(solution)/shard_map/ppermute | solution.py:12
  17.3 1.6 %collective-permute-start.4 = (f32[32]{0:T(128)S(1)}, f32[32]{0:T(128)S(1)}, u32[]{:S(2)}, u32[]{:S(2)}) collective-permute-start(f32[32]{0:T(128)S(1)} %get-tuple-element.14), channel_id=1, source_target_pairs={{0,8},{4,12},{8,0},{12,4},{16,24},{20,28},{24,16},{28,20},{1,9},{5... | collective-permute-start | bytes 392 | tf_op jit(solution)/shard_map/ppermute | solution.py:18
  19.4 1.5 %collective-permute-done.4 = f32[32]{0:T(128)S(1)} collective-permute-done((f32[32]{0:T(128)S(1)}, f32[32]{0:T(128)S(1)}, u32[]{:S(2)}, u32[]{:S(2)}) %collective-permute-start.4) | collective-permute-done | bytes 160 | tf_op jit(solution)/shard_map/ppermute | solution.py:18
  23.0 3.5 %fusion.79 = (bf16[128,4352]{1,0:T(8,128)(2,1)S(1)}, f32[128,4352]{1,0:T(8,128)S(1)}) fusion(f32[4352]{0:T(1024)S(1)} %get-tuple-element.8, bf16[128,4352]{1,0:T(8,128)(2,1)} %param.9, f32[4352]{0:T(1024)S(1)} %get-tuple-element.9, bf16[3,4352]{1,0:T(4,128)(2,1)S(1)} %collective-permute-done, f32[4352]{0:T(1024)S(1)} %get-tuple-element.10, ...), kind=kLoop, calls=%fused_computation.167 | loop fusion | flops 12255232 | bytes 4569600 | tf_op jit(solution)/shard_map/convert.2
  27.1 3.3 %reshape_reshape.3 = bf16[2,64,64,64]{3,2,1,0:T(8,128)(2,1)} reshape(bf16[128,4096]{1,0:T(8,128)(2,1)S(1)} %multiply_convert_fusion.5) | data formatting | bytes 2097152 | tf_op jit(solution)/shard_map/reshape;reshape | solution.py:160
  30.4 3.3 %copy.46 = bf16[2,64,64,64]{1,3,2,0:T(8,128)(2,1)S(1)} copy(bf16[2,64,64,64]{3,2,1,0:T(8,128)(2,1)} %reshape_reshape.3) | data formatting | bytes 2097152 | tf_op jit(solution)/shard_map/reshape;reshape | solution.py:160
  36.3 1.5 %collective-permute-start.1 = (bf16[32,128,64]{1,2,0:T(8,128)(2,1)S(1)}, bf16[32,128,64]{1,2,0:T(8,128)(2,1)S(1)}, u32[]{:S(2)}, u32[]{:S(2)}) collective-permute-start(bf16[32,128,64]{1,2,0:T(8,128)(2,1)S(1)} %get-tuple-element.26), channel_id=1, source_target_pairs={{0,4},{4,0},{8,12},{12,8},{16,20},{20,16},{24,28},{28,24},{1,5},{5... | collective-permute-start | bytes 1572872 | tf_op jit(solution)/shard_map/ppermute | solution.py:18
  38.5 2.4 %slice_bitcast_fusion.4 = (f32[64,128,64]{1,2,0:T(8,128)}, f32[64,128,64]{1,2,0:T(8,128)}) fusion(f32[2,64,128,64]{2,3,1,0:T(8,128)S(1)} %get-tuple-element.72), kind=kLoop, calls=%fused_computation.26 | loop fusion | bytes 8388608 | tf_op jit(solution)/shard_map/mul | solution.py:202
  40.9 10.3 %collective-permute-done.1 = bf16[32,128,64]{1,2,0:T(8,128)(2,1)S(1)} collective-permute-done((bf16[32,128,64]{1,2,0:T(8,128)(2,1)S(1)}, bf16[32,128,64]{1,2,0:T(8,128)(2,1)S(1)}, u32[]{:S(2)}, u32[]{:S(2)}) %collective-permute-start.1) | collective-permute-done | bytes 524320 | tf_op jit(solution)/shard_map/ppermute | solution.py:18
  53.0 3.3 %reshape.194 = bf16[2,64,64,64]{3,2,1,0:T(8,128)(2,1)} reshape(bf16[128,4096]{1,0:T(8,128)(2,1)S(1)} %copy-done.11) | data formatting | bytes 2097152 | tf_op jit(solution)/shard_map/reshape | solution.py:182
  56.3 3.3 %copy.55 = bf16[2,64,64,64]{1,3,2,0:T(8,128)(2,1)S(1)} copy(bf16[2,64,64,64]{3,2,1,0:T(8,128)(2,1)} %reshape.194) | data formatting | bytes 2097152 | tf_op jit(solution)/shard_map/reshape | solution.py:182
  62.0 3.8 %multiply_reduce_fusion.2 = (f32[2,64]{1,0:T(2,128)S(1)}, f32[2,64,64]{2,1,0:T(8,128)S(1)}) fusion(f32[2,64,64]{2,1,0:T(8,128)S(1)} %fusion.87, f32[2,64,64]{2,1,0:T(8,128)S(1)} %copy.44, pred[64,64]{1,0:T(8,128)(4,1)S(1)} %iota_compare_fusion, f32[2,64]{1,0:T(2,128)S(1)} %copy-done.27, bf16[2,64,64,64]{1,3,2,0:T(8,128)(2,1)S(1)} %copy.55, ...), kind=kOutput, calls=%fused_computation.10 | convolution fusion | flops 72343424 | bytes 2200576 | tf_op jit(solution)/shard_map/vmap(thp,shp->hts)/dot_general | solution.py:35
  65.8 2.3 %fusion.30 = (bf16[32,128,64]{1,2,0:T(8,128)(2,1)S(1)}, bf16[32,128,64]{1,2,0:T(8,128)(2,1)S(1)}, f32[1,32,128,64]{2,3,1,0:T(8,128)S(1)}, f32[1,32,128,64]{2,3,1,0:T(8,128)S(1)}, f32[1,32,128,64]{2,3,1,0:T(8,128)S(1)}) fusion(bf16[32,128,64]{1,2,0:T(8,128)(2,1)} %collective-permute-done.3, f32[32]{0:T(128)S(1)} %copy-done.21, f32[]{:T(128)S(6)} %sub.97, ...), kind=kLoop, calls=%fused_computation.67 | loop fusion | flops 7602176 | bytes 7865232 | tf_op jit(solution)/shard_map/convert_element_type | solution.py:120
  69.6 5.1 %collective-permute-start.11 = (bf16[32,128,64]{1,2,0:T(8,128)(2,1)S(1)}, bf16[32,128,64]{1,2,0:T(8,128)(2,1)S(1)}, u32[]{:S(2)}, u32[]{:S(2)}) collective-permute-start(bf16[32,128,64]{1,2,0:T(8,128)(2,1)S(1)} %get-tuple-element.25), channel_id=1, source_target_pairs={{0,8},{4,12},{8,0},{12,4},{16,24},{20,28},{24,16},{28,20},{1,9},{5... | collective-permute-start | bytes 1572872 | tf_op jit(solution)/shard_map/ppermute | solution.py:18
  77.9 3.9 %collective-permute-done.11 = bf16[32,128,64]{1,2,0:T(8,128)(2,1)S(1)} collective-permute-done((bf16[32,128,64]{1,2,0:T(8,128)(2,1)S(1)}, bf16[32,128,64]{1,2,0:T(8,128)(2,1)S(1)}, u32[]{:S(2)}, u32[]{:S(2)}) %collective-permute-start.11) | collective-permute-done | bytes 524320 | tf_op jit(solution)/shard_map/ppermute | solution.py:18
  91.1 1.7 %add_convert_fusion = bf16[2,64,128,64]{2,3,1,0:T(8,128)(2,1)S(1)} fusion(f32[64,128,64]{1,2,0:T(8,128)S(1)} %get-tuple-element.20, f32[2,64]{1,0:T(2,128)S(1)} %get-tuple-element.49, f32[64,128,64]{1,2,0:T(8,128)S(1)} %get-tuple-element.21, f32[2,64]{1,0:T(2,128)S(1)} %get-tuple-element.50, f32[64,128,64]{1,2,0:T(8,128)S(1)} %get-tuple-element.19, ...), kind=kLoop, calls=%fused_computation.13 | loop fusion | flops 10485760 | bytes 12585472 | tf_op jit(solution)/shard_map/convert_element_type | solution.py:204
  92.8 2.0 %fusion.3 = f32[2,64,128]{2,1,0:T(8,128)S(1)} fusion(bf16[2,64,64,64]{1,3,2,0:T(8,128)(2,1)S(1)} %copy-done.8, bf16[2,64,128,64]{2,3,1,0:T(8,128)(2,1)S(1)} %add_convert_fusion, f32[2,64,64]{1,2,0:T(8,128)S(1)} %copy.50), kind=kOutput, calls=%fused_computation.9 | convolution fusion | flops 136298496 | bytes 3244032 | tf_op jit(solution)/shard_map/chnp,cthp->cthn/dot_general | solution.py:35
  94.9 1.5 %fusion.6 = f32[2,64,64,64]{3,2,1,0:T(8,128)S(1)} fusion(bf16[2,64,128,64]{2,3,1,0:T(8,128)(2,1)S(1)} %add_convert_fusion, f32[2,64,64]{1,2,0:T(8,128)S(1)} %copy.50, f32[2,64,128]{2,1,0:T(8,128)S(1)} %convert_element_type.135), kind=kOutput, calls=%fused_computation.19 | convolution fusion | flops 136314880 | bytes 4292608 | tf_op jit(solution)/shard_map/cthn,chnp->cthp/dot_general | solution.py:35
  100.9 9.0 %collective-permute-start.19 = (f32[8,12,64]{2,0,1:T(8,128)S(1)}, f32[8,12,64]{2,0,1:T(8,128)S(1)}, u32[]{:S(2)}, u32[]{:S(2)}) collective-permute-start(f32[8,12,64]{2,0,1:T(8,128)S(1)} %fusion.73), channel_id=1, source_target_pairs={{0,8},{4,12},{8,0},{12,4},{16,24},{20,28},{24,16},{28,20},{1,9},{5... | collective-permute-start | bytes 73736 | tf_op jit(solution)/shard_map/ppermute | solution.py:18
  109.9 3.5 %fusion.2 = bf16[2,64,64,64]{1,3,2,0:T(8,128)(2,1)} fusion(bf16[2,64,64,64]{1,3,2,0:T(8,128)(2,1)S(1)} %copy-done.6, f32[2,64,64,64]{3,2,1,0:T(8,128)S(1)} %fusion.6, f32[64]{0:T(128)S(1)} %copy-done.31, f32[2,64]{1,0:T(2,128)S(1)} %copy-done.26, f32[2,64,64]{2,1,0:T(8,128)S(1)} %fusion.87, f32[2,64,64]{2,1,0:T(8,128)S(1)} %copy.44, ...), kind=kOutput, calls=%fused_computation.7 | convolution fusion | flops 72876032 | bytes 4264704 | tf_op jit(solution)/shard_map/vmap(hts,shp->thp)/dot_general | solution.py:35
  113.4 3.3 %copy.51 = bf16[2,64,64,64]{3,2,1,0:T(8,128)(2,1)S(1)} copy(bf16[2,64,64,64]{1,3,2,0:T(8,128)(2,1)} %fusion.2) | data formatting | bytes 2097152 | tf_op jit(solution)/shard_map/convert_element_type | solution.py:225
  116.8 2.5 %reshape.193 = bf16[128,4096]{1,0:T(8,128)(2,1)} reshape(bf16[2,64,64,64]{3,2,1,0:T(8,128)(2,1)S(1)} %copy.51) | data formatting | bytes 2097152 | tf_op jit(solution)/shard_map/reshape | solution.py:226
  119.3 9.2 %collective-permute-start.20 = (f32[8,12,64]{2,0,1:T(8,128)S(1)}, f32[8,12,64]{2,0,1:T(8,128)S(1)}, u32[]{:S(2)}, u32[]{:S(2)}) collective-permute-start(f32[8,12,64]{2,0,1:T(8,128)S(1)} %add.178), channel_id=1, source_target_pairs={{0,16},{4,20},{8,24},{12,28},{16,0},{20,4},{24,8},{28,12},{1,17},{... | collective-permute-start | bytes 73736 | tf_op jit(solution)/shard_map/ppermute | solution.py:18
  (164 shorter events, 41.2 us)
Async XLA Ops:
  2.5 14.2 %collective-permute-start.2 = (f32[32]{0:T(128)S(1)}, f32[32]{0:T(128)S(1)}, u32[]{:S(2)}, u32[]{:S(2)}) collective-permute-start(f32[32]{0:T(128)S(1)} %get-tuple-element.67), channel_id=1, source_target_pairs={{0,4},{4,0},{8,12},{12,8},{16,20},{20,16},{24,28},{28,24},{1,5},{5... | collective-permute-start | bytes 392 | tf_op jit(solution)/shard_map/ppermute | solution.py:18
  5.4 11.2 %collective-permute-start.10 = (f32[32]{0:T(128)S(1)}, f32[32]{0:T(128)S(1)}, u32[]{:S(2)}, u32[]{:S(2)}) collective-permute-start(f32[32]{0:T(128)S(1)} %get-tuple-element.68), channel_id=1, source_target_pairs={{0,4},{4,0},{8,12},{12,8},{16,20},{20,16},{24,28},{28,24},{1,5},{5... | collective-permute-start | bytes 392 | tf_op jit(solution)/shard_map/ppermute | solution.py:18
  6.4 16.7 %collective-permute-start = (bf16[3,4352]{1,0:T(4,128)(2,1)S(1)}, bf16[3,4352]{1,0:T(4,128)(2,1)S(1)}, u32[]{:S(2)}, u32[]{:S(2)}) collective-permute-start(bf16[3,4352]{1,0:T(4,128)(2,1)S(1)} %slice.131), channel_id=1, source_target_pairs={{0,4},{4,8},{8,12},{12,16},{16,20},{20,24},{24,28},{1,5},{5,9},{9,... | collective-permute-start | bytes 78344 | tf_op jit(solution)/shard_map/ppermute | solution.py:12
  17.3 3.5 %collective-permute-start.4 = (f32[32]{0:T(128)S(1)}, f32[32]{0:T(128)S(1)}, u32[]{:S(2)}, u32[]{:S(2)}) collective-permute-start(f32[32]{0:T(128)S(1)} %get-tuple-element.14), channel_id=1, source_target_pairs={{0,8},{4,12},{8,0},{12,4},{16,24},{20,28},{24,16},{28,20},{1,9},{5... | collective-permute-start | bytes 392 | tf_op jit(solution)/shard_map/ppermute | solution.py:18
  18.9 3.5 %collective-permute-start.12 = (f32[32]{0:T(128)S(1)}, f32[32]{0:T(128)S(1)}, u32[]{:S(2)}, u32[]{:S(2)}) collective-permute-start(f32[32]{0:T(128)S(1)} %get-tuple-element.64), channel_id=1, source_target_pairs={{0,8},{4,12},{8,0},{12,4},{16,24},{20,28},{24,16},{28,20},{1,9},{5... | collective-permute-start | bytes 392 | tf_op jit(solution)/shard_map/ppermute | solution.py:18
  35.1 16.1 %copy-start.2 = (f32[64,128,64]{1,2,0:T(8,128)}, f32[64,128,64]{1,2,0:T(8,128)S(1)}, u32[]{:S(2)}) copy-start(f32[64,128,64]{1,2,0:T(8,128)S(1)} %get-tuple-element.71) | copy-start | bytes 6291460
  36.3 14.9 %collective-permute-start.1 = (bf16[32,128,64]{1,2,0:T(8,128)(2,1)S(1)}, bf16[32,128,64]{1,2,0:T(8,128)(2,1)S(1)}, u32[]{:S(2)}, u32[]{:S(2)}) collective-permute-start(bf16[32,128,64]{1,2,0:T(8,128)(2,1)S(1)} %get-tuple-element.26), channel_id=1, source_target_pairs={{0,4},{4,0},{8,12},{12,8},{16,20},{20,16},{24,28},{28,24},{1,5},{5... | collective-permute-start | bytes 1572872 | tf_op jit(solution)/shard_map/ppermute | solution.py:18
  37.8 27.9 %collective-permute-start.9 = (bf16[32,128,64]{1,2,0:T(8,128)(2,1)}, bf16[32,128,64]{1,2,0:T(8,128)(2,1)S(1)}, u32[]{:S(2)}, u32[]{:S(2)}) collective-permute-start(bf16[32,128,64]{1,2,0:T(8,128)(2,1)} %get-tuple-element.27), channel_id=1, source_target_pairs={{0,4},{4,0},{8,12},{12,8},{16,20},{20,16},{24,28},{28,24},{1,5},{5... | collective-permute-start | bytes 1572872 | tf_op jit(solution)/shard_map/ppermute | solution.py:18
  52.4 13.4 %collective-permute-start.3 = (bf16[32,128,64]{1,2,0:T(8,128)(2,1)}, bf16[32,128,64]{1,2,0:T(8,128)(2,1)}, u32[]{:S(2)}, u32[]{:S(2)}) collective-permute-start(bf16[32,128,64]{1,2,0:T(8,128)(2,1)} %fusion.75), channel_id=1, source_target_pairs={{0,8},{4,12},{8,0},{12,4},{16,24},{20,28},{24,16},{28,20},{1,9},{5... | collective-permute-start | bytes 1572872 | tf_op jit(solution)/shard_map/ppermute | solution.py:18
  68.2 8.2 %collective-permute-start.5 = (bf16[16,128,64]{1,2,0:T(8,128)(2,1)S(1)}, bf16[16,128,64]{1,2,0:T(8,128)(2,1)S(1)}, u32[]{:S(2)}, u32[]{:S(2)}) collective-permute-start(bf16[16,128,64]{1,2,0:T(8,128)(2,1)S(1)} %get-tuple-element.33), channel_id=1, source_target_pairs={{8,16},{12,20},{9,17},{13,21},{10,18},{14,22},{11,19},{15,23}} | collective-permute-start | bytes 786440 | tf_op jit(solution)/shard_map/ppermute | solution.py:105
  68.8 8.2 %collective-permute-start.7 = (bf16[16,128,64]{1,2,0:T(8,128)(2,1)S(1)}, bf16[16,128,64]{1,2,0:T(8,128)(2,1)S(1)}, u32[]{:S(2)}, u32[]{:S(2)}) collective-permute-start(bf16[16,128,64]{1,2,0:T(8,128)(2,1)S(1)} %get-tuple-element.34), channel_id=1, source_target_pairs={{8,16},{12,20},{9,17},{13,21},{10,18},{14,22},{11,19},{15,23}} | collective-permute-start | bytes 786440 | tf_op jit(solution)/shard_map/ppermute | solution.py:105
  69.6 12.2 %collective-permute-start.11 = (bf16[32,128,64]{1,2,0:T(8,128)(2,1)S(1)}, bf16[32,128,64]{1,2,0:T(8,128)(2,1)S(1)}, u32[]{:S(2)}, u32[]{:S(2)}) collective-permute-start(bf16[32,128,64]{1,2,0:T(8,128)(2,1)S(1)} %get-tuple-element.25), channel_id=1, source_target_pairs={{0,8},{4,12},{8,0},{12,4},{16,24},{20,28},{24,16},{28,20},{1,9},{5... | collective-permute-start | bytes 1572872 | tf_op jit(solution)/shard_map/ppermute | solution.py:18
  76.4 8.0 %collective-permute-start.6 = (bf16[16,128,64]{1,2,0:T(8,128)(2,1)S(1)}, bf16[16,128,64]{1,2,0:T(8,128)(2,1)S(1)}, u32[]{:S(2)}, u32[]{:S(2)}) collective-permute-start(bf16[16,128,64]{1,2,0:T(8,128)(2,1)S(1)} %collective-permute-done.5), channel_id=1, source_target_pairs={{16,24},{20,28},{17,25},{21,29},{18,26},{22,30},{19,27},{23,31}} | collective-permute-start | bytes 786440 | tf_op jit(solution)/shard_map/ppermute | solution.py:106
  77.1 8.1 %collective-permute-start.8 = (bf16[16,128,64]{1,2,0:T(8,128)(2,1)S(1)}, bf16[16,128,64]{1,2,0:T(8,128)(2,1)S(1)}, u32[]{:S(2)}, u32[]{:S(2)}) collective-permute-start(bf16[16,128,64]{1,2,0:T(8,128)(2,1)S(1)} %collective-permute-done.7), channel_id=1, source_target_pairs={{16,24},{20,28},{17,25},{21,29},{18,26},{22,30},{19,27},{23,31}} | collective-permute-start | bytes 786440 | tf_op jit(solution)/shard_map/ppermute | solution.py:106
  82.7 1.8 %collective-permute-start.13 = (bf16[16,128,64]{1,2,0:T(8,128)(2,1)S(1)}, bf16[16,128,64]{1,2,0:T(8,128)(2,1)S(1)}, u32[]{:S(2)}, u32[]{:S(2)}) collective-permute-start(bf16[16,128,64]{1,2,0:T(8,128)(2,1)S(1)} %get-tuple-element.37), channel_id=1, source_target_pairs={{8,16},{12,20},{9,17},{13,21},{10,18},{14,22},{11,19},{15,23}} | collective-permute-start | bytes 786440 | tf_op jit(solution)/shard_map/ppermute | solution.py:105
  83.6 1.6 %collective-permute-start.15 = (bf16[16,128,64]{1,2,0:T(8,128)(2,1)S(1)}, bf16[16,128,64]{1,2,0:T(8,128)(2,1)S(1)}, u32[]{:S(2)}, u32[]{:S(2)}) collective-permute-start(bf16[16,128,64]{1,2,0:T(8,128)(2,1)S(1)} %get-tuple-element.38), channel_id=1, source_target_pairs={{8,16},{12,20},{9,17},{13,21},{10,18},{14,22},{11,19},{15,23}} | collective-permute-start | bytes 786440 | tf_op jit(solution)/shard_map/ppermute | solution.py:105
  84.5 1.6 %collective-permute-start.14 = (bf16[16,128,64]{1,2,0:T(8,128)(2,1)S(1)}, bf16[16,128,64]{1,2,0:T(8,128)(2,1)S(1)}, u32[]{:S(2)}, u32[]{:S(2)}) collective-permute-start(bf16[16,128,64]{1,2,0:T(8,128)(2,1)S(1)} %collective-permute-done.13), channel_id=1, source_target_pairs={{16,24},{20,28},{17,25},{21,29},{18,26},{22,30},{19,27},{23,31}} | collective-permute-start | bytes 786440 | tf_op jit(solution)/shard_map/ppermute | solution.py:106
  85.2 0.9 collective-permute-start.16
  94.8 15.1 %copy-start.6 = (bf16[2,64,64,64]{1,3,2,0:T(8,128)(2,1)S(1)}, bf16[2,64,64,64]{1,3,2,0:T(8,128)(2,1)}, u32[]{:S(2)}) copy-start(bf16[2,64,64,64]{1,3,2,0:T(8,128)(2,1)} %copy-done.4) | copy-start | bytes 3145732
  94.8 15.1 %copy-start.26 = (f32[2,64]{1,0:T(2,128)S(1)}, f32[2,64]{1,0:T(2,128)}, u32[]{:S(2)}) copy-start(f32[2,64]{1,0:T(2,128)} %broadcast_multiply_fusion) | copy-start | bytes 1540
  96.7 4.2 %collective-permute-start.18 = (f32[8,12,64]{2,0,1:T(8,128)S(1)}, f32[8,12,64]{2,0,1:T(8,128)S(1)}, u32[]{:S(2)}, u32[]{:S(2)}) collective-permute-start(f32[8,12,64]{2,0,1:T(8,128)S(1)} %pad_maximum_fusion.2), channel_id=1, source_target_pairs={{0,4},{4,0},{8,12},{12,8},{16,20},{20,16},{24,28},{28,24},{1,5},{5... | collective-permute-start | bytes 73736 | tf_op jit(solution)/shard_map/ppermute | solution.py:18
  98.3 30.2 %collective-permute-start.17 = (f32[3,128]{1,0:T(4,128)S(1)}, f32[3,128]{1,0:T(4,128)S(1)}, u32[]{:S(2)}, u32[]{:S(2)}) collective-permute-start(f32[3,128]{1,0:T(4,128)S(1)} %slice.199), channel_id=1, source_target_pairs={{4,0},{8,4},{12,8},{16,12},{20,16},{24,20},{28,24},{5,1},{9,5},{13... | collective-permute-start | bytes 4616 | tf_op jit(solution)/shard_map/ppermute | solution.py:12
  100.9 18.4 %collective-permute-start.19 = (f32[8,12,64]{2,0,1:T(8,128)S(1)}, f32[8,12,64]{2,0,1:T(8,128)S(1)}, u32[]{:S(2)}, u32[]{:S(2)}) collective-permute-start(f32[8,12,64]{2,0,1:T(8,128)S(1)} %fusion.73), channel_id=1, source_target_pairs={{0,8},{4,12},{8,0},{12,4},{16,24},{20,28},{24,16},{28,20},{1,9},{5... | collective-permute-start | bytes 73736 | tf_op jit(solution)/shard_map/ppermute | solution.py:18
  119.3 11.3 %collective-permute-start.20 = (f32[8,12,64]{2,0,1:T(8,128)S(1)}, f32[8,12,64]{2,0,1:T(8,128)S(1)}, u32[]{:S(2)}, u32[]{:S(2)}) collective-permute-start(f32[8,12,64]{2,0,1:T(8,128)S(1)} %add.178), channel_id=1, source_target_pairs={{0,16},{4,20},{8,24},{12,28},{16,0},{20,4},{24,8},{28,12},{1,17},{... | collective-permute-start | bytes 73736 | tf_op jit(solution)/shard_map/ppermute | solution.py:18
  (32 other events, 200.5 us)

commit v13 on v12

--- a/solution.py
+++ b/solution.py
@@ -199,14 +199,8 @@
     local_weight = exact("cds,csh->cdh", onehot, weight_rows[:, 1 : 1 + low_levels]) * fade_pairs
     lead_fade = jnp.exp(before)
     cross_weight = weight_rows[:, 1 + low_levels : 1 + low_levels + depth] * lead_fade[:, None, :]
-    terms = [local_weight[:, d, :, None, None] * states[d][None] for d in range(groups)]
-    terms += [cross_weight[:, l, :, None, None] * cross[l][None] for l in range(depth)]
-    mixed = sum(terms[1:], terms[0]).astype(jnp.bfloat16)
     scaled = jnp.exp(cumuls) / state_dim
     query_faded = (c_groups[:, :, None, :] * scaled[:, :, :, None]).astype(jnp.bfloat16)
-    y_cross = contract("cthn,chnp->cthp", query_faded, mixed)
-    backed = contract("chnp,cthp->cthn", mixed, grad_groups)
-    grad_cross = jnp.sum(backed * scaled[:, :, :, None], axis=2)
     gram = contract("cthn,cthp->chnp", query_faded, grad_groups)
     inner_pairs = jnp.sum(states[None] * gram[:, None], axis=(3, 4))
     level_local = exact("cds,cdh->csh", onehot, fade_pairs * inner_pairs)
@@ -220,6 +214,15 @@
         axis=1,
     )
     grads = exact("ck,clh->klh", picked, level_rest)
+    grad_first = exact("gk,gh->kh", picked, level_zero)
+    local_grads = jnp.concatenate([grad_first[:, None, :], grads], axis=1)
+    local_grads, states, cross = lax.optimization_barrier((local_grads, states, cross))
+    terms = [local_weight[:, d, :, None, None] * states[d][None] for d in range(groups)]
+    terms += [cross_weight[:, l, :, None, None] * cross[l][None] for l in range(depth)]
+    mixed = sum(terms[1:], terms[0]).astype(jnp.bfloat16)
+    y_cross = contract("cthn,chnp->cthp", query_faded, mixed)
+    backed = contract("chnp,cthp->cthn", mixed, grad_groups)
+    grad_cross = jnp.sum(backed * scaled[:, :, :, None], axis=2)
     ssm_out = (
         (y_inner + y_cross + skip[None, None, :, None] * x_groups)
         .astype(jnp.bfloat16)
@@ -233,8 +236,6 @@
     for offset in range(taps):
         lagged = taps - 1 - offset
         grad_c_in = grad_c_in + query_taps[offset][None, :] * extended[lagged : lagged + length]
-    grad_first = exact("gk,gh->kh", picked, level_zero)
-    local_grads = jnp.concatenate([grad_first[:, None, :], grads], axis=1)
     summed = all_sum(local_grads, "seq")
     level_update = level_table + summed / math.sqrt(length * devices)
     return (ssm_out, grad_c_in, level_update)

time: 132 us -> 141 us (1.068)
  matrix products: 15.6 us -> 22.3 us
  local copies, waits for them, and re-layouts: 30.6 us -> 25.4 us
  other arithmetic: 20.9 us -> 25.8 us
  starting transfers between devices: 43.4 us -> 45.4 us
    dot_general x6, matrix products: 13 us -> 19.8 us  [contract(): return jnp.einsum(form, left, right, preferred_element_type=jnp.float32)]
    mul x2, local copies, waits for them, and re-layouts: 0.59 us -> 3.74 us  [local(): cross_weight[:, l, :, None, None] * cross[l][None]]
    mul x2 -> x0, local copies, waits for them, and re-layouts: 2.96 us -> none  [the longest x1 2.4 us: local(): local_weight[:, d, :, None, None] * states[d][None]]
    convert_element_type x1, other arithmetic: 1.71 us -> 4.37 us  [local(): mixed = sum(terms[1:], terms[0]).astype(jnp.bfloat16)]
    reshape x2 -> x1, local copies, waits for them, and re-layouts: 6.6 us -> 4.27 us  [local(): grad_groups = late_cotangent.reshape(groups, group_len, heads, head_dim)]
    reduce_sum x1, other arithmetic: 1.29 us -> 3.59 us  [local(): jnp.sum(cross[None] * gram[:, None], axis=(3, 4))]
    unnamed x70 -> x54, local copies, waits for them, and re-layouts: 2.23 us -> 0.12 us
    ppermute x11, starting transfers between devices: 32.5 us -> 34.4 us  [from_partner(): return lax.ppermute(value, axis, pairs)]
  transfers between devices with their start and end apart: 21 -> 21, of which waited for: 6 -> 4; matrix products, arithmetic and copies ran while one was open for 29% -> 36% of each run, Pallas kernels for 0% -> 0%
where the time goes in v13:
time: 141 us; the launch traced here: 140 us
  starting transfers between devices  45.4 us (32%)
  other arithmetic  25.8 us (18%)
  local copies, waits for them, and re-layouts  25.4 us (18%)
  matrix products  22.3 us (16%)
  waiting for transfers between devices  19.5 us (14%)
    ppermute x11, starting transfers between devices, from_partner(): return lax.ppermute(value, axis, pairs)  34.4 us
    dot_general x6, matrix products, contract(): return jnp.einsum(form, left, right, preferred_element_type=jnp.float32)  19.8 us
    ppermute x11, waiting for transfers between devices, from_partner(): return lax.ppermute(value, axis, pairs)  19.5 us
    another operation x2, local copies, waits for them, and re-layouts, local(): x_groups = x_act.reshape(groups, group_len, heads, head_dim)  5.3 us
    ppermute x2, starting transfers between devices, shifted(): lax.ppermute(value, axis, [(source, source + steps) for source in range(l...  5.15 us
    convert_element_type x1, other arithmetic, local(): mixed = sum(terms[1:], terms[0]).astype(jnp.bfloat16)  4.37 us
    reshape x1, local copies, waits for them, and re-layouts, local(): grad_groups = late_cotangent.reshape(groups, group_len, heads, head_dim)  4.27 us
    mul x2, local copies, waits for them, and re-layouts, local(): cross_weight[:, l, :, None, None] * cross[l][None]  3.74 us
  transfers between devices with their start and end apart: 21, of which 4 were waited for; matrix products, arithmetic and copies ran while one was open for 36% of the time, Pallas kernels for 0%

profile of v13, /device:TPU:0, one launch (start us, length us, event | category | flops | bytes accessed | tf_op | source)
XLA Modules:
  0.0 139.9 jit_solution(7595383410793128654)
XLA Ops:
  2.5 2.9 %collective-permute-start.2 = (f32[32]{0:T(128)S(1)}, f32[32]{0:T(128)S(1)}, u32[]{:S(2)}, u32[]{:S(2)}) collective-permute-start(f32[32]{0:T(128)S(1)} %get-tuple-element.73), channel_id=1, source_target_pairs={{0,4},{4,0},{8,12},{12,8},{16,20},{20,16},{24,28},{28,24},{1,5},{5... | collective-permute-start | bytes 392 | tf_op jit(solution)/shard_map/ppermute | solution.py:18
  6.4 3.9 %collective-permute-start = (bf16[3,4352]{1,0:T(4,128)(2,1)S(1)}, bf16[3,4352]{1,0:T(4,128)(2,1)S(1)}, u32[]{:S(2)}, u32[]{:S(2)}) collective-permute-start(bf16[3,4352]{1,0:T(4,128)(2,1)S(1)} %slice.131), channel_id=1, source_target_pairs={{0,4},{4,8},{8,12},{12,16},{16,20},{20,24},{24,28},{1,5},{5,9},{9,... | collective-permute-start | bytes 78344 | tf_op jit(solution)/shard_map/ppermute | solution.py:12
  17.4 1.6 %collective-permute-start.4 = (f32[32]{0:T(128)S(1)}, f32[32]{0:T(128)S(1)}, u32[]{:S(2)}, u32[]{:S(2)}) collective-permute-start(f32[32]{0:T(128)S(1)} %get-tuple-element.20), channel_id=1, source_target_pairs={{0,8},{4,12},{8,0},{12,4},{16,24},{20,28},{24,16},{28,20},{1,9},{5... | collective-permute-start | bytes 392 | tf_op jit(solution)/shard_map/ppermute | solution.py:18
  19.5 3.4 %fusion.82 = (bf16[128,4352]{1,0:T(8,128)(2,1)S(1)}, f32[128,4352]{1,0:T(8,128)S(1)}) fusion(f32[4352]{0:T(1024)S(1)} %get-tuple-element.14, bf16[128,4352]{1,0:T(8,128)(2,1)} %param.9, f32[4352]{0:T(1024)S(1)} %get-tuple-element.15, bf16[3,4352]{1,0:T(4,128)(2,1)S(1)} %collective-permute-done, f32[4352]{0:T(1024)S(1)} %get-tuple-element.16, ...), kind=kLoop, calls=%fused_computation.170 | loop fusion | flops 12255232 | bytes 4569600 | tf_op jit(solution)/shard_map/convert.2
  23.4 2.3 %reshape_reshape.3 = bf16[2,64,64,64]{3,2,1,0:T(8,128)(2,1)S(1)} reshape(bf16[128,4096]{1,0:T(8,128)(2,1)S(1)} %multiply_convert_fusion.5) | data formatting | bytes 2097152 | tf_op jit(solution)/shard_map/reshape;reshape | solution.py:160
  25.7 3.0 %copy.46 = bf16[2,64,64,64]{1,3,2,0:T(8,128)(2,1)} copy(bf16[2,64,64,64]{3,2,1,0:T(8,128)(2,1)S(1)} %reshape_reshape.3) | data formatting | bytes 2097152 | tf_op jit(solution)/shard_map/reshape;reshape | solution.py:160
  28.8 4.4 %multiply_reduce_fusion.4 = (f32[64,128,64]{1,2,0:T(8,128)S(1)}, f32[2,64,128,64]{2,3,1,0:T(8,128)}) fusion(f32[2,64]{1,0:T(2,128)S(1)} %get-tuple-element.62, bf16[2,64,128,1]{2,1,3,0:T(8,128)(2,1)S(1)} %bitcast.96, bf16[2,64,64,64]{1,3,2,0:T(8,128)(2,1)} %copy.46, f32[2,64,64]{1,2,0:T(8,128)S(1)} %copy.49), kind=kOutput, calls=%fused_computation.14 | convolution fusion | flops 137363456 | bytes 7406080 | tf_op jit(solution)/shard_map/vmap(sn,shp->hnp)/dot_general | solution.py:35
  37.6 11.5 %collective-permute-done.1 = bf16[32,128,64]{1,2,0:T(8,128)(2,1)S(1)} collective-permute-done((bf16[32,128,64]{1,2,0:T(8,128)(2,1)S(1)}, bf16[32,128,64]{1,2,0:T(8,128)(2,1)S(1)}, u32[]{:S(2)}, u32[]{:S(2)}) %collective-permute-start.1) | collective-permute-done | bytes 524320 | tf_op jit(solution)/shard_map/ppermute | solution.py:18
  51.8 4.3 %reshape.193 = bf16[2,64,64,64]{3,2,1,0:T(8,128)(2,1)} reshape(bf16[128,4096]{1,0:T(8,128)(2,1)} %param.17) | data formatting | bytes 2097152 | tf_op jit(solution)/shard_map/reshape | solution.py:182
  56.1 5.5 %multiply_reduce_fusion.2 = (f32[2,64,64]{2,1,0:T(8,128)S(1)}, f32[2,64]{1,0:T(2,128)S(1)}) fusion(f32[2,64]{1,0:T(2,128)} %get-tuple-element.53, f32[2,64,64]{2,1,0:T(8,128)S(1)} %copy.44, pred[64,64]{1,0:T(8,128)(4,1)S(1)} %iota_compare_fusion, f32[2,64,64]{2,1,0:T(8,128)S(1)} %fusion.90, bf16[2,64,64,64]{1,3,2,0:T(8,128)(2,1)} %copy.46, ...), kind=kOutput, calls=%fused_computation.10 | convolution fusion | flops 72343424 | bytes 2200576 | tf_op jit(solution)/shard_map/vmap(thp,shp->hts)/dot_general | solution.py:35
  61.6 2.8 %fusion.6 = f32[2,64,128,64]{2,3,1,0:T(8,128)S(1)} fusion(f32[2,64,64]{1,2,0:T(8,128)S(1)} %copy.52, f32[2,64,128]{2,1,0:T(8,128)S(1)} %convert_element_type.120, bf16[2,64,64,64]{3,2,1,0:T(8,128)(2,1)S(1)} %copy-done.3), kind=kOutput, calls=%fused_computation.19 | convolution fusion | flops 136314880 | bytes 5341184 | tf_op jit(solution)/shard_map/cthn,cthp->chnp/dot_general | solution.py:35
  64.5 2.7 %fusion.34 = (bf16[32,128,64]{1,2,0:T(8,128)(2,1)S(1)}, bf16[32,128,64]{1,2,0:T(8,128)(2,1)S(1)}, f32[1,32,128,64]{2,3,1,0:T(8,128)S(1)}, f32[1,32,128,64]{2,3,1,0:T(8,128)S(1)}, f32[1,32,128,64]{2,3,1,0:T(8,128)S(1)}) fusion(bf16[32,128,64]{1,2,0:T(8,128)(2,1)} %collective-permute-done.3, f32[32]{0:T(128)S(1)} %copy-done.14, f32[]{:T(128)S(6)} %sub.97, ...), kind=kLoop, calls=%fused_computation.71 | loop fusion | flops 7602176 | bytes 7865232 | tf_op jit(solution)/shard_map/convert_element_type | solution.py:120
  68.9 5.1 %collective-permute-start.11 = (bf16[32,128,64]{1,2,0:T(8,128)(2,1)S(1)}, bf16[32,128,64]{1,2,0:T(8,128)(2,1)S(1)}, u32[]{:S(2)}, u32[]{:S(2)}) collective-permute-start(bf16[32,128,64]{1,2,0:T(8,128)(2,1)S(1)} %get-tuple-element.31), channel_id=1, source_target_pairs={{0,8},{4,12},{8,0},{12,4},{16,24},{20,28},{24,16},{28,20},{1,9},{5... | collective-permute-start | bytes 1572872 | tf_op jit(solution)/shard_map/ppermute | solution.py:18
  77.1 4.0 %collective-permute-done.11 = bf16[32,128,64]{1,2,0:T(8,128)(2,1)S(1)} collective-permute-done((bf16[32,128,64]{1,2,0:T(8,128)(2,1)S(1)}, bf16[32,128,64]{1,2,0:T(8,128)(2,1)S(1)}, u32[]{:S(2)}, u32[]{:S(2)}) %collective-permute-start.11) | collective-permute-done | bytes 524320 | tf_op jit(solution)/shard_map/ppermute | solution.py:18
  86.9 3.6 %multiply_reduce_fusion = f32[2,3,64]{2,1,0:T(4,128)S(1)} fusion(f32[2,64,128,64]{2,3,1,0:T(8,128)} %copy-done.1, f32[3,64,128,64]{2,3,1,0:T(8,128)S(1)} %maximum_maximum_fusion), kind=kLoop, calls=%fused_computation | loop fusion | flops 6291072 | bytes 10487296 | tf_op jit(solution)/shard_map/reduce_sum | solution.py:207
  91.5 3.7 %slice_bitcast_fusion.2 = (f32[64,128,64]{1,2,0:T(8,128)S(1)}, f32[64,128,64]{1,2,0:T(8,128)}, f32[64,128,64]{1,2,0:T(8,128)}, f32[64,128,64]{1,2,0:T(8,128)}, f32[64,128,64]{1,2,0:T(8,128)}) fusion(f32[3,64,128,64]{2,3,1,0:T(8,128)S(1)} %maximum_maximum_fusion, f32[2,64,128,64]{2,3,1,0:T(8,128)S(1)} %copy-done), kind=kLoop, calls=%fused_computation.24 | loop fusion | bytes 20971520 | tf_op jit(solution)/shard_map/mul | solution.py:221
  95.2 4.4 %add_convert_fusion = bf16[2,64,128,64]{2,3,1,0:T(8,128)(2,1)S(1)} fusion(f32[64,128,64]{1,2,0:T(8,128)} %get-tuple-element.26, f32[2,64]{1,0:T(2,128)S(1)} %get-tuple-element.55, f32[64,128,64]{1,2,0:T(8,128)} %get-tuple-element.27, f32[2,64]{1,0:T(2,128)S(1)} %get-tuple-element.56, f32[64,128,64]{1,2,0:T(8,128)S(1)} %get-tuple-element.25, ...), kind=kLoop, calls=%fused_computation.11 | loop fusion | flops 10485760 | bytes 12585472 | tf_op jit(solution)/shard_map/convert_element_type | solution.py:222
  99.6 2.0 %fusion.3 = f32[2,64,128]{2,1,0:T(8,128)S(1)} fusion(bf16[2,64,128,64]{2,3,1,0:T(8,128)(2,1)S(1)} %add_convert_fusion, f32[2,64,64]{1,2,0:T(8,128)S(1)} %copy.52, bf16[2,64,64,64]{3,2,1,0:T(8,128)(2,1)S(1)} %copy-done.4), kind=kOutput, calls=%fused_computation.9 | convolution fusion | flops 136298496 | bytes 3244032 | tf_op jit(solution)/shard_map/chnp,cthp->cthn/dot_general | solution.py:35
  104.6 2.6 %collective-permute-done.18 = f32[8,12,64]{2,0,1:T(8,128)S(1)} collective-permute-done((f32[8,12,64]{2,0,1:T(8,128)S(1)}, f32[8,12,64]{2,0,1:T(8,128)S(1)}, u32[]{:S(2)}, u32[]{:S(2)}) %collective-permute-start.18) | collective-permute-done | bytes 24608 | tf_op jit(solution)/shard_map/ppermute | solution.py:18
  107.3 10.2 %collective-permute-start.19 = (f32[8,12,64]{2,0,1:T(8,128)S(1)}, f32[8,12,64]{2,0,1:T(8,128)S(1)}, u32[]{:S(2)}, u32[]{:S(2)}) collective-permute-start(f32[8,12,64]{2,0,1:T(8,128)S(1)} %add.177), channel_id=1, source_target_pairs={{0,8},{4,12},{8,0},{12,4},{16,24},{20,28},{24,16},{28,20},{1,9},{5... | collective-permute-start | bytes 73736 | tf_op jit(solution)/shard_map/ppermute | solution.py:18
  117.5 3.5 %fusion.2 = bf16[2,64,64,64]{1,3,2,0:T(8,128)(2,1)} fusion(bf16[2,64,64,64]{1,3,2,0:T(8,128)(2,1)S(1)} %copy-done.2, f32[2,64,64,64]{3,2,1,0:T(8,128)S(1)} %fusion.5, f32[64]{0:T(128)S(1)} %copy-done.23, f32[2,64]{1,0:T(2,128)S(1)} %copy-done.19, f32[2,64,64]{2,1,0:T(8,128)S(1)} %fusion.90, f32[2,64,64]{2,1,0:T(8,128)S(1)} %copy.44, ...), kind=kOutput, calls=%fused_computation.7 | convolution fusion | flops 72876032 | bytes 4264704 | tf_op jit(solution)/shard_map/vmap(hts,shp->thp)/dot_general | solution.py:35
  121.0 3.3 %copy.55 = bf16[2,64,64,64]{3,2,1,0:T(8,128)(2,1)S(1)} copy(bf16[2,64,64,64]{1,3,2,0:T(8,128)(2,1)} %fusion.2) | data formatting | bytes 2097152 | tf_op jit(solution)/shard_map/convert_element_type | solution.py:228
  124.3 2.5 %reshape.194 = bf16[128,4096]{1,0:T(8,128)(2,1)} reshape(bf16[2,64,64,64]{3,2,1,0:T(8,128)(2,1)S(1)} %copy.55) | data formatting | bytes 2097152 | tf_op jit(solution)/shard_map/reshape | solution.py:229
  126.8 10.4 %collective-permute-start.20 = (f32[8,12,64]{2,0,1:T(8,128)S(1)}, f32[8,12,64]{2,0,1:T(8,128)S(1)}, u32[]{:S(2)}, u32[]{:S(2)}) collective-permute-start(f32[8,12,64]{2,0,1:T(8,128)S(1)} %add.178), channel_id=1, source_target_pairs={{0,16},{4,20},{8,24},{12,28},{16,0},{20,4},{24,8},{28,12},{1,17},{... | collective-permute-start | bytes 73736 | tf_op jit(solution)/shard_map/ppermute | solution.py:18
  (147 shorter events, 35.1 us)
Async XLA Ops:
  2.5 14.3 %collective-permute-start.2 = (f32[32]{0:T(128)S(1)}, f32[32]{0:T(128)S(1)}, u32[]{:S(2)}, u32[]{:S(2)}) collective-permute-start(f32[32]{0:T(128)S(1)} %get-tuple-element.73), channel_id=1, source_target_pairs={{0,4},{4,0},{8,12},{12,8},{16,20},{20,16},{24,28},{28,24},{1,5},{5... | collective-permute-start | bytes 392 | tf_op jit(solution)/shard_map/ppermute | solution.py:18
  5.4 11.4 %collective-permute-start.10 = (f32[32]{0:T(128)S(1)}, f32[32]{0:T(128)S(1)}, u32[]{:S(2)}, u32[]{:S(2)}) collective-permute-start(f32[32]{0:T(128)S(1)} %get-tuple-element.74), channel_id=1, source_target_pairs={{0,4},{4,0},{8,12},{12,8},{16,20},{20,16},{24,28},{28,24},{1,5},{5... | collective-permute-start | bytes 392 | tf_op jit(solution)/shard_map/ppermute | solution.py:18
  6.4 13.1 %collective-permute-start = (bf16[3,4352]{1,0:T(4,128)(2,1)S(1)}, bf16[3,4352]{1,0:T(4,128)(2,1)S(1)}, u32[]{:S(2)}, u32[]{:S(2)}) collective-permute-start(bf16[3,4352]{1,0:T(4,128)(2,1)S(1)} %slice.131), channel_id=1, source_target_pairs={{0,4},{4,8},{8,12},{12,16},{16,20},{20,24},{24,28},{1,5},{5,9},{9,... | collective-permute-start | bytes 78344 | tf_op jit(solution)/shard_map/ppermute | solution.py:12
  17.4 18.9 %collective-permute-start.4 = (f32[32]{0:T(128)S(1)}, f32[32]{0:T(128)S(1)}, u32[]{:S(2)}, u32[]{:S(2)}) collective-permute-start(f32[32]{0:T(128)S(1)} %get-tuple-element.20), channel_id=1, source_target_pairs={{0,8},{4,12},{8,0},{12,4},{16,24},{20,28},{24,16},{28,20},{1,9},{5... | collective-permute-start | bytes 392 | tf_op jit(solution)/shard_map/ppermute | solution.py:18
  19.0 16.7 %collective-permute-start.12 = (f32[32]{0:T(128)S(1)}, f32[32]{0:T(128)S(1)}, u32[]{:S(2)}, u32[]{:S(2)}) collective-permute-start(f32[32]{0:T(128)S(1)} %get-tuple-element.70), channel_id=1, source_target_pairs={{0,8},{4,12},{8,0},{12,4},{16,24},{20,28},{24,16},{28,20},{1,9},{5... | collective-permute-start | bytes 392 | tf_op jit(solution)/shard_map/ppermute | solution.py:18
  34.2 14.9 %collective-permute-start.1 = (bf16[32,128,64]{1,2,0:T(8,128)(2,1)S(1)}, bf16[32,128,64]{1,2,0:T(8,128)(2,1)S(1)}, u32[]{:S(2)}, u32[]{:S(2)}) collective-permute-start(bf16[32,128,64]{1,2,0:T(8,128)(2,1)S(1)} %get-tuple-element.33), channel_id=1, source_target_pairs={{0,4},{4,0},{8,12},{12,8},{16,20},{20,16},{24,28},{28,24},{1,5},{5... | collective-permute-start | bytes 1572872 | tf_op jit(solution)/shard_map/ppermute | solution.py:18
  36.9 27.5 %collective-permute-start.9 = (bf16[32,128,64]{1,2,0:T(8,128)(2,1)}, bf16[32,128,64]{1,2,0:T(8,128)(2,1)S(1)}, u32[]{:S(2)}, u32[]{:S(2)}) collective-permute-start(bf16[32,128,64]{1,2,0:T(8,128)(2,1)} %get-tuple-element.32), channel_id=1, source_target_pairs={{0,4},{4,0},{8,12},{12,8},{16,20},{20,16},{24,28},{28,24},{1,5},{5... | collective-permute-start | bytes 1572872 | tf_op jit(solution)/shard_map/ppermute | solution.py:18
  50.2 14.2 %collective-permute-start.3 = (bf16[32,128,64]{1,2,0:T(8,128)(2,1)}, bf16[32,128,64]{1,2,0:T(8,128)(2,1)}, u32[]{:S(2)}, u32[]{:S(2)}) collective-permute-start(bf16[32,128,64]{1,2,0:T(8,128)(2,1)} %fusion.78), channel_id=1, source_target_pairs={{0,8},{4,12},{8,0},{12,4},{16,24},{20,28},{24,16},{28,20},{1,9},{5... | collective-permute-start | bytes 1572872 | tf_op jit(solution)/shard_map/ppermute | solution.py:18
  67.2 8.5 %collective-permute-start.5 = (bf16[16,128,64]{1,2,0:T(8,128)(2,1)S(1)}, bf16[16,128,64]{1,2,0:T(8,128)(2,1)S(1)}, u32[]{:S(2)}, u32[]{:S(2)}) collective-permute-start(bf16[16,128,64]{1,2,0:T(8,128)(2,1)S(1)} %get-tuple-element.39), channel_id=1, source_target_pairs={{8,16},{12,20},{9,17},{13,21},{10,18},{14,22},{11,19},{15,23}} | collective-permute-start | bytes 786440 | tf_op jit(solution)/shard_map/ppermute | solution.py:105
  68.0 8.4 %collective-permute-start.7 = (bf16[16,128,64]{1,2,0:T(8,128)(2,1)S(1)}, bf16[16,128,64]{1,2,0:T(8,128)(2,1)S(1)}, u32[]{:S(2)}, u32[]{:S(2)}) collective-permute-start(bf16[16,128,64]{1,2,0:T(8,128)(2,1)S(1)} %get-tuple-element.40), channel_id=1, source_target_pairs={{8,16},{12,20},{9,17},{13,21},{10,18},{14,22},{11,19},{15,23}} | collective-permute-start | bytes 786440 | tf_op jit(solution)/shard_map/ppermute | solution.py:105
  68.9 12.2 %collective-permute-start.11 = (bf16[32,128,64]{1,2,0:T(8,128)(2,1)S(1)}, bf16[32,128,64]{1,2,0:T(8,128)(2,1)S(1)}, u32[]{:S(2)}, u32[]{:S(2)}) collective-permute-start(bf16[32,128,64]{1,2,0:T(8,128)(2,1)S(1)} %get-tuple-element.31), channel_id=1, source_target_pairs={{0,8},{4,12},{8,0},{12,4},{16,24},{20,28},{24,16},{28,20},{1,9},{5... | collective-permute-start | bytes 1572872 | tf_op jit(solution)/shard_map/ppermute | solution.py:18
  75.7 8.0 %collective-permute-start.6 = (bf16[16,128,64]{1,2,0:T(8,128)(2,1)S(1)}, bf16[16,128,64]{1,2,0:T(8,128)(2,1)S(1)}, u32[]{:S(2)}, u32[]{:S(2)}) collective-permute-start(bf16[16,128,64]{1,2,0:T(8,128)(2,1)S(1)} %collective-permute-done.5), channel_id=1, source_target_pairs={{16,24},{20,28},{17,25},{21,29},{18,26},{22,30},{19,27},{23,31}} | collective-permute-start | bytes 786440 | tf_op jit(solution)/shard_map/ppermute | solution.py:106
  76.4 8.1 %collective-permute-start.8 = (bf16[16,128,64]{1,2,0:T(8,128)(2,1)S(1)}, bf16[16,128,64]{1,2,0:T(8,128)(2,1)S(1)}, u32[]{:S(2)}, u32[]{:S(2)}) collective-permute-start(bf16[16,128,64]{1,2,0:T(8,128)(2,1)S(1)} %collective-permute-done.7), channel_id=1, source_target_pairs={{16,24},{20,28},{17,25},{21,29},{18,26},{22,30},{19,27},{23,31}} | collective-permute-start | bytes 786440 | tf_op jit(solution)/shard_map/ppermute | solution.py:106
  82.0 1.8 %collective-permute-start.13 = (bf16[16,128,64]{1,2,0:T(8,128)(2,1)S(1)}, bf16[16,128,64]{1,2,0:T(8,128)(2,1)S(1)}, u32[]{:S(2)}, u32[]{:S(2)}) collective-permute-start(bf16[16,128,64]{1,2,0:T(8,128)(2,1)S(1)} %get-tuple-element.43), channel_id=1, source_target_pairs={{8,16},{12,20},{9,17},{13,21},{10,18},{14,22},{11,19},{15,23}} | collective-permute-start | bytes 786440 | tf_op jit(solution)/shard_map/ppermute | solution.py:105
  82.9 1.6 %collective-permute-start.15 = (bf16[16,128,64]{1,2,0:T(8,128)(2,1)S(1)}, bf16[16,128,64]{1,2,0:T(8,128)(2,1)S(1)}, u32[]{:S(2)}, u32[]{:S(2)}) collective-permute-start(bf16[16,128,64]{1,2,0:T(8,128)(2,1)S(1)} %get-tuple-element.44), channel_id=1, source_target_pairs={{8,16},{12,20},{9,17},{13,21},{10,18},{14,22},{11,19},{15,23}} | collective-permute-start | bytes 786440 | tf_op jit(solution)/shard_map/ppermute | solution.py:105
  83.8 1.6 %collective-permute-start.14 = (bf16[16,128,64]{1,2,0:T(8,128)(2,1)S(1)}, bf16[16,128,64]{1,2,0:T(8,128)(2,1)S(1)}, u32[]{:S(2)}, u32[]{:S(2)}) collective-permute-start(bf16[16,128,64]{1,2,0:T(8,128)(2,1)S(1)} %collective-permute-done.13), channel_id=1, source_target_pairs={{16,24},{20,28},{17,25},{21,29},{18,26},{22,30},{19,27},{23,31}} | collective-permute-start | bytes 786440 | tf_op jit(solution)/shard_map/ppermute | solution.py:106
  84.5 0.9 collective-permute-start.16
  101.6 15.9 %copy-start.2 = (bf16[2,64,64,64]{1,3,2,0:T(8,128)(2,1)S(1)}, bf16[2,64,64,64]{1,3,2,0:T(8,128)(2,1)}, u32[]{:S(2)}) copy-start(bf16[2,64,64,64]{1,3,2,0:T(8,128)(2,1)} %copy.46) | copy-start | bytes 3145732
  101.6 15.9 %copy-start.19 = (f32[2,64]{1,0:T(2,128)S(1)}, f32[2,64]{1,0:T(2,128)}, u32[]{:S(2)}) copy-start(f32[2,64]{1,0:T(2,128)} %broadcast_multiply_fusion) | copy-start | bytes 1540
  101.6 15.9 %copy-start.23 = (f32[64]{0:T(128)S(1)}, f32[64]{0:T(128)}, u32[]{:S(2)}) copy-start(f32[64]{0:T(128)} %param.14) | copy-start | bytes 772
  103.1 4.2 %collective-permute-start.18 = (f32[8,12,64]{2,0,1:T(8,128)S(1)}, f32[8,12,64]{2,0,1:T(8,128)S(1)}, u32[]{:S(2)}, u32[]{:S(2)}) collective-permute-start(f32[8,12,64]{2,0,1:T(8,128)S(1)} %pad_maximum_fusion.2), channel_id=1, source_target_pairs={{0,4},{4,0},{8,12},{12,8},{16,20},{20,16},{24,28},{28,24},{1,5},{5... | collective-permute-start | bytes 73736 | tf_op jit(solution)/shard_map/ppermute | solution.py:18
  103.3 33.9 %collective-permute-start.17 = (f32[3,128]{1,0:T(4,128)S(1)}, f32[3,128]{1,0:T(4,128)S(1)}, u32[]{:S(2)}, u32[]{:S(2)}) collective-permute-start(f32[3,128]{1,0:T(4,128)S(1)} %slice.194), channel_id=1, source_target_pairs={{4,0},{8,4},{12,8},{16,12},{20,16},{24,20},{28,24},{5,1},{9,5},{13... | collective-permute-start | bytes 4616 | tf_op jit(solution)/shard_map/ppermute | solution.py:12
  107.3 19.5 %collective-permute-start.19 = (f32[8,12,64]{2,0,1:T(8,128)S(1)}, f32[8,12,64]{2,0,1:T(8,128)S(1)}, u32[]{:S(2)}, u32[]{:S(2)}) collective-permute-start(f32[8,12,64]{2,0,1:T(8,128)S(1)} %add.177), channel_id=1, source_target_pairs={{0,8},{4,12},{8,0},{12,4},{16,24},{20,28},{24,16},{28,20},{1,9},{5... | collective-permute-start | bytes 73736 | tf_op jit(solution)/shard_map/ppermute | solution.py:18
  126.8 12.5 %collective-permute-start.20 = (f32[8,12,64]{2,0,1:T(8,128)S(1)}, f32[8,12,64]{2,0,1:T(8,128)S(1)}, u32[]{:S(2)}, u32[]{:S(2)}) collective-permute-start(f32[8,12,64]{2,0,1:T(8,128)S(1)} %add.178), channel_id=1, source_target_pairs={{0,16},{4,20},{8,24},{12,28},{16,0},{20,4},{24,8},{28,12},{1,17},{... | collective-permute-start | bytes 73736 | tf_op jit(solution)/shard_map/ppermute | solution.py:18
  (24 other events, 154.0 us)

commit v14 on v12

--- a/solution.py
+++ b/solution.py
@@ -171,11 +171,11 @@
     devices = lax.axis_size("seq")
     depth = devices.bit_length() - 1
     myself = lax.axis_index("seq")
-    chunks = 2 if heads % 2 == 0 else 1
-    width = heads // chunks
+    chunks = min(3, heads)
+    bounds = [k * heads // chunks for k in range(chunks + 1)]
     pieces = [
-        exchange(dev_state[k * width : (k + 1) * width], dev_decay[k * width : (k + 1) * width], depth, myself)
-        for k in range(chunks)
+        exchange(dev_state[low:high], dev_decay[low:high], depth, myself)
+        for low, high in zip(bounds[:-1], bounds[1:])
     ]
     cross = jnp.concatenate([piece for piece, _ in pieces], axis=1)
     late_cotangent = lax.optimization_barrier((cotangent, pieces[0][1]))[0]

time: 132 us -> 146 us (1.11)
  starting transfers between devices: 43.4 us -> 55.3 us
  local copies, waits for them, and re-layouts: 30.6 us -> 32.6 us
  waiting for transfers between devices: 19.4 us -> 17.7 us
    ppermute x11 -> x15, starting transfers between devices: 32.5 us -> 46.4 us  [from_partner(): return lax.ppermute(value, axis, pairs)]
    ppermute x2, starting transfers between devices: 5.15 us -> 3.28 us  [shifted(): lax.ppermute(value, axis, [(source, source + steps) for source in range(l...]
    reshape x2, local copies, waits for them, and re-layouts: 6.6 us -> 8.45 us  [local(): grad_groups = late_cotangent.reshape(groups, group_len, heads, head_dim)]
    ppermute x11 -> x15, waiting for transfers between devices: 19.3 us -> 17.7 us  [from_partner(): return lax.ppermute(value, axis, pairs)]
  transfers between devices with their start and end apart: 21 -> 25, of which waited for: 6 -> 6; matrix products, arithmetic and copies ran while one was open for 29% -> 30% of each run, Pallas kernels for 0% -> 0%
where the time goes in v14:
time: 146 us; the launch traced here: 145 us
  starting transfers between devices  55.3 us (38%)
  local copies, waits for them, and re-layouts  32.6 us (22%)
  other arithmetic  21.8 us (15%)
  waiting for transfers between devices  17.7 us (12%)
  matrix products  16.1 us (11%)
  between operations  1.58 us (1%)
    ppermute x15, starting transfers between devices, from_partner(): return lax.ppermute(value, axis, pairs)  46.4 us
    ppermute x15, waiting for transfers between devices, from_partner(): return lax.ppermute(value, axis, pairs)  17.7 us
    dot_general x6, matrix products, contract(): return jnp.einsum(form, left, right, preferred_element_type=jnp.float32)  14.1 us
    reshape x2, local copies, waits for them, and re-layouts, local(): grad_groups = late_cotangent.reshape(groups, group_len, heads, head_dim)  8.45 us
    another operation x2, local copies, waits for them, and re-layouts, local(): x_groups = x_act.reshape(groups, group_len, heads, head_dim)  6.58 us
    another operation x1, other arithmetic  3.56 us
    convert_element_type x1, local copies, waits for them, and re-layouts, local(): ssm_out = (y_inner + y_cross + skip[None, None, :, None] * x_groups).asty...  3.31 us
    ppermute x2, starting transfers between devices, shifted(): lax.ppermute(value, axis, [(source, source + steps) for source in range(l...  3.28 us
  transfers between devices with their start and end apart: 25, of which 6 were waited for; matrix products, arithmetic and copies ran while one was open for 30% of the time, Pallas kernels for 0%

profile of v14, /device:TPU:0, one launch (start us, length us, event | category | flops | bytes accessed | tf_op | source)
XLA Modules:
  0.0 145.1 jit_solution(11563941282981705633)
XLA Ops:
  2.5 2.9 %collective-permute-start.2 = (f32[21]{0:T(128)S(1)}, f32[21]{0:T(128)S(1)}, u32[]{:S(2)}, u32[]{:S(2)}) collective-permute-start(f32[21]{0:T(128)S(1)} %get-tuple-element.70), channel_id=1, source_target_pairs={{0,4},{4,0},{8,12},{12,8},{16,20},{20,16},{24,28},{28,24},{1,5},{5... | collective-permute-start | bytes 260 | tf_op jit(solution)/shard_map/ppermute | solution.py:18
  5.6 1.9 %collective-permute-start.14 = (f32[22]{0:T(128)S(1)}, f32[22]{0:T(128)S(1)}, u32[]{:S(2)}, u32[]{:S(2)}) collective-permute-start(f32[22]{0:T(128)S(1)} %slice.156), channel_id=1, source_target_pairs={{0,4},{4,0},{8,12},{12,8},{16,20},{20,16},{24,28},{28,24},{1,5},{5... | collective-permute-start | bytes 272 | tf_op jit(solution)/shard_map/ppermute | solution.py:18
  8.4 2.0 %collective-permute-start = (bf16[3,4352]{1,0:T(4,128)(2,1)S(1)}, bf16[3,4352]{1,0:T(4,128)(2,1)S(1)}, u32[]{:S(2)}, u32[]{:S(2)}) collective-permute-start(bf16[3,4352]{1,0:T(4,128)(2,1)S(1)} %slice.131), channel_id=1, source_target_pairs={{0,4},{4,8},{8,12},{12,16},{16,20},{20,24},{24,28},{1,5},{5,9},{9,... | collective-permute-start | bytes 78344 | tf_op jit(solution)/shard_map/ppermute | solution.py:12
  17.6 2.0 %collective-permute-start.4 = (f32[21]{0:T(128)S(1)}, f32[21]{0:T(128)S(1)}, u32[]{:S(2)}, u32[]{:S(2)}) collective-permute-start(f32[21]{0:T(128)S(1)} %get-tuple-element.14), channel_id=1, source_target_pairs={{0,8},{4,12},{8,0},{12,4},{16,24},{20,28},{24,16},{28,20},{1,9},{5... | collective-permute-start | bytes 260 | tf_op jit(solution)/shard_map/ppermute | solution.py:18
  20.3 2.0 %collective-permute-start.16 = (f32[22]{0:T(128)S(1)}, f32[22]{0:T(128)S(1)}, u32[]{:S(2)}, u32[]{:S(2)}) collective-permute-start(f32[22]{0:T(128)S(1)} %get-tuple-element.18), channel_id=1, source_target_pairs={{0,8},{4,12},{8,0},{12,4},{16,24},{20,28},{24,16},{28,20},{1,9},{5... | collective-permute-start | bytes 272 | tf_op jit(solution)/shard_map/ppermute | solution.py:18
  24.4 3.6 %fusion.92 = (bf16[128,4352]{1,0:T(8,128)(2,1)S(1)}, f32[128,4352]{1,0:T(8,128)S(1)}) fusion(f32[4352]{0:T(1024)S(1)} %get-tuple-element.8, bf16[128,4352]{1,0:T(8,128)(2,1)} %param.9, f32[4352]{0:T(1024)S(1)} %get-tuple-element.9, bf16[3,4352]{1,0:T(4,128)(2,1)S(1)} %collective-permute-done, f32[4352]{0:T(1024)S(1)} %get-tuple-element.10, ...), kind=kLoop, calls=%fused_computation.190 | loop fusion | flops 12255232 | bytes 4569600 | tf_op jit(solution)/shard_map/convert.2
  28.6 3.3 %reshape_reshape.3 = bf16[2,64,64,64]{3,2,1,0:T(8,128)(2,1)} reshape(bf16[128,4096]{1,0:T(8,128)(2,1)S(1)} %multiply_convert_fusion.5) | data formatting | bytes 2097152 | tf_op jit(solution)/shard_map/reshape;reshape | solution.py:160
  31.8 3.3 %copy.46 = bf16[2,64,64,64]{1,3,2,0:T(8,128)(2,1)S(1)} copy(bf16[2,64,64,64]{3,2,1,0:T(8,128)(2,1)} %reshape_reshape.3) | data formatting | bytes 2097152 | tf_op jit(solution)/shard_map/reshape;reshape | solution.py:160
  38.4 2.9 %collective-permute-start.13 = (bf16[22,128,64]{1,2,0:T(8,128)(2,1)}, bf16[22,128,64]{1,2,0:T(8,128)(2,1)S(1)}, u32[]{:S(2)}, u32[]{:S(2)}) collective-permute-start(bf16[22,128,64]{1,2,0:T(8,128)(2,1)} %slice.287), channel_id=1, source_target_pairs={{0,4},{4,0},{8,12},{12,8},{16,20},{20,16},{24,28},{28,24},{1,5},{5... | collective-permute-start | bytes 1081352 | tf_op jit(solution)/shard_map/ppermute | solution.py:18
  41.4 2.0 %collective-permute-start.7 = (bf16[21,128,64]{1,2,0:T(8,128)(2,1)}, bf16[21,128,64]{1,2,0:T(8,128)(2,1)S(1)}, u32[]{:S(2)}, u32[]{:S(2)}) collective-permute-start(bf16[21,128,64]{1,2,0:T(8,128)(2,1)} %get-tuple-element.29), channel_id=1, source_target_pairs={{0,4},{4,0},{8,12},{12,8},{16,20},{20,16},{24,28},{28,24},{1,5},{5... | collective-permute-start | bytes 1032200 | tf_op jit(solution)/shard_map/ppermute | solution.py:18
  43.4 2.4 %slice_bitcast_fusion.4 = (f32[64,128,64]{1,2,0:T(8,128)}, f32[64,128,64]{1,2,0:T(8,128)}) fusion(f32[2,64,128,64]{2,3,1,0:T(8,128)S(1)} %get-tuple-element.80), kind=kLoop, calls=%fused_computation.26 | loop fusion | bytes 8388608 | tf_op jit(solution)/shard_map/mul | solution.py:202
  45.7 12.4 %collective-permute-done.1 = bf16[21,128,64]{1,2,0:T(8,128)(2,1)S(1)} collective-permute-done((bf16[21,128,64]{1,2,0:T(8,128)(2,1)S(1)}, bf16[21,128,64]{1,2,0:T(8,128)(2,1)S(1)}, u32[]{:S(2)}, u32[]{:S(2)}) %collective-permute-start.1) | collective-permute-done | bytes 344096 | tf_op jit(solution)/shard_map/ppermute | solution.py:18
  60.8 4.2 %reshape.170 = bf16[2,64,64,64]{3,2,1,0:T(8,128)(2,1)} reshape(bf16[128,4096]{1,0:T(8,128)(2,1)} %param.17) | data formatting | bytes 2097152 | tf_op jit(solution)/shard_map/reshape | solution.py:182
  65.0 4.2 %copy.55 = bf16[2,64,64,64]{1,3,2,0:T(8,128)(2,1)} copy(bf16[2,64,64,64]{3,2,1,0:T(8,128)(2,1)} %reshape.170) | data formatting | bytes 2097152 | tf_op jit(solution)/shard_map/reshape | solution.py:182
  69.2 4.9 %multiply_reduce_fusion.2 = (f32[2,64]{1,0:T(2,128)S(1)}, f32[2,64,64]{2,1,0:T(8,128)S(1)}) fusion(f32[2,64,64]{2,1,0:T(8,128)S(1)} %fusion.99, f32[2,64,64]{2,1,0:T(8,128)S(1)} %copy.44, pred[64,64]{1,0:T(8,128)(4,1)S(1)} %iota_compare_fusion, f32[2,64]{1,0:T(2,128)} %get-tuple-element.49, bf16[2,64,64,64]{1,3,2,0:T(8,128)(2,1)} %copy.55, ...), kind=kOutput, calls=%fused_computation.10 | convolution fusion | flops 72343424 | bytes 2200576 | tf_op jit(solution)/shard_map/vmap(thp,shp->hts)/dot_general | solution.py:35
  77.9 1.7 %fusion.41 = (bf16[21,128,64]{1,2,0:T(8,128)(2,1)S(1)}, bf16[21,128,64]{1,2,0:T(8,128)(2,1)S(1)}, f32[1,21,128,64]{2,3,1,0:T(8,128)S(1)}, f32[1,21,128,64]{2,3,1,0:T(8,128)S(1)}, f32[1,21,128,64]{2,3,1,0:T(8,128)S(1)}) fusion(bf16[21,128,64]{1,2,0:T(8,128)(2,1)} %collective-permute-done.3, f32[21]{0:T(128)S(1)} %copy-done.21, f32[]{:T(128)S(6)} %sub.101, ...), kind=kLoop, calls=%fused_computation.85 | loop fusion | flops 4988928 | bytes 5161564 | tf_op jit(solution)/shard_map/convert_element_type | solution.py:120
  81.0 2.5 %collective-permute-done.15 = bf16[22,128,64]{1,2,0:T(8,128)(2,1)S(1)} collective-permute-done((bf16[22,128,64]{1,2,0:T(8,128)(2,1)S(1)}, bf16[22,128,64]{1,2,0:T(8,128)(2,1)S(1)}, u32[]{:S(2)}, u32[]{:S(2)}) %collective-permute-start.15) | collective-permute-done | bytes 360480 | tf_op jit(solution)/shard_map/ppermute | solution.py:18
  97.7 2.0 %fusion.3 = f32[2,64,128]{2,1,0:T(8,128)S(1)} fusion(bf16[2,64,64,64]{1,3,2,0:T(8,128)(2,1)S(1)} %copy-done.7, bf16[2,64,128,64]{2,3,1,0:T(8,128)(2,1)S(1)} %add_convert_fusion, f32[2,64,64]{1,2,0:T(8,128)S(1)} %copy.50), kind=kOutput, calls=%fused_computation.9 | convolution fusion | flops 136298496 | bytes 3244032 | tf_op jit(solution)/shard_map/chnp,cthp->cthn/dot_general | solution.py:35
  101.6 1.8 %collective-permute-start.22 = (f32[8,12,64]{2,0,1:T(8,128)S(1)}, f32[8,12,64]{2,0,1:T(8,128)S(1)}, u32[]{:S(2)}, u32[]{:S(2)}) collective-permute-start(f32[8,12,64]{2,0,1:T(8,128)S(1)} %pad_maximum_fusion.2), channel_id=1, source_target_pairs={{0,4},{4,0},{8,12},{12,8},{16,20},{20,16},{24,28},{28,24},{1,5},{5... | collective-permute-start | bytes 73736 | tf_op jit(solution)/shard_map/ppermute | solution.py:18
  105.8 17.7 %collective-permute-start.23 = (f32[8,12,64]{2,0,1:T(8,128)S(1)}, f32[8,12,64]{2,0,1:T(8,128)S(1)}, u32[]{:S(2)}, u32[]{:S(2)}) collective-permute-start(f32[8,12,64]{2,0,1:T(8,128)S(1)} %fusion.84), channel_id=1, source_target_pairs={{0,8},{4,12},{8,0},{12,4},{16,24},{20,28},{24,16},{28,20},{1,9},{5... | collective-permute-start | bytes 73736 | tf_op jit(solution)/shard_map/ppermute | solution.py:18
  123.5 3.5 %fusion.2 = bf16[2,64,64,64]{1,3,2,0:T(8,128)(2,1)} fusion(bf16[2,64,64,64]{1,3,2,0:T(8,128)(2,1)S(1)} %copy-done.5, f32[2,64,64,64]{3,2,1,0:T(8,128)S(1)} %fusion.6, f32[64]{0:T(128)S(1)} %copy-done.37, f32[2,64]{1,0:T(2,128)S(1)} %copy-done.32, f32[2,64,64]{2,1,0:T(8,128)S(1)} %fusion.99, f32[2,64,64]{2,1,0:T(8,128)S(1)} %copy.44, ...), kind=kOutput, calls=%fused_computation.7 | convolution fusion | flops 72876032 | bytes 4264704 | tf_op jit(solution)/shard_map/vmap(hts,shp->thp)/dot_general | solution.py:35
  127.0 3.3 %copy.51 = bf16[2,64,64,64]{3,2,1,0:T(8,128)(2,1)S(1)} copy(bf16[2,64,64,64]{1,3,2,0:T(8,128)(2,1)} %fusion.2) | data formatting | bytes 2097152 | tf_op jit(solution)/shard_map/convert_element_type | solution.py:225
  130.3 2.5 %reshape.169 = bf16[128,4096]{1,0:T(8,128)(2,1)} reshape(bf16[2,64,64,64]{3,2,1,0:T(8,128)(2,1)S(1)} %copy.51) | data formatting | bytes 2097152 | tf_op jit(solution)/shard_map/reshape | solution.py:226
  132.8 9.5 %collective-permute-start.24 = (f32[8,12,64]{2,0,1:T(8,128)S(1)}, f32[8,12,64]{2,0,1:T(8,128)S(1)}, u32[]{:S(2)}, u32[]{:S(2)}) collective-permute-start(f32[8,12,64]{2,0,1:T(8,128)S(1)} %add.216), channel_id=1, source_target_pairs={{0,16},{4,20},{8,24},{12,28},{16,0},{20,4},{24,8},{28,12},{1,17},{... | collective-permute-start | bytes 73736 | tf_op jit(solution)/shard_map/ppermute | solution.py:18
  (186 shorter events, 44.8 us)
Async XLA Ops:
  2.5 14.4 %collective-permute-start.2 = (f32[21]{0:T(128)S(1)}, f32[21]{0:T(128)S(1)}, u32[]{:S(2)}, u32[]{:S(2)}) collective-permute-start(f32[21]{0:T(128)S(1)} %get-tuple-element.70), channel_id=1, source_target_pairs={{0,4},{4,0},{8,12},{12,8},{16,20},{20,16},{24,28},{28,24},{1,5},{5... | collective-permute-start | bytes 260 | tf_op jit(solution)/shard_map/ppermute | solution.py:18
  5.4 11.5 %collective-permute-start.8 = (f32[21]{0:T(128)S(1)}, f32[21]{0:T(128)S(1)}, u32[]{:S(2)}, u32[]{:S(2)}) collective-permute-start(f32[21]{0:T(128)S(1)} %get-tuple-element.71), channel_id=1, source_target_pairs={{0,4},{4,0},{8,12},{12,8},{16,20},{20,16},{24,28},{28,24},{1,5},{5... | collective-permute-start | bytes 260 | tf_op jit(solution)/shard_map/ppermute | solution.py:18
  5.6 14.1 %collective-permute-start.14 = (f32[22]{0:T(128)S(1)}, f32[22]{0:T(128)S(1)}, u32[]{:S(2)}, u32[]{:S(2)}) collective-permute-start(f32[22]{0:T(128)S(1)} %slice.156), channel_id=1, source_target_pairs={{0,4},{4,0},{8,12},{12,8},{16,20},{20,16},{24,28},{28,24},{1,5},{5... | collective-permute-start | bytes 272 | tf_op jit(solution)/shard_map/ppermute | solution.py:18
  8.4 16.0 %collective-permute-start = (bf16[3,4352]{1,0:T(4,128)(2,1)S(1)}, bf16[3,4352]{1,0:T(4,128)(2,1)S(1)}, u32[]{:S(2)}, u32[]{:S(2)}) collective-permute-start(bf16[3,4352]{1,0:T(4,128)(2,1)S(1)} %slice.131), channel_id=1, source_target_pairs={{0,4},{4,8},{8,12},{12,16},{16,20},{20,24},{24,28},{1,5},{5,9},{9,... | collective-permute-start | bytes 78344 | tf_op jit(solution)/shard_map/ppermute | solution.py:12
  17.6 4.7 %collective-permute-start.4 = (f32[21]{0:T(128)S(1)}, f32[21]{0:T(128)S(1)}, u32[]{:S(2)}, u32[]{:S(2)}) collective-permute-start(f32[21]{0:T(128)S(1)} %get-tuple-element.14), channel_id=1, source_target_pairs={{0,8},{4,12},{8,0},{12,4},{16,24},{20,28},{24,16},{28,20},{1,9},{5... | collective-permute-start | bytes 260 | tf_op jit(solution)/shard_map/ppermute | solution.py:18
  19.6 3.5 %collective-permute-start.10 = (f32[21]{0:T(128)S(1)}, f32[21]{0:T(128)S(1)}, u32[]{:S(2)}, u32[]{:S(2)}) collective-permute-start(f32[21]{0:T(128)S(1)} %get-tuple-element.67), channel_id=1, source_target_pairs={{0,8},{4,12},{8,0},{12,4},{16,24},{20,28},{24,16},{28,20},{1,9},{5... | collective-permute-start | bytes 260 | tf_op jit(solution)/shard_map/ppermute | solution.py:18
  20.3 3.5 %collective-permute-start.16 = (f32[22]{0:T(128)S(1)}, f32[22]{0:T(128)S(1)}, u32[]{:S(2)}, u32[]{:S(2)}) collective-permute-start(f32[22]{0:T(128)S(1)} %get-tuple-element.18), channel_id=1, source_target_pairs={{0,8},{4,12},{8,0},{12,4},{16,24},{20,28},{24,16},{28,20},{1,9},{5... | collective-permute-start | bytes 272 | tf_op jit(solution)/shard_map/ppermute | solution.py:18
  38.4 37.3 %collective-permute-start.13 = (bf16[22,128,64]{1,2,0:T(8,128)(2,1)}, bf16[22,128,64]{1,2,0:T(8,128)(2,1)S(1)}, u32[]{:S(2)}, u32[]{:S(2)}) collective-permute-start(bf16[22,128,64]{1,2,0:T(8,128)(2,1)} %slice.287), channel_id=1, source_target_pairs={{0,4},{4,0},{8,12},{12,8},{16,20},{20,16},{24,28},{28,24},{1,5},{5... | collective-permute-start | bytes 1081352 | tf_op jit(solution)/shard_map/ppermute | solution.py:18
  41.3 16.9 %collective-permute-start.1 = (bf16[21,128,64]{1,2,0:T(8,128)(2,1)S(1)}, bf16[21,128,64]{1,2,0:T(8,128)(2,1)S(1)}, u32[]{:S(2)}, u32[]{:S(2)}) collective-permute-start(bf16[21,128,64]{1,2,0:T(8,128)(2,1)S(1)} %get-tuple-element.28), channel_id=1, source_target_pairs={{0,4},{4,0},{8,12},{12,8},{16,20},{20,16},{24,28},{28,24},{1,5},{5... | collective-permute-start | bytes 1032200 | tf_op jit(solution)/shard_map/ppermute | solution.py:18
  41.4 36.5 %collective-permute-start.7 = (bf16[21,128,64]{1,2,0:T(8,128)(2,1)}, bf16[21,128,64]{1,2,0:T(8,128)(2,1)S(1)}, u32[]{:S(2)}, u32[]{:S(2)}) collective-permute-start(bf16[21,128,64]{1,2,0:T(8,128)(2,1)} %get-tuple-element.29), channel_id=1, source_target_pairs={{0,4},{4,0},{8,12},{12,8},{16,20},{20,16},{24,28},{28,24},{1,5},{5... | collective-permute-start | bytes 1032200 | tf_op jit(solution)/shard_map/ppermute | solution.py:18
  59.2 18.7 %collective-permute-start.3 = (bf16[21,128,64]{1,2,0:T(8,128)(2,1)}, bf16[21,128,64]{1,2,0:T(8,128)(2,1)}, u32[]{:S(2)}, u32[]{:S(2)}) collective-permute-start(bf16[21,128,64]{1,2,0:T(8,128)(2,1)} %fusion.86), channel_id=1, source_target_pairs={{0,8},{4,12},{8,0},{12,4},{16,24},{20,28},{24,16},{28,20},{1,9},{5... | collective-permute-start | bytes 1032200 | tf_op jit(solution)/shard_map/ppermute | solution.py:18
  76.0 7.5 %collective-permute-start.15 = (bf16[22,128,64]{1,2,0:T(8,128)(2,1)S(1)}, bf16[22,128,64]{1,2,0:T(8,128)(2,1)S(1)}, u32[]{:S(2)}, u32[]{:S(2)}) collective-permute-start(bf16[22,128,64]{1,2,0:T(8,128)(2,1)S(1)} %fusion.87), channel_id=1, source_target_pairs={{0,8},{4,12},{8,0},{12,4},{16,24},{20,28},{24,16},{28,20},{1,9},{5... | collective-permute-start | bytes 1081352 | tf_op jit(solution)/shard_map/ppermute | solution.py:18
  79.8 8.5 %collective-permute-start.9 = (bf16[21,128,64]{1,2,0:T(8,128)(2,1)S(1)}, bf16[21,128,64]{1,2,0:T(8,128)(2,1)S(1)}, u32[]{:S(2)}, u32[]{:S(2)}) collective-permute-start(bf16[21,128,64]{1,2,0:T(8,128)(2,1)S(1)} %get-tuple-element.27), channel_id=1, source_target_pairs={{0,8},{4,12},{8,0},{12,4},{16,24},{20,28},{24,16},{28,20},{1,9},{5... | collective-permute-start | bytes 1032200 | tf_op jit(solution)/shard_map/ppermute | solution.py:18
  84.1 2.6 %collective-permute-start.17 = (bf16[11,128,64]{1,2,0:T(8,128)(2,1)S(1)}, bf16[11,128,64]{1,2,0:T(8,128)(2,1)S(1)}, u32[]{:S(2)}, u32[]{:S(2)}) collective-permute-start(bf16[11,128,64]{1,2,0:T(8,128)(2,1)S(1)} %get-tuple-element.35), channel_id=1, source_target_pairs={{8,16},{12,20},{9,17},{13,21},{10,18},{14,22},{11,19},{15,23}} | collective-permute-start | bytes 540680 | tf_op jit(solution)/shard_map/ppermute | solution.py:105
  84.8 2.6 %collective-permute-start.19 = (bf16[11,128,64]{1,2,0:T(8,128)(2,1)S(1)}, bf16[11,128,64]{1,2,0:T(8,128)(2,1)S(1)}, u32[]{:S(2)}, u32[]{:S(2)}) collective-permute-start(bf16[11,128,64]{1,2,0:T(8,128)(2,1)S(1)} %get-tuple-element.36), channel_id=1, source_target_pairs={{8,16},{12,20},{9,17},{13,21},{10,18},{14,22},{11,19},{15,23}} | collective-permute-start | bytes 540680 | tf_op jit(solution)/shard_map/ppermute | solution.py:105
  85.7 3.8 %collective-permute-start.5 = (bf16[21,128,64]{1,2,0:T(8,128)(2,1)S(1)}, bf16[21,128,64]{1,2,0:T(8,128)(2,1)S(1)}, u32[]{:S(2)}, u32[]{:S(2)}) collective-permute-start(bf16[21,128,64]{1,2,0:T(8,128)(2,1)S(1)} %get-tuple-element.26), channel_id=1, source_target_pairs={{8,16},{12,20},{9,17},{13,21},{10,18},{14,22},{11,19},{15,23}} | collective-permute-start | bytes 1032200 | tf_op jit(solution)/shard_map/ppermute | solution.py:105
  86.7 3.5 %collective-permute-start.18 = (bf16[11,128,64]{1,2,0:T(8,128)(2,1)S(1)}, bf16[11,128,64]{1,2,0:T(8,128)(2,1)S(1)}, u32[]{:S(2)}, u32[]{:S(2)}) collective-permute-start(bf16[11,128,64]{1,2,0:T(8,128)(2,1)S(1)} %collective-permute-done.17), channel_id=1, source_target_pairs={{16,24},{20,28},{17,25},{21,29},{18,26},{22,30},{19,27},{23,31}} | collective-permute-start | bytes 540680 | tf_op jit(solution)/shard_map/ppermute | solution.py:106
  87.4 2.9 %collective-permute-start.20 = (bf16[11,128,64]{1,2,0:T(8,128)(2,1)S(1)}, bf16[11,128,64]{1,2,0:T(8,128)(2,1)S(1)}, u32[]{:S(2)}, u32[]{:S(2)}) collective-permute-start(bf16[11,128,64]{1,2,0:T(8,128)(2,1)S(1)} %collective-permute-done.19), channel_id=1, source_target_pairs={{16,24},{20,28},{17,25},{21,29},{18,26},{22,30},{19,27},{23,31}} | collective-permute-start | bytes 540680 | tf_op jit(solution)/shard_map/ppermute | solution.py:106
  88.8 1.5 %collective-permute-start.11 = (bf16[21,128,64]{1,2,0:T(8,128)(2,1)S(1)}, bf16[21,128,64]{1,2,0:T(8,128)(2,1)S(1)}, u32[]{:S(2)}, u32[]{:S(2)}) collective-permute-start(bf16[21,128,64]{1,2,0:T(8,128)(2,1)S(1)} %get-tuple-element.41), channel_id=1, source_target_pairs={{8,16},{12,20},{9,17},{13,21},{10,18},{14,22},{11,19},{15,23}} | collective-permute-start | bytes 1032200 | tf_op jit(solution)/shard_map/ppermute | solution.py:105
  89.5 1.6 %collective-permute-start.6 = (bf16[21,128,64]{1,2,0:T(8,128)(2,1)S(1)}, bf16[21,128,64]{1,2,0:T(8,128)(2,1)S(1)}, u32[]{:S(2)}, u32[]{:S(2)}) collective-permute-start(bf16[21,128,64]{1,2,0:T(8,128)(2,1)S(1)} %collective-permute-done.5), channel_id=1, source_target_pairs={{16,24},{20,28},{17,25},{21,29},{18,26},{22,30},{19,27},{23,31}} | collective-permute-start | bytes 1032200 | tf_op jit(solution)/shard_map/ppermute | solution.py:106
  101.6 4.2 %collective-permute-start.22 = (f32[8,12,64]{2,0,1:T(8,128)S(1)}, f32[8,12,64]{2,0,1:T(8,128)S(1)}, u32[]{:S(2)}, u32[]{:S(2)}) collective-permute-start(f32[8,12,64]{2,0,1:T(8,128)S(1)} %pad_maximum_fusion.2), channel_id=1, source_target_pairs={{0,4},{4,0},{8,12},{12,8},{16,20},{20,16},{24,28},{28,24},{1,5},{5... | collective-permute-start | bytes 73736 | tf_op jit(solution)/shard_map/ppermute | solution.py:18
  103.5 38.8 %collective-permute-start.21 = (f32[3,128]{1,0:T(4,128)S(1)}, f32[3,128]{1,0:T(4,128)S(1)}, u32[]{:S(2)}, u32[]{:S(2)}) collective-permute-start(f32[3,128]{1,0:T(4,128)S(1)} %slice.198), channel_id=1, source_target_pairs={{4,0},{8,4},{12,8},{16,12},{20,16},{24,20},{28,24},{5,1},{9,5},{13... | collective-permute-start | bytes 4616 | tf_op jit(solution)/shard_map/ppermute | solution.py:12
  105.8 27.1 %collective-permute-start.23 = (f32[8,12,64]{2,0,1:T(8,128)S(1)}, f32[8,12,64]{2,0,1:T(8,128)S(1)}, u32[]{:S(2)}, u32[]{:S(2)}) collective-permute-start(f32[8,12,64]{2,0,1:T(8,128)S(1)} %fusion.84), channel_id=1, source_target_pairs={{0,8},{4,12},{8,0},{12,4},{16,24},{20,28},{24,16},{28,20},{1,9},{5... | collective-permute-start | bytes 73736 | tf_op jit(solution)/shard_map/ppermute | solution.py:18
  132.8 11.6 %collective-permute-start.24 = (f32[8,12,64]{2,0,1:T(8,128)S(1)}, f32[8,12,64]{2,0,1:T(8,128)S(1)}, u32[]{:S(2)}, u32[]{:S(2)}) collective-permute-start(f32[8,12,64]{2,0,1:T(8,128)S(1)} %add.216), channel_id=1, source_target_pairs={{0,16},{4,20},{8,24},{12,28},{16,0},{20,4},{24,8},{28,12},{1,17},{... | collective-permute-start | bytes 73736 | tf_op jit(solution)/shard_map/ppermute | solution.py:18
  (41 other events, 342.4 us)

commit v15 on v13

--- a/solution.py
+++ b/solution.py
@@ -216,7 +216,10 @@
     grads = exact("ck,clh->klh", picked, level_rest)
     grad_first = exact("gk,gh->kh", picked, level_zero)
     local_grads = jnp.concatenate([grad_first[:, None, :], grads], axis=1)
-    local_grads, states, cross = lax.optimization_barrier((local_grads, states, cross))
+    partial = local_grads
+    if depth > 0:
+        partial = partial + from_partner(partial, "seq", 0)
+    partial, states, cross = lax.optimization_barrier((partial, states, cross))
     terms = [local_weight[:, d, :, None, None] * states[d][None] for d in range(groups)]
     terms += [cross_weight[:, l, :, None, None] * cross[l][None] for l in range(depth)]
     mixed = sum(terms[1:], terms[0]).astype(jnp.bfloat16)
@@ -236,7 +239,9 @@
     for offset in range(taps):
         lagged = taps - 1 - offset
         grad_c_in = grad_c_in + query_taps[offset][None, :] * extended[lagged : lagged + length]
-    summed = all_sum(local_grads, "seq")
+    summed = partial
+    for distance in range(1, depth):
+        summed = summed + from_partner(summed, "seq", distance)
     level_update = level_table + summed / math.sqrt(length * devices)
     return (ssm_out, grad_c_in, level_update)
 

time: 141 us -> 143 us (1.014)
  waiting for transfers between devices: 19.5 us -> 21 us
where the time goes in v15:
time: 143 us; the launch traced here: 142 us
  starting transfers between devices  46 us (32%)
  other arithmetic  25.8 us (18%)
  local copies, waits for them, and re-layouts  25.4 us (18%)
  matrix products  22.3 us (16%)
  waiting for transfers between devices  21 us (15%)
    ppermute x11, starting transfers between devices, from_partner(): return lax.ppermute(value, axis, pairs)  35 us
    ppermute x11, waiting for transfers between devices, from_partner(): return lax.ppermute(value, axis, pairs)  20.9 us
    dot_general x6, matrix products, contract(): return jnp.einsum(form, left, right, preferred_element_type=jnp.float32)  19.8 us
    another operation x2, local copies, waits for them, and re-layouts, local(): x_groups = x_act.reshape(groups, group_len, heads, head_dim)  5.3 us
    ppermute x2, starting transfers between devices, shifted(): lax.ppermute(value, axis, [(source, source + steps) for source in range(l...  5.15 us
    convert_element_type x1, other arithmetic, local(): mixed = sum(terms[1:], terms[0]).astype(jnp.bfloat16)  4.37 us
    reshape x1, local copies, waits for them, and re-layouts, local(): grad_groups = late_cotangent.reshape(groups, group_len, heads, head_dim)  4.27 us
    mul x2, local copies, waits for them, and re-layouts, local(): cross_weight[:, l, :, None, None] * cross[l][None]  3.74 us
  transfers between devices with their start and end apart: 21, of which 4 were waited for; matrix products, arithmetic and copies ran while one was open for 36% of the time, Pallas kernels for 0%

profile of v15, /device:TPU:0, one launch (start us, length us, event | category | flops | bytes accessed | tf_op | source)
XLA Modules:
  0.0 142.0 jit_solution(10726079121266530571)
XLA Ops:
  2.5 2.9 %collective-permute-start.2 = (f32[32]{0:T(128)S(1)}, f32[32]{0:T(128)S(1)}, u32[]{:S(2)}, u32[]{:S(2)}) collective-permute-start(f32[32]{0:T(128)S(1)} %get-tuple-element.73), channel_id=1, source_target_pairs={{0,4},{4,0},{8,12},{12,8},{16,20},{20,16},{24,28},{28,24},{1,5},{5... | collective-permute-start | bytes 392 | tf_op jit(solution)/shard_map/ppermute | solution.py:18
  6.4 3.9 %collective-permute-start = (bf16[3,4352]{1,0:T(4,128)(2,1)S(1)}, bf16[3,4352]{1,0:T(4,128)(2,1)S(1)}, u32[]{:S(2)}, u32[]{:S(2)}) collective-permute-start(bf16[3,4352]{1,0:T(4,128)(2,1)S(1)} %slice.131), channel_id=1, source_target_pairs={{0,4},{4,8},{8,12},{12,16},{16,20},{20,24},{24,28},{1,5},{5,9},{9,... | collective-permute-start | bytes 78344 | tf_op jit(solution)/shard_map/ppermute | solution.py:12
  17.4 1.6 %collective-permute-start.4 = (f32[32]{0:T(128)S(1)}, f32[32]{0:T(128)S(1)}, u32[]{:S(2)}, u32[]{:S(2)}) collective-permute-start(f32[32]{0:T(128)S(1)} %get-tuple-element.20), channel_id=1, source_target_pairs={{0,8},{4,12},{8,0},{12,4},{16,24},{20,28},{24,16},{28,20},{1,9},{5... | collective-permute-start | bytes 392 | tf_op jit(solution)/shard_map/ppermute | solution.py:18
  19.5 3.4 %fusion.83 = (bf16[128,4352]{1,0:T(8,128)(2,1)S(1)}, f32[128,4352]{1,0:T(8,128)S(1)}) fusion(f32[4352]{0:T(1024)S(1)} %get-tuple-element.14, bf16[128,4352]{1,0:T(8,128)(2,1)} %param.9, f32[4352]{0:T(1024)S(1)} %get-tuple-element.15, bf16[3,4352]{1,0:T(4,128)(2,1)S(1)} %collective-permute-done, f32[4352]{0:T(1024)S(1)} %get-tuple-element.16, ...), kind=kLoop, calls=%fused_computation.171 | loop fusion | flops 12255232 | bytes 4569600 | tf_op jit(solution)/shard_map/convert.2
  23.4 2.3 %reshape_reshape.3 = bf16[2,64,64,64]{3,2,1,0:T(8,128)(2,1)S(1)} reshape(bf16[128,4096]{1,0:T(8,128)(2,1)S(1)} %multiply_convert_fusion.5) | data formatting | bytes 2097152 | tf_op jit(solution)/shard_map/reshape;reshape | solution.py:160
  25.7 3.0 %copy.46 = bf16[2,64,64,64]{1,3,2,0:T(8,128)(2,1)} copy(bf16[2,64,64,64]{3,2,1,0:T(8,128)(2,1)S(1)} %reshape_reshape.3) | data formatting | bytes 2097152 | tf_op jit(solution)/shard_map/reshape;reshape | solution.py:160
  28.8 4.4 %multiply_reduce_fusion.4 = (f32[64,128,64]{1,2,0:T(8,128)S(1)}, f32[2,64,128,64]{2,3,1,0:T(8,128)}) fusion(f32[2,64]{1,0:T(2,128)S(1)} %get-tuple-element.62, bf16[2,64,128,1]{2,1,3,0:T(8,128)(2,1)S(1)} %bitcast.96, bf16[2,64,64,64]{1,3,2,0:T(8,128)(2,1)} %copy.46, f32[2,64,64]{1,2,0:T(8,128)S(1)} %copy.49), kind=kOutput, calls=%fused_computation.14 | convolution fusion | flops 137363456 | bytes 7406080 | tf_op jit(solution)/shard_map/vmap(sn,shp->hnp)/dot_general | solution.py:35
  37.6 11.5 %collective-permute-done.1 = bf16[32,128,64]{1,2,0:T(8,128)(2,1)S(1)} collective-permute-done((bf16[32,128,64]{1,2,0:T(8,128)(2,1)S(1)}, bf16[32,128,64]{1,2,0:T(8,128)(2,1)S(1)}, u32[]{:S(2)}, u32[]{:S(2)}) %collective-permute-start.1) | collective-permute-done | bytes 524320 | tf_op jit(solution)/shard_map/ppermute | solution.py:18
  51.8 4.3 %reshape.193 = bf16[2,64,64,64]{3,2,1,0:T(8,128)(2,1)} reshape(bf16[128,4096]{1,0:T(8,128)(2,1)} %param.17) | data formatting | bytes 2097152 | tf_op jit(solution)/shard_map/reshape | solution.py:182
  56.1 5.5 %multiply_reduce_fusion.2 = (f32[2,64,64]{2,1,0:T(8,128)S(1)}, f32[2,64]{1,0:T(2,128)S(1)}) fusion(f32[2,64]{1,0:T(2,128)} %get-tuple-element.53, f32[2,64,64]{2,1,0:T(8,128)S(1)} %copy.44, pred[64,64]{1,0:T(8,128)(4,1)S(1)} %iota_compare_fusion, f32[2,64,64]{2,1,0:T(8,128)S(1)} %fusion.91, bf16[2,64,64,64]{1,3,2,0:T(8,128)(2,1)} %copy.46, ...), kind=kOutput, calls=%fused_computation.10 | convolution fusion | flops 72343424 | bytes 2200576 | tf_op jit(solution)/shard_map/vmap(thp,shp->hts)/dot_general | solution.py:35
  61.6 2.8 %fusion.6 = f32[2,64,128,64]{2,3,1,0:T(8,128)S(1)} fusion(f32[2,64,64]{1,2,0:T(8,128)S(1)} %copy.52, f32[2,64,128]{2,1,0:T(8,128)S(1)} %convert_element_type.120, bf16[2,64,64,64]{3,2,1,0:T(8,128)(2,1)S(1)} %copy-done.3), kind=kOutput, calls=%fused_computation.19 | convolution fusion | flops 136314880 | bytes 5341184 | tf_op jit(solution)/shard_map/cthn,cthp->chnp/dot_general | solution.py:35
  64.5 2.7 %fusion.34 = (bf16[32,128,64]{1,2,0:T(8,128)(2,1)S(1)}, bf16[32,128,64]{1,2,0:T(8,128)(2,1)S(1)}, f32[1,32,128,64]{2,3,1,0:T(8,128)S(1)}, f32[1,32,128,64]{2,3,1,0:T(8,128)S(1)}, f32[1,32,128,64]{2,3,1,0:T(8,128)S(1)}) fusion(bf16[32,128,64]{1,2,0:T(8,128)(2,1)} %collective-permute-done.3, f32[32]{0:T(128)S(1)} %copy-done.14, f32[]{:T(128)S(6)} %sub.97, ...), kind=kLoop, calls=%fused_computation.71 | loop fusion | flops 7602176 | bytes 7865232 | tf_op jit(solution)/shard_map/convert_element_type | solution.py:120
  68.9 5.1 %collective-permute-start.11 = (bf16[32,128,64]{1,2,0:T(8,128)(2,1)S(1)}, bf16[32,128,64]{1,2,0:T(8,128)(2,1)S(1)}, u32[]{:S(2)}, u32[]{:S(2)}) collective-permute-start(bf16[32,128,64]{1,2,0:T(8,128)(2,1)S(1)} %get-tuple-element.31), channel_id=1, source_target_pairs={{0,8},{4,12},{8,0},{12,4},{16,24},{20,28},{24,16},{28,20},{1,9},{5... | collective-permute-start | bytes 1572872 | tf_op jit(solution)/shard_map/ppermute | solution.py:18
  77.1 4.0 %collective-permute-done.11 = bf16[32,128,64]{1,2,0:T(8,128)(2,1)S(1)} collective-permute-done((bf16[32,128,64]{1,2,0:T(8,128)(2,1)S(1)}, bf16[32,128,64]{1,2,0:T(8,128)(2,1)S(1)}, u32[]{:S(2)}, u32[]{:S(2)}) %collective-permute-start.11) | collective-permute-done | bytes 524320 | tf_op jit(solution)/shard_map/ppermute | solution.py:18
  86.9 3.6 %multiply_reduce_fusion = f32[2,3,64]{2,1,0:T(4,128)S(1)} fusion(f32[2,64,128,64]{2,3,1,0:T(8,128)} %copy-done.1, f32[3,64,128,64]{2,3,1,0:T(8,128)S(1)} %maximum_maximum_fusion), kind=kLoop, calls=%fused_computation | loop fusion | flops 6291072 | bytes 10487296 | tf_op jit(solution)/shard_map/reduce_sum | solution.py:207
  91.5 4.1 %collective-permute-done.17 = f32[8,12,64]{2,0,1:T(8,128)S(1)} collective-permute-done((f32[8,12,64]{2,0,1:T(8,128)S(1)}, f32[8,12,64]{2,0,1:T(8,128)S(1)}, u32[]{:S(2)}, u32[]{:S(2)}) %collective-permute-start.17) | collective-permute-done | bytes 24608 | tf_op jit(solution)/shard_map/ppermute | solution.py:18
  95.6 3.7 %slice_bitcast_fusion.2 = (f32[64,128,64]{1,2,0:T(8,128)S(1)}, f32[64,128,64]{1,2,0:T(8,128)}, f32[64,128,64]{1,2,0:T(8,128)}, f32[64,128,64]{1,2,0:T(8,128)}, f32[64,128,64]{1,2,0:T(8,128)}) fusion(f32[3,64,128,64]{2,3,1,0:T(8,128)S(1)} %maximum_maximum_fusion, f32[2,64,128,64]{2,3,1,0:T(8,128)S(1)} %copy-done), kind=kLoop, calls=%fused_computation.24 | loop fusion | bytes 20971520 | tf_op jit(solution)/shard_map/mul | solution.py:224
  99.4 4.4 %add_convert_fusion = bf16[2,64,128,64]{2,3,1,0:T(8,128)(2,1)S(1)} fusion(f32[64,128,64]{1,2,0:T(8,128)} %get-tuple-element.26, f32[2,64]{1,0:T(2,128)S(1)} %get-tuple-element.55, f32[64,128,64]{1,2,0:T(8,128)} %get-tuple-element.27, f32[2,64]{1,0:T(2,128)S(1)} %get-tuple-element.56, f32[64,128,64]{1,2,0:T(8,128)S(1)} %get-tuple-element.25, ...), kind=kLoop, calls=%fused_computation.11 | loop fusion | flops 10485760 | bytes 12585472 | tf_op jit(solution)/shard_map/convert_element_type | solution.py:225
  103.7 2.0 %fusion.3 = f32[2,64,128]{2,1,0:T(8,128)S(1)} fusion(bf16[2,64,128,64]{2,3,1,0:T(8,128)(2,1)S(1)} %add_convert_fusion, f32[2,64,64]{1,2,0:T(8,128)S(1)} %copy.52, bf16[2,64,64,64]{3,2,1,0:T(8,128)(2,1)S(1)} %copy-done.4), kind=kOutput, calls=%fused_computation.9 | convolution fusion | flops 136298496 | bytes 3244032 | tf_op jit(solution)/shard_map/chnp,cthp->cthn/dot_general | solution.py:35
  108.7 10.8 %collective-permute-start.19 = (f32[8,12,64]{2,0,1:T(8,128)S(1)}, f32[8,12,64]{2,0,1:T(8,128)S(1)}, u32[]{:S(2)}, u32[]{:S(2)}) collective-permute-start(f32[8,12,64]{2,0,1:T(8,128)S(1)} %fusion.77), channel_id=1, source_target_pairs={{0,8},{4,12},{8,0},{12,4},{16,24},{20,28},{24,16},{28,20},{1,9},{5... | collective-permute-start | bytes 73736 | tf_op jit(solution)/shard_map/ppermute | solution.py:18
  119.5 3.5 %fusion.2 = bf16[2,64,64,64]{1,3,2,0:T(8,128)(2,1)} fusion(bf16[2,64,64,64]{1,3,2,0:T(8,128)(2,1)S(1)} %copy-done.2, f32[2,64,64,64]{3,2,1,0:T(8,128)S(1)} %fusion.5, f32[64]{0:T(128)S(1)} %copy-done.23, f32[2,64]{1,0:T(2,128)S(1)} %copy-done.19, f32[2,64,64]{2,1,0:T(8,128)S(1)} %fusion.91, f32[2,64,64]{2,1,0:T(8,128)S(1)} %copy.44, ...), kind=kOutput, calls=%fused_computation.7 | convolution fusion | flops 72876032 | bytes 4264704 | tf_op jit(solution)/shard_map/vmap(hts,shp->thp)/dot_general | solution.py:35
  123.0 3.3 %copy.55 = bf16[2,64,64,64]{3,2,1,0:T(8,128)(2,1)S(1)} copy(bf16[2,64,64,64]{1,3,2,0:T(8,128)(2,1)} %fusion.2) | data formatting | bytes 2097152 | tf_op jit(solution)/shard_map/convert_element_type | solution.py:231
  126.4 2.5 %reshape.194 = bf16[128,4096]{1,0:T(8,128)(2,1)} reshape(bf16[2,64,64,64]{3,2,1,0:T(8,128)(2,1)S(1)} %copy.55) | data formatting | bytes 2097152 | tf_op jit(solution)/shard_map/reshape | solution.py:232
  128.9 10.4 %collective-permute-start.20 = (f32[8,12,64]{2,0,1:T(8,128)S(1)}, f32[8,12,64]{2,0,1:T(8,128)S(1)}, u32[]{:S(2)}, u32[]{:S(2)}) collective-permute-start(f32[8,12,64]{2,0,1:T(8,128)S(1)} %add.178), channel_id=1, source_target_pairs={{0,16},{4,20},{8,24},{12,28},{16,0},{20,4},{24,8},{28,12},{1,17},{... | collective-permute-start | bytes 73736 | tf_op jit(solution)/shard_map/ppermute | solution.py:18
  (147 shorter events, 35.1 us)
Async XLA Ops:
  2.5 14.3 %collective-permute-start.2 = (f32[32]{0:T(128)S(1)}, f32[32]{0:T(128)S(1)}, u32[]{:S(2)}, u32[]{:S(2)}) collective-permute-start(f32[32]{0:T(128)S(1)} %get-tuple-element.73), channel_id=1, source_target_pairs={{0,4},{4,0},{8,12},{12,8},{16,20},{20,16},{24,28},{28,24},{1,5},{5... | collective-permute-start | bytes 392 | tf_op jit(solution)/shard_map/ppermute | solution.py:18
  5.4 11.4 %collective-permute-start.10 = (f32[32]{0:T(128)S(1)}, f32[32]{0:T(128)S(1)}, u32[]{:S(2)}, u32[]{:S(2)}) collective-permute-start(f32[32]{0:T(128)S(1)} %get-tuple-element.74), channel_id=1, source_target_pairs={{0,4},{4,0},{8,12},{12,8},{16,20},{20,16},{24,28},{28,24},{1,5},{5... | collective-permute-start | bytes 392 | tf_op jit(solution)/shard_map/ppermute | solution.py:18
  6.4 13.1 %collective-permute-start = (bf16[3,4352]{1,0:T(4,128)(2,1)S(1)}, bf16[3,4352]{1,0:T(4,128)(2,1)S(1)}, u32[]{:S(2)}, u32[]{:S(2)}) collective-permute-start(bf16[3,4352]{1,0:T(4,128)(2,1)S(1)} %slice.131), channel_id=1, source_target_pairs={{0,4},{4,8},{8,12},{12,16},{16,20},{20,24},{24,28},{1,5},{5,9},{9,... | collective-permute-start | bytes 78344 | tf_op jit(solution)/shard_map/ppermute | solution.py:12
  17.4 18.9 %collective-permute-start.4 = (f32[32]{0:T(128)S(1)}, f32[32]{0:T(128)S(1)}, u32[]{:S(2)}, u32[]{:S(2)}) collective-permute-start(f32[32]{0:T(128)S(1)} %get-tuple-element.20), channel_id=1, source_target_pairs={{0,8},{4,12},{8,0},{12,4},{16,24},{20,28},{24,16},{28,20},{1,9},{5... | collective-permute-start | bytes 392 | tf_op jit(solution)/shard_map/ppermute | solution.py:18
  19.0 16.7 %collective-permute-start.12 = (f32[32]{0:T(128)S(1)}, f32[32]{0:T(128)S(1)}, u32[]{:S(2)}, u32[]{:S(2)}) collective-permute-start(f32[32]{0:T(128)S(1)} %get-tuple-element.70), channel_id=1, source_target_pairs={{0,8},{4,12},{8,0},{12,4},{16,24},{20,28},{24,16},{28,20},{1,9},{5... | collective-permute-start | bytes 392 | tf_op jit(solution)/shard_map/ppermute | solution.py:18
  34.2 14.9 %collective-permute-start.1 = (bf16[32,128,64]{1,2,0:T(8,128)(2,1)S(1)}, bf16[32,128,64]{1,2,0:T(8,128)(2,1)S(1)}, u32[]{:S(2)}, u32[]{:S(2)}) collective-permute-start(bf16[32,128,64]{1,2,0:T(8,128)(2,1)S(1)} %get-tuple-element.33), channel_id=1, source_target_pairs={{0,4},{4,0},{8,12},{12,8},{16,20},{20,16},{24,28},{28,24},{1,5},{5... | collective-permute-start | bytes 1572872 | tf_op jit(solution)/shard_map/ppermute | solution.py:18
  36.9 27.5 %collective-permute-start.9 = (bf16[32,128,64]{1,2,0:T(8,128)(2,1)}, bf16[32,128,64]{1,2,0:T(8,128)(2,1)S(1)}, u32[]{:S(2)}, u32[]{:S(2)}) collective-permute-start(bf16[32,128,64]{1,2,0:T(8,128)(2,1)} %get-tuple-element.32), channel_id=1, source_target_pairs={{0,4},{4,0},{8,12},{12,8},{16,20},{20,16},{24,28},{28,24},{1,5},{5... | collective-permute-start | bytes 1572872 | tf_op jit(solution)/shard_map/ppermute | solution.py:18
  50.2 14.2 %collective-permute-start.3 = (bf16[32,128,64]{1,2,0:T(8,128)(2,1)}, bf16[32,128,64]{1,2,0:T(8,128)(2,1)}, u32[]{:S(2)}, u32[]{:S(2)}) collective-permute-start(bf16[32,128,64]{1,2,0:T(8,128)(2,1)} %fusion.79), channel_id=1, source_target_pairs={{0,8},{4,12},{8,0},{12,4},{16,24},{20,28},{24,16},{28,20},{1,9},{5... | collective-permute-start | bytes 1572872 | tf_op jit(solution)/shard_map/ppermute | solution.py:18
  67.2 8.5 %collective-permute-start.5 = (bf16[16,128,64]{1,2,0:T(8,128)(2,1)S(1)}, bf16[16,128,64]{1,2,0:T(8,128)(2,1)S(1)}, u32[]{:S(2)}, u32[]{:S(2)}) collective-permute-start(bf16[16,128,64]{1,2,0:T(8,128)(2,1)S(1)} %get-tuple-element.39), channel_id=1, source_target_pairs={{8,16},{12,20},{9,17},{13,21},{10,18},{14,22},{11,19},{15,23}} | collective-permute-start | bytes 786440 | tf_op jit(solution)/shard_map/ppermute | solution.py:105
  68.0 8.4 %collective-permute-start.7 = (bf16[16,128,64]{1,2,0:T(8,128)(2,1)S(1)}, bf16[16,128,64]{1,2,0:T(8,128)(2,1)S(1)}, u32[]{:S(2)}, u32[]{:S(2)}) collective-permute-start(bf16[16,128,64]{1,2,0:T(8,128)(2,1)S(1)} %get-tuple-element.40), channel_id=1, source_target_pairs={{8,16},{12,20},{9,17},{13,21},{10,18},{14,22},{11,19},{15,23}} | collective-permute-start | bytes 786440 | tf_op jit(solution)/shard_map/ppermute | solution.py:105
  68.9 12.2 %collective-permute-start.11 = (bf16[32,128,64]{1,2,0:T(8,128)(2,1)S(1)}, bf16[32,128,64]{1,2,0:T(8,128)(2,1)S(1)}, u32[]{:S(2)}, u32[]{:S(2)}) collective-permute-start(bf16[32,128,64]{1,2,0:T(8,128)(2,1)S(1)} %get-tuple-element.31), channel_id=1, source_target_pairs={{0,8},{4,12},{8,0},{12,4},{16,24},{20,28},{24,16},{28,20},{1,9},{5... | collective-permute-start | bytes 1572872 | tf_op jit(solution)/shard_map/ppermute | solution.py:18
  75.7 8.0 %collective-permute-start.6 = (bf16[16,128,64]{1,2,0:T(8,128)(2,1)S(1)}, bf16[16,128,64]{1,2,0:T(8,128)(2,1)S(1)}, u32[]{:S(2)}, u32[]{:S(2)}) collective-permute-start(bf16[16,128,64]{1,2,0:T(8,128)(2,1)S(1)} %collective-permute-done.5), channel_id=1, source_target_pairs={{16,24},{20,28},{17,25},{21,29},{18,26},{22,30},{19,27},{23,31}} | collective-permute-start | bytes 786440 | tf_op jit(solution)/shard_map/ppermute | solution.py:106
  76.4 8.1 %collective-permute-start.8 = (bf16[16,128,64]{1,2,0:T(8,128)(2,1)S(1)}, bf16[16,128,64]{1,2,0:T(8,128)(2,1)S(1)}, u32[]{:S(2)}, u32[]{:S(2)}) collective-permute-start(bf16[16,128,64]{1,2,0:T(8,128)(2,1)S(1)} %collective-permute-done.7), channel_id=1, source_target_pairs={{16,24},{20,28},{17,25},{21,29},{18,26},{22,30},{19,27},{23,31}} | collective-permute-start | bytes 786440 | tf_op jit(solution)/shard_map/ppermute | solution.py:106
  82.0 1.8 %collective-permute-start.13 = (bf16[16,128,64]{1,2,0:T(8,128)(2,1)S(1)}, bf16[16,128,64]{1,2,0:T(8,128)(2,1)S(1)}, u32[]{:S(2)}, u32[]{:S(2)}) collective-permute-start(bf16[16,128,64]{1,2,0:T(8,128)(2,1)S(1)} %get-tuple-element.43), channel_id=1, source_target_pairs={{8,16},{12,20},{9,17},{13,21},{10,18},{14,22},{11,19},{15,23}} | collective-permute-start | bytes 786440 | tf_op jit(solution)/shard_map/ppermute | solution.py:105
  82.9 1.6 %collective-permute-start.15 = (bf16[16,128,64]{1,2,0:T(8,128)(2,1)S(1)}, bf16[16,128,64]{1,2,0:T(8,128)(2,1)S(1)}, u32[]{:S(2)}, u32[]{:S(2)}) collective-permute-start(bf16[16,128,64]{1,2,0:T(8,128)(2,1)S(1)} %get-tuple-element.44), channel_id=1, source_target_pairs={{8,16},{12,20},{9,17},{13,21},{10,18},{14,22},{11,19},{15,23}} | collective-permute-start | bytes 786440 | tf_op jit(solution)/shard_map/ppermute | solution.py:105
  83.8 1.6 %collective-permute-start.14 = (bf16[16,128,64]{1,2,0:T(8,128)(2,1)S(1)}, bf16[16,128,64]{1,2,0:T(8,128)(2,1)S(1)}, u32[]{:S(2)}, u32[]{:S(2)}) collective-permute-start(bf16[16,128,64]{1,2,0:T(8,128)(2,1)S(1)} %collective-permute-done.13), channel_id=1, source_target_pairs={{16,24},{20,28},{17,25},{21,29},{18,26},{22,30},{19,27},{23,31}} | collective-permute-start | bytes 786440 | tf_op jit(solution)/shard_map/ppermute | solution.py:106
  84.5 0.9 collective-permute-start.16
  91.4 4.2 %collective-permute-start.17 = (f32[8,12,64]{2,0,1:T(8,128)S(1)}, f32[8,12,64]{2,0,1:T(8,128)S(1)}, u32[]{:S(2)}, u32[]{:S(2)}) collective-permute-start(f32[8,12,64]{2,0,1:T(8,128)S(1)} %pad_maximum_fusion.2), channel_id=1, source_target_pairs={{0,4},{4,0},{8,12},{12,8},{16,20},{20,16},{24,28},{28,24},{1,5},{5... | collective-permute-start | bytes 73736 | tf_op jit(solution)/shard_map/ppermute | solution.py:18
  105.7 13.8 %copy-start.2 = (bf16[2,64,64,64]{1,3,2,0:T(8,128)(2,1)S(1)}, bf16[2,64,64,64]{1,3,2,0:T(8,128)(2,1)}, u32[]{:S(2)}) copy-start(bf16[2,64,64,64]{1,3,2,0:T(8,128)(2,1)} %copy.46) | copy-start | bytes 3145732
  105.7 13.8 %copy-start.19 = (f32[2,64]{1,0:T(2,128)S(1)}, f32[2,64]{1,0:T(2,128)}, u32[]{:S(2)}) copy-start(f32[2,64]{1,0:T(2,128)} %broadcast_multiply_fusion) | copy-start | bytes 1540
  107.4 31.9 %collective-permute-start.18 = (f32[3,128]{1,0:T(4,128)S(1)}, f32[3,128]{1,0:T(4,128)S(1)}, u32[]{:S(2)}, u32[]{:S(2)}) collective-permute-start(f32[3,128]{1,0:T(4,128)S(1)} %slice.194), channel_id=1, source_target_pairs={{4,0},{8,4},{12,8},{16,12},{20,16},{24,20},{28,24},{5,1},{9,5},{13... | collective-permute-start | bytes 4616 | tf_op jit(solution)/shard_map/ppermute | solution.py:12
  108.7 20.1 %collective-permute-start.19 = (f32[8,12,64]{2,0,1:T(8,128)S(1)}, f32[8,12,64]{2,0,1:T(8,128)S(1)}, u32[]{:S(2)}, u32[]{:S(2)}) collective-permute-start(f32[8,12,64]{2,0,1:T(8,128)S(1)} %fusion.77), channel_id=1, source_target_pairs={{0,8},{4,12},{8,0},{12,4},{16,24},{20,28},{24,16},{28,20},{1,9},{5... | collective-permute-start | bytes 73736 | tf_op jit(solution)/shard_map/ppermute | solution.py:18
  126.4 15.0 %copy-start.5 = (f32[8,12,64]{2,0,1:T(8,128)S(1)}, f32[8,12,64]{2,0,1:T(8,128)}, u32[]{:S(2)}) copy-start(f32[8,12,64]{2,0,1:T(8,128)} %param.15) | copy-start | bytes 73732
  128.9 12.5 %collective-permute-start.20 = (f32[8,12,64]{2,0,1:T(8,128)S(1)}, f32[8,12,64]{2,0,1:T(8,128)S(1)}, u32[]{:S(2)}, u32[]{:S(2)}) collective-permute-start(f32[8,12,64]{2,0,1:T(8,128)S(1)} %add.178), channel_id=1, source_target_pairs={{0,16},{4,20},{8,24},{12,28},{16,0},{20,4},{24,8},{28,12},{1,17},{... | collective-permute-start | bytes 73736 | tf_op jit(solution)/shard_map/ppermute | solution.py:18
  (24 other events, 152.8 us)

commit v16 on v12

--- a/solution.py
+++ b/solution.py
@@ -108,7 +108,7 @@
     return jnp.concatenate(received, axis=0)
 
 
-def exchange(block, block_decay, depth, myself):
+def exchange(block, block_decay, depth, myself, decays):
     leading = jnp.zeros_like(block_decay)
     found_all = []
     first = None
@@ -120,8 +120,8 @@
                 sent = relay(block.astype(jnp.bfloat16), "seq", bit_pos)
             other, other_decay = (sent.astype(jnp.float32), jnp.zeros_like(block_decay))
         else:
-            sent, other_decay = from_partner((block.astype(jnp.bfloat16), block_decay), "seq", bit_pos)
-            other = sent.astype(jnp.float32)
+            sent = from_partner(block.astype(jnp.bfloat16), "seq", bit_pos)
+            other, other_decay = (sent.astype(jnp.float32), decays[bit_pos])
         first = sent if first is None else first
         upper = jnp.zeros_like(block_decay) + (jnp.right_shift(myself, bit_pos) & 1).astype(
             jnp.float32
@@ -171,10 +171,21 @@
     devices = lax.axis_size("seq")
     depth = devices.bit_length() - 1
     myself = lax.axis_index("seq")
+    decays = []
+    running = dev_decay
+    for bit_pos in range(depth - 1):
+        decays.append(from_partner(running, "seq", bit_pos))
+        running = running + decays[-1]
     chunks = 2 if heads % 2 == 0 else 1
     width = heads // chunks
     pieces = [
-        exchange(dev_state[k * width : (k + 1) * width], dev_decay[k * width : (k + 1) * width], depth, myself)
+        exchange(
+            dev_state[k * width : (k + 1) * width],
+            dev_decay[k * width : (k + 1) * width],
+            depth,
+            myself,
+            [decay[k * width : (k + 1) * width] for decay in decays],
+        )
         for k in range(chunks)
     ]
     cross = jnp.concatenate([piece for piece, _ in pieces], axis=1)

time: 132 us -> 130 us (0.985)
    ppermute x11 -> x9, starting transfers between devices: 32.5 us -> 34.7 us  [from_partner(): return lax.ppermute(value, axis, pairs)]
    ppermute x2, starting transfers between devices: 5.15 us -> 3.22 us  [shifted(): lax.ppermute(value, axis, [(source, source + steps) for source in range(l...]
    ppermute x11 -> x9, waiting for transfers between devices: 19.3 us -> 18.1 us  [from_partner(): return lax.ppermute(value, axis, pairs)]
  transfers between devices with their start and end apart: 21 -> 19, of which waited for: 6 -> 5; matrix products, arithmetic and copies ran while one was open for 29% -> 28% of each run, Pallas kernels for 0% -> 0%
where the time goes in v16:
time: 130 us; the launch traced here: 129 us
  starting transfers between devices  43.6 us (34%)
  local copies, waits for them, and re-layouts  30.6 us (24%)
  other arithmetic  19.6 us (15%)
  waiting for transfers between devices  18.1 us (14%)
  matrix products  15.5 us (12%)
  between operations  1.46 us (1%)
    ppermute x9, starting transfers between devices, from_partner(): return lax.ppermute(value, axis, pairs)  34.7 us
    ppermute x9, waiting for transfers between devices, from_partner(): return lax.ppermute(value, axis, pairs)  18.1 us
    dot_general x6, matrix products, contract(): return jnp.einsum(form, left, right, preferred_element_type=jnp.float32)  12.9 us
    reshape x2, local copies, waits for them, and re-layouts, local(): grad_groups = late_cotangent.reshape(groups, group_len, heads, head_dim)  6.6 us
    another operation x2, local copies, waits for them, and re-layouts, local(): x_groups = x_act.reshape(groups, group_len, heads, head_dim)  6.57 us
    another operation x1, other arithmetic  3.47 us
    convert_element_type x1, local copies, waits for them, and re-layouts, local(): ssm_out = (y_inner + y_cross + skip[None, None, :, None] * x_groups).asty...  3.31 us
    ppermute x2, starting transfers between devices, shifted(): lax.ppermute(value, axis, [(source, source + steps) for source in range(l...  3.22 us
  transfers between devices with their start and end apart: 19, of which 5 were waited for; matrix products, arithmetic and copies ran while one was open for 28% of the time, Pallas kernels for 0%

profile of v16, /device:TPU:0, one launch (start us, length us, event | category | flops | bytes accessed | tf_op | source)
XLA Modules:
  0.0 128.9 jit_solution(14401385358332741832)
XLA Ops:
  2.4 3.0 %collective-permute-start.2 = (f32[64]{0:T(128)S(1)}, f32[64]{0:T(128)S(1)}, u32[]{:S(2)}, u32[]{:S(2)}) collective-permute-start(f32[64]{0:T(128)S(1)} %get-tuple-element.41), channel_id=1, source_target_pairs={{0,4},{4,0},{8,12},{12,8},{16,20},{20,16},{24,28},{28,24},{1,5},{5... | collective-permute-start | bytes 776 | tf_op jit(solution)/shard_map/ppermute | solution.py:18
  6.3 1.9 %collective-permute-start = (bf16[3,4352]{1,0:T(4,128)(2,1)S(1)}, bf16[3,4352]{1,0:T(4,128)(2,1)S(1)}, u32[]{:S(2)}, u32[]{:S(2)}) collective-permute-start(bf16[3,4352]{1,0:T(4,128)(2,1)S(1)} %slice.143), channel_id=1, source_target_pairs={{0,4},{4,8},{8,12},{12,16},{16,20},{20,24},{24,28},{1,5},{5,9},{9,... | collective-permute-start | bytes 78344 | tf_op jit(solution)/shard_map/ppermute | solution.py:12
  14.0 2.2 %collective-permute-start.4 = (f32[64]{0:T(128)S(1)}, f32[64]{0:T(128)S(1)}, u32[]{:S(2)}, u32[]{:S(2)}) collective-permute-start(f32[64]{0:T(128)S(1)} %add.153), channel_id=1, source_target_pairs={{0,8},{4,12},{8,0},{12,4},{16,24},{20,28},{24,16},{28,20},{1,9},{5... | collective-permute-start | bytes 776 | tf_op jit(solution)/shard_map/ppermute | solution.py:18
  18.3 3.5 %fusion.77 = (bf16[128,4352]{1,0:T(8,128)(2,1)S(1)}, f32[128,4352]{1,0:T(8,128)S(1)}) fusion(f32[4352]{0:T(1024)S(1)} %get-tuple-element.8, bf16[128,4352]{1,0:T(8,128)(2,1)} %param.9, f32[4352]{0:T(1024)S(1)} %get-tuple-element.9, bf16[3,4352]{1,0:T(4,128)(2,1)S(1)} %collective-permute-done, f32[4352]{0:T(1024)S(1)} %get-tuple-element.10, ...), kind=kLoop, calls=%fused_computation.169 | loop fusion | flops 12255232 | bytes 4569600 | tf_op jit(solution)/shard_map/convert.2
  22.4 3.3 %reshape_reshape.3 = bf16[2,64,64,64]{3,2,1,0:T(8,128)(2,1)} reshape(bf16[128,4096]{1,0:T(8,128)(2,1)S(1)} %multiply_convert_fusion.5) | data formatting | bytes 2097152 | tf_op jit(solution)/shard_map/reshape;reshape | solution.py:160
  25.7 3.3 %copy.46 = bf16[2,64,64,64]{1,3,2,0:T(8,128)(2,1)S(1)} copy(bf16[2,64,64,64]{3,2,1,0:T(8,128)(2,1)} %reshape_reshape.3) | data formatting | bytes 2097152 | tf_op jit(solution)/shard_map/reshape;reshape | solution.py:160
  31.6 2.9 %collective-permute-start.1 = (bf16[32,128,64]{1,2,0:T(8,128)(2,1)S(1)}, bf16[32,128,64]{1,2,0:T(8,128)(2,1)S(1)}, u32[]{:S(2)}, u32[]{:S(2)}) collective-permute-start(bf16[32,128,64]{1,2,0:T(8,128)(2,1)S(1)} %get-tuple-element.22), channel_id=1, source_target_pairs={{0,4},{4,0},{8,12},{12,8},{16,20},{20,16},{24,28},{28,24},{1,5},{5... | collective-permute-start | bytes 1572872 | tf_op jit(solution)/shard_map/ppermute | solution.py:18
  34.7 2.4 %slice_bitcast_fusion.4 = (f32[64,128,64]{1,2,0:T(8,128)}, f32[64,128,64]{1,2,0:T(8,128)}) fusion(f32[2,64,128,64]{2,3,1,0:T(8,128)S(1)} %get-tuple-element.70), kind=kLoop, calls=%fused_computation.26 | loop fusion | bytes 8388608 | tf_op jit(solution)/shard_map/mul | solution.py:213
  37.1 10.3 %collective-permute-done.1 = bf16[32,128,64]{1,2,0:T(8,128)(2,1)S(1)} collective-permute-done((bf16[32,128,64]{1,2,0:T(8,128)(2,1)S(1)}, bf16[32,128,64]{1,2,0:T(8,128)(2,1)S(1)}, u32[]{:S(2)}, u32[]{:S(2)}) %collective-permute-start.1) | collective-permute-done | bytes 524320 | tf_op jit(solution)/shard_map/ppermute | solution.py:18
  48.5 1.6 %collective-permute-start.3 = (bf16[32,128,64]{1,2,0:T(8,128)(2,1)}, bf16[32,128,64]{1,2,0:T(8,128)(2,1)}, u32[]{:S(2)}, u32[]{:S(2)}) collective-permute-start(bf16[32,128,64]{1,2,0:T(8,128)(2,1)} %fusion.75), channel_id=1, source_target_pairs={{0,8},{4,12},{8,0},{12,4},{16,24},{20,28},{24,16},{28,20},{1,9},{5... | collective-permute-start | bytes 1572872 | tf_op jit(solution)/shard_map/ppermute | solution.py:18
  50.1 3.3 %reshape.194 = bf16[2,64,64,64]{3,2,1,0:T(8,128)(2,1)} reshape(bf16[128,4096]{1,0:T(8,128)(2,1)S(1)} %copy-done.11) | data formatting | bytes 2097152 | tf_op jit(solution)/shard_map/reshape | solution.py:193
  53.4 3.3 %copy.55 = bf16[2,64,64,64]{1,3,2,0:T(8,128)(2,1)S(1)} copy(bf16[2,64,64,64]{3,2,1,0:T(8,128)(2,1)} %reshape.194) | data formatting | bytes 2097152 | tf_op jit(solution)/shard_map/reshape | solution.py:193
  59.1 3.8 %multiply_reduce_fusion.2 = (f32[2,64]{1,0:T(2,128)S(1)}, f32[2,64,64]{2,1,0:T(8,128)S(1)}) fusion(f32[2,64,64]{2,1,0:T(8,128)S(1)} %fusion.84, f32[2,64,64]{2,1,0:T(8,128)S(1)} %copy.44, pred[64,64]{1,0:T(8,128)(4,1)S(1)} %iota_compare_fusion, f32[2,64]{1,0:T(2,128)S(1)} %copy-done.27, bf16[2,64,64,64]{1,3,2,0:T(8,128)(2,1)S(1)} %copy.55, ...), kind=kOutput, calls=%fused_computation.10 | convolution fusion | flops 72343424 | bytes 2200576 | tf_op jit(solution)/shard_map/vmap(thp,shp->hts)/dot_general | solution.py:35
  62.9 2.3 %fusion.30 = (bf16[32,128,64]{1,2,0:T(8,128)(2,1)S(1)}, bf16[32,128,64]{1,2,0:T(8,128)(2,1)S(1)}, f32[1,32,128,64]{2,3,1,0:T(8,128)S(1)}, f32[1,32,128,64]{2,3,1,0:T(8,128)S(1)}, f32[1,32,128,64]{2,3,1,0:T(8,128)S(1)}) fusion(bf16[32,128,64]{1,2,0:T(8,128)(2,1)} %collective-permute-done.3, f32[32]{0:T(128)S(1)} %copy-done.25, f32[]{:T(128)S(6)} %sub.97, ...), kind=kLoop, calls=%fused_computation.67 | loop fusion | flops 7602176 | bytes 7865232 | tf_op jit(solution)/shard_map/convert_element_type | solution.py:120
  66.7 4.6 %collective-permute-start.10 = (bf16[32,128,64]{1,2,0:T(8,128)(2,1)S(1)}, bf16[32,128,64]{1,2,0:T(8,128)(2,1)S(1)}, u32[]{:S(2)}, u32[]{:S(2)}) collective-permute-start(bf16[32,128,64]{1,2,0:T(8,128)(2,1)S(1)} %get-tuple-element.21), channel_id=1, source_target_pairs={{0,8},{4,12},{8,0},{12,4},{16,24},{20,28},{24,16},{28,20},{1,9},{5... | collective-permute-start | bytes 1572872 | tf_op jit(solution)/shard_map/ppermute | solution.py:18
  74.6 3.9 %collective-permute-done.10 = bf16[32,128,64]{1,2,0:T(8,128)(2,1)S(1)} collective-permute-done((bf16[32,128,64]{1,2,0:T(8,128)(2,1)S(1)}, bf16[32,128,64]{1,2,0:T(8,128)(2,1)S(1)}, u32[]{:S(2)}, u32[]{:S(2)}) %collective-permute-start.10) | collective-permute-done | bytes 524320 | tf_op jit(solution)/shard_map/ppermute | solution.py:18
  87.7 1.7 %add_convert_fusion = bf16[2,64,128,64]{2,3,1,0:T(8,128)(2,1)S(1)} fusion(f32[64,128,64]{1,2,0:T(8,128)S(1)} %get-tuple-element.16, f32[2,64]{1,0:T(2,128)S(1)} %get-tuple-element.45, f32[64,128,64]{1,2,0:T(8,128)S(1)} %get-tuple-element.17, f32[2,64]{1,0:T(2,128)S(1)} %get-tuple-element.46, f32[64,128,64]{1,2,0:T(8,128)S(1)} %get-tuple-element.15, ...), kind=kLoop, calls=%fused_computation.13 | loop fusion | flops 10485760 | bytes 12585472 | tf_op jit(solution)/shard_map/convert_element_type | solution.py:215
  89.5 2.0 %fusion.3 = f32[2,64,128]{2,1,0:T(8,128)S(1)} fusion(bf16[2,64,64,64]{1,3,2,0:T(8,128)(2,1)S(1)} %copy-done.8, bf16[2,64,128,64]{2,3,1,0:T(8,128)(2,1)S(1)} %add_convert_fusion, f32[2,64,64]{1,2,0:T(8,128)S(1)} %copy.50), kind=kOutput, calls=%fused_computation.9 | convolution fusion | flops 136298496 | bytes 3244032 | tf_op jit(solution)/shard_map/chnp,cthp->cthn/dot_general | solution.py:35
  95.8 1.7 %collective-permute-done.16 = f32[8,12,64]{2,0,1:T(8,128)S(1)} collective-permute-done((f32[8,12,64]{2,0,1:T(8,128)S(1)}, f32[8,12,64]{2,0,1:T(8,128)S(1)}, u32[]{:S(2)}, u32[]{:S(2)}) %collective-permute-start.16) | collective-permute-done | bytes 24608 | tf_op jit(solution)/shard_map/ppermute | solution.py:18
  97.5 9.6 %collective-permute-start.17 = (f32[8,12,64]{2,0,1:T(8,128)S(1)}, f32[8,12,64]{2,0,1:T(8,128)S(1)}, u32[]{:S(2)}, u32[]{:S(2)}) collective-permute-start(f32[8,12,64]{2,0,1:T(8,128)S(1)} %fusion.73), channel_id=1, source_target_pairs={{0,8},{4,12},{8,0},{12,4},{16,24},{20,28},{24,16},{28,20},{1,9},{5... | collective-permute-start | bytes 73736 | tf_op jit(solution)/shard_map/ppermute | solution.py:18
  107.1 3.4 %fusion.2 = bf16[2,64,64,64]{1,3,2,0:T(8,128)(2,1)} fusion(bf16[2,64,64,64]{1,3,2,0:T(8,128)(2,1)S(1)} %copy-done.6, f32[2,64,64,64]{3,2,1,0:T(8,128)S(1)} %fusion.6, f32[64]{0:T(128)S(1)} %copy-done.31, f32[2,64]{1,0:T(2,128)S(1)} %copy-done.26, f32[2,64,64]{2,1,0:T(8,128)S(1)} %fusion.84, f32[2,64,64]{2,1,0:T(8,128)S(1)} %copy.44, ...), kind=kOutput, calls=%fused_computation.7 | convolution fusion | flops 72876032 | bytes 4264704 | tf_op jit(solution)/shard_map/vmap(hts,shp->thp)/dot_general | solution.py:35
  110.6 3.3 %copy.51 = bf16[2,64,64,64]{3,2,1,0:T(8,128)(2,1)S(1)} copy(bf16[2,64,64,64]{1,3,2,0:T(8,128)(2,1)} %fusion.2) | data formatting | bytes 2097152 | tf_op jit(solution)/shard_map/convert_element_type | solution.py:236
  113.9 2.5 %reshape.193 = bf16[128,4096]{1,0:T(8,128)(2,1)} reshape(bf16[2,64,64,64]{3,2,1,0:T(8,128)(2,1)S(1)} %copy.51) | data formatting | bytes 2097152 | tf_op jit(solution)/shard_map/reshape | solution.py:237
  116.4 9.8 %collective-permute-start.18 = (f32[8,12,64]{2,0,1:T(8,128)S(1)}, f32[8,12,64]{2,0,1:T(8,128)S(1)}, u32[]{:S(2)}, u32[]{:S(2)}) collective-permute-start(f32[8,12,64]{2,0,1:T(8,128)S(1)} %add.182), channel_id=1, source_target_pairs={{0,16},{4,20},{8,24},{12,28},{16,0},{20,4},{24,8},{28,12},{1,17},{... | collective-permute-start | bytes 73736 | tf_op jit(solution)/shard_map/ppermute | solution.py:18
  (158 shorter events, 38.0 us)
Async XLA Ops:
  2.4 11.6 %collective-permute-start.2 = (f32[64]{0:T(128)S(1)}, f32[64]{0:T(128)S(1)}, u32[]{:S(2)}, u32[]{:S(2)}) collective-permute-start(f32[64]{0:T(128)S(1)} %get-tuple-element.41), channel_id=1, source_target_pairs={{0,4},{4,0},{8,12},{12,8},{16,20},{20,16},{24,28},{28,24},{1,5},{5... | collective-permute-start | bytes 776 | tf_op jit(solution)/shard_map/ppermute | solution.py:18
  6.3 12.0 %collective-permute-start = (bf16[3,4352]{1,0:T(4,128)(2,1)S(1)}, bf16[3,4352]{1,0:T(4,128)(2,1)S(1)}, u32[]{:S(2)}, u32[]{:S(2)}) collective-permute-start(bf16[3,4352]{1,0:T(4,128)(2,1)S(1)} %slice.143), channel_id=1, source_target_pairs={{0,4},{4,8},{8,12},{12,16},{16,20},{20,24},{24,28},{1,5},{5,9},{9,... | collective-permute-start | bytes 78344 | tf_op jit(solution)/shard_map/ppermute | solution.py:12
  14.0 3.7 %collective-permute-start.4 = (f32[64]{0:T(128)S(1)}, f32[64]{0:T(128)S(1)}, u32[]{:S(2)}, u32[]{:S(2)}) collective-permute-start(f32[64]{0:T(128)S(1)} %add.153), channel_id=1, source_target_pairs={{0,8},{4,12},{8,0},{12,4},{16,24},{20,28},{24,16},{28,20},{1,9},{5... | collective-permute-start | bytes 776 | tf_op jit(solution)/shard_map/ppermute | solution.py:18
  30.4 17.0 %copy-start.2 = (f32[64,128,64]{1,2,0:T(8,128)}, f32[64,128,64]{1,2,0:T(8,128)S(1)}, u32[]{:S(2)}) copy-start(f32[64,128,64]{1,2,0:T(8,128)S(1)} %get-tuple-element.69) | copy-start | bytes 6291460
  31.6 15.8 %collective-permute-start.1 = (bf16[32,128,64]{1,2,0:T(8,128)(2,1)S(1)}, bf16[32,128,64]{1,2,0:T(8,128)(2,1)S(1)}, u32[]{:S(2)}, u32[]{:S(2)}) collective-permute-start(bf16[32,128,64]{1,2,0:T(8,128)(2,1)S(1)} %get-tuple-element.22), channel_id=1, source_target_pairs={{0,4},{4,0},{8,12},{12,8},{16,20},{20,16},{24,28},{28,24},{1,5},{5... | collective-permute-start | bytes 1572872 | tf_op jit(solution)/shard_map/ppermute | solution.py:18
  34.5 28.3 %collective-permute-start.9 = (bf16[32,128,64]{1,2,0:T(8,128)(2,1)}, bf16[32,128,64]{1,2,0:T(8,128)(2,1)S(1)}, u32[]{:S(2)}, u32[]{:S(2)}) collective-permute-start(bf16[32,128,64]{1,2,0:T(8,128)(2,1)} %get-tuple-element.23), channel_id=1, source_target_pairs={{0,4},{4,0},{8,12},{12,8},{16,20},{20,16},{24,28},{28,24},{1,5},{5... | collective-permute-start | bytes 1572872 | tf_op jit(solution)/shard_map/ppermute | solution.py:18
  48.5 14.3 %collective-permute-start.3 = (bf16[32,128,64]{1,2,0:T(8,128)(2,1)}, bf16[32,128,64]{1,2,0:T(8,128)(2,1)}, u32[]{:S(2)}, u32[]{:S(2)}) collective-permute-start(bf16[32,128,64]{1,2,0:T(8,128)(2,1)} %fusion.75), channel_id=1, source_target_pairs={{0,8},{4,12},{8,0},{12,4},{16,24},{20,28},{24,16},{28,20},{1,9},{5... | collective-permute-start | bytes 1572872 | tf_op jit(solution)/shard_map/ppermute | solution.py:18
  65.3 7.7 %collective-permute-start.5 = (bf16[16,128,64]{1,2,0:T(8,128)(2,1)S(1)}, bf16[16,128,64]{1,2,0:T(8,128)(2,1)S(1)}, u32[]{:S(2)}, u32[]{:S(2)}) collective-permute-start(bf16[16,128,64]{1,2,0:T(8,128)(2,1)S(1)} %get-tuple-element.29), channel_id=1, source_target_pairs={{8,16},{12,20},{9,17},{13,21},{10,18},{14,22},{11,19},{15,23}} | collective-permute-start | bytes 786440 | tf_op jit(solution)/shard_map/ppermute | solution.py:105
  66.0 7.7 %collective-permute-start.7 = (bf16[16,128,64]{1,2,0:T(8,128)(2,1)S(1)}, bf16[16,128,64]{1,2,0:T(8,128)(2,1)S(1)}, u32[]{:S(2)}, u32[]{:S(2)}) collective-permute-start(bf16[16,128,64]{1,2,0:T(8,128)(2,1)S(1)} %get-tuple-element.30), channel_id=1, source_target_pairs={{8,16},{12,20},{9,17},{13,21},{10,18},{14,22},{11,19},{15,23}} | collective-permute-start | bytes 786440 | tf_op jit(solution)/shard_map/ppermute | solution.py:105
  66.7 11.8 %collective-permute-start.10 = (bf16[32,128,64]{1,2,0:T(8,128)(2,1)S(1)}, bf16[32,128,64]{1,2,0:T(8,128)(2,1)S(1)}, u32[]{:S(2)}, u32[]{:S(2)}) collective-permute-start(bf16[32,128,64]{1,2,0:T(8,128)(2,1)S(1)} %get-tuple-element.21), channel_id=1, source_target_pairs={{0,8},{4,12},{8,0},{12,4},{16,24},{20,28},{24,16},{28,20},{1,9},{5... | collective-permute-start | bytes 1572872 | tf_op jit(solution)/shard_map/ppermute | solution.py:18
  73.0 8.0 %collective-permute-start.6 = (bf16[16,128,64]{1,2,0:T(8,128)(2,1)S(1)}, bf16[16,128,64]{1,2,0:T(8,128)(2,1)S(1)}, u32[]{:S(2)}, u32[]{:S(2)}) collective-permute-start(bf16[16,128,64]{1,2,0:T(8,128)(2,1)S(1)} %collective-permute-done.5), channel_id=1, source_target_pairs={{16,24},{20,28},{17,25},{21,29},{18,26},{22,30},{19,27},{23,31}} | collective-permute-start | bytes 786440 | tf_op jit(solution)/shard_map/ppermute | solution.py:106
  73.7 8.1 %collective-permute-start.8 = (bf16[16,128,64]{1,2,0:T(8,128)(2,1)S(1)}, bf16[16,128,64]{1,2,0:T(8,128)(2,1)S(1)}, u32[]{:S(2)}, u32[]{:S(2)}) collective-permute-start(bf16[16,128,64]{1,2,0:T(8,128)(2,1)S(1)} %collective-permute-done.7), channel_id=1, source_target_pairs={{16,24},{20,28},{17,25},{21,29},{18,26},{22,30},{19,27},{23,31}} | collective-permute-start | bytes 786440 | tf_op jit(solution)/shard_map/ppermute | solution.py:106
  79.3 1.8 %collective-permute-start.11 = (bf16[16,128,64]{1,2,0:T(8,128)(2,1)S(1)}, bf16[16,128,64]{1,2,0:T(8,128)(2,1)S(1)}, u32[]{:S(2)}, u32[]{:S(2)}) collective-permute-start(bf16[16,128,64]{1,2,0:T(8,128)(2,1)S(1)} %get-tuple-element.33), channel_id=1, source_target_pairs={{8,16},{12,20},{9,17},{13,21},{10,18},{14,22},{11,19},{15,23}} | collective-permute-start | bytes 786440 | tf_op jit(solution)/shard_map/ppermute | solution.py:105
  80.3 1.6 %collective-permute-start.13 = (bf16[16,128,64]{1,2,0:T(8,128)(2,1)S(1)}, bf16[16,128,64]{1,2,0:T(8,128)(2,1)S(1)}, u32[]{:S(2)}, u32[]{:S(2)}) collective-permute-start(bf16[16,128,64]{1,2,0:T(8,128)(2,1)S(1)} %get-tuple-element.34), channel_id=1, source_target_pairs={{8,16},{12,20},{9,17},{13,21},{10,18},{14,22},{11,19},{15,23}} | collective-permute-start | bytes 786440 | tf_op jit(solution)/shard_map/ppermute | solution.py:105
  81.1 1.6 %collective-permute-start.12 = (bf16[16,128,64]{1,2,0:T(8,128)(2,1)S(1)}, bf16[16,128,64]{1,2,0:T(8,128)(2,1)S(1)}, u32[]{:S(2)}, u32[]{:S(2)}) collective-permute-start(bf16[16,128,64]{1,2,0:T(8,128)(2,1)S(1)} %collective-permute-done.11), channel_id=1, source_target_pairs={{16,24},{20,28},{17,25},{21,29},{18,26},{22,30},{19,27},{23,31}} | collective-permute-start | bytes 786440 | tf_op jit(solution)/shard_map/ppermute | solution.py:106
  81.9 0.9 collective-permute-start.14
  91.5 15.6 %copy-start.6 = (bf16[2,64,64,64]{1,3,2,0:T(8,128)(2,1)S(1)}, bf16[2,64,64,64]{1,3,2,0:T(8,128)(2,1)}, u32[]{:S(2)}) copy-start(bf16[2,64,64,64]{1,3,2,0:T(8,128)(2,1)} %copy-done.4) | copy-start | bytes 3145732
  91.5 15.6 %copy-start.26 = (f32[2,64]{1,0:T(2,128)S(1)}, f32[2,64]{1,0:T(2,128)}, u32[]{:S(2)}) copy-start(f32[2,64]{1,0:T(2,128)} %broadcast_multiply_fusion) | copy-start | bytes 1540
  91.5 15.6 %copy-start.31 = (f32[64]{0:T(128)S(1)}, f32[64]{0:T(128)}, u32[]{:S(2)}) copy-start(f32[64]{0:T(128)} %param.14) | copy-start | bytes 772
  93.4 4.2 %collective-permute-start.16 = (f32[8,12,64]{2,0,1:T(8,128)S(1)}, f32[8,12,64]{2,0,1:T(8,128)S(1)}, u32[]{:S(2)}, u32[]{:S(2)}) collective-permute-start(f32[8,12,64]{2,0,1:T(8,128)S(1)} %pad_maximum_fusion.2), channel_id=1, source_target_pairs={{0,4},{4,0},{8,12},{12,8},{16,20},{20,16},{24,28},{28,24},{1,5},{5... | collective-permute-start | bytes 73736 | tf_op jit(solution)/shard_map/ppermute | solution.py:18
  94.5 31.7 %collective-permute-start.15 = (f32[3,128]{1,0:T(4,128)S(1)}, f32[3,128]{1,0:T(4,128)S(1)}, u32[]{:S(2)}, u32[]{:S(2)}) collective-permute-start(f32[3,128]{1,0:T(4,128)S(1)} %slice.215), channel_id=1, source_target_pairs={{4,0},{8,4},{12,8},{16,12},{20,16},{24,20},{28,24},{5,1},{9,5},{13... | collective-permute-start | bytes 4616 | tf_op jit(solution)/shard_map/ppermute | solution.py:12
  97.5 18.9 %collective-permute-start.17 = (f32[8,12,64]{2,0,1:T(8,128)S(1)}, f32[8,12,64]{2,0,1:T(8,128)S(1)}, u32[]{:S(2)}, u32[]{:S(2)}) collective-permute-start(f32[8,12,64]{2,0,1:T(8,128)S(1)} %fusion.73), channel_id=1, source_target_pairs={{0,8},{4,12},{8,0},{12,4},{16,24},{20,28},{24,16},{28,20},{1,9},{5... | collective-permute-start | bytes 73736 | tf_op jit(solution)/shard_map/ppermute | solution.py:18
  113.9 14.4 %copy-start.12 = (f32[8,12,64]{2,0,1:T(8,128)S(1)}, f32[8,12,64]{2,0,1:T(8,128)}, u32[]{:S(2)}) copy-start(f32[8,12,64]{2,0,1:T(8,128)} %param.15) | copy-start | bytes 73732
  116.4 11.9 %collective-permute-start.18 = (f32[8,12,64]{2,0,1:T(8,128)S(1)}, f32[8,12,64]{2,0,1:T(8,128)S(1)}, u32[]{:S(2)}, u32[]{:S(2)}) collective-permute-start(f32[8,12,64]{2,0,1:T(8,128)S(1)} %add.182), channel_id=1, source_target_pairs={{0,16},{4,20},{8,24},{12,28},{16,0},{20,4},{24,8},{28,12},{1,17},{... | collective-permute-start | bytes 73736 | tf_op jit(solution)/shard_map/ppermute | solution.py:18
  (30 other events, 175.0 us)

commit v17 on v16

--- a/solution.py
+++ b/solution.py
@@ -97,7 +97,7 @@
 def relay(value, axis, bit_pos):
     half = 2**bit_pos
     step = half // 2
-    parts = 2 if value.shape[0] % 2 == 0 else 1
+    parts = 1
     size = value.shape[0] // parts
     received = []
     for index in range(parts):

time: 130 us -> 136 us (1.046)
  matrix products: 15.5 us -> 19.2 us
  local copies, waits for them, and re-layouts: 30.6 us -> 32.4 us
  starting transfers between devices: 43.6 us -> 45.3 us
    ppermute x9, starting transfers between devices: 34.7 us -> 39 us  [from_partner(): return lax.ppermute(value, axis, pairs)]
    dot_general x6, matrix products: 12.9 us -> 16.7 us  [contract(): return jnp.einsum(form, left, right, preferred_element_type=jnp.float32)]
    mul x1, local copies, waits for them, and re-layouts: 2.39 us -> 4.81 us  [local(): local_weight[:, d, :, None, None] * states[d][None]]
    reshape x2, local copies, waits for them, and re-layouts: 6.6 us -> 8.45 us  [local(): grad_groups = late_cotangent.reshape(groups, group_len, heads, head_dim)]
    unnamed x70 -> x58, local copies, waits for them, and re-layouts: 2.24 us -> 0.72 us
    ppermute x4 -> x2, starting transfers between devices: 2.84 us -> 1.52 us  [relay(): lax.ppermute(piece, axis, [(source, source + step) for source in range(ha...]
    ppermute x4 -> x2, starting transfers between devices: 2.88 us -> 1.57 us  [relay(): lax.ppermute(first, axis, [(source, source + step) for source in range(ha...]
  transfers between devices with their start and end apart: 19 -> 15, of which waited for: 5 -> 5; matrix products, arithmetic and copies ran while one was open for 28% -> 41% of each run, Pallas kernels for 0% -> 0%
where the time goes in v17:
time: 136 us
  starting transfers between devices  45.3 us (33%)
  local copies, waits for them, and re-layouts  32.4 us (24%)
  other arithmetic  20.2 us (15%)
  matrix products  19.2 us (14%)
  waiting for transfers between devices  17.3 us (13%)
    ppermute x9, starting transfers between devices, from_partner(): return lax.ppermute(value, axis, pairs)  39 us
    ppermute x9, waiting for transfers between devices, from_partner(): return lax.ppermute(value, axis, pairs)  17.2 us
    dot_general x6, matrix products, contract(): return jnp.einsum(form, left, right, preferred_element_type=jnp.float32)  16.7 us
    reshape x2, local copies, waits for them, and re-layouts, local(): grad_groups = late_cotangent.reshape(groups, group_len, heads, head_dim)  8.45 us
    another operation x2, local copies, waits for them, and re-layouts, local(): x_groups = x_act.reshape(groups, group_len, heads, head_dim)  5.25 us
    mul x1, local copies, waits for them, and re-layouts, local(): local_weight[:, d, :, None, None] * states[d][None]  4.81 us
    another operation x1, other arithmetic  3.48 us
    convert_element_type x1, local copies, waits for them, and re-layouts, local(): ssm_out = (y_inner + y_cross + skip[None, None, :, None] * x_groups).asty...  3.31 us
  transfers between devices with their start and end apart: 15, of which 5 were waited for; matrix products, arithmetic and copies ran while one was open for 41% of the time, Pallas kernels for 0%

profile of v17, /device:TPU:0, one launch (start us, length us, event | category | flops | bytes accessed | tf_op | source)
XLA Modules:
  0.0 135.6 jit_solution(609408557801870590)
XLA Ops:
  2.9 2.9 %collective-permute-start.2 = (f32[64]{0:T(128)S(1)}, f32[64]{0:T(128)S(1)}, u32[]{:S(2)}, u32[]{:S(2)}) collective-permute-start(f32[64]{0:T(128)S(1)} %get-tuple-element.37), channel_id=1, source_target_pairs={{0,4},{4,0},{8,12},{12,8},{16,20},{20,16},{24,28},{28,24},{1,5},{5... | collective-permute-start | bytes 776 | tf_op jit(solution)/shard_map/ppermute | solution.py:18
  6.8 1.9 %collective-permute-start = (bf16[3,4352]{1,0:T(4,128)(2,1)S(1)}, bf16[3,4352]{1,0:T(4,128)(2,1)S(1)}, u32[]{:S(2)}, u32[]{:S(2)}) collective-permute-start(bf16[3,4352]{1,0:T(4,128)(2,1)S(1)} %slice.131), channel_id=1, source_target_pairs={{0,4},{4,8},{8,12},{12,16},{16,20},{20,24},{24,28},{1,5},{5,9},{9,... | collective-permute-start | bytes 78344 | tf_op jit(solution)/shard_map/ppermute | solution.py:12
  13.9 3.5 %fusion.77 = (bf16[128,4352]{1,0:T(8,128)(2,1)S(1)}, f32[128,4352]{1,0:T(8,128)S(1)}) fusion(f32[4352]{0:T(1024)S(1)} %get-tuple-element.8, bf16[128,4352]{1,0:T(8,128)(2,1)} %param.9, f32[4352]{0:T(1024)S(1)} %get-tuple-element.9, bf16[3,4352]{1,0:T(4,128)(2,1)S(1)} %collective-permute-done, f32[4352]{0:T(1024)S(1)} %get-tuple-element.10, ...), kind=kLoop, calls=%fused_computation.165 | loop fusion | flops 12255232 | bytes 4569600 | tf_op jit(solution)/shard_map/convert.2
  18.0 2.3 %reshape_reshape.3 = bf16[2,64,64,64]{3,2,1,0:T(8,128)(2,1)S(1)} reshape(bf16[128,4096]{1,0:T(8,128)(2,1)S(1)} %multiply_convert_fusion.5) | data formatting | bytes 2097152 | tf_op jit(solution)/shard_map/reshape;reshape | solution.py:160
  20.3 3.0 %copy.46 = bf16[2,64,64,64]{1,3,2,0:T(8,128)(2,1)} copy(bf16[2,64,64,64]{3,2,1,0:T(8,128)(2,1)S(1)} %reshape_reshape.3) | data formatting | bytes 2097152 | tf_op jit(solution)/shard_map/reshape;reshape | solution.py:160
  23.2 4.4 %multiply_reduce_fusion.4 = (f32[64,128,64]{1,2,0:T(8,128)S(1)}, f32[2,64,128,64]{2,3,1,0:T(8,128)}) fusion(f32[2,64]{1,0:T(2,128)S(1)} %get-tuple-element.48, bf16[2,64,128,1]{2,1,3,0:T(8,128)(2,1)S(1)} %bitcast.95, bf16[2,64,64,64]{1,3,2,0:T(8,128)(2,1)} %copy.46, f32[2,64,64]{1,2,0:T(8,128)S(1)} %copy.49), kind=kOutput, calls=%fused_computation.14 | convolution fusion | flops 137363456 | bytes 7406080 | tf_op jit(solution)/shard_map/vmap(sn,shp->hnp)/dot_general | solution.py:35
  28.8 3.0 %collective-permute-start.1 = (bf16[32,128,64]{1,2,0:T(8,128)(2,1)}, bf16[32,128,64]{1,2,0:T(8,128)(2,1)S(1)}, u32[]{:S(2)}, u32[]{:S(2)}) collective-permute-start(bf16[32,128,64]{1,2,0:T(8,128)(2,1)} %get-tuple-element.22), channel_id=1, source_target_pairs={{0,4},{4,0},{8,12},{12,8},{16,20},{20,16},{24,28},{28,24},{1,5},{5... | collective-permute-start | bytes 1572872 | tf_op jit(solution)/shard_map/ppermute | solution.py:18
  33.1 1.6 %collective-permute-start.4 = (f32[64]{0:T(128)S(1)}, f32[64]{0:T(128)S(1)}, u32[]{:S(2)}, u32[]{:S(2)}) collective-permute-start(f32[64]{0:T(128)S(1)} %add.147), channel_id=1, source_target_pairs={{0,8},{4,12},{8,0},{12,4},{16,24},{20,28},{24,16},{28,20},{1,9},{5... | collective-permute-start | bytes 776 | tf_op jit(solution)/shard_map/ppermute | solution.py:18
  37.3 7.6 %collective-permute-done.1 = bf16[32,128,64]{1,2,0:T(8,128)(2,1)S(1)} collective-permute-done((bf16[32,128,64]{1,2,0:T(8,128)(2,1)}, bf16[32,128,64]{1,2,0:T(8,128)(2,1)S(1)}, u32[]{:S(2)}, u32[]{:S(2)}) %collective-permute-start.1) | collective-permute-done | bytes 524320 | tf_op jit(solution)/shard_map/ppermute | solution.py:18
  46.1 1.6 %collective-permute-start.3 = (bf16[32,128,64]{1,2,0:T(8,128)(2,1)}, bf16[32,128,64]{1,2,0:T(8,128)(2,1)}, u32[]{:S(2)}, u32[]{:S(2)}) collective-permute-start(bf16[32,128,64]{1,2,0:T(8,128)(2,1)} %fusion.75), channel_id=1, source_target_pairs={{0,8},{4,12},{8,0},{12,4},{16,24},{20,28},{24,16},{28,20},{1,9},{5... | collective-permute-start | bytes 1572872 | tf_op jit(solution)/shard_map/ppermute | solution.py:18
  47.8 4.8 %slice_bitcast_fusion.4 = (f32[64,128,64]{1,2,0:T(8,128)}, f32[64,128,64]{1,2,0:T(8,128)}) fusion(f32[2,64,128,64]{2,3,1,0:T(8,128)} %get-tuple-element.66), kind=kLoop, calls=%fused_computation.26 | loop fusion | bytes 8388608 | tf_op jit(solution)/shard_map/mul | solution.py:213
  52.6 4.2 %reshape.130 = bf16[2,64,64,64]{3,2,1,0:T(8,128)(2,1)} reshape(bf16[128,4096]{1,0:T(8,128)(2,1)} %param.17) | data formatting | bytes 2097152 | tf_op jit(solution)/shard_map/reshape | solution.py:193
  56.8 4.2 %copy.55 = bf16[2,64,64,64]{1,3,2,0:T(8,128)(2,1)} copy(bf16[2,64,64,64]{3,2,1,0:T(8,128)(2,1)} %reshape.130) | data formatting | bytes 2097152 | tf_op jit(solution)/shard_map/reshape | solution.py:193
  61.1 2.3 %fusion.30 = (bf16[32,128,64]{1,2,0:T(8,128)(2,1)S(1)}, bf16[32,128,64]{1,2,0:T(8,128)(2,1)S(1)}, f32[1,32,128,64]{2,3,1,0:T(8,128)S(1)}, f32[1,32,128,64]{2,3,1,0:T(8,128)S(1)}, f32[1,32,128,64]{2,3,1,0:T(8,128)S(1)}) fusion(bf16[32,128,64]{1,2,0:T(8,128)(2,1)} %collective-permute-done.3, f32[32]{0:T(128)S(1)} %get-tuple-element.63, f32[]{:T(128)S(6)} %sub.97, ...), kind=kLoop, calls=%fused_computation.67 | loop fusion | flops 7602176 | bytes 7865232 | tf_op jit(solution)/shard_map/convert_element_type | solution.py:120
  63.9 3.8 %multiply_reduce_fusion.2 = (f32[2,64]{1,0:T(2,128)S(1)}, f32[2,64,64]{2,1,0:T(8,128)S(1)}) fusion(f32[2,64,64]{2,1,0:T(8,128)S(1)} %fusion.82, f32[2,64,64]{2,1,0:T(8,128)S(1)} %copy.44, pred[64,64]{1,0:T(8,128)(4,1)S(1)} %iota_compare_fusion, f32[2,64]{1,0:T(2,128)S(1)} %copy-done.21, bf16[2,64,64,64]{1,3,2,0:T(8,128)(2,1)S(1)} %copy-done.3, ...), kind=kOutput, calls=%fused_computation.10 | convolution fusion | flops 72343424 | bytes 2200576 | tf_op jit(solution)/shard_map/vmap(thp,shp->hts)/dot_general | solution.py:35
  68.3 5.8 %collective-permute-done.8 = bf16[32,128,64]{1,2,0:T(8,128)(2,1)S(1)} collective-permute-done((bf16[32,128,64]{1,2,0:T(8,128)(2,1)S(1)}, bf16[32,128,64]{1,2,0:T(8,128)(2,1)S(1)}, u32[]{:S(2)}, u32[]{:S(2)}) %collective-permute-start.8) | collective-permute-done | bytes 524320 | tf_op jit(solution)/shard_map/ppermute | solution.py:18
  86.1 1.7 %add_convert_fusion = bf16[2,64,128,64]{2,3,1,0:T(8,128)(2,1)S(1)} fusion(f32[64,128,64]{1,2,0:T(8,128)S(1)} %get-tuple-element.16, f32[2,64]{1,0:T(2,128)S(1)} %get-tuple-element.41, f32[64,128,64]{1,2,0:T(8,128)S(1)} %get-tuple-element.17, f32[2,64]{1,0:T(2,128)S(1)} %get-tuple-element.42, f32[64,128,64]{1,2,0:T(8,128)S(1)} %get-tuple-element.15, ...), kind=kLoop, calls=%fused_computation.13 | loop fusion | flops 10485760 | bytes 12585472 | tf_op jit(solution)/shard_map/convert_element_type | solution.py:215
  87.8 2.0 %fusion.3 = f32[2,64,128]{2,1,0:T(8,128)S(1)} fusion(bf16[2,64,64,64]{1,3,2,0:T(8,128)(2,1)S(1)} %copy-done.4, bf16[2,64,128,64]{2,3,1,0:T(8,128)(2,1)S(1)} %add_convert_fusion, f32[2,64,64]{1,2,0:T(8,128)S(1)} %copy.50), kind=kOutput, calls=%fused_computation.9 | convolution fusion | flops 136298496 | bytes 3244032 | tf_op jit(solution)/shard_map/chnp,cthp->cthn/dot_general | solution.py:35
  89.8 1.5 %fusion.6 = f32[2,64,64,64]{3,2,1,0:T(8,128)S(1)} fusion(bf16[2,64,128,64]{2,3,1,0:T(8,128)(2,1)S(1)} %add_convert_fusion, f32[2,64,64]{1,2,0:T(8,128)S(1)} %copy.50, f32[2,64,128]{2,1,0:T(8,128)S(1)} %convert_element_type.121), kind=kOutput, calls=%fused_computation.19 | convolution fusion | flops 136314880 | bytes 4292608 | tf_op jit(solution)/shard_map/cthn,chnp->cthp/dot_general | solution.py:35
  95.9 12.8 %collective-permute-start.13 = (f32[8,12,64]{2,0,1:T(8,128)S(1)}, f32[8,12,64]{2,0,1:T(8,128)S(1)}, u32[]{:S(2)}, u32[]{:S(2)}) collective-permute-start(f32[8,12,64]{2,0,1:T(8,128)S(1)} %fusion.73), channel_id=1, source_target_pairs={{0,8},{4,12},{8,0},{12,4},{16,24},{20,28},{24,16},{28,20},{1,9},{5... | collective-permute-start | bytes 73736 | tf_op jit(solution)/shard_map/ppermute | solution.py:18
  108.7 3.5 %fusion.2 = bf16[2,64,64,64]{1,3,2,0:T(8,128)(2,1)} fusion(bf16[2,64,64,64]{1,3,2,0:T(8,128)(2,1)S(1)} %copy-done.2, f32[2,64,64,64]{3,2,1,0:T(8,128)S(1)} %fusion.6, f32[64]{0:T(128)S(1)} %copy-done.25, f32[2,64]{1,0:T(2,128)S(1)} %copy-done.20, f32[2,64,64]{2,1,0:T(8,128)S(1)} %fusion.82, f32[2,64,64]{2,1,0:T(8,128)S(1)} %copy.44, ...), kind=kOutput, calls=%fused_computation.7 | convolution fusion | flops 72876032 | bytes 4264704 | tf_op jit(solution)/shard_map/vmap(hts,shp->thp)/dot_general | solution.py:35
  112.1 3.3 %copy.51 = bf16[2,64,64,64]{3,2,1,0:T(8,128)(2,1)S(1)} copy(bf16[2,64,64,64]{1,3,2,0:T(8,128)(2,1)} %fusion.2) | data formatting | bytes 2097152 | tf_op jit(solution)/shard_map/convert_element_type | solution.py:236
  115.5 2.5 %reshape.129 = bf16[128,4096]{1,0:T(8,128)(2,1)} reshape(bf16[2,64,64,64]{3,2,1,0:T(8,128)(2,1)S(1)} %copy.51) | data formatting | bytes 2097152 | tf_op jit(solution)/shard_map/reshape | solution.py:237
  118.0 14.9 %collective-permute-start.14 = (f32[8,12,64]{2,0,1:T(8,128)S(1)}, f32[8,12,64]{2,0,1:T(8,128)S(1)}, u32[]{:S(2)}, u32[]{:S(2)}) collective-permute-start(f32[8,12,64]{2,0,1:T(8,128)S(1)} %add.174), channel_id=1, source_target_pairs={{0,16},{4,20},{8,24},{12,28},{16,0},{20,4},{24,8},{28,12},{1,17},{... | collective-permute-start | bytes 73736 | tf_op jit(solution)/shard_map/ppermute | solution.py:18
  (132 shorter events, 35.2 us)
Async XLA Ops:
  2.9 14.4 %copy-start.10 = (f32[2,1,64]{2,1,0:T(1,128)}, f32[2,1,64]{2,1,0:T(1,128)S(1)}, u32[]{:S(2)}) copy-start(f32[2,1,64]{2,1,0:T(1,128)S(1)} %get-tuple-element.12) | copy-start | bytes 1540
  2.9 30.1 %collective-permute-start.2 = (f32[64]{0:T(128)S(1)}, f32[64]{0:T(128)S(1)}, u32[]{:S(2)}, u32[]{:S(2)}) collective-permute-start(f32[64]{0:T(128)S(1)} %get-tuple-element.37), channel_id=1, source_target_pairs={{0,4},{4,0},{8,12},{12,8},{16,20},{20,16},{24,28},{28,24},{1,5},{5... | collective-permute-start | bytes 776 | tf_op jit(solution)/shard_map/ppermute | solution.py:18
  6.8 7.1 %collective-permute-start = (bf16[3,4352]{1,0:T(4,128)(2,1)S(1)}, bf16[3,4352]{1,0:T(4,128)(2,1)S(1)}, u32[]{:S(2)}, u32[]{:S(2)}) collective-permute-start(bf16[3,4352]{1,0:T(4,128)(2,1)S(1)} %slice.131), channel_id=1, source_target_pairs={{0,4},{4,8},{8,12},{12,16},{16,20},{20,24},{24,28},{1,5},{5,9},{9,... | collective-permute-start | bytes 78344 | tf_op jit(solution)/shard_map/ppermute | solution.py:12
  28.8 16.1 %collective-permute-start.1 = (bf16[32,128,64]{1,2,0:T(8,128)(2,1)}, bf16[32,128,64]{1,2,0:T(8,128)(2,1)S(1)}, u32[]{:S(2)}, u32[]{:S(2)}) collective-permute-start(bf16[32,128,64]{1,2,0:T(8,128)(2,1)} %get-tuple-element.22), channel_id=1, source_target_pairs={{0,4},{4,0},{8,12},{12,8},{16,20},{20,16},{24,28},{28,24},{1,5},{5... | collective-permute-start | bytes 1572872 | tf_op jit(solution)/shard_map/ppermute | solution.py:18
  33.1 3.6 %collective-permute-start.4 = (f32[64]{0:T(128)S(1)}, f32[64]{0:T(128)S(1)}, u32[]{:S(2)}, u32[]{:S(2)}) collective-permute-start(f32[64]{0:T(128)S(1)} %add.147), channel_id=1, source_target_pairs={{0,8},{4,12},{8,0},{12,4},{16,24},{20,28},{24,16},{28,20},{1,9},{5... | collective-permute-start | bytes 776 | tf_op jit(solution)/shard_map/ppermute | solution.py:18
  37.3 23.7 %collective-permute-start.7 = (bf16[32,128,64]{1,2,0:T(8,128)(2,1)}, bf16[32,128,64]{1,2,0:T(8,128)(2,1)S(1)}, u32[]{:S(2)}, u32[]{:S(2)}) collective-permute-start(bf16[32,128,64]{1,2,0:T(8,128)(2,1)} %get-tuple-element.23), channel_id=1, source_target_pairs={{0,4},{4,0},{8,12},{12,8},{16,20},{20,16},{24,28},{28,24},{1,5},{5... | collective-permute-start | bytes 1572872 | tf_op jit(solution)/shard_map/ppermute | solution.py:18
  46.1 15.0 %collective-permute-start.3 = (bf16[32,128,64]{1,2,0:T(8,128)(2,1)}, bf16[32,128,64]{1,2,0:T(8,128)(2,1)}, u32[]{:S(2)}, u32[]{:S(2)}) collective-permute-start(bf16[32,128,64]{1,2,0:T(8,128)(2,1)} %fusion.75), channel_id=1, source_target_pairs={{0,8},{4,12},{8,0},{12,4},{16,24},{20,28},{24,16},{28,20},{1,9},{5... | collective-permute-start | bytes 1572872 | tf_op jit(solution)/shard_map/ppermute | solution.py:18
  63.3 10.8 %collective-permute-start.8 = (bf16[32,128,64]{1,2,0:T(8,128)(2,1)S(1)}, bf16[32,128,64]{1,2,0:T(8,128)(2,1)S(1)}, u32[]{:S(2)}, u32[]{:S(2)}) collective-permute-start(bf16[32,128,64]{1,2,0:T(8,128)(2,1)S(1)} %get-tuple-element.21), channel_id=1, source_target_pairs={{0,8},{4,12},{8,0},{12,4},{16,24},{20,28},{24,16},{28,20},{1,9},{5... | collective-permute-start | bytes 1572872 | tf_op jit(solution)/shard_map/ppermute | solution.py:18
  67.6 9.7 %collective-permute-start.5 = (bf16[32,128,64]{1,2,0:T(8,128)(2,1)S(1)}, bf16[32,128,64]{1,2,0:T(8,128)(2,1)S(1)}, u32[]{:S(2)}, u32[]{:S(2)}) collective-permute-start(bf16[32,128,64]{1,2,0:T(8,128)(2,1)S(1)} %get-tuple-element.20), channel_id=1, source_target_pairs={{8,16},{12,20},{9,17},{13,21},{10,18},{14,22},{11,19},{15,23}} | collective-permute-start | bytes 1572872 | tf_op jit(solution)/shard_map/ppermute | solution.py:105
  74.9 4.2 %collective-permute-start.9 = (bf16[32,128,64]{1,2,0:T(8,128)(2,1)S(1)}, bf16[32,128,64]{1,2,0:T(8,128)(2,1)S(1)}, u32[]{:S(2)}, u32[]{:S(2)}) collective-permute-start(bf16[32,128,64]{1,2,0:T(8,128)(2,1)S(1)} %get-tuple-element.30), channel_id=1, source_target_pairs={{8,16},{12,20},{9,17},{13,21},{10,18},{14,22},{11,19},{15,23}} | collective-permute-start | bytes 1572872 | tf_op jit(solution)/shard_map/ppermute | solution.py:105
  77.3 3.6 %collective-permute-start.6 = (bf16[32,128,64]{1,2,0:T(8,128)(2,1)S(1)}, bf16[32,128,64]{1,2,0:T(8,128)(2,1)S(1)}, u32[]{:S(2)}, u32[]{:S(2)}) collective-permute-start(bf16[32,128,64]{1,2,0:T(8,128)(2,1)S(1)} %collective-permute-done.5), channel_id=1, source_target_pairs={{16,24},{20,28},{17,25},{21,29},{18,26},{22,30},{19,27},{23,31}} | collective-permute-start | bytes 1572872 | tf_op jit(solution)/shard_map/ppermute | solution.py:106
  79.1 2.0 %collective-permute-start.10 = (bf16[32,128,64]{1,2,0:T(8,128)(2,1)S(1)}, bf16[32,128,64]{1,2,0:T(8,128)(2,1)S(1)}, u32[]{:S(2)}, u32[]{:S(2)}) collective-permute-start(bf16[32,128,64]{1,2,0:T(8,128)(2,1)S(1)} %collective-permute-done.9), channel_id=1, source_target_pairs={{16,24},{20,28},{17,25},{21,29},{18,26},{22,30},{19,27},{23,31}} | collective-permute-start | bytes 1572872 | tf_op jit(solution)/shard_map/ppermute | solution.py:106
  89.8 18.9 %copy-start.2 = (bf16[2,64,64,64]{1,3,2,0:T(8,128)(2,1)S(1)}, bf16[2,64,64,64]{1,3,2,0:T(8,128)(2,1)}, u32[]{:S(2)}) copy-start(bf16[2,64,64,64]{1,3,2,0:T(8,128)(2,1)} %copy.46) | copy-start | bytes 3145732
  89.8 18.9 %copy-start.20 = (f32[2,64]{1,0:T(2,128)S(1)}, f32[2,64]{1,0:T(2,128)}, u32[]{:S(2)}) copy-start(f32[2,64]{1,0:T(2,128)} %broadcast_multiply_fusion) | copy-start | bytes 1540
  89.8 18.9 %copy-start.25 = (f32[64]{0:T(128)S(1)}, f32[64]{0:T(128)}, u32[]{:S(2)}) copy-start(f32[64]{0:T(128)} %param.14) | copy-start | bytes 772
  91.7 4.2 %collective-permute-start.12 = (f32[8,12,64]{2,0,1:T(8,128)S(1)}, f32[8,12,64]{2,0,1:T(8,128)S(1)}, u32[]{:S(2)}, u32[]{:S(2)}) collective-permute-start(f32[8,12,64]{2,0,1:T(8,128)S(1)} %pad_maximum_fusion.2), channel_id=1, source_target_pairs={{0,4},{4,0},{8,12},{12,8},{16,20},{20,16},{24,28},{28,24},{1,5},{5... | collective-permute-start | bytes 73736 | tf_op jit(solution)/shard_map/ppermute | solution.py:18
  93.3 39.6 %collective-permute-start.11 = (f32[3,128]{1,0:T(4,128)S(1)}, f32[3,128]{1,0:T(4,128)S(1)}, u32[]{:S(2)}, u32[]{:S(2)}) collective-permute-start(f32[3,128]{1,0:T(4,128)S(1)} %slice.195), channel_id=1, source_target_pairs={{4,0},{8,4},{12,8},{16,12},{20,16},{24,20},{28,24},{5,1},{9,5},{13... | collective-permute-start | bytes 4616 | tf_op jit(solution)/shard_map/ppermute | solution.py:12
  95.9 22.1 %collective-permute-start.13 = (f32[8,12,64]{2,0,1:T(8,128)S(1)}, f32[8,12,64]{2,0,1:T(8,128)S(1)}, u32[]{:S(2)}, u32[]{:S(2)}) collective-permute-start(f32[8,12,64]{2,0,1:T(8,128)S(1)} %fusion.73), channel_id=1, source_target_pairs={{0,8},{4,12},{8,0},{12,4},{16,24},{20,28},{24,16},{28,20},{1,9},{5... | collective-permute-start | bytes 73736 | tf_op jit(solution)/shard_map/ppermute | solution.py:18
  115.5 17.5 %copy-start.15 = (f32[128]{0:T(128)S(1)}, f32[128]{0:T(128)}, u32[]{:S(2)}) copy-start(f32[128]{0:T(128)} %get-tuple-element.31) | copy-start | bytes 1540
  115.5 17.5 %copy-start.16 = (f32[128]{0:T(128)S(1)}, f32[128]{0:T(128)}, u32[]{:S(2)}) copy-start(f32[128]{0:T(128)} %get-tuple-element.32) | copy-start | bytes 1540
  115.5 17.5 %copy-start.17 = (f32[128]{0:T(128)S(1)}, f32[128]{0:T(128)}, u32[]{:S(2)}) copy-start(f32[128]{0:T(128)} %get-tuple-element.33) | copy-start | bytes 1540
  115.5 17.5 %copy-start.18 = (f32[128]{0:T(128)S(1)}, f32[128]{0:T(128)}, u32[]{:S(2)}) copy-start(f32[128]{0:T(128)} %get-tuple-element.34) | copy-start | bytes 1540
  115.5 19.5 %copy-start.7 = (f32[8,12,64]{2,0,1:T(8,128)S(1)}, f32[8,12,64]{2,0,1:T(8,128)}, u32[]{:S(2)}) copy-start(f32[8,12,64]{2,0,1:T(8,128)} %param.15) | copy-start | bytes 73732
  118.0 17.0 %collective-permute-start.14 = (f32[8,12,64]{2,0,1:T(8,128)S(1)}, f32[8,12,64]{2,0,1:T(8,128)S(1)}, u32[]{:S(2)}, u32[]{:S(2)}) collective-permute-start(f32[8,12,64]{2,0,1:T(8,128)S(1)} %add.174), channel_id=1, source_target_pairs={{0,16},{4,20},{8,24},{12,28},{16,0},{20,4},{24,8},{28,12},{1,17},{... | collective-permute-start | bytes 73736 | tf_op jit(solution)/shard_map/ppermute | solution.py:18
  (20 other events, 70.4 us)

commit v18 on v17

--- a/solution.py
+++ b/solution.py
@@ -97,7 +97,7 @@
 def relay(value, axis, bit_pos):
     half = 2**bit_pos
     step = half // 2
-    parts = 1
+    parts = 4 if value.shape[0] % 4 == 0 else 1
     size = value.shape[0] // parts
     received = []
     for index in range(parts):

time: 136 us -> 137 us (level)
  starting transfers between devices: 45.3 us -> 49 us
  matrix products: 19.2 us -> 15.6 us
  local copies, waits for them, and re-layouts: 32.4 us -> 30.7 us
  waiting for transfers between devices: 17.3 us -> 19 us
    ppermute x9, starting transfers between devices: 39 us -> 35 us  [from_partner(): return lax.ppermute(value, axis, pairs)]
    ppermute x2 -> x8, starting transfers between devices: 1.57 us -> 5.52 us  [relay(): lax.ppermute(first, axis, [(source, source + step) for source in range(ha...]
    ppermute x2 -> x8, starting transfers between devices: 1.52 us -> 5.35 us  [relay(): lax.ppermute(piece, axis, [(source, source + step) for source in range(ha...]
    dot_general x6, matrix products: 16.7 us -> 13 us  [contract(): return jnp.einsum(form, left, right, preferred_element_type=jnp.float32)]
    mul x1, local copies, waits for them, and re-layouts: 4.81 us -> 2.38 us  [local(): local_weight[:, d, :, None, None] * states[d][None]]
    reshape x2, local copies, waits for them, and re-layouts: 8.45 us -> 6.61 us  [local(): grad_groups = late_cotangent.reshape(groups, group_len, heads, head_dim)]
    ppermute x9, waiting for transfers between devices: 17.2 us -> 19 us  [from_partner(): return lax.ppermute(value, axis, pairs)]
    unnamed x58 -> x72, local copies, waits for them, and re-layouts: 0.72 us -> 2.23 us
  transfers between devices with their start and end apart: 15 -> 27, of which waited for: 5 -> 5; matrix products, arithmetic and copies ran while one was open for 41% -> 27% of each run, Pallas kernels for 0% -> 0%
where the time goes in v18:
time: 137 us; the launch traced here: 136 us
  starting transfers between devices  49 us (36%)
  local copies, waits for them, and re-layouts  30.7 us (22%)
  other arithmetic  19.9 us (15%)
  waiting for transfers between devices  19 us (14%)
  matrix products  15.6 us (11%)
  between operations  1.64 us (1%)
    ppermute x9, starting transfers between devices, from_partner(): return lax.ppermute(value, axis, pairs)  35 us
    ppermute x9, waiting for transfers between devices, from_partner(): return lax.ppermute(value, axis, pairs)  19 us
    dot_general x6, matrix products, contract(): return jnp.einsum(form, left, right, preferred_element_type=jnp.float32)  13 us
    reshape x2, local copies, waits for them, and re-layouts, local(): grad_groups = late_cotangent.reshape(groups, group_len, heads, head_dim)  6.61 us
    another operation x2, local copies, waits for them, and re-layouts, local(): x_groups = x_act.reshape(groups, group_len, heads, head_dim)  6.58 us
    ppermute x8, starting transfers between devices, relay(): lax.ppermute(first, axis, [(source, source + step) for source in range(ha...  5.52 us
    ppermute x8, starting transfers between devices, relay(): lax.ppermute(piece, axis, [(source, source + step) for source in range(ha...  5.35 us
    another operation x1, other arithmetic  3.48 us
  transfers between devices with their start and end apart: 27, of which 5 were waited for; matrix products, arithmetic and copies ran while one was open for 27% of the time, Pallas kernels for 0%

profile of v18, /device:TPU:0, one launch (start us, length us, event | category | flops | bytes accessed | tf_op | source)
XLA Modules:
  0.0 135.8 jit_solution(1550390312208193689)
XLA Ops:
  2.4 3.0 %collective-permute-start.2 = (f32[64]{0:T(128)S(1)}, f32[64]{0:T(128)S(1)}, u32[]{:S(2)}, u32[]{:S(2)}) collective-permute-start(f32[64]{0:T(128)S(1)} %get-tuple-element.45), channel_id=1, source_target_pairs={{0,4},{4,0},{8,12},{12,8},{16,20},{20,16},{24,28},{28,24},{1,5},{5... | collective-permute-start | bytes 776 | tf_op jit(solution)/shard_map/ppermute | solution.py:18
  6.3 1.9 %collective-permute-start = (bf16[3,4352]{1,0:T(4,128)(2,1)S(1)}, bf16[3,4352]{1,0:T(4,128)(2,1)S(1)}, u32[]{:S(2)}, u32[]{:S(2)}) collective-permute-start(bf16[3,4352]{1,0:T(4,128)(2,1)S(1)} %slice.155), channel_id=1, source_target_pairs={{0,4},{4,8},{8,12},{12,16},{16,20},{20,24},{24,28},{1,5},{5,9},{9,... | collective-permute-start | bytes 78344 | tf_op jit(solution)/shard_map/ppermute | solution.py:12
  14.1 2.2 %collective-permute-start.4 = (f32[64]{0:T(128)S(1)}, f32[64]{0:T(128)S(1)}, u32[]{:S(2)}, u32[]{:S(2)}) collective-permute-start(f32[64]{0:T(128)S(1)} %add.165), channel_id=1, source_target_pairs={{0,8},{4,12},{8,0},{12,4},{16,24},{20,28},{24,16},{28,20},{1,9},{5... | collective-permute-start | bytes 776 | tf_op jit(solution)/shard_map/ppermute | solution.py:18
  18.4 3.5 %fusion.77 = (bf16[128,4352]{1,0:T(8,128)(2,1)S(1)}, f32[128,4352]{1,0:T(8,128)S(1)}) fusion(f32[4352]{0:T(1024)S(1)} %get-tuple-element.8, bf16[128,4352]{1,0:T(8,128)(2,1)} %param.9, f32[4352]{0:T(1024)S(1)} %get-tuple-element.9, bf16[3,4352]{1,0:T(4,128)(2,1)S(1)} %collective-permute-done, f32[4352]{0:T(1024)S(1)} %get-tuple-element.10, ...), kind=kLoop, calls=%fused_computation.173 | loop fusion | flops 12255232 | bytes 4569600 | tf_op jit(solution)/shard_map/convert.2
  22.5 3.3 %reshape_reshape.3 = bf16[2,64,64,64]{3,2,1,0:T(8,128)(2,1)} reshape(bf16[128,4096]{1,0:T(8,128)(2,1)S(1)} %multiply_convert_fusion.5) | data formatting | bytes 2097152 | tf_op jit(solution)/shard_map/reshape;reshape | solution.py:160
  25.8 3.3 %copy.46 = bf16[2,64,64,64]{1,3,2,0:T(8,128)(2,1)S(1)} copy(bf16[2,64,64,64]{3,2,1,0:T(8,128)(2,1)} %reshape_reshape.3) | data formatting | bytes 2097152 | tf_op jit(solution)/shard_map/reshape;reshape | solution.py:160
  31.7 2.9 %collective-permute-start.1 = (bf16[32,128,64]{1,2,0:T(8,128)(2,1)S(1)}, bf16[32,128,64]{1,2,0:T(8,128)(2,1)S(1)}, u32[]{:S(2)}, u32[]{:S(2)}) collective-permute-start(bf16[32,128,64]{1,2,0:T(8,128)(2,1)S(1)} %get-tuple-element.22), channel_id=1, source_target_pairs={{0,4},{4,0},{8,12},{12,8},{16,20},{20,16},{24,28},{28,24},{1,5},{5... | collective-permute-start | bytes 1572872 | tf_op jit(solution)/shard_map/ppermute | solution.py:18
  34.8 2.4 %slice_bitcast_fusion.4 = (f32[64,128,64]{1,2,0:T(8,128)}, f32[64,128,64]{1,2,0:T(8,128)}) fusion(f32[2,64,128,64]{2,3,1,0:T(8,128)S(1)} %get-tuple-element.74), kind=kLoop, calls=%fused_computation.26 | loop fusion | bytes 8388608 | tf_op jit(solution)/shard_map/mul | solution.py:213
  37.2 10.3 %collective-permute-done.1 = bf16[32,128,64]{1,2,0:T(8,128)(2,1)S(1)} collective-permute-done((bf16[32,128,64]{1,2,0:T(8,128)(2,1)S(1)}, bf16[32,128,64]{1,2,0:T(8,128)(2,1)S(1)}, u32[]{:S(2)}, u32[]{:S(2)}) %collective-permute-start.1) | collective-permute-done | bytes 524320 | tf_op jit(solution)/shard_map/ppermute | solution.py:18
  48.7 1.6 %collective-permute-start.3 = (bf16[32,128,64]{1,2,0:T(8,128)(2,1)}, bf16[32,128,64]{1,2,0:T(8,128)(2,1)}, u32[]{:S(2)}, u32[]{:S(2)}) collective-permute-start(bf16[32,128,64]{1,2,0:T(8,128)(2,1)} %fusion.75), channel_id=1, source_target_pairs={{0,8},{4,12},{8,0},{12,4},{16,24},{20,28},{24,16},{28,20},{1,9},{5... | collective-permute-start | bytes 1572872 | tf_op jit(solution)/shard_map/ppermute | solution.py:18
  50.3 3.3 %reshape.246 = bf16[2,64,64,64]{3,2,1,0:T(8,128)(2,1)} reshape(bf16[128,4096]{1,0:T(8,128)(2,1)S(1)} %copy-done.11) | data formatting | bytes 2097152 | tf_op jit(solution)/shard_map/reshape | solution.py:193
  53.6 3.3 %copy.55 = bf16[2,64,64,64]{1,3,2,0:T(8,128)(2,1)S(1)} copy(bf16[2,64,64,64]{3,2,1,0:T(8,128)(2,1)} %reshape.246) | data formatting | bytes 2097152 | tf_op jit(solution)/shard_map/reshape | solution.py:193
  59.3 3.8 %multiply_reduce_fusion.2 = (f32[2,64]{1,0:T(2,128)S(1)}, f32[2,64,64]{2,1,0:T(8,128)S(1)}) fusion(f32[2,64,64]{2,1,0:T(8,128)S(1)} %fusion.84, f32[2,64,64]{2,1,0:T(8,128)S(1)} %copy.44, pred[64,64]{1,0:T(8,128)(4,1)S(1)} %iota_compare_fusion, f32[2,64]{1,0:T(2,128)S(1)} %copy-done.27, bf16[2,64,64,64]{1,3,2,0:T(8,128)(2,1)S(1)} %copy.55, ...), kind=kOutput, calls=%fused_computation.10 | convolution fusion | flops 72343424 | bytes 2200576 | tf_op jit(solution)/shard_map/vmap(thp,shp->hts)/dot_general | solution.py:35
  63.1 2.3 %fusion.30 = (bf16[32,128,64]{1,2,0:T(8,128)(2,1)S(1)}, bf16[32,128,64]{1,2,0:T(8,128)(2,1)S(1)}, f32[1,32,128,64]{2,3,1,0:T(8,128)S(1)}, f32[1,32,128,64]{2,3,1,0:T(8,128)S(1)}, f32[1,32,128,64]{2,3,1,0:T(8,128)S(1)}) fusion(bf16[32,128,64]{1,2,0:T(8,128)(2,1)} %collective-permute-done.3, f32[32]{0:T(128)S(1)} %copy-done.25, f32[]{:T(128)S(6)} %sub.97, ...), kind=kLoop, calls=%fused_computation.67 | loop fusion | flops 7602176 | bytes 7865232 | tf_op jit(solution)/shard_map/convert_element_type | solution.py:120
  70.9 5.8 %collective-permute-start.14 = (bf16[32,128,64]{1,2,0:T(8,128)(2,1)S(1)}, bf16[32,128,64]{1,2,0:T(8,128)(2,1)S(1)}, u32[]{:S(2)}, u32[]{:S(2)}) collective-permute-start(bf16[32,128,64]{1,2,0:T(8,128)(2,1)S(1)} %get-tuple-element.21), channel_id=1, source_target_pairs={{0,8},{4,12},{8,0},{12,4},{16,24},{20,28},{24,16},{28,20},{1,9},{5... | collective-permute-start | bytes 1572872 | tf_op jit(solution)/shard_map/ppermute | solution.py:18
  79.0 4.8 %collective-permute-done.14 = bf16[32,128,64]{1,2,0:T(8,128)(2,1)S(1)} collective-permute-done((bf16[32,128,64]{1,2,0:T(8,128)(2,1)S(1)}, bf16[32,128,64]{1,2,0:T(8,128)(2,1)S(1)}, u32[]{:S(2)}, u32[]{:S(2)}) %collective-permute-start.14) | collective-permute-done | bytes 524320 | tf_op jit(solution)/shard_map/ppermute | solution.py:18
  95.5 1.7 %add_convert_fusion = bf16[2,64,128,64]{2,3,1,0:T(8,128)(2,1)S(1)} fusion(f32[64,128,64]{1,2,0:T(8,128)S(1)} %get-tuple-element.16, f32[2,64]{1,0:T(2,128)S(1)} %get-tuple-element.49, f32[64,128,64]{1,2,0:T(8,128)S(1)} %get-tuple-element.17, f32[2,64]{1,0:T(2,128)S(1)} %get-tuple-element.50, f32[64,128,64]{1,2,0:T(8,128)S(1)} %get-tuple-element.15, ...), kind=kLoop, calls=%fused_computation.13 | loop fusion | flops 10485760 | bytes 12585472 | tf_op jit(solution)/shard_map/convert_element_type | solution.py:215
  97.2 2.0 %fusion.3 = f32[2,64,128]{2,1,0:T(8,128)S(1)} fusion(bf16[2,64,64,64]{1,3,2,0:T(8,128)(2,1)S(1)} %copy-done.8, bf16[2,64,128,64]{2,3,1,0:T(8,128)(2,1)S(1)} %add_convert_fusion, f32[2,64,64]{1,2,0:T(8,128)S(1)} %copy.50), kind=kOutput, calls=%fused_computation.9 | convolution fusion | flops 136298496 | bytes 3244032 | tf_op jit(solution)/shard_map/chnp,cthp->cthn/dot_general | solution.py:35
  103.6 1.7 %collective-permute-done.24 = f32[8,12,64]{2,0,1:T(8,128)S(1)} collective-permute-done((f32[8,12,64]{2,0,1:T(8,128)S(1)}, f32[8,12,64]{2,0,1:T(8,128)S(1)}, u32[]{:S(2)}, u32[]{:S(2)}) %collective-permute-start.24) | collective-permute-done | bytes 24608 | tf_op jit(solution)/shard_map/ppermute | solution.py:18
  105.3 10.9 %collective-permute-start.25 = (f32[8,12,64]{2,0,1:T(8,128)S(1)}, f32[8,12,64]{2,0,1:T(8,128)S(1)}, u32[]{:S(2)}, u32[]{:S(2)}) collective-permute-start(f32[8,12,64]{2,0,1:T(8,128)S(1)} %fusion.73), channel_id=1, source_target_pairs={{0,8},{4,12},{8,0},{12,4},{16,24},{20,28},{24,16},{28,20},{1,9},{5... | collective-permute-start | bytes 73736 | tf_op jit(solution)/shard_map/ppermute | solution.py:18
  116.2 3.5 %fusion.2 = bf16[2,64,64,64]{1,3,2,0:T(8,128)(2,1)} fusion(bf16[2,64,64,64]{1,3,2,0:T(8,128)(2,1)S(1)} %copy-done.6, f32[2,64,64,64]{3,2,1,0:T(8,128)S(1)} %fusion.6, f32[64]{0:T(128)S(1)} %copy-done.32, f32[2,64]{1,0:T(2,128)S(1)} %copy-done.26, f32[2,64,64]{2,1,0:T(8,128)S(1)} %fusion.84, f32[2,64,64]{2,1,0:T(8,128)S(1)} %copy.44, ...), kind=kOutput, calls=%fused_computation.7 | convolution fusion | flops 72876032 | bytes 4264704 | tf_op jit(solution)/shard_map/vmap(hts,shp->thp)/dot_general | solution.py:35
  119.7 3.3 %copy.51 = bf16[2,64,64,64]{3,2,1,0:T(8,128)(2,1)S(1)} copy(bf16[2,64,64,64]{1,3,2,0:T(8,128)(2,1)} %fusion.2) | data formatting | bytes 2097152 | tf_op jit(solution)/shard_map/convert_element_type | solution.py:236
  123.1 2.5 %reshape.245 = bf16[128,4096]{1,0:T(8,128)(2,1)} reshape(bf16[2,64,64,64]{3,2,1,0:T(8,128)(2,1)S(1)} %copy.51) | data formatting | bytes 2097152 | tf_op jit(solution)/shard_map/reshape | solution.py:237
  125.6 7.5 %collective-permute-start.26 = (f32[8,12,64]{2,0,1:T(8,128)S(1)}, f32[8,12,64]{2,0,1:T(8,128)S(1)}, u32[]{:S(2)}, u32[]{:S(2)}) collective-permute-start(f32[8,12,64]{2,0,1:T(8,128)S(1)} %add.198), channel_id=1, source_target_pairs={{0,16},{4,20},{8,24},{12,28},{16,0},{20,4},{24,8},{28,12},{1,17},{... | collective-permute-start | bytes 73736 | tf_op jit(solution)/shard_map/ppermute | solution.py:18
  (180 shorter events, 43.4 us)
Async XLA Ops:
  2.4 11.6 %collective-permute-start.2 = (f32[64]{0:T(128)S(1)}, f32[64]{0:T(128)S(1)}, u32[]{:S(2)}, u32[]{:S(2)}) collective-permute-start(f32[64]{0:T(128)S(1)} %get-tuple-element.45), channel_id=1, source_target_pairs={{0,4},{4,0},{8,12},{12,8},{16,20},{20,16},{24,28},{28,24},{1,5},{5... | collective-permute-start | bytes 776 | tf_op jit(solution)/shard_map/ppermute | solution.py:18
  6.3 12.1 %collective-permute-start = (bf16[3,4352]{1,0:T(4,128)(2,1)S(1)}, bf16[3,4352]{1,0:T(4,128)(2,1)S(1)}, u32[]{:S(2)}, u32[]{:S(2)}) collective-permute-start(bf16[3,4352]{1,0:T(4,128)(2,1)S(1)} %slice.155), channel_id=1, source_target_pairs={{0,4},{4,8},{8,12},{12,16},{16,20},{20,24},{24,28},{1,5},{5,9},{9,... | collective-permute-start | bytes 78344 | tf_op jit(solution)/shard_map/ppermute | solution.py:12
  14.1 3.7 %collective-permute-start.4 = (f32[64]{0:T(128)S(1)}, f32[64]{0:T(128)S(1)}, u32[]{:S(2)}, u32[]{:S(2)}) collective-permute-start(f32[64]{0:T(128)S(1)} %add.165), channel_id=1, source_target_pairs={{0,8},{4,12},{8,0},{12,4},{16,24},{20,28},{24,16},{28,20},{1,9},{5... | collective-permute-start | bytes 776 | tf_op jit(solution)/shard_map/ppermute | solution.py:18
  31.7 15.8 %collective-permute-start.1 = (bf16[32,128,64]{1,2,0:T(8,128)(2,1)S(1)}, bf16[32,128,64]{1,2,0:T(8,128)(2,1)S(1)}, u32[]{:S(2)}, u32[]{:S(2)}) collective-permute-start(bf16[32,128,64]{1,2,0:T(8,128)(2,1)S(1)} %get-tuple-element.22), channel_id=1, source_target_pairs={{0,4},{4,0},{8,12},{12,8},{16,20},{20,16},{24,28},{28,24},{1,5},{5... | collective-permute-start | bytes 1572872 | tf_op jit(solution)/shard_map/ppermute | solution.py:18
  34.6 28.4 %collective-permute-start.13 = (bf16[32,128,64]{1,2,0:T(8,128)(2,1)}, bf16[32,128,64]{1,2,0:T(8,128)(2,1)S(1)}, u32[]{:S(2)}, u32[]{:S(2)}) collective-permute-start(bf16[32,128,64]{1,2,0:T(8,128)(2,1)} %get-tuple-element.23), channel_id=1, source_target_pairs={{0,4},{4,0},{8,12},{12,8},{16,20},{20,16},{24,28},{28,24},{1,5},{5... | collective-permute-start | bytes 1572872 | tf_op jit(solution)/shard_map/ppermute | solution.py:18
  48.7 14.4 %collective-permute-start.3 = (bf16[32,128,64]{1,2,0:T(8,128)(2,1)}, bf16[32,128,64]{1,2,0:T(8,128)(2,1)}, u32[]{:S(2)}, u32[]{:S(2)}) collective-permute-start(bf16[32,128,64]{1,2,0:T(8,128)(2,1)} %fusion.75), channel_id=1, source_target_pairs={{0,8},{4,12},{8,0},{12,4},{16,24},{20,28},{24,16},{28,20},{1,9},{5... | collective-permute-start | bytes 1572872 | tf_op jit(solution)/shard_map/ppermute | solution.py:18
  65.5 3.6 %collective-permute-start.5 = (bf16[8,128,64]{1,2,0:T(8,128)(2,1)S(1)}, bf16[8,128,64]{1,2,0:T(8,128)(2,1)S(1)}, u32[]{:S(2)}, u32[]{:S(2)}) collective-permute-start(bf16[8,128,64]{1,2,0:T(8,128)(2,1)S(1)} %get-tuple-element.29), channel_id=1, source_target_pairs={{8,16},{12,20},{9,17},{13,21},{10,18},{14,22},{11,19},{15,23}} | collective-permute-start | bytes 393224 | tf_op jit(solution)/shard_map/ppermute | solution.py:105
  67.1 9.6 %collective-permute-start.11 = (bf16[8,128,64]{1,2,0:T(8,128)(2,1)S(1)}, bf16[8,128,64]{1,2,0:T(8,128)(2,1)S(1)}, u32[]{:S(2)}, u32[]{:S(2)}) collective-permute-start(bf16[8,128,64]{1,2,0:T(8,128)(2,1)S(1)} %get-tuple-element.30), channel_id=1, source_target_pairs={{8,16},{12,20},{9,17},{13,21},{10,18},{14,22},{11,19},{15,23}} | collective-permute-start | bytes 393224 | tf_op jit(solution)/shard_map/ppermute | solution.py:105
  67.8 9.6 %collective-permute-start.9 = (bf16[8,128,64]{1,2,0:T(8,128)(2,1)S(1)}, bf16[8,128,64]{1,2,0:T(8,128)(2,1)S(1)}, u32[]{:S(2)}, u32[]{:S(2)}) collective-permute-start(bf16[8,128,64]{1,2,0:T(8,128)(2,1)S(1)} %get-tuple-element.31), channel_id=1, source_target_pairs={{8,16},{12,20},{9,17},{13,21},{10,18},{14,22},{11,19},{15,23}} | collective-permute-start | bytes 393224 | tf_op jit(solution)/shard_map/ppermute | solution.py:105
  68.5 9.6 %collective-permute-start.7 = (bf16[8,128,64]{1,2,0:T(8,128)(2,1)S(1)}, bf16[8,128,64]{1,2,0:T(8,128)(2,1)S(1)}, u32[]{:S(2)}, u32[]{:S(2)}) collective-permute-start(bf16[8,128,64]{1,2,0:T(8,128)(2,1)S(1)} %get-tuple-element.32), channel_id=1, source_target_pairs={{8,16},{12,20},{9,17},{13,21},{10,18},{14,22},{11,19},{15,23}} | collective-permute-start | bytes 393224 | tf_op jit(solution)/shard_map/ppermute | solution.py:105
  69.2 9.8 %collective-permute-start.6 = (bf16[8,128,64]{1,2,0:T(8,128)(2,1)S(1)}, bf16[8,128,64]{1,2,0:T(8,128)(2,1)S(1)}, u32[]{:S(2)}, u32[]{:S(2)}) collective-permute-start(bf16[8,128,64]{1,2,0:T(8,128)(2,1)S(1)} %collective-permute-done.5), channel_id=1, source_target_pairs={{16,24},{20,28},{17,25},{21,29},{18,26},{22,30},{19,27},{23,31}} | collective-permute-start | bytes 393224 | tf_op jit(solution)/shard_map/ppermute | solution.py:106
  70.9 13.0 %collective-permute-start.14 = (bf16[32,128,64]{1,2,0:T(8,128)(2,1)S(1)}, bf16[32,128,64]{1,2,0:T(8,128)(2,1)S(1)}, u32[]{:S(2)}, u32[]{:S(2)}) collective-permute-start(bf16[32,128,64]{1,2,0:T(8,128)(2,1)S(1)} %get-tuple-element.21), channel_id=1, source_target_pairs={{0,8},{4,12},{8,0},{12,4},{16,24},{20,28},{24,16},{28,20},{1,9},{5... | collective-permute-start | bytes 1572872 | tf_op jit(solution)/shard_map/ppermute | solution.py:18
  76.7 2.3 %collective-permute-start.12 = (bf16[8,128,64]{1,2,0:T(8,128)(2,1)S(1)}, bf16[8,128,64]{1,2,0:T(8,128)(2,1)S(1)}, u32[]{:S(2)}, u32[]{:S(2)}) collective-permute-start(bf16[8,128,64]{1,2,0:T(8,128)(2,1)S(1)} %collective-permute-done.11), channel_id=1, source_target_pairs={{16,24},{20,28},{17,25},{21,29},{18,26},{22,30},{19,27},{23,31}} | collective-permute-start | bytes 393224 | tf_op jit(solution)/shard_map/ppermute | solution.py:106
  78.1 7.3 %collective-permute-start.8 = (bf16[8,128,64]{1,2,0:T(8,128)(2,1)S(1)}, bf16[8,128,64]{1,2,0:T(8,128)(2,1)S(1)}, u32[]{:S(2)}, u32[]{:S(2)}) collective-permute-start(bf16[8,128,64]{1,2,0:T(8,128)(2,1)S(1)} %collective-permute-done.7), channel_id=1, source_target_pairs={{16,24},{20,28},{17,25},{21,29},{18,26},{22,30},{19,27},{23,31}} | collective-permute-start | bytes 393224 | tf_op jit(solution)/shard_map/ppermute | solution.py:106
  84.7 2.7 %collective-permute-start.15 = (bf16[8,128,64]{1,2,0:T(8,128)(2,1)S(1)}, bf16[8,128,64]{1,2,0:T(8,128)(2,1)S(1)}, u32[]{:S(2)}, u32[]{:S(2)}) collective-permute-start(bf16[8,128,64]{1,2,0:T(8,128)(2,1)S(1)} %get-tuple-element.35), channel_id=1, source_target_pairs={{8,16},{12,20},{9,17},{13,21},{10,18},{14,22},{11,19},{15,23}} | collective-permute-start | bytes 393224 | tf_op jit(solution)/shard_map/ppermute | solution.py:105
  85.4 2.9 %collective-permute-start.21 = (bf16[8,128,64]{1,2,0:T(8,128)(2,1)S(1)}, bf16[8,128,64]{1,2,0:T(8,128)(2,1)S(1)}, u32[]{:S(2)}, u32[]{:S(2)}) collective-permute-start(bf16[8,128,64]{1,2,0:T(8,128)(2,1)S(1)} %get-tuple-element.36), channel_id=1, source_target_pairs={{8,16},{12,20},{9,17},{13,21},{10,18},{14,22},{11,19},{15,23}} | collective-permute-start | bytes 393224 | tf_op jit(solution)/shard_map/ppermute | solution.py:105
  86.1 2.9 %collective-permute-start.19 = (bf16[8,128,64]{1,2,0:T(8,128)(2,1)S(1)}, bf16[8,128,64]{1,2,0:T(8,128)(2,1)S(1)}, u32[]{:S(2)}, u32[]{:S(2)}) collective-permute-start(bf16[8,128,64]{1,2,0:T(8,128)(2,1)S(1)} %get-tuple-element.37), channel_id=1, source_target_pairs={{8,16},{12,20},{9,17},{13,21},{10,18},{14,22},{11,19},{15,23}} | collective-permute-start | bytes 393224 | tf_op jit(solution)/shard_map/ppermute | solution.py:105
  86.8 2.9 %collective-permute-start.17 = (bf16[8,128,64]{1,2,0:T(8,128)(2,1)S(1)}, bf16[8,128,64]{1,2,0:T(8,128)(2,1)S(1)}, u32[]{:S(2)}, u32[]{:S(2)}) collective-permute-start(bf16[8,128,64]{1,2,0:T(8,128)(2,1)S(1)} %get-tuple-element.38), channel_id=1, source_target_pairs={{8,16},{12,20},{9,17},{13,21},{10,18},{14,22},{11,19},{15,23}} | collective-permute-start | bytes 393224 | tf_op jit(solution)/shard_map/ppermute | solution.py:105
  87.4 2.9 %collective-permute-start.16 = (bf16[8,128,64]{1,2,0:T(8,128)(2,1)S(1)}, bf16[8,128,64]{1,2,0:T(8,128)(2,1)S(1)}, u32[]{:S(2)}, u32[]{:S(2)}) collective-permute-start(bf16[8,128,64]{1,2,0:T(8,128)(2,1)S(1)} %collective-permute-done.15), channel_id=1, source_target_pairs={{16,24},{20,28},{17,25},{21,29},{18,26},{22,30},{19,27},{23,31}} | collective-permute-start | bytes 393224 | tf_op jit(solution)/shard_map/ppermute | solution.py:106
  88.3 2.1 %collective-permute-start.22 = (bf16[8,128,64]{1,2,0:T(8,128)(2,1)S(1)}, bf16[8,128,64]{1,2,0:T(8,128)(2,1)S(1)}, u32[]{:S(2)}, u32[]{:S(2)}) collective-permute-start(bf16[8,128,64]{1,2,0:T(8,128)(2,1)S(1)} %collective-permute-done.21), channel_id=1, source_target_pairs={{16,24},{20,28},{17,25},{21,29},{18,26},{22,30},{19,27},{23,31}} | collective-permute-start | bytes 393224 | tf_op jit(solution)/shard_map/ppermute | solution.py:106
  101.1 4.2 %collective-permute-start.24 = (f32[8,12,64]{2,0,1:T(8,128)S(1)}, f32[8,12,64]{2,0,1:T(8,128)S(1)}, u32[]{:S(2)}, u32[]{:S(2)}) collective-permute-start(f32[8,12,64]{2,0,1:T(8,128)S(1)} %pad_maximum_fusion.2), channel_id=1, source_target_pairs={{0,4},{4,0},{8,12},{12,8},{16,20},{20,16},{24,28},{28,24},{1,5},{5... | collective-permute-start | bytes 73736 | tf_op jit(solution)/shard_map/ppermute | solution.py:18
  102.3 30.8 %collective-permute-start.23 = (f32[3,128]{1,0:T(4,128)S(1)}, f32[3,128]{1,0:T(4,128)S(1)}, u32[]{:S(2)}, u32[]{:S(2)}) collective-permute-start(f32[3,128]{1,0:T(4,128)S(1)} %slice.235), channel_id=1, source_target_pairs={{4,0},{8,4},{12,8},{16,12},{20,16},{24,20},{28,24},{5,1},{9,5},{13... | collective-permute-start | bytes 4616 | tf_op jit(solution)/shard_map/ppermute | solution.py:12
  105.3 20.2 %collective-permute-start.25 = (f32[8,12,64]{2,0,1:T(8,128)S(1)}, f32[8,12,64]{2,0,1:T(8,128)S(1)}, u32[]{:S(2)}, u32[]{:S(2)}) collective-permute-start(f32[8,12,64]{2,0,1:T(8,128)S(1)} %fusion.73), channel_id=1, source_target_pairs={{0,8},{4,12},{8,0},{12,4},{16,24},{20,28},{24,16},{28,20},{1,9},{5... | collective-permute-start | bytes 73736 | tf_op jit(solution)/shard_map/ppermute | solution.py:18
  125.6 9.6 %collective-permute-start.26 = (f32[8,12,64]{2,0,1:T(8,128)S(1)}, f32[8,12,64]{2,0,1:T(8,128)S(1)}, u32[]{:S(2)}, u32[]{:S(2)}) collective-permute-start(f32[8,12,64]{2,0,1:T(8,128)S(1)} %add.198), channel_id=1, source_target_pairs={{0,16},{4,20},{8,24},{12,28},{16,0},{20,4},{24,8},{28,12},{1,17},{... | collective-permute-start | bytes 73736 | tf_op jit(solution)/shard_map/ppermute | solution.py:18
  (39 other events, 271.7 us)

commit v19 on v16

--- a/solution.py
+++ b/solution.py
@@ -26,9 +26,19 @@
 
 
 def all_sum(value, axis):
-    for distance in range(lax.axis_size(axis).bit_length() - 1):
-        value = value + from_partner(value, axis, distance)
-    return value
+    count = lax.axis_size(axis)
+    if count > 8:
+        for distance in range(count.bit_length() - 1):
+            value = value + from_partner(value, axis, distance)
+        return value
+    received = [value] + [
+        lax.ppermute(value, axis, [(source, (source + shift) % count) for source in range(count)])
+        for shift in range(1, count)
+    ]
+    stacked = jnp.stack(received, axis=0)
+    myself = lax.axis_index(axis)
+    order = (myself - jnp.arange(count, dtype=jnp.int32)) % count
+    return jnp.sum(jnp.take(stacked, order, axis=0), axis=0)
 
 
 def contract(form, left, right):

time: 130 us -> 146 us (1.12)
  waiting for transfers between devices: 18.1 us -> 26.3 us
  starting transfers between devices: 43.6 us -> 51.1 us
    ppermute x0 -> x7, starting transfers between devices: none -> 27.8 us  [all_sum(): lax.ppermute(value, axis, [(source, (source + shift) % count) for source...]
    ppermute x9 -> x6, starting transfers between devices: 34.7 us -> 14.3 us  [from_partner(): return lax.ppermute(value, axis, pairs)]
    ppermute x0 -> x7, waiting for transfers between devices: none -> 11.3 us  [all_sum(): lax.ppermute(value, axis, [(source, (source + shift) % count) for source...]
    ppermute x9 -> x6, waiting for transfers between devices: 18.1 us -> 14.9 us  [from_partner(): return lax.ppermute(value, axis, pairs)]
  transfers between devices with their start and end apart: 19 -> 23, of which waited for: 5 -> 6; matrix products, arithmetic and copies ran while one was open for 28% -> 29% of each run, Pallas kernels for 0% -> 0%
where the time goes in v19:
time: 146 us; the launch traced here: 145 us
  starting transfers between devices  51.1 us (35%)
  local copies, waits for them, and re-layouts  30.7 us (21%)
  waiting for transfers between devices  26.3 us (18%)
  other arithmetic  20.3 us (14%)
  matrix products  15.5 us (11%)
  between operations  1.61 us (1%)
    ppermute x7, starting transfers between devices, all_sum(): lax.ppermute(value, axis, [(source, (source + shift) % count) for source...  27.8 us
    ppermute x6, waiting for transfers between devices, from_partner(): return lax.ppermute(value, axis, pairs)  14.9 us
    ppermute x6, starting transfers between devices, from_partner(): return lax.ppermute(value, axis, pairs)  14.3 us
    dot_general x6, matrix products, contract(): return jnp.einsum(form, left, right, preferred_element_type=jnp.float32)  13 us
    ppermute x7, waiting for transfers between devices, all_sum(): lax.ppermute(value, axis, [(source, (source + shift) % count) for source...  11.3 us
    reshape x2, local copies, waits for them, and re-layouts, local(): grad_groups = late_cotangent.reshape(groups, group_len, heads, head_dim)  6.6 us
    another operation x2, local copies, waits for them, and re-layouts, local(): x_groups = x_act.reshape(groups, group_len, heads, head_dim)  6.57 us
    another operation x1, other arithmetic  3.48 us
  transfers between devices with their start and end apart: 23, of which 6 were waited for; matrix products, arithmetic and copies ran while one was open for 29% of the time, Pallas kernels for 0%

profile of v19, /device:TPU:0, one launch (start us, length us, event | category | flops | bytes accessed | tf_op | source)
XLA Modules:
  0.0 145.5 jit_solution(13086500673090416228)
XLA Ops:
  2.4 3.0 %collective-permute-start.2 = (f32[64]{0:T(128)S(1)}, f32[64]{0:T(128)S(1)}, u32[]{:S(2)}, u32[]{:S(2)}) collective-permute-start(f32[64]{0:T(128)S(1)} %get-tuple-element.41), channel_id=1, source_target_pairs={{0,4},{4,0},{8,12},{12,8},{16,20},{20,16},{24,28},{28,24},{1,5},{5... | collective-permute-start | bytes 776 | tf_op jit(solution)/shard_map/ppermute | solution.py:18
  14.6 2.2 %collective-permute-start.4 = (f32[64]{0:T(128)S(1)}, f32[64]{0:T(128)S(1)}, u32[]{:S(2)}, u32[]{:S(2)}) collective-permute-start(f32[64]{0:T(128)S(1)} %add.176), channel_id=1, source_target_pairs={{0,8},{4,12},{8,0},{12,4},{16,24},{20,28},{24,16},{28,20},{1,9},{5... | collective-permute-start | bytes 776 | tf_op jit(solution)/shard_map/ppermute | solution.py:18
  18.9 3.5 %fusion.79 = (bf16[128,4352]{1,0:T(8,128)(2,1)S(1)}, f32[128,4352]{1,0:T(8,128)S(1)}) fusion(f32[4352]{0:T(1024)S(1)} %get-tuple-element.8, bf16[128,4352]{1,0:T(8,128)(2,1)} %param.9, f32[4352]{0:T(1024)S(1)} %get-tuple-element.9, bf16[3,4352]{1,0:T(4,128)(2,1)S(1)} %collective-permute-done, f32[4352]{0:T(1024)S(1)} %get-tuple-element.10, ...), kind=kLoop, calls=%fused_computation.191 | loop fusion | flops 12255232 | bytes 4569600 | tf_op jit(solution)/shard_map/convert.2
  23.0 3.3 %reshape_reshape.3 = bf16[2,64,64,64]{3,2,1,0:T(8,128)(2,1)} reshape(bf16[128,4096]{1,0:T(8,128)(2,1)S(1)} %multiply_convert_fusion.5) | data formatting | bytes 2097152 | tf_op jit(solution)/shard_map/reshape;reshape | solution.py:170
  26.3 3.3 %copy.46 = bf16[2,64,64,64]{1,3,2,0:T(8,128)(2,1)S(1)} copy(bf16[2,64,64,64]{3,2,1,0:T(8,128)(2,1)} %reshape_reshape.3) | data formatting | bytes 2097152 | tf_op jit(solution)/shard_map/reshape;reshape | solution.py:170
  32.2 2.9 %collective-permute-start.1 = (bf16[32,128,64]{1,2,0:T(8,128)(2,1)S(1)}, bf16[32,128,64]{1,2,0:T(8,128)(2,1)S(1)}, u32[]{:S(2)}, u32[]{:S(2)}) collective-permute-start(bf16[32,128,64]{1,2,0:T(8,128)(2,1)S(1)} %get-tuple-element.22), channel_id=1, source_target_pairs={{0,4},{4,0},{8,12},{12,8},{16,20},{20,16},{24,28},{28,24},{1,5},{5... | collective-permute-start | bytes 1572872 | tf_op jit(solution)/shard_map/ppermute | solution.py:18
  35.3 2.4 %slice_bitcast_fusion.4 = (f32[64,128,64]{1,2,0:T(8,128)}, f32[64,128,64]{1,2,0:T(8,128)}) fusion(f32[2,64,128,64]{2,3,1,0:T(8,128)S(1)} %get-tuple-element.70), kind=kLoop, calls=%fused_computation.27 | loop fusion | bytes 8388608 | tf_op jit(solution)/shard_map/mul | solution.py:223
  37.7 10.3 %collective-permute-done.1 = bf16[32,128,64]{1,2,0:T(8,128)(2,1)S(1)} collective-permute-done((bf16[32,128,64]{1,2,0:T(8,128)(2,1)S(1)}, bf16[32,128,64]{1,2,0:T(8,128)(2,1)S(1)}, u32[]{:S(2)}, u32[]{:S(2)}) %collective-permute-start.1) | collective-permute-done | bytes 524320 | tf_op jit(solution)/shard_map/ppermute | solution.py:18
  50.7 3.3 %reshape.248 = bf16[2,64,64,64]{3,2,1,0:T(8,128)(2,1)} reshape(bf16[128,4096]{1,0:T(8,128)(2,1)S(1)} %copy-done.11) | data formatting | bytes 2097152 | tf_op jit(solution)/shard_map/reshape | solution.py:203
  54.0 3.3 %copy.55 = bf16[2,64,64,64]{1,3,2,0:T(8,128)(2,1)S(1)} copy(bf16[2,64,64,64]{3,2,1,0:T(8,128)(2,1)} %reshape.248) | data formatting | bytes 2097152 | tf_op jit(solution)/shard_map/reshape | solution.py:203
  59.7 3.8 %multiply_reduce_fusion.2 = (f32[2,64]{1,0:T(2,128)S(1)}, f32[2,64,64]{2,1,0:T(8,128)S(1)}) fusion(f32[2,64,64]{2,1,0:T(8,128)S(1)} %fusion.86, f32[2,64,64]{2,1,0:T(8,128)S(1)} %copy.44, pred[64,64]{1,0:T(8,128)(4,1)S(1)} %iota_compare_fusion, f32[2,64]{1,0:T(2,128)S(1)} %copy-done.29, bf16[2,64,64,64]{1,3,2,0:T(8,128)(2,1)S(1)} %copy.55, ...), kind=kOutput, calls=%fused_computation.11 | convolution fusion | flops 72343424 | bytes 2200576 | tf_op jit(solution)/shard_map/vmap(thp,shp->hts)/dot_general | solution.py:45
  63.6 2.3 %fusion.30 = (bf16[32,128,64]{1,2,0:T(8,128)(2,1)S(1)}, bf16[32,128,64]{1,2,0:T(8,128)(2,1)S(1)}, f32[1,32,128,64]{2,3,1,0:T(8,128)S(1)}, f32[1,32,128,64]{2,3,1,0:T(8,128)S(1)}, f32[1,32,128,64]{2,3,1,0:T(8,128)S(1)}) fusion(bf16[32,128,64]{1,2,0:T(8,128)(2,1)} %collective-permute-done.3, f32[32]{0:T(128)S(1)} %copy-done.27, f32[]{:T(128)S(6)} %sub.116, ...), kind=kLoop, calls=%fused_computation.68 | loop fusion | flops 7602176 | bytes 7865232 | tf_op jit(solution)/shard_map/convert_element_type | solution.py:130
  67.4 4.6 %collective-permute-start.10 = (bf16[32,128,64]{1,2,0:T(8,128)(2,1)S(1)}, bf16[32,128,64]{1,2,0:T(8,128)(2,1)S(1)}, u32[]{:S(2)}, u32[]{:S(2)}) collective-permute-start(bf16[32,128,64]{1,2,0:T(8,128)(2,1)S(1)} %get-tuple-element.21), channel_id=1, source_target_pairs={{0,8},{4,12},{8,0},{12,4},{16,24},{20,28},{24,16},{28,20},{1,9},{5... | collective-permute-start | bytes 1572872 | tf_op jit(solution)/shard_map/ppermute | solution.py:18
  75.2 3.9 %collective-permute-done.10 = bf16[32,128,64]{1,2,0:T(8,128)(2,1)S(1)} collective-permute-done((bf16[32,128,64]{1,2,0:T(8,128)(2,1)S(1)}, bf16[32,128,64]{1,2,0:T(8,128)(2,1)S(1)}, u32[]{:S(2)}, u32[]{:S(2)}) %collective-permute-start.10) | collective-permute-done | bytes 524320 | tf_op jit(solution)/shard_map/ppermute | solution.py:18
  88.1 18.7 %collective-permute-start.21 = (f32[8,12,64]{2,0,1:T(8,128)S(1)}, f32[8,12,64]{2,0,1:T(8,128)S(1)}, u32[]{:S(2)}, u32[]{:S(2)}) collective-permute-start(f32[8,12,64]{2,0,1:T(8,128)S(1)} %pad_maximum_fusion.2), channel_id=1, source_target_pairs={{0,24},{4,28},{8,0},{12,4},{16,8},{20,12},{24,16},{28,20},{1,25},{... | collective-permute-start | bytes 73736 | tf_op jit(solution)/shard_map/ppermute | solution.py:35
  106.8 4.2 %collective-permute-start.19 = (f32[8,12,64]{2,0,1:T(8,128)S(1)}, f32[8,12,64]{2,0,1:T(8,128)S(1)}, u32[]{:S(2)}, u32[]{:S(2)}) collective-permute-start(f32[8,12,64]{2,0,1:T(8,128)S(1)} %pad_maximum_fusion.2), channel_id=1, source_target_pairs={{0,16},{4,20},{8,24},{12,28},{16,0},{20,4},{24,8},{28,12},{1,17},{... | collective-permute-start | bytes 73736 | tf_op jit(solution)/shard_map/ppermute | solution.py:35
  112.7 2.0 %fusion.3 = f32[2,64,128]{2,1,0:T(8,128)S(1)} fusion(bf16[2,64,64,64]{1,3,2,0:T(8,128)(2,1)S(1)} %copy-done.8, bf16[2,64,128,64]{2,3,1,0:T(8,128)(2,1)S(1)} %add_convert_fusion, f32[2,64,64]{1,2,0:T(8,128)S(1)} %copy.50), kind=kOutput, calls=%fused_computation.10 | convolution fusion | flops 136298496 | bytes 3244032 | tf_op jit(solution)/shard_map/chnp,cthp->cthn/dot_general | solution.py:45
  117.8 3.5 %fusion.2 = bf16[2,64,64,64]{1,3,2,0:T(8,128)(2,1)} fusion(bf16[2,64,64,64]{1,3,2,0:T(8,128)(2,1)S(1)} %copy-done.6, f32[2,64,64,64]{3,2,1,0:T(8,128)S(1)} %fusion.6, f32[64]{0:T(128)S(1)} %copy-done.34, f32[2,64]{1,0:T(2,128)S(1)} %copy-done.28, f32[2,64,64]{2,1,0:T(8,128)S(1)} %fusion.86, f32[2,64,64]{2,1,0:T(8,128)S(1)} %copy.44, ...), kind=kOutput, calls=%fused_computation.8 | convolution fusion | flops 72876032 | bytes 4264704 | tf_op jit(solution)/shard_map/vmap(hts,shp->thp)/dot_general | solution.py:45
  121.2 3.3 %copy.51 = bf16[2,64,64,64]{3,2,1,0:T(8,128)(2,1)S(1)} copy(bf16[2,64,64,64]{1,3,2,0:T(8,128)(2,1)} %fusion.2) | data formatting | bytes 2097152 | tf_op jit(solution)/shard_map/convert_element_type | solution.py:246
  124.6 2.5 %reshape.247 = bf16[128,4096]{1,0:T(8,128)(2,1)} reshape(bf16[2,64,64,64]{3,2,1,0:T(8,128)(2,1)S(1)} %copy.51) | data formatting | bytes 2097152 | tf_op jit(solution)/shard_map/reshape | solution.py:247
  127.1 2.6 %collective-permute-start.16 = (f32[8,12,64]{2,0,1:T(8,128)S(1)}, f32[8,12,64]{2,0,1:T(8,128)S(1)}, u32[]{:S(2)}, u32[]{:S(2)}) collective-permute-start(f32[8,12,64]{2,0,1:T(8,128)S(1)} %pad_maximum_fusion.2), channel_id=1, source_target_pairs={{0,4},{4,8},{8,12},{12,16},{16,20},{20,24},{24,28},{28,0},{1,5},{5... | collective-permute-start | bytes 73736 | tf_op jit(solution)/shard_map/ppermute | solution.py:35
  130.4 3.5 %collective-permute-done.16 = f32[8,12,64]{2,0,1:T(8,128)S(1)} collective-permute-done((f32[8,12,64]{2,0,1:T(8,128)S(1)}, f32[8,12,64]{2,0,1:T(8,128)S(1)}, u32[]{:S(2)}, u32[]{:S(2)}) %collective-permute-start.16) | collective-permute-done | bytes 24608 | tf_op jit(solution)/shard_map/ppermute | solution.py:35
  135.6 4.4 %collective-permute-done.17 = f32[8,12,64]{2,0,1:T(8,128)S(1)} collective-permute-done((f32[8,12,64]{2,0,1:T(8,128)S(1)}, f32[8,12,64]{2,0,1:T(8,128)S(1)}, u32[]{:S(2)}, u32[]{:S(2)}) %collective-permute-start.17) | collective-permute-done | bytes 24608 | tf_op jit(solution)/shard_map/ppermute | solution.py:35
  140.7 3.4 %collective-permute-done.22 = f32[8,12,64]{2,0,1:T(8,128)S(1)} collective-permute-done((f32[8,12,64]{2,0,1:T(8,128)S(1)}, f32[8,12,64]{2,0,1:T(8,128)S(1)}, u32[]{:S(2)}, u32[]{:S(2)}) %collective-permute-start.22) | collective-permute-done | bytes 24608 | tf_op jit(solution)/shard_map/ppermute | solution.py:35
  (183 shorter events, 43.8 us)
Async XLA Ops:
  2.4 12.1 %collective-permute-start.2 = (f32[64]{0:T(128)S(1)}, f32[64]{0:T(128)S(1)}, u32[]{:S(2)}, u32[]{:S(2)}) collective-permute-start(f32[64]{0:T(128)S(1)} %get-tuple-element.41), channel_id=1, source_target_pairs={{0,4},{4,0},{8,12},{12,8},{16,20},{20,16},{24,28},{28,24},{1,5},{5... | collective-permute-start | bytes 776 | tf_op jit(solution)/shard_map/ppermute | solution.py:18
  6.3 12.6 %collective-permute-start = (bf16[3,4352]{1,0:T(4,128)(2,1)S(1)}, bf16[3,4352]{1,0:T(4,128)(2,1)S(1)}, u32[]{:S(2)}, u32[]{:S(2)}) collective-permute-start(bf16[3,4352]{1,0:T(4,128)(2,1)S(1)} %slice.143), channel_id=1, source_target_pairs={{0,4},{4,8},{8,12},{12,16},{16,20},{20,24},{24,28},{1,5},{5,9},{9,... | collective-permute-start | bytes 78344 | tf_op jit(solution)/shard_map/ppermute | solution.py:12
  14.6 3.7 %collective-permute-start.4 = (f32[64]{0:T(128)S(1)}, f32[64]{0:T(128)S(1)}, u32[]{:S(2)}, u32[]{:S(2)}) collective-permute-start(f32[64]{0:T(128)S(1)} %add.176), channel_id=1, source_target_pairs={{0,8},{4,12},{8,0},{12,4},{16,24},{20,28},{24,16},{28,20},{1,9},{5... | collective-permute-start | bytes 776 | tf_op jit(solution)/shard_map/ppermute | solution.py:18
  32.2 15.8 %collective-permute-start.1 = (bf16[32,128,64]{1,2,0:T(8,128)(2,1)S(1)}, bf16[32,128,64]{1,2,0:T(8,128)(2,1)S(1)}, u32[]{:S(2)}, u32[]{:S(2)}) collective-permute-start(bf16[32,128,64]{1,2,0:T(8,128)(2,1)S(1)} %get-tuple-element.22), channel_id=1, source_target_pairs={{0,4},{4,0},{8,12},{12,8},{16,20},{20,16},{24,28},{28,24},{1,5},{5... | collective-permute-start | bytes 1572872 | tf_op jit(solution)/shard_map/ppermute | solution.py:18
  35.1 28.4 %collective-permute-start.9 = (bf16[32,128,64]{1,2,0:T(8,128)(2,1)}, bf16[32,128,64]{1,2,0:T(8,128)(2,1)S(1)}, u32[]{:S(2)}, u32[]{:S(2)}) collective-permute-start(bf16[32,128,64]{1,2,0:T(8,128)(2,1)} %get-tuple-element.23), channel_id=1, source_target_pairs={{0,4},{4,0},{8,12},{12,8},{16,20},{20,16},{24,28},{28,24},{1,5},{5... | collective-permute-start | bytes 1572872 | tf_op jit(solution)/shard_map/ppermute | solution.py:18
  49.2 14.3 %collective-permute-start.3 = (bf16[32,128,64]{1,2,0:T(8,128)(2,1)}, bf16[32,128,64]{1,2,0:T(8,128)(2,1)}, u32[]{:S(2)}, u32[]{:S(2)}) collective-permute-start(bf16[32,128,64]{1,2,0:T(8,128)(2,1)} %fusion.77), channel_id=1, source_target_pairs={{0,8},{4,12},{8,0},{12,4},{16,24},{20,28},{24,16},{28,20},{1,9},{5... | collective-permute-start | bytes 1572872 | tf_op jit(solution)/shard_map/ppermute | solution.py:18
  65.9 7.8 %collective-permute-start.5 = (bf16[16,128,64]{1,2,0:T(8,128)(2,1)S(1)}, bf16[16,128,64]{1,2,0:T(8,128)(2,1)S(1)}, u32[]{:S(2)}, u32[]{:S(2)}) collective-permute-start(bf16[16,128,64]{1,2,0:T(8,128)(2,1)S(1)} %get-tuple-element.29), channel_id=1, source_target_pairs={{8,16},{12,20},{9,17},{13,21},{10,18},{14,22},{11,19},{15,23}} | collective-permute-start | bytes 786440 | tf_op jit(solution)/shard_map/ppermute | solution.py:115
  66.6 7.8 %collective-permute-start.7 = (bf16[16,128,64]{1,2,0:T(8,128)(2,1)S(1)}, bf16[16,128,64]{1,2,0:T(8,128)(2,1)S(1)}, u32[]{:S(2)}, u32[]{:S(2)}) collective-permute-start(bf16[16,128,64]{1,2,0:T(8,128)(2,1)S(1)} %get-tuple-element.30), channel_id=1, source_target_pairs={{8,16},{12,20},{9,17},{13,21},{10,18},{14,22},{11,19},{15,23}} | collective-permute-start | bytes 786440 | tf_op jit(solution)/shard_map/ppermute | solution.py:115
  67.4 11.8 %collective-permute-start.10 = (bf16[32,128,64]{1,2,0:T(8,128)(2,1)S(1)}, bf16[32,128,64]{1,2,0:T(8,128)(2,1)S(1)}, u32[]{:S(2)}, u32[]{:S(2)}) collective-permute-start(bf16[32,128,64]{1,2,0:T(8,128)(2,1)S(1)} %get-tuple-element.21), channel_id=1, source_target_pairs={{0,8},{4,12},{8,0},{12,4},{16,24},{20,28},{24,16},{28,20},{1,9},{5... | collective-permute-start | bytes 1572872 | tf_op jit(solution)/shard_map/ppermute | solution.py:18
  73.7 8.0 %collective-permute-start.6 = (bf16[16,128,64]{1,2,0:T(8,128)(2,1)S(1)}, bf16[16,128,64]{1,2,0:T(8,128)(2,1)S(1)}, u32[]{:S(2)}, u32[]{:S(2)}) collective-permute-start(bf16[16,128,64]{1,2,0:T(8,128)(2,1)S(1)} %collective-permute-done.5), channel_id=1, source_target_pairs={{16,24},{20,28},{17,25},{21,29},{18,26},{22,30},{19,27},{23,31}} | collective-permute-start | bytes 786440 | tf_op jit(solution)/shard_map/ppermute | solution.py:116
  74.4 8.1 %collective-permute-start.8 = (bf16[16,128,64]{1,2,0:T(8,128)(2,1)S(1)}, bf16[16,128,64]{1,2,0:T(8,128)(2,1)S(1)}, u32[]{:S(2)}, u32[]{:S(2)}) collective-permute-start(bf16[16,128,64]{1,2,0:T(8,128)(2,1)S(1)} %collective-permute-done.7), channel_id=1, source_target_pairs={{16,24},{20,28},{17,25},{21,29},{18,26},{22,30},{19,27},{23,31}} | collective-permute-start | bytes 786440 | tf_op jit(solution)/shard_map/ppermute | solution.py:116
  80.0 1.8 %collective-permute-start.11 = (bf16[16,128,64]{1,2,0:T(8,128)(2,1)S(1)}, bf16[16,128,64]{1,2,0:T(8,128)(2,1)S(1)}, u32[]{:S(2)}, u32[]{:S(2)}) collective-permute-start(bf16[16,128,64]{1,2,0:T(8,128)(2,1)S(1)} %get-tuple-element.33), channel_id=1, source_target_pairs={{8,16},{12,20},{9,17},{13,21},{10,18},{14,22},{11,19},{15,23}} | collective-permute-start | bytes 786440 | tf_op jit(solution)/shard_map/ppermute | solution.py:115
  80.9 1.6 %collective-permute-start.13 = (bf16[16,128,64]{1,2,0:T(8,128)(2,1)S(1)}, bf16[16,128,64]{1,2,0:T(8,128)(2,1)S(1)}, u32[]{:S(2)}, u32[]{:S(2)}) collective-permute-start(bf16[16,128,64]{1,2,0:T(8,128)(2,1)S(1)} %get-tuple-element.34), channel_id=1, source_target_pairs={{8,16},{12,20},{9,17},{13,21},{10,18},{14,22},{11,19},{15,23}} | collective-permute-start | bytes 786440 | tf_op jit(solution)/shard_map/ppermute | solution.py:115
  81.8 1.6 %collective-permute-start.12 = (bf16[16,128,64]{1,2,0:T(8,128)(2,1)S(1)}, bf16[16,128,64]{1,2,0:T(8,128)(2,1)S(1)}, u32[]{:S(2)}, u32[]{:S(2)}) collective-permute-start(bf16[16,128,64]{1,2,0:T(8,128)(2,1)S(1)} %collective-permute-done.11), channel_id=1, source_target_pairs={{16,24},{20,28},{17,25},{21,29},{18,26},{22,30},{19,27},{23,31}} | collective-permute-start | bytes 786440 | tf_op jit(solution)/shard_map/ppermute | solution.py:116
  82.5 0.9 collective-permute-start.14
  86.1 24.8 %copy-start.9 = (f32[64,128,64]{1,2,0:T(8,128)S(1)}, f32[64,128,64]{1,2,0:T(8,128)}, u32[]{:S(2)}) copy-start(f32[64,128,64]{1,2,0:T(8,128)} %get-tuple-element.18) | copy-start | bytes 6291460
  88.1 52.6 %collective-permute-start.21 = (f32[8,12,64]{2,0,1:T(8,128)S(1)}, f32[8,12,64]{2,0,1:T(8,128)S(1)}, u32[]{:S(2)}, u32[]{:S(2)}) collective-permute-start(f32[8,12,64]{2,0,1:T(8,128)S(1)} %pad_maximum_fusion.2), channel_id=1, source_target_pairs={{0,24},{4,28},{8,0},{12,4},{16,8},{20,12},{24,16},{28,20},{1,25},{... | collective-permute-start | bytes 73736 | tf_op jit(solution)/shard_map/ppermute | solution.py:35
  106.8 33.9 %collective-permute-start.20 = (f32[8,12,64]{2,0,1:T(8,128)S(1)}, f32[8,12,64]{2,0,1:T(8,128)S(1)}, u32[]{:S(2)}, u32[]{:S(2)}) collective-permute-start(f32[8,12,64]{2,0,1:T(8,128)S(1)} %pad_maximum_fusion.2), channel_id=1, source_target_pairs={{0,20},{4,24},{8,28},{12,0},{16,4},{20,8},{24,12},{28,16},{1,21},{... | collective-permute-start | bytes 73736 | tf_op jit(solution)/shard_map/ppermute | solution.py:35
  106.8 33.8 %collective-permute-start.19 = (f32[8,12,64]{2,0,1:T(8,128)S(1)}, f32[8,12,64]{2,0,1:T(8,128)S(1)}, u32[]{:S(2)}, u32[]{:S(2)}) collective-permute-start(f32[8,12,64]{2,0,1:T(8,128)S(1)} %pad_maximum_fusion.2), channel_id=1, source_target_pairs={{0,16},{4,20},{8,24},{12,28},{16,0},{20,4},{24,8},{28,12},{1,17},{... | collective-permute-start | bytes 73736 | tf_op jit(solution)/shard_map/ppermute | solution.py:35
  111.0 29.7 %collective-permute-start.18 = (f32[8,12,64]{2,0,1:T(8,128)S(1)}, f32[8,12,64]{2,0,1:T(8,128)S(1)}, u32[]{:S(2)}, u32[]{:S(2)}) collective-permute-start(f32[8,12,64]{2,0,1:T(8,128)S(1)} %pad_maximum_fusion.2), channel_id=1, source_target_pairs={{0,12},{4,16},{8,20},{12,24},{16,28},{20,0},{24,4},{28,8},{1,13},{... | collective-permute-start | bytes 73736 | tf_op jit(solution)/shard_map/ppermute | solution.py:35
  116.4 10.7 %collective-permute-start.15 = (f32[3,128]{1,0:T(4,128)S(1)}, f32[3,128]{1,0:T(4,128)S(1)}, u32[]{:S(2)}, u32[]{:S(2)}) collective-permute-start(f32[3,128]{1,0:T(4,128)S(1)} %slice.217), channel_id=1, source_target_pairs={{4,0},{8,4},{12,8},{16,12},{20,16},{24,20},{28,24},{5,1},{9,5},{13... | collective-permute-start | bytes 4616 | tf_op jit(solution)/shard_map/ppermute | solution.py:12
  127.1 6.8 %collective-permute-start.16 = (f32[8,12,64]{2,0,1:T(8,128)S(1)}, f32[8,12,64]{2,0,1:T(8,128)S(1)}, u32[]{:S(2)}, u32[]{:S(2)}) collective-permute-start(f32[8,12,64]{2,0,1:T(8,128)S(1)} %pad_maximum_fusion.2), channel_id=1, source_target_pairs={{0,4},{4,8},{8,12},{12,16},{16,20},{20,24},{24,28},{28,0},{1,5},{5... | collective-permute-start | bytes 73736 | tf_op jit(solution)/shard_map/ppermute | solution.py:35
  133.9 6.2 %collective-permute-start.17 = (f32[8,12,64]{2,0,1:T(8,128)S(1)}, f32[8,12,64]{2,0,1:T(8,128)S(1)}, u32[]{:S(2)}, u32[]{:S(2)}) collective-permute-start(f32[8,12,64]{2,0,1:T(8,128)S(1)} %pad_maximum_fusion.2), channel_id=1, source_target_pairs={{0,8},{4,12},{8,16},{12,20},{16,24},{20,28},{24,0},{28,4},{1,9},{5... | collective-permute-start | bytes 73736 | tf_op jit(solution)/shard_map/ppermute | solution.py:35
  140.1 4.1 %collective-permute-start.22 = (f32[8,12,64]{2,0,1:T(8,128)S(1)}, f32[8,12,64]{2,0,1:T(8,128)S(1)}, u32[]{:S(2)}, u32[]{:S(2)}) collective-permute-start(f32[8,12,64]{2,0,1:T(8,128)S(1)} %pad_maximum_fusion.2), channel_id=1, source_target_pairs={{0,28},{4,0},{8,4},{12,8},{16,12},{20,16},{24,20},{28,24},{1,29},{... | collective-permute-start | bytes 73736 | tf_op jit(solution)/shard_map/ppermute | solution.py:35
  (37 other events, 250.5 us)

commit v20 on v18

--- a/solution.py
+++ b/solution.py
@@ -94,10 +94,9 @@
     return (joined, block_decay + other_decay, leading + upper * other_decay, found)
 
 
-def relay(value, axis, bit_pos):
+def relay(value, axis, bit_pos, parts):
     half = 2**bit_pos
     step = half // 2
-    parts = 4 if value.shape[0] % 4 == 0 else 1
     size = value.shape[0] // parts
     received = []
     for index in range(parts):
@@ -108,16 +107,34 @@
     return jnp.concatenate(received, axis=0)
 
 
-def exchange(block, block_decay, depth, myself, decays):
-    leading = jnp.zeros_like(block_decay)
+def exchange(block, block_decay, depth, myself, decays, start=0, leading=None):
+    leading = jnp.zeros_like(block_decay) if leading is None else leading
     found_all = []
     first = None
-    for bit_pos in range(depth):
+    for bit_pos in range(start, depth):
+        if start == 0 and bit_pos == 1 and depth > 2 and block.shape[0] % 2 == 0:
+            size = block.shape[0] // 2
+            rest = [
+                exchange(
+                    block[index * size : (index + 1) * size],
+                    block_decay[index * size : (index + 1) * size],
+                    depth,
+                    myself,
+                    [decay[index * size : (index + 1) * size] for decay in decays],
+                    1,
+                    leading[index * size : (index + 1) * size],
+                )[0]
+                for index in range(2)
+            ]
+            later_found = jnp.concatenate(rest, axis=1)
+            found_all.extend(later_found[index] for index in range(depth - 1))
+            break
         if bit_pos == depth - 1:
             if bit_pos == 0:
                 sent = upward(block.astype(jnp.bfloat16), "seq", bit_pos)
             else:
-                sent = relay(block.astype(jnp.bfloat16), "seq", bit_pos)
+                parts = 2 if start == 0 and block.shape[0] % 2 == 0 else 1
+                sent = relay(block.astype(jnp.bfloat16), "seq", bit_pos, parts)
             other, other_decay = (sent.astype(jnp.float32), jnp.zeros_like(block_decay))
         else:
             sent = from_partner(block.astype(jnp.bfloat16), "seq", bit_pos)

time: 137 us -> 141 us (1.029)
  waiting for transfers between devices: 19 us -> 24.7 us
    ppermute x9 -> x11, waiting for transfers between devices: 19 us -> 24.7 us  [from_partner(): return lax.ppermute(value, axis, pairs)]
    ppermute x9 -> x11, starting transfers between devices: 35 us -> 39.3 us  [from_partner(): return lax.ppermute(value, axis, pairs)]
    ppermute x8 -> x4, starting transfers between devices: 5.52 us -> 2.89 us  [relay(): lax.ppermute(first, axis, [(source, source + step) for source in range(ha...]
    ppermute x8 -> x4, starting transfers between devices: 5.35 us -> 2.84 us  [relay(): lax.ppermute(piece, axis, [(source, source + step) for source in range(ha...]
    add x0 -> x1, other arithmetic: none -> 1.98 us  [combine(): grown * (other * jnp.exp(block_decay)[..., None, None] + block)]
    slice x2, local copies, waits for them, and re-layouts: 0.07 us -> 1.77 us  [exchange(): block[index * size:(index + 1) * size]]
  transfers between devices with their start and end apart: 27 -> 21, of which waited for: 5 -> 6; matrix products, arithmetic and copies ran while one was open for 27% -> 27% of each run, Pallas kernels for 0% -> 0%
where the time goes in v20:
time: 141 us; the launch traced here: 140 us
  starting transfers between devices  48.3 us (34%)
  local copies, waits for them, and re-layouts  30.4 us (22%)
  waiting for transfers between devices  24.7 us (18%)
  other arithmetic  19.2 us (14%)
  matrix products  16.3 us (12%)
    ppermute x11, starting transfers between devices, from_partner(): return lax.ppermute(value, axis, pairs)  39.3 us
    ppermute x11, waiting for transfers between devices, from_partner(): return lax.ppermute(value, axis, pairs)  24.7 us
    dot_general x6, matrix products, contract(): return jnp.einsum(form, left, right, preferred_element_type=jnp.float32)  14.3 us
    another operation x2, local copies, waits for them, and re-layouts, local(): x_groups = x_act.reshape(groups, group_len, heads, head_dim)  6.56 us
    reshape x2, local copies, waits for them, and re-layouts, local(): grad_groups = late_cotangent.reshape(groups, group_len, heads, head_dim)  5.24 us
    another operation x1, other arithmetic  3.58 us
    convert_element_type x1, local copies, waits for them, and re-layouts, local(): ssm_out = (y_inner + y_cross + skip[None, None, :, None] * x_groups).asty...  3.31 us
    ppermute x2, starting transfers between devices, shifted(): lax.ppermute(value, axis, [(source, source + steps) for source in range(l...  3.22 us
  transfers between devices with their start and end apart: 21, of which 6 were waited for; matrix products, arithmetic and copies ran while one was open for 27% of the time, Pallas kernels for 0%

profile of v20, /device:TPU:0, one launch (start us, length us, event | category | flops | bytes accessed | tf_op | source)
XLA Modules:
  0.0 140.3 jit_solution(7825409876551837186)
XLA Ops:
  2.4 3.0 %collective-permute-start.2 = (f32[64]{0:T(128)S(1)}, f32[64]{0:T(128)S(1)}, u32[]{:S(2)}, u32[]{:S(2)}) collective-permute-start(f32[64]{0:T(128)S(1)} %get-tuple-element.46), channel_id=1, source_target_pairs={{0,4},{4,0},{8,12},{12,8},{16,20},{20,16},{24,28},{28,24},{1,5},{5... | collective-permute-start | bytes 776 | tf_op jit(solution)/shard_map/ppermute | solution.py:18
  6.3 1.9 %collective-permute-start = (bf16[3,4352]{1,0:T(4,128)(2,1)S(1)}, bf16[3,4352]{1,0:T(4,128)(2,1)S(1)}, u32[]{:S(2)}, u32[]{:S(2)}) collective-permute-start(bf16[3,4352]{1,0:T(4,128)(2,1)S(1)} %slice.185), channel_id=1, source_target_pairs={{0,4},{4,8},{8,12},{12,16},{16,20},{20,24},{24,28},{1,5},{5,9},{9,... | collective-permute-start | bytes 78344 | tf_op jit(solution)/shard_map/ppermute | solution.py:12
  14.9 2.1 %collective-permute-start.4 = (f32[64]{0:T(128)S(1)}, f32[64]{0:T(128)S(1)}, u32[]{:S(2)}, u32[]{:S(2)}) collective-permute-start(f32[64]{0:T(128)S(1)} %add.181), channel_id=1, source_target_pairs={{0,8},{4,12},{8,0},{12,4},{16,24},{20,28},{24,16},{28,20},{1,9},{5... | collective-permute-start | bytes 776 | tf_op jit(solution)/shard_map/ppermute | solution.py:18
  18.6 3.6 %fusion.87 = (bf16[128,4352]{1,0:T(8,128)(2,1)S(1)}, f32[128,4352]{1,0:T(8,128)S(1)}) fusion(f32[4352]{0:T(1024)S(1)} %get-tuple-element.8, bf16[128,4352]{1,0:T(8,128)(2,1)} %param.9, f32[4352]{0:T(1024)S(1)} %get-tuple-element.9, bf16[3,4352]{1,0:T(4,128)(2,1)S(1)} %collective-permute-done, f32[4352]{0:T(1024)S(1)} %get-tuple-element.10, ...), kind=kLoop, calls=%fused_computation.199 | loop fusion | flops 12255232 | bytes 4569600 | tf_op jit(solution)/shard_map/convert.2
  22.8 3.2 %reshape_reshape.3 = bf16[2,64,64,64]{3,2,1,0:T(8,128)(2,1)} reshape(bf16[128,4096]{1,0:T(8,128)(2,1)S(1)} %multiply_convert_fusion.5) | data formatting | bytes 2097152 | tf_op jit(solution)/shard_map/reshape;reshape | solution.py:177
  26.0 3.3 %copy.46 = bf16[2,64,64,64]{1,3,2,0:T(8,128)(2,1)S(1)} copy(bf16[2,64,64,64]{3,2,1,0:T(8,128)(2,1)} %reshape_reshape.3) | data formatting | bytes 2097152 | tf_op jit(solution)/shard_map/reshape;reshape | solution.py:177
  30.9 3.0 %collective-permute-start.1 = (bf16[32,128,64]{1,2,0:T(8,128)(2,1)S(1)}, bf16[32,128,64]{1,2,0:T(8,128)(2,1)S(1)}, u32[]{:S(2)}, u32[]{:S(2)}) collective-permute-start(bf16[32,128,64]{1,2,0:T(8,128)(2,1)S(1)} %get-tuple-element.22), channel_id=1, source_target_pairs={{0,4},{4,0},{8,12},{12,8},{16,20},{20,16},{24,28},{28,24},{1,5},{5... | collective-permute-start | bytes 1572872 | tf_op jit(solution)/shard_map/ppermute | solution.py:18
  34.2 2.4 %slice_bitcast_fusion.4 = (f32[64,128,64]{1,2,0:T(8,128)}, f32[64,128,64]{1,2,0:T(8,128)}) fusion(f32[2,64,128,64]{2,3,1,0:T(8,128)S(1)} %get-tuple-element.87), kind=kLoop, calls=%fused_computation.26 | loop fusion | bytes 8388608 | tf_op jit(solution)/shard_map/mul | solution.py:230
  36.6 10.2 %collective-permute-done.1 = bf16[32,128,64]{1,2,0:T(8,128)(2,1)S(1)} collective-permute-done((bf16[32,128,64]{1,2,0:T(8,128)(2,1)S(1)}, bf16[32,128,64]{1,2,0:T(8,128)(2,1)S(1)}, u32[]{:S(2)}, u32[]{:S(2)}) %collective-permute-start.1) | collective-permute-done | bytes 524320 | tf_op jit(solution)/shard_map/ppermute | solution.py:18
  46.8 8.6 %collective-permute-done.10 = bf16[32,128,64]{1,2,0:T(8,128)(2,1)S(1)} collective-permute-done((bf16[32,128,64]{1,2,0:T(8,128)(2,1)S(1)}, bf16[32,128,64]{1,2,0:T(8,128)(2,1)S(1)}, u32[]{:S(2)}, u32[]{:S(2)}) %collective-permute-start.10) | collective-permute-done | bytes 524320 | tf_op jit(solution)/shard_map/ppermute | solution.py:18
  55.4 2.0 %fusion.24 = (f32[32,128,64]{1,2,0:T(8,128)S(1)}, f32[32,128,64]{1,2,0:T(8,128)S(1)}, f32[1,32,128,64]{2,3,1,0:T(8,128)}, f32[1,32,128,64]{2,3,1,0:T(8,128)}) fusion(bf16[32,128,64]{1,2,0:T(8,128)(2,1)S(1)} %collective-permute-done.1, f32[64,128,64]{1,2,0:T(8,128)S(1)} %get-tuple-element.86, f32[32]{0:T(128)S(1)} %get-tuple-element.77, f32[]{:T(128)S(6)} %sub.98, ...), kind=kLoop, calls=%fused_computation.55 | loop fusion | flops 4718592 | bytes 7340552 | tf_op jit(solution)/shard_map/add | solution.py:91
  58.3 1.6 %collective-permute-start.3 = (bf16[16,128,64]{1,2,0:T(8,128)(2,1)}, bf16[16,128,64]{1,2,0:T(8,128)(2,1)}, u32[]{:S(2)}, u32[]{:S(2)}) collective-permute-start(bf16[16,128,64]{1,2,0:T(8,128)(2,1)} %get-tuple-element.28), channel_id=1, source_target_pairs={{0,8},{4,12},{8,0},{12,4},{16,24},{20,28},{24,16},{28,20},{1,9},{5... | collective-permute-start | bytes 786440 | tf_op jit(solution)/shard_map/ppermute | solution.py:18
  63.2 2.3 %reshape.142 = bf16[2,64,64,64]{3,2,1,0:T(8,128)(2,1)S(1)} reshape(bf16[128,4096]{1,0:T(8,128)(2,1)S(1)} %copy-done.15) | data formatting | bytes 2097152 | tf_op jit(solution)/shard_map/reshape | solution.py:210
  65.5 3.0 %copy.55 = bf16[2,64,64,64]{1,3,2,0:T(8,128)(2,1)} copy(bf16[2,64,64,64]{3,2,1,0:T(8,128)(2,1)S(1)} %reshape.142) | data formatting | bytes 2097152 | tf_op jit(solution)/shard_map/reshape | solution.py:210
  68.5 2.9 %fusion.5 = f32[2,64,128,64]{2,3,1,0:T(8,128)S(1)} fusion(bf16[2,64,64,64]{1,3,2,0:T(8,128)(2,1)} %copy.55, f32[2,64,64]{1,2,0:T(8,128)S(1)} %copy.50, f32[2,64,128]{2,1,0:T(8,128)S(1)} %convert_element_type.157), kind=kOutput, calls=%fused_computation.18 | convolution fusion | flops 136314880 | bytes 5341184 | tf_op jit(solution)/shard_map/cthn,cthp->chnp/dot_general | solution.py:35
  71.4 3.8 %multiply_reduce_fusion.2 = (f32[2,64]{1,0:T(2,128)S(1)}, f32[2,64,64]{2,1,0:T(8,128)S(1)}) fusion(f32[2,64,64]{2,1,0:T(8,128)S(1)} %fusion.94, f32[2,64,64]{2,1,0:T(8,128)S(1)} %copy.44, pred[64,64]{1,0:T(8,128)(4,1)S(1)} %iota_compare_fusion, f32[2,64]{1,0:T(2,128)S(1)} %copy-done.21, bf16[2,64,64,64]{1,3,2,0:T(8,128)(2,1)S(1)} %copy-done.5, ...), kind=kOutput, calls=%fused_computation.10 | convolution fusion | flops 72343424 | bytes 2200576 | tf_op jit(solution)/shard_map/vmap(thp,shp->hts)/dot_general | solution.py:35
  79.3 1.8 %collective-permute-done.14 = bf16[16,128,64]{1,2,0:T(8,128)(2,1)} collective-permute-done((bf16[16,128,64]{1,2,0:T(8,128)(2,1)}, bf16[16,128,64]{1,2,0:T(8,128)(2,1)}, u32[]{:S(2)}, u32[]{:S(2)}) %collective-permute-start.14) | collective-permute-done | bytes 262176 | tf_op jit(solution)/shard_map/ppermute | solution.py:18
  93.0 1.7 %add_convert_fusion = bf16[2,64,128,64]{2,3,1,0:T(8,128)(2,1)S(1)} fusion(f32[64,128,64]{1,2,0:T(8,128)S(1)} %get-tuple-element.16, f32[2,64]{1,0:T(2,128)S(1)} %get-tuple-element.50, f32[64,128,64]{1,2,0:T(8,128)S(1)} %get-tuple-element.17, f32[2,64]{1,0:T(2,128)S(1)} %get-tuple-element.51, f32[64,128,64]{1,2,0:T(8,128)S(1)} %get-tuple-element.15, ...), kind=kLoop, calls=%fused_computation.13 | loop fusion | flops 10485760 | bytes 12585472 | tf_op jit(solution)/shard_map/convert_element_type | solution.py:232
  94.7 2.0 %fusion.3 = f32[2,64,128]{2,1,0:T(8,128)S(1)} fusion(bf16[2,64,64,64]{1,3,2,0:T(8,128)(2,1)S(1)} %copy-done.6, bf16[2,64,128,64]{2,3,1,0:T(8,128)(2,1)S(1)} %add_convert_fusion, f32[2,64,64]{1,2,0:T(8,128)S(1)} %copy.50), kind=kOutput, calls=%fused_computation.9 | convolution fusion | flops 136298496 | bytes 3244032 | tf_op jit(solution)/shard_map/chnp,cthp->cthn/dot_general | solution.py:35
  102.7 15.1 %collective-permute-start.19 = (f32[8,12,64]{2,0,1:T(8,128)S(1)}, f32[8,12,64]{2,0,1:T(8,128)S(1)}, u32[]{:S(2)}, u32[]{:S(2)}) collective-permute-start(f32[8,12,64]{2,0,1:T(8,128)S(1)} %fusion.85), channel_id=1, source_target_pairs={{0,8},{4,12},{8,0},{12,4},{16,24},{20,28},{24,16},{28,20},{1,9},{5... | collective-permute-start | bytes 73736 | tf_op jit(solution)/shard_map/ppermute | solution.py:18
  117.8 3.5 %fusion.2 = bf16[2,64,64,64]{1,3,2,0:T(8,128)(2,1)} fusion(bf16[2,64,64,64]{1,3,2,0:T(8,128)(2,1)S(1)} %copy-done.4, f32[2,64,64,64]{3,2,1,0:T(8,128)S(1)} %fusion.6, f32[64]{0:T(128)S(1)} %copy-done.25, f32[2,64]{1,0:T(2,128)S(1)} %copy-done.20, f32[2,64,64]{2,1,0:T(8,128)S(1)} %fusion.94, f32[2,64,64]{2,1,0:T(8,128)S(1)} %copy.44, ...), kind=kOutput, calls=%fused_computation.7 | convolution fusion | flops 72876032 | bytes 4264704 | tf_op jit(solution)/shard_map/vmap(hts,shp->thp)/dot_general | solution.py:35
  121.3 3.3 %copy.51 = bf16[2,64,64,64]{3,2,1,0:T(8,128)(2,1)S(1)} copy(bf16[2,64,64,64]{1,3,2,0:T(8,128)(2,1)} %fusion.2) | data formatting | bytes 2097152 | tf_op jit(solution)/shard_map/convert_element_type | solution.py:253
  124.7 2.5 %reshape.141 = bf16[128,4096]{1,0:T(8,128)(2,1)} reshape(bf16[2,64,64,64]{3,2,1,0:T(8,128)(2,1)S(1)} %copy.51) | data formatting | bytes 2097152 | tf_op jit(solution)/shard_map/reshape | solution.py:254
  127.1 10.4 %collective-permute-start.20 = (f32[8,12,64]{2,0,1:T(8,128)S(1)}, f32[8,12,64]{2,0,1:T(8,128)S(1)}, u32[]{:S(2)}, u32[]{:S(2)}) collective-permute-start(f32[8,12,64]{2,0,1:T(8,128)S(1)} %add.218), channel_id=1, source_target_pairs={{0,16},{4,20},{8,24},{12,28},{16,0},{20,4},{24,8},{28,12},{1,17},{... | collective-permute-start | bytes 73736 | tf_op jit(solution)/shard_map/ppermute | solution.py:18
  (149 shorter events, 41.8 us)
Async XLA Ops:
  2.4 12.3 %collective-permute-start.2 = (f32[64]{0:T(128)S(1)}, f32[64]{0:T(128)S(1)}, u32[]{:S(2)}, u32[]{:S(2)}) collective-permute-start(f32[64]{0:T(128)S(1)} %get-tuple-element.46), channel_id=1, source_target_pairs={{0,4},{4,0},{8,12},{12,8},{16,20},{20,16},{24,28},{28,24},{1,5},{5... | collective-permute-start | bytes 776 | tf_op jit(solution)/shard_map/ppermute | solution.py:18
  6.3 12.3 %collective-permute-start = (bf16[3,4352]{1,0:T(4,128)(2,1)S(1)}, bf16[3,4352]{1,0:T(4,128)(2,1)S(1)}, u32[]{:S(2)}, u32[]{:S(2)}) collective-permute-start(bf16[3,4352]{1,0:T(4,128)(2,1)S(1)} %slice.185), channel_id=1, source_target_pairs={{0,4},{4,8},{8,12},{12,16},{16,20},{20,24},{24,28},{1,5},{5,9},{9,... | collective-permute-start | bytes 78344 | tf_op jit(solution)/shard_map/ppermute | solution.py:12
  14.9 3.6 %collective-permute-start.4 = (f32[64]{0:T(128)S(1)}, f32[64]{0:T(128)S(1)}, u32[]{:S(2)}, u32[]{:S(2)}) collective-permute-start(f32[64]{0:T(128)S(1)} %add.181), channel_id=1, source_target_pairs={{0,8},{4,12},{8,0},{12,4},{16,24},{20,28},{24,16},{28,20},{1,9},{5... | collective-permute-start | bytes 776 | tf_op jit(solution)/shard_map/ppermute | solution.py:18
  30.9 15.9 %collective-permute-start.1 = (bf16[32,128,64]{1,2,0:T(8,128)(2,1)S(1)}, bf16[32,128,64]{1,2,0:T(8,128)(2,1)S(1)}, u32[]{:S(2)}, u32[]{:S(2)}) collective-permute-start(bf16[32,128,64]{1,2,0:T(8,128)(2,1)S(1)} %get-tuple-element.22), channel_id=1, source_target_pairs={{0,4},{4,0},{8,12},{12,8},{16,20},{20,16},{24,28},{28,24},{1,5},{5... | collective-permute-start | bytes 1572872 | tf_op jit(solution)/shard_map/ppermute | solution.py:18
  34.0 21.4 %collective-permute-start.10 = (bf16[32,128,64]{1,2,0:T(8,128)(2,1)S(1)}, bf16[32,128,64]{1,2,0:T(8,128)(2,1)S(1)}, u32[]{:S(2)}, u32[]{:S(2)}) collective-permute-start(bf16[32,128,64]{1,2,0:T(8,128)(2,1)S(1)} %get-tuple-element.23), channel_id=1, source_target_pairs={{0,4},{4,0},{8,12},{12,8},{16,20},{20,16},{24,28},{28,24},{1,5},{5... | collective-permute-start | bytes 1572872 | tf_op jit(solution)/shard_map/ppermute | solution.py:18
  58.3 17.8 %collective-permute-start.3 = (bf16[16,128,64]{1,2,0:T(8,128)(2,1)}, bf16[16,128,64]{1,2,0:T(8,128)(2,1)}, u32[]{:S(2)}, u32[]{:S(2)}) collective-permute-start(bf16[16,128,64]{1,2,0:T(8,128)(2,1)} %get-tuple-element.28), channel_id=1, source_target_pairs={{0,8},{4,12},{8,0},{12,4},{16,24},{20,28},{24,16},{28,20},{1,9},{5... | collective-permute-start | bytes 786440 | tf_op jit(solution)/shard_map/ppermute | solution.py:18
  59.9 16.3 %collective-permute-start.7 = (bf16[16,128,64]{1,2,0:T(8,128)(2,1)}, bf16[16,128,64]{1,2,0:T(8,128)(2,1)}, u32[]{:S(2)}, u32[]{:S(2)}) collective-permute-start(bf16[16,128,64]{1,2,0:T(8,128)(2,1)} %get-tuple-element.29), channel_id=1, source_target_pairs={{0,8},{4,12},{8,0},{12,4},{16,24},{20,28},{24,16},{28,20},{1,9},{5... | collective-permute-start | bytes 786440 | tf_op jit(solution)/shard_map/ppermute | solution.py:18
  61.2 18.1 %collective-permute-start.11 = (bf16[16,128,64]{1,2,0:T(8,128)(2,1)}, bf16[16,128,64]{1,2,0:T(8,128)(2,1)}, u32[]{:S(2)}, u32[]{:S(2)}) collective-permute-start(bf16[16,128,64]{1,2,0:T(8,128)(2,1)} %get-tuple-element.32), channel_id=1, source_target_pairs={{0,8},{4,12},{8,0},{12,4},{16,24},{20,28},{24,16},{28,20},{1,9},{5... | collective-permute-start | bytes 786440 | tf_op jit(solution)/shard_map/ppermute | solution.py:18
  62.8 18.4 %collective-permute-start.14 = (bf16[16,128,64]{1,2,0:T(8,128)(2,1)}, bf16[16,128,64]{1,2,0:T(8,128)(2,1)}, u32[]{:S(2)}, u32[]{:S(2)}) collective-permute-start(bf16[16,128,64]{1,2,0:T(8,128)(2,1)} %get-tuple-element.33), channel_id=1, source_target_pairs={{0,8},{4,12},{8,0},{12,4},{16,24},{20,28},{24,16},{28,20},{1,9},{5... | collective-permute-start | bytes 786440 | tf_op jit(solution)/shard_map/ppermute | solution.py:18
  77.9 6.2 %collective-permute-start.5 = (bf16[16,128,64]{1,2,0:T(8,128)(2,1)S(1)}, bf16[16,128,64]{1,2,0:T(8,128)(2,1)S(1)}, u32[]{:S(2)}, u32[]{:S(2)}) collective-permute-start(bf16[16,128,64]{1,2,0:T(8,128)(2,1)S(1)} %get-tuple-element.26), channel_id=1, source_target_pairs={{8,16},{12,20},{9,17},{13,21},{10,18},{14,22},{11,19},{15,23}} | collective-permute-start | bytes 786440 | tf_op jit(solution)/shard_map/ppermute | solution.py:104
  78.6 6.6 %collective-permute-start.8 = (bf16[16,128,64]{1,2,0:T(8,128)(2,1)S(1)}, bf16[16,128,64]{1,2,0:T(8,128)(2,1)S(1)}, u32[]{:S(2)}, u32[]{:S(2)}) collective-permute-start(bf16[16,128,64]{1,2,0:T(8,128)(2,1)S(1)} %get-tuple-element.27), channel_id=1, source_target_pairs={{8,16},{12,20},{9,17},{13,21},{10,18},{14,22},{11,19},{15,23}} | collective-permute-start | bytes 786440 | tf_op jit(solution)/shard_map/ppermute | solution.py:104
  82.7 3.6 %collective-permute-start.12 = (bf16[16,128,64]{1,2,0:T(8,128)(2,1)S(1)}, bf16[16,128,64]{1,2,0:T(8,128)(2,1)S(1)}, u32[]{:S(2)}, u32[]{:S(2)}) collective-permute-start(bf16[16,128,64]{1,2,0:T(8,128)(2,1)S(1)} %get-tuple-element.30), channel_id=1, source_target_pairs={{8,16},{12,20},{9,17},{13,21},{10,18},{14,22},{11,19},{15,23}} | collective-permute-start | bytes 786440 | tf_op jit(solution)/shard_map/ppermute | solution.py:104
  83.5 3.4 %collective-permute-start.15 = (bf16[16,128,64]{1,2,0:T(8,128)(2,1)S(1)}, bf16[16,128,64]{1,2,0:T(8,128)(2,1)S(1)}, u32[]{:S(2)}, u32[]{:S(2)}) collective-permute-start(bf16[16,128,64]{1,2,0:T(8,128)(2,1)S(1)} %get-tuple-element.31), channel_id=1, source_target_pairs={{8,16},{12,20},{9,17},{13,21},{10,18},{14,22},{11,19},{15,23}} | collective-permute-start | bytes 786440 | tf_op jit(solution)/shard_map/ppermute | solution.py:104
  84.2 3.4 %collective-permute-start.6 = (bf16[16,128,64]{1,2,0:T(8,128)(2,1)S(1)}, bf16[16,128,64]{1,2,0:T(8,128)(2,1)S(1)}, u32[]{:S(2)}, u32[]{:S(2)}) collective-permute-start(bf16[16,128,64]{1,2,0:T(8,128)(2,1)S(1)} %collective-permute-done.5), channel_id=1, source_target_pairs={{16,24},{20,28},{17,25},{21,29},{18,26},{22,30},{19,27},{23,31}} | collective-permute-start | bytes 786440 | tf_op jit(solution)/shard_map/ppermute | solution.py:105
  85.3 2.5 %collective-permute-start.9 = (bf16[16,128,64]{1,2,0:T(8,128)(2,1)S(1)}, bf16[16,128,64]{1,2,0:T(8,128)(2,1)S(1)}, u32[]{:S(2)}, u32[]{:S(2)}) collective-permute-start(bf16[16,128,64]{1,2,0:T(8,128)(2,1)S(1)} %collective-permute-done.8), channel_id=1, source_target_pairs={{16,24},{20,28},{17,25},{21,29},{18,26},{22,30},{19,27},{23,31}} | collective-permute-start | bytes 786440 | tf_op jit(solution)/shard_map/ppermute | solution.py:105
  86.2 1.6 %collective-permute-start.13 = (bf16[16,128,64]{1,2,0:T(8,128)(2,1)S(1)}, bf16[16,128,64]{1,2,0:T(8,128)(2,1)S(1)}, u32[]{:S(2)}, u32[]{:S(2)}) collective-permute-start(bf16[16,128,64]{1,2,0:T(8,128)(2,1)S(1)} %collective-permute-done.12), channel_id=1, source_target_pairs={{16,24},{20,28},{17,25},{21,29},{18,26},{22,30},{19,27},{23,31}} | collective-permute-start | bytes 786440 | tf_op jit(solution)/shard_map/ppermute | solution.py:105
  86.9 1.0 collective-permute-start.16
  96.7 21.1 %copy-start.4 = (bf16[2,64,64,64]{1,3,2,0:T(8,128)(2,1)S(1)}, bf16[2,64,64,64]{1,3,2,0:T(8,128)(2,1)}, u32[]{:S(2)}) copy-start(bf16[2,64,64,64]{1,3,2,0:T(8,128)(2,1)} %copy-done.2) | copy-start | bytes 3145732
  96.7 21.1 %copy-start.20 = (f32[2,64]{1,0:T(2,128)S(1)}, f32[2,64]{1,0:T(2,128)}, u32[]{:S(2)}) copy-start(f32[2,64]{1,0:T(2,128)} %broadcast_multiply_fusion) | copy-start | bytes 1540
  96.7 21.1 %copy-start.25 = (f32[64]{0:T(128)S(1)}, f32[64]{0:T(128)}, u32[]{:S(2)}) copy-start(f32[64]{0:T(128)} %param.14) | copy-start | bytes 772
  98.6 4.2 %collective-permute-start.18 = (f32[8,12,64]{2,0,1:T(8,128)S(1)}, f32[8,12,64]{2,0,1:T(8,128)S(1)}, u32[]{:S(2)}, u32[]{:S(2)}) collective-permute-start(f32[8,12,64]{2,0,1:T(8,128)S(1)} %pad_maximum_fusion.2), channel_id=1, source_target_pairs={{0,4},{4,0},{8,12},{12,8},{16,20},{20,16},{24,28},{28,24},{1,5},{5... | collective-permute-start | bytes 73736 | tf_op jit(solution)/shard_map/ppermute | solution.py:18
  100.2 37.4 %collective-permute-start.17 = (f32[3,128]{1,0:T(4,128)S(1)}, f32[3,128]{1,0:T(4,128)S(1)}, u32[]{:S(2)}, u32[]{:S(2)}) collective-permute-start(f32[3,128]{1,0:T(4,128)S(1)} %slice.267), channel_id=1, source_target_pairs={{4,0},{8,4},{12,8},{16,12},{20,16},{24,20},{28,24},{5,1},{9,5},{13... | collective-permute-start | bytes 4616 | tf_op jit(solution)/shard_map/ppermute | solution.py:12
  102.7 24.4 %collective-permute-start.19 = (f32[8,12,64]{2,0,1:T(8,128)S(1)}, f32[8,12,64]{2,0,1:T(8,128)S(1)}, u32[]{:S(2)}, u32[]{:S(2)}) collective-permute-start(f32[8,12,64]{2,0,1:T(8,128)S(1)} %fusion.85), channel_id=1, source_target_pairs={{0,8},{4,12},{8,0},{12,4},{16,24},{20,28},{24,16},{28,20},{1,9},{5... | collective-permute-start | bytes 73736 | tf_op jit(solution)/shard_map/ppermute | solution.py:18
  127.1 12.5 %collective-permute-start.20 = (f32[8,12,64]{2,0,1:T(8,128)S(1)}, f32[8,12,64]{2,0,1:T(8,128)S(1)}, u32[]{:S(2)}, u32[]{:S(2)}) collective-permute-start(f32[8,12,64]{2,0,1:T(8,128)S(1)} %add.218), channel_id=1, source_target_pairs={{0,16},{4,20},{8,24},{12,28},{16,0},{20,4},{24,8},{28,12},{1,17},{... | collective-permute-start | bytes 73736 | tf_op jit(solution)/shard_map/ppermute | solution.py:18
  (25 other events, 142.7 us)

commit v21 on v16

--- a/solution.py
+++ b/solution.py
@@ -189,7 +189,7 @@
         for k in range(chunks)
     ]
     cross = jnp.concatenate([piece for piece, _ in pieces], axis=1)
-    late_cotangent = lax.optimization_barrier((cotangent, pieces[0][1]))[0]
+    late_cotangent = lax.optimization_barrier((cotangent, pieces[-1][1]))[0]
     grad_groups = late_cotangent.reshape(groups, group_len, heads, head_dim)
     y_inner, grad_inner, level_zero = jax.vmap(local_group)(
         x_groups, b_groups, c_groups, cumuls, grad_groups, weight_rows[:, 0]

time: 130 us -> 137 us (1.054)
  waiting for transfers between devices: 18.1 us -> 25.7 us
    ppermute x9, waiting for transfers between devices: 18.1 us -> 25.7 us  [from_partner(): return lax.ppermute(value, axis, pairs)]
  transfers between devices with their start and end apart: 19 -> 19, of which waited for: 5 -> 6; matrix products, arithmetic and copies ran while one was open for 28% -> 27% of each run, Pallas kernels for 0% -> 0%
where the time goes in v21:
time: 137 us
  starting transfers between devices  44.8 us (33%)
  local copies, waits for them, and re-layouts  29.5 us (22%)
  waiting for transfers between devices  25.7 us (19%)
  other arithmetic  19.7 us (14%)
  matrix products  15.5 us (11%)
  between operations  1.46 us (1%)
    ppermute x9, starting transfers between devices, from_partner(): return lax.ppermute(value, axis, pairs)  35.8 us
    ppermute x9, waiting for transfers between devices, from_partner(): return lax.ppermute(value, axis, pairs)  25.7 us
    dot_general x6, matrix products, contract(): return jnp.einsum(form, left, right, preferred_element_type=jnp.float32)  12.9 us
    reshape x2, local copies, waits for them, and re-layouts, local(): grad_groups = late_cotangent.reshape(groups, group_len, heads, head_dim)  6.6 us
    another operation x2, local copies, waits for them, and re-layouts, local(): x_groups = x_act.reshape(groups, group_len, heads, head_dim)  6.57 us
    another operation x1, other arithmetic  3.48 us
    convert_element_type x1, local copies, waits for them, and re-layouts, local(): ssm_out = (y_inner + y_cross + skip[None, None, :, None] * x_groups).asty...  3.31 us
    ppermute x2, starting transfers between devices, shifted(): lax.ppermute(value, axis, [(source, source + steps) for source in range(l...  3.22 us
  transfers between devices with their start and end apart: 19, of which 6 were waited for; matrix products, arithmetic and copies ran while one was open for 27% of the time, Pallas kernels for 0%

profile of v21, /device:TPU:0, one launch (start us, length us, event | category | flops | bytes accessed | tf_op | source)
XLA Modules:
  0.0 136.6 jit_solution(9578722736856912009)
XLA Ops:
  2.4 3.0 %collective-permute-start.2 = (f32[64]{0:T(128)S(1)}, f32[64]{0:T(128)S(1)}, u32[]{:S(2)}, u32[]{:S(2)}) collective-permute-start(f32[64]{0:T(128)S(1)} %get-tuple-element.41), channel_id=1, source_target_pairs={{0,4},{4,0},{8,12},{12,8},{16,20},{20,16},{24,28},{28,24},{1,5},{5... | collective-permute-start | bytes 776 | tf_op jit(solution)/shard_map/ppermute | solution.py:18
  6.3 1.9 %collective-permute-start = (bf16[3,4352]{1,0:T(4,128)(2,1)S(1)}, bf16[3,4352]{1,0:T(4,128)(2,1)S(1)}, u32[]{:S(2)}, u32[]{:S(2)}) collective-permute-start(bf16[3,4352]{1,0:T(4,128)(2,1)S(1)} %slice.143), channel_id=1, source_target_pairs={{0,4},{4,8},{8,12},{12,16},{16,20},{20,24},{24,28},{1,5},{5,9},{9,... | collective-permute-start | bytes 78344 | tf_op jit(solution)/shard_map/ppermute | solution.py:12
  14.0 2.2 %collective-permute-start.4 = (f32[64]{0:T(128)S(1)}, f32[64]{0:T(128)S(1)}, u32[]{:S(2)}, u32[]{:S(2)}) collective-permute-start(f32[64]{0:T(128)S(1)} %add.153), channel_id=1, source_target_pairs={{0,8},{4,12},{8,0},{12,4},{16,24},{20,28},{24,16},{28,20},{1,9},{5... | collective-permute-start | bytes 776 | tf_op jit(solution)/shard_map/ppermute | solution.py:18
  18.4 3.5 %fusion.77 = (bf16[128,4352]{1,0:T(8,128)(2,1)S(1)}, f32[128,4352]{1,0:T(8,128)S(1)}) fusion(f32[4352]{0:T(1024)S(1)} %get-tuple-element.8, bf16[128,4352]{1,0:T(8,128)(2,1)} %param.9, f32[4352]{0:T(1024)S(1)} %get-tuple-element.9, bf16[3,4352]{1,0:T(4,128)(2,1)S(1)} %collective-permute-done, f32[4352]{0:T(1024)S(1)} %get-tuple-element.10, ...), kind=kLoop, calls=%fused_computation.169 | loop fusion | flops 12255232 | bytes 4569600 | tf_op jit(solution)/shard_map/convert.2
  22.5 3.3 %reshape_reshape.3 = bf16[2,64,64,64]{3,2,1,0:T(8,128)(2,1)} reshape(bf16[128,4096]{1,0:T(8,128)(2,1)S(1)} %multiply_convert_fusion.5) | data formatting | bytes 2097152 | tf_op jit(solution)/shard_map/reshape;reshape | solution.py:160
  25.7 3.3 %copy.46 = bf16[2,64,64,64]{1,3,2,0:T(8,128)(2,1)S(1)} copy(bf16[2,64,64,64]{3,2,1,0:T(8,128)(2,1)} %reshape_reshape.3) | data formatting | bytes 2097152 | tf_op jit(solution)/shard_map/reshape;reshape | solution.py:160
  30.6 3.0 %collective-permute-start.1 = (bf16[32,128,64]{1,2,0:T(8,128)(2,1)S(1)}, bf16[32,128,64]{1,2,0:T(8,128)(2,1)S(1)}, u32[]{:S(2)}, u32[]{:S(2)}) collective-permute-start(bf16[32,128,64]{1,2,0:T(8,128)(2,1)S(1)} %get-tuple-element.22), channel_id=1, source_target_pairs={{0,4},{4,0},{8,12},{12,8},{16,20},{20,16},{24,28},{28,24},{1,5},{5... | collective-permute-start | bytes 1572872 | tf_op jit(solution)/shard_map/ppermute | solution.py:18
  33.7 2.4 %slice_bitcast_fusion.4 = (f32[64,128,64]{1,2,0:T(8,128)}, f32[64,128,64]{1,2,0:T(8,128)}) fusion(f32[2,64,128,64]{2,3,1,0:T(8,128)S(1)} %get-tuple-element.70), kind=kLoop, calls=%fused_computation.26 | loop fusion | bytes 8388608 | tf_op jit(solution)/shard_map/mul | solution.py:213
  36.2 10.2 %collective-permute-done.1 = bf16[32,128,64]{1,2,0:T(8,128)(2,1)S(1)} collective-permute-done((bf16[32,128,64]{1,2,0:T(8,128)(2,1)S(1)}, bf16[32,128,64]{1,2,0:T(8,128)(2,1)S(1)}, u32[]{:S(2)}, u32[]{:S(2)}) %collective-permute-start.1) | collective-permute-done | bytes 524320 | tf_op jit(solution)/shard_map/ppermute | solution.py:18
  47.7 1.6 %collective-permute-start.3 = (bf16[32,128,64]{1,2,0:T(8,128)(2,1)}, bf16[32,128,64]{1,2,0:T(8,128)(2,1)}, u32[]{:S(2)}, u32[]{:S(2)}) collective-permute-start(bf16[32,128,64]{1,2,0:T(8,128)(2,1)} %fusion.75), channel_id=1, source_target_pairs={{0,8},{4,12},{8,0},{12,4},{16,24},{20,28},{24,16},{28,20},{1,9},{5... | collective-permute-start | bytes 1572872 | tf_op jit(solution)/shard_map/ppermute | solution.py:18
  49.2 5.9 %collective-permute-done.9 = bf16[32,128,64]{1,2,0:T(8,128)(2,1)S(1)} collective-permute-done((bf16[32,128,64]{1,2,0:T(8,128)(2,1)S(1)}, bf16[32,128,64]{1,2,0:T(8,128)(2,1)S(1)}, u32[]{:S(2)}, u32[]{:S(2)}) %collective-permute-start.9) | collective-permute-done | bytes 524320 | tf_op jit(solution)/shard_map/ppermute | solution.py:18
  55.1 3.3 %reshape.194 = bf16[2,64,64,64]{3,2,1,0:T(8,128)(2,1)} reshape(bf16[128,4096]{1,0:T(8,128)(2,1)S(1)} %copy-done.11) | data formatting | bytes 2097152 | tf_op jit(solution)/shard_map/reshape | solution.py:193
  58.4 3.3 %copy.55 = bf16[2,64,64,64]{1,3,2,0:T(8,128)(2,1)S(1)} copy(bf16[2,64,64,64]{3,2,1,0:T(8,128)(2,1)} %reshape.194) | data formatting | bytes 2097152 | tf_op jit(solution)/shard_map/reshape | solution.py:193
  64.1 3.8 %multiply_reduce_fusion.2 = (f32[2,64]{1,0:T(2,128)S(1)}, f32[2,64,64]{2,1,0:T(8,128)S(1)}) fusion(f32[2,64,64]{2,1,0:T(8,128)S(1)} %fusion.84, f32[2,64,64]{2,1,0:T(8,128)S(1)} %copy.44, pred[64,64]{1,0:T(8,128)(4,1)S(1)} %iota_compare_fusion, f32[2,64]{1,0:T(2,128)S(1)} %copy-done.27, bf16[2,64,64,64]{1,3,2,0:T(8,128)(2,1)S(1)} %copy.55, ...), kind=kOutput, calls=%fused_computation.10 | convolution fusion | flops 72343424 | bytes 2200576 | tf_op jit(solution)/shard_map/vmap(thp,shp->hts)/dot_general | solution.py:35
  67.9 2.3 %fusion.30 = (bf16[32,128,64]{1,2,0:T(8,128)(2,1)S(1)}, bf16[32,128,64]{1,2,0:T(8,128)(2,1)S(1)}, f32[1,32,128,64]{2,3,1,0:T(8,128)S(1)}, f32[1,32,128,64]{2,3,1,0:T(8,128)S(1)}, f32[1,32,128,64]{2,3,1,0:T(8,128)S(1)}) fusion(bf16[32,128,64]{1,2,0:T(8,128)(2,1)} %collective-permute-done.3, f32[32]{0:T(128)S(1)} %copy-done.25, f32[]{:T(128)S(6)} %sub.97, ...), kind=kLoop, calls=%fused_computation.67 | loop fusion | flops 7602176 | bytes 7865232 | tf_op jit(solution)/shard_map/convert_element_type | solution.py:120
  71.7 5.1 %collective-permute-start.10 = (bf16[32,128,64]{1,2,0:T(8,128)(2,1)S(1)}, bf16[32,128,64]{1,2,0:T(8,128)(2,1)S(1)}, u32[]{:S(2)}, u32[]{:S(2)}) collective-permute-start(bf16[32,128,64]{1,2,0:T(8,128)(2,1)S(1)} %get-tuple-element.21), channel_id=1, source_target_pairs={{0,8},{4,12},{8,0},{12,4},{16,24},{20,28},{24,16},{28,20},{1,9},{5... | collective-permute-start | bytes 1572872 | tf_op jit(solution)/shard_map/ppermute | solution.py:18
  80.0 6.1 %collective-permute-done.10 = bf16[32,128,64]{1,2,0:T(8,128)(2,1)S(1)} collective-permute-done((bf16[32,128,64]{1,2,0:T(8,128)(2,1)S(1)}, bf16[32,128,64]{1,2,0:T(8,128)(2,1)S(1)}, u32[]{:S(2)}, u32[]{:S(2)}) %collective-permute-start.10) | collective-permute-done | bytes 524320 | tf_op jit(solution)/shard_map/ppermute | solution.py:18
  95.4 1.7 %add_convert_fusion = bf16[2,64,128,64]{2,3,1,0:T(8,128)(2,1)S(1)} fusion(f32[64,128,64]{1,2,0:T(8,128)S(1)} %get-tuple-element.16, f32[2,64]{1,0:T(2,128)S(1)} %get-tuple-element.45, f32[64,128,64]{1,2,0:T(8,128)S(1)} %get-tuple-element.17, f32[2,64]{1,0:T(2,128)S(1)} %get-tuple-element.46, f32[64,128,64]{1,2,0:T(8,128)S(1)} %get-tuple-element.15, ...), kind=kLoop, calls=%fused_computation.13 | loop fusion | flops 10485760 | bytes 12585472 | tf_op jit(solution)/shard_map/convert_element_type | solution.py:215
  97.1 2.0 %fusion.3 = f32[2,64,128]{2,1,0:T(8,128)S(1)} fusion(bf16[2,64,64,64]{1,3,2,0:T(8,128)(2,1)S(1)} %copy-done.8, bf16[2,64,128,64]{2,3,1,0:T(8,128)(2,1)S(1)} %add_convert_fusion, f32[2,64,64]{1,2,0:T(8,128)S(1)} %copy.50), kind=kOutput, calls=%fused_computation.9 | convolution fusion | flops 136298496 | bytes 3244032 | tf_op jit(solution)/shard_map/chnp,cthp->cthn/dot_general | solution.py:35
  105.2 9.5 %collective-permute-start.17 = (f32[8,12,64]{2,0,1:T(8,128)S(1)}, f32[8,12,64]{2,0,1:T(8,128)S(1)}, u32[]{:S(2)}, u32[]{:S(2)}) collective-permute-start(f32[8,12,64]{2,0,1:T(8,128)S(1)} %fusion.73), channel_id=1, source_target_pairs={{0,8},{4,12},{8,0},{12,4},{16,24},{20,28},{24,16},{28,20},{1,9},{5... | collective-permute-start | bytes 73736 | tf_op jit(solution)/shard_map/ppermute | solution.py:18
  114.7 3.4 %fusion.2 = bf16[2,64,64,64]{1,3,2,0:T(8,128)(2,1)} fusion(bf16[2,64,64,64]{1,3,2,0:T(8,128)(2,1)S(1)} %copy-done.6, f32[2,64,64,64]{3,2,1,0:T(8,128)S(1)} %fusion.6, f32[64]{0:T(128)S(1)} %copy-done.31, f32[2,64]{1,0:T(2,128)S(1)} %copy-done.26, f32[2,64,64]{2,1,0:T(8,128)S(1)} %fusion.84, f32[2,64,64]{2,1,0:T(8,128)S(1)} %copy.44, ...), kind=kOutput, calls=%fused_computation.7 | convolution fusion | flops 72876032 | bytes 4264704 | tf_op jit(solution)/shard_map/vmap(hts,shp->thp)/dot_general | solution.py:35
  118.1 3.3 %copy.51 = bf16[2,64,64,64]{3,2,1,0:T(8,128)(2,1)S(1)} copy(bf16[2,64,64,64]{1,3,2,0:T(8,128)(2,1)} %fusion.2) | data formatting | bytes 2097152 | tf_op jit(solution)/shard_map/convert_element_type | solution.py:236
  121.5 2.5 %reshape.193 = bf16[128,4096]{1,0:T(8,128)(2,1)} reshape(bf16[2,64,64,64]{3,2,1,0:T(8,128)(2,1)S(1)} %copy.51) | data formatting | bytes 2097152 | tf_op jit(solution)/shard_map/reshape | solution.py:237
  124.0 9.9 %collective-permute-start.18 = (f32[8,12,64]{2,0,1:T(8,128)S(1)}, f32[8,12,64]{2,0,1:T(8,128)S(1)}, u32[]{:S(2)}, u32[]{:S(2)}) collective-permute-start(f32[8,12,64]{2,0,1:T(8,128)S(1)} %add.182), channel_id=1, source_target_pairs={{0,16},{4,20},{8,24},{12,28},{16,0},{20,4},{24,8},{28,12},{1,17},{... | collective-permute-start | bytes 73736 | tf_op jit(solution)/shard_map/ppermute | solution.py:18
  (158 shorter events, 38.8 us)
Async XLA Ops:
  2.4 11.6 %collective-permute-start.2 = (f32[64]{0:T(128)S(1)}, f32[64]{0:T(128)S(1)}, u32[]{:S(2)}, u32[]{:S(2)}) collective-permute-start(f32[64]{0:T(128)S(1)} %get-tuple-element.41), channel_id=1, source_target_pairs={{0,4},{4,0},{8,12},{12,8},{16,20},{20,16},{24,28},{28,24},{1,5},{5... | collective-permute-start | bytes 776 | tf_op jit(solution)/shard_map/ppermute | solution.py:18
  6.3 12.1 %collective-permute-start = (bf16[3,4352]{1,0:T(4,128)(2,1)S(1)}, bf16[3,4352]{1,0:T(4,128)(2,1)S(1)}, u32[]{:S(2)}, u32[]{:S(2)}) collective-permute-start(bf16[3,4352]{1,0:T(4,128)(2,1)S(1)} %slice.143), channel_id=1, source_target_pairs={{0,4},{4,8},{8,12},{12,16},{16,20},{20,24},{24,28},{1,5},{5,9},{9,... | collective-permute-start | bytes 78344 | tf_op jit(solution)/shard_map/ppermute | solution.py:12
  14.0 3.7 %collective-permute-start.4 = (f32[64]{0:T(128)S(1)}, f32[64]{0:T(128)S(1)}, u32[]{:S(2)}, u32[]{:S(2)}) collective-permute-start(f32[64]{0:T(128)S(1)} %add.153), channel_id=1, source_target_pairs={{0,8},{4,12},{8,0},{12,4},{16,24},{20,28},{24,16},{28,20},{1,9},{5... | collective-permute-start | bytes 776 | tf_op jit(solution)/shard_map/ppermute | solution.py:18
  30.4 16.1 %copy-start.2 = (f32[64,128,64]{1,2,0:T(8,128)}, f32[64,128,64]{1,2,0:T(8,128)S(1)}, u32[]{:S(2)}) copy-start(f32[64,128,64]{1,2,0:T(8,128)S(1)} %get-tuple-element.69) | copy-start | bytes 6291460
  30.6 15.9 %collective-permute-start.1 = (bf16[32,128,64]{1,2,0:T(8,128)(2,1)S(1)}, bf16[32,128,64]{1,2,0:T(8,128)(2,1)S(1)}, u32[]{:S(2)}, u32[]{:S(2)}) collective-permute-start(bf16[32,128,64]{1,2,0:T(8,128)(2,1)S(1)} %get-tuple-element.22), channel_id=1, source_target_pairs={{0,4},{4,0},{8,12},{12,8},{16,20},{20,16},{24,28},{28,24},{1,5},{5... | collective-permute-start | bytes 1572872 | tf_op jit(solution)/shard_map/ppermute | solution.py:18
  33.6 21.4 %collective-permute-start.9 = (bf16[32,128,64]{1,2,0:T(8,128)(2,1)S(1)}, bf16[32,128,64]{1,2,0:T(8,128)(2,1)S(1)}, u32[]{:S(2)}, u32[]{:S(2)}) collective-permute-start(bf16[32,128,64]{1,2,0:T(8,128)(2,1)S(1)} %get-tuple-element.23), channel_id=1, source_target_pairs={{0,4},{4,0},{8,12},{12,8},{16,20},{20,16},{24,28},{28,24},{1,5},{5... | collective-permute-start | bytes 1572872 | tf_op jit(solution)/shard_map/ppermute | solution.py:18
  36.1 19.0 %copy-start.11 = (bf16[128,4096]{1,0:T(8,128)(2,1)S(1)}, bf16[128,4096]{1,0:T(8,128)(2,1)}, u32[]{:S(2)}) copy-start(bf16[128,4096]{1,0:T(8,128)(2,1)} %param.17) | copy-start | bytes 3145732
  47.7 20.2 %collective-permute-start.3 = (bf16[32,128,64]{1,2,0:T(8,128)(2,1)}, bf16[32,128,64]{1,2,0:T(8,128)(2,1)}, u32[]{:S(2)}, u32[]{:S(2)}) collective-permute-start(bf16[32,128,64]{1,2,0:T(8,128)(2,1)} %fusion.75), channel_id=1, source_target_pairs={{0,8},{4,12},{8,0},{12,4},{16,24},{20,28},{24,16},{28,20},{1,9},{5... | collective-permute-start | bytes 1572872 | tf_op jit(solution)/shard_map/ppermute | solution.py:18
  70.3 8.2 %collective-permute-start.5 = (bf16[16,128,64]{1,2,0:T(8,128)(2,1)S(1)}, bf16[16,128,64]{1,2,0:T(8,128)(2,1)S(1)}, u32[]{:S(2)}, u32[]{:S(2)}) collective-permute-start(bf16[16,128,64]{1,2,0:T(8,128)(2,1)S(1)} %get-tuple-element.29), channel_id=1, source_target_pairs={{8,16},{12,20},{9,17},{13,21},{10,18},{14,22},{11,19},{15,23}} | collective-permute-start | bytes 786440 | tf_op jit(solution)/shard_map/ppermute | solution.py:105
  70.9 8.2 %collective-permute-start.7 = (bf16[16,128,64]{1,2,0:T(8,128)(2,1)S(1)}, bf16[16,128,64]{1,2,0:T(8,128)(2,1)S(1)}, u32[]{:S(2)}, u32[]{:S(2)}) collective-permute-start(bf16[16,128,64]{1,2,0:T(8,128)(2,1)S(1)} %get-tuple-element.30), channel_id=1, source_target_pairs={{8,16},{12,20},{9,17},{13,21},{10,18},{14,22},{11,19},{15,23}} | collective-permute-start | bytes 786440 | tf_op jit(solution)/shard_map/ppermute | solution.py:105
  71.7 14.5 %collective-permute-start.10 = (bf16[32,128,64]{1,2,0:T(8,128)(2,1)S(1)}, bf16[32,128,64]{1,2,0:T(8,128)(2,1)S(1)}, u32[]{:S(2)}, u32[]{:S(2)}) collective-permute-start(bf16[32,128,64]{1,2,0:T(8,128)(2,1)S(1)} %get-tuple-element.21), channel_id=1, source_target_pairs={{0,8},{4,12},{8,0},{12,4},{16,24},{20,28},{24,16},{28,20},{1,9},{5... | collective-permute-start | bytes 1572872 | tf_op jit(solution)/shard_map/ppermute | solution.py:18
  78.5 10.3 %collective-permute-start.6 = (bf16[16,128,64]{1,2,0:T(8,128)(2,1)S(1)}, bf16[16,128,64]{1,2,0:T(8,128)(2,1)S(1)}, u32[]{:S(2)}, u32[]{:S(2)}) collective-permute-start(bf16[16,128,64]{1,2,0:T(8,128)(2,1)S(1)} %collective-permute-done.5), channel_id=1, source_target_pairs={{16,24},{20,28},{17,25},{21,29},{18,26},{22,30},{19,27},{23,31}} | collective-permute-start | bytes 786440 | tf_op jit(solution)/shard_map/ppermute | solution.py:106
  79.2 10.3 %collective-permute-start.8 = (bf16[16,128,64]{1,2,0:T(8,128)(2,1)S(1)}, bf16[16,128,64]{1,2,0:T(8,128)(2,1)S(1)}, u32[]{:S(2)}, u32[]{:S(2)}) collective-permute-start(bf16[16,128,64]{1,2,0:T(8,128)(2,1)S(1)} %collective-permute-done.7), channel_id=1, source_target_pairs={{16,24},{20,28},{17,25},{21,29},{18,26},{22,30},{19,27},{23,31}} | collective-permute-start | bytes 786440 | tf_op jit(solution)/shard_map/ppermute | solution.py:106
  87.0 1.8 %collective-permute-start.11 = (bf16[16,128,64]{1,2,0:T(8,128)(2,1)S(1)}, bf16[16,128,64]{1,2,0:T(8,128)(2,1)S(1)}, u32[]{:S(2)}, u32[]{:S(2)}) collective-permute-start(bf16[16,128,64]{1,2,0:T(8,128)(2,1)S(1)} %get-tuple-element.33), channel_id=1, source_target_pairs={{8,16},{12,20},{9,17},{13,21},{10,18},{14,22},{11,19},{15,23}} | collective-permute-start | bytes 786440 | tf_op jit(solution)/shard_map/ppermute | solution.py:105
  88.0 1.6 %collective-permute-start.13 = (bf16[16,128,64]{1,2,0:T(8,128)(2,1)S(1)}, bf16[16,128,64]{1,2,0:T(8,128)(2,1)S(1)}, u32[]{:S(2)}, u32[]{:S(2)}) collective-permute-start(bf16[16,128,64]{1,2,0:T(8,128)(2,1)S(1)} %get-tuple-element.34), channel_id=1, source_target_pairs={{8,16},{12,20},{9,17},{13,21},{10,18},{14,22},{11,19},{15,23}} | collective-permute-start | bytes 786440 | tf_op jit(solution)/shard_map/ppermute | solution.py:105
  88.8 1.6 %collective-permute-start.12 = (bf16[16,128,64]{1,2,0:T(8,128)(2,1)S(1)}, bf16[16,128,64]{1,2,0:T(8,128)(2,1)S(1)}, u32[]{:S(2)}, u32[]{:S(2)}) collective-permute-start(bf16[16,128,64]{1,2,0:T(8,128)(2,1)S(1)} %collective-permute-done.11), channel_id=1, source_target_pairs={{16,24},{20,28},{17,25},{21,29},{18,26},{22,30},{19,27},{23,31}} | collective-permute-start | bytes 786440 | tf_op jit(solution)/shard_map/ppermute | solution.py:106
  89.6 0.9 collective-permute-start.14
  99.2 15.5 %copy-start.6 = (bf16[2,64,64,64]{1,3,2,0:T(8,128)(2,1)S(1)}, bf16[2,64,64,64]{1,3,2,0:T(8,128)(2,1)}, u32[]{:S(2)}) copy-start(bf16[2,64,64,64]{1,3,2,0:T(8,128)(2,1)} %copy-done.4) | copy-start | bytes 3145732
  99.2 15.5 %copy-start.26 = (f32[2,64]{1,0:T(2,128)S(1)}, f32[2,64]{1,0:T(2,128)}, u32[]{:S(2)}) copy-start(f32[2,64]{1,0:T(2,128)} %broadcast_multiply_fusion) | copy-start | bytes 1540
  99.2 15.5 %copy-start.31 = (f32[64]{0:T(128)S(1)}, f32[64]{0:T(128)}, u32[]{:S(2)}) copy-start(f32[64]{0:T(128)} %param.14) | copy-start | bytes 772
  101.1 4.2 %collective-permute-start.16 = (f32[8,12,64]{2,0,1:T(8,128)S(1)}, f32[8,12,64]{2,0,1:T(8,128)S(1)}, u32[]{:S(2)}, u32[]{:S(2)}) collective-permute-start(f32[8,12,64]{2,0,1:T(8,128)S(1)} %pad_maximum_fusion.2), channel_id=1, source_target_pairs={{0,4},{4,0},{8,12},{12,8},{16,20},{20,16},{24,28},{28,24},{1,5},{5... | collective-permute-start | bytes 73736 | tf_op jit(solution)/shard_map/ppermute | solution.py:18
  102.7 31.2 %collective-permute-start.15 = (f32[3,128]{1,0:T(4,128)S(1)}, f32[3,128]{1,0:T(4,128)S(1)}, u32[]{:S(2)}, u32[]{:S(2)}) collective-permute-start(f32[3,128]{1,0:T(4,128)S(1)} %slice.215), channel_id=1, source_target_pairs={{4,0},{8,4},{12,8},{16,12},{20,16},{24,20},{28,24},{5,1},{9,5},{13... | collective-permute-start | bytes 4616 | tf_op jit(solution)/shard_map/ppermute | solution.py:12
  105.2 18.8 %collective-permute-start.17 = (f32[8,12,64]{2,0,1:T(8,128)S(1)}, f32[8,12,64]{2,0,1:T(8,128)S(1)}, u32[]{:S(2)}, u32[]{:S(2)}) collective-permute-start(f32[8,12,64]{2,0,1:T(8,128)S(1)} %fusion.73), channel_id=1, source_target_pairs={{0,8},{4,12},{8,0},{12,4},{16,24},{20,28},{24,16},{28,20},{1,9},{5... | collective-permute-start | bytes 73736 | tf_op jit(solution)/shard_map/ppermute | solution.py:18
  124.0 12.0 %collective-permute-start.18 = (f32[8,12,64]{2,0,1:T(8,128)S(1)}, f32[8,12,64]{2,0,1:T(8,128)S(1)}, u32[]{:S(2)}, u32[]{:S(2)}) collective-permute-start(f32[8,12,64]{2,0,1:T(8,128)S(1)} %add.182), channel_id=1, source_target_pairs={{0,16},{4,20},{8,24},{12,28},{16,0},{20,4},{24,8},{28,12},{1,17},{... | collective-permute-start | bytes 73736 | tf_op jit(solution)/shard_map/ppermute | solution.py:18
  (30 other events, 185.6 us)
